TPU v7x, 256 devices: a whole 4x4x8 slice. The times are simulated.
256 devices in a mesh: pipe: 2 (over x_hi), ctx: 16 (over y, x_lo, core), dp: 8 (over z).
Axes of the slice: x: 4 (x_hi: 2, x_lo: 2; x = x_hi * 2 + x_lo), y: 4, z: 8, core: 2. Of those that a mesh axis runs over, the one named last changes fastest.
Arguments:
- patches: bfloat16 [1, 8, 2048, 1024], P(None, 'dp', 'ctx'), may hold values from -6 to 6
- lengths: int32 [1, 8], P(None, 'dp'), may hold values from 512 to 2048, as said below
- norm_gain: float32 [2, 1024], P('pipe'), may hold values from 0.1 to 1.9
- norm_bias: float32 [2, 1024], P('pipe'), may hold values from -3 to 3
- w_qkv: bfloat16 [2, 1024, 3072], P('pipe', None, 'dp')
- w_out: bfloat16 [2, 1024, 1024], P('pipe'), may hold values from -0.1875 to 0.1875
- out_bias: float32 [2, 1024], P('pipe'), may hold values from -3 to 3
- scale_gain: float32 [2, 1024], P('pipe'), may hold values from 0.3 to 1.5
Outputs:
- section_outputs: bfloat16 [2, 1, 8, 2048, 1024], P('pipe', None, 'dp', 'ctx')
Inputs may be any that keep to these rules, and one draw needn't show every extreme that they name: `lengths`: every volume has at least 512 real tokens, and in every draw some volume fills all 2048 slots.
All inputs are finite; a program needn't handle non-finite values.
Results may differ from a plain program's by a relative error of at most 0.017.
The roundings to bfloat16 on the way count: a program that leaves them out, or rounds other values in their place, can miss the bound.
Values may be sent and summed in bfloat16 or wider, within the bound.
No kernel may reach another device: no remote copies, remote signals or barrier semaphores. Data moves between devices by JAX's collectives and lax.ppermute only.
A program may use at most 128 MiB of HBM per device.

v0:
```python
import jax
import jax.numpy as jnp
from jax import lax
from jax.sharding import PartitionSpec as P

HEADS = 16


epsilon = 1e-06
masked_score = -1e30


def normalize(hidden, gain, shift):
    values = hidden.astype(jnp.float32)
    row_mean = jnp.mean(values, axis=-1, keepdims=True)
    centered = values - row_mean
    variance = jnp.mean(centered * centered, axis=-1, keepdims=True)
    return (centered * lax.rsqrt(variance + epsilon) * gain + shift).astype(jnp.bfloat16)


def head_attention(qkv, length, score_scale):
    queries, key_rows, value_rows = qkv[0], qkv[1], qkv[2]
    count = qkv.shape[-1]
    scores = (
        jnp.einsum("dq,dk->qk", queries, key_rows, preferred_element_type=jnp.float32)
        * score_scale
    )
    valid = jnp.arange(count, dtype=jnp.int32) < length
    top = jnp.max(jnp.where(valid[None, :], scores, masked_score), axis=-1)
    weights = jnp.where(valid[None, :], jnp.exp(scores - top[:, None]), 0.0)
    totals = jnp.sum(weights, axis=-1)
    context = jnp.einsum(
        "qk,dk->dq", weights.astype(jnp.bfloat16), value_rows, preferred_element_type=jnp.float32
    )
    return (context / totals[None, :]).astype(jnp.bfloat16)


def sublayer(current, length, qkv_mine, qkv_other, out_full, gain, shift, out_shift, layer_scale):
    tok_rows, width = current.shape
    head_width = width // HEADS
    ctx_count = lax.axis_size("ctx")
    core = lax.axis_index("ctx") % 2
    half = width // 2
    normed = normalize(current, gain, shift)
    normed_mine = lax.dynamic_slice_in_dim(normed, core * half, half, axis=1)
    normed_other = lax.dynamic_slice_in_dim(normed, (1 - core) * half, half, axis=1)
    projected = jnp.einsum(
        "tk,kphf->hpft", normed_mine, qkv_mine.reshape(half, 3, HEADS, head_width),
        preferred_element_type=jnp.float32,
    ) + jnp.einsum(
        "tk,kphf->hpft", normed_other, qkv_other.reshape(half, 3, HEADS, head_width),
        preferred_element_type=jnp.float32,
    )
    projected = projected.astype(jnp.bfloat16)
    gathered = lax.all_to_all(projected, "ctx", 0, 3, tiled=True)
    context = head_attention(gathered[0], length, head_width ** (-0.5))
    context = jnp.transpose(context.reshape(head_width, ctx_count, tok_rows), (1, 0, 2))
    spread = lax.all_to_all(context, "ctx", 0, 0, tiled=True).reshape(width, tok_rows)
    mixed = jnp.einsum("ft,fo->to", spread, out_full, preferred_element_type=jnp.float32)
    mixed = mixed + out_shift
    return (current.astype(jnp.float32) + layer_scale * mixed).astype(jnp.bfloat16)


def per_device(patches, lengths, norm_gain, norm_bias, w_qkv, w_out, out_bias, scale_gain):
    section_index = lax.axis_index("pipe")
    section_count = lax.axis_size("pipe")
    core = lax.axis_index("ctx") % 2
    width = w_qkv.shape[1]
    half = width // 2
    rows_mine = lax.dynamic_slice_in_dim(w_qkv[0], core * half, half, axis=0)
    qkv_mine = lax.all_gather(rows_mine, "dp", axis=1, tiled=True)
    sibling = [(i, i ^ 1) for i in range(lax.axis_size("ctx"))]
    qkv_other = lax.ppermute(qkv_mine, "ctx", sibling)
    args = (qkv_mine, qkv_other, w_out[0], norm_gain[0], norm_bias[0], out_bias[0], scale_gain[0])
    length = lengths[0, 0]
    current = patches[0, 0]
    outputs = []
    for turn_index in range(section_count):
        produced = sublayer(current, length, *args)
        outputs.append(produced)
        if turn_index + 1 < section_count:
            pairs = [(i, i + 1) for i in range(section_count - 1)]
            current = lax.ppermute(produced, "pipe", pairs)
    result = outputs[0]
    for turn_index in range(1, section_count):
        result = jnp.where(section_index == turn_index, outputs[turn_index], result)
    return result[None, None, None]


def solution(mesh):
    in_specs = (
        P(None, "dp", "ctx", None),
        P(None, "dp"),
        P("pipe", None),
        P("pipe", None),
        P("pipe", None, "dp"),
        P("pipe", None, None),
        P("pipe", None),
        P("pipe", None),
    )
    out_specs = P("pipe", None, "dp", "ctx", None)
    return jax.shard_map(
        per_device, mesh=mesh, in_specs=in_specs, out_specs=out_specs, check_vma=False
    )
```

profile of v0, /device:TPU:4, one launch (start us, length us, event | category | flops | bytes accessed | tf_op | source)
XLA Modules:
  0.0 182.9 jit_solution(12311057242982659959)
XLA Ops:
  6.5 0.0 copy-start
  6.5 0.0 all-gather.3.cloned.1.call-start
  6.5 1.9 %constant_dynamic-slice_fusion = bf16[1,512,384]{2,1,0:T(8,128)(2,1)} fusion(bf16[1,1024,384]{2,1,0:T(8,128)(2,1)} %param.12, s32[]{:T(128)S(6)} %select_n.43), kind=kLoop, calls=%fused_computation.84 | loop fusion | bytes 786436 | tf_op jit(solution)/shard_map/dynamic_slice | solution.py:70
  8.5 0.0 all-gather.3.cloned.1.call-update
  8.5 49.5 %all-gather.3.cloned.1.call-done = bf16[1,512,3072]{2,1,0:T(8,128)(2,1)} async-done(((bf16[1,512,384]{2,1,0:T(8,128)(2,1)}), bf16[1,512,3072]{2,1,0:T(8,128)(2,1)}) %all-gather.3.cloned.1.call-update) | async-done | bytes 3145744 | tf_op jit(solution)/shard_map/all_gather | solution.py:71
  58.0 0.0 collective-permute-start
  58.0 1.1 convert_reduce_fusion.1
  59.1 1.2 fusion.73
  60.2 1.2 fusion.76
  61.5 4.7 %copy.21 = bf16[1,512,3072]{1,2,0:T(8,128)(2,1)} copy(bf16[1,512,3072]{2,1,0:T(8,128)(2,1)} %all-gather.3.cloned.1.call-done) | data formatting | bytes 6291456 | tf_op jit(solution)/shard_map/all_gather | solution.py:71
  66.1 4.0 %fusion.95 = f32[3,16,64,128]{3,2,1,0:T(8,128)} fusion(bf16[512,3,16,64]{0,3,2,1:T(8,128)(2,1)} %bitcast.146, bf16[128,1024]{1,0:T(8,128)(2,1)S(1)} %fusion.76, s32[]{:T(128)S(6)} %select_n.43), kind=kOutput, calls=%fused_computation.73 | convolution fusion | flops 402653184 | bytes 4849668 | tf_op jit(solution)/shard_map/tk,kphf->hpft/dot_general | solution.py:47
  70.2 0.0 collective-permute-done
  70.2 4.7 %copy.22 = bf16[512,3072]{0,1:T(8,128)(2,1)} copy(bf16[512,3072]{1,0:T(8,128)(2,1)} %collective-permute-done) | data formatting | bytes 6291456 | tf_op jit(solution)/shard_map/ppermute | solution.py:73
  74.9 3.3 %fusion.26 = bf16[16,3,64,128]{3,2,0,1:T(8,128)(2,1)S(1)} fusion(f32[3,16,64,128]{3,2,1,0:T(8,128)} %fusion.95, bf16[512,3,16,64]{0,3,2,1:T(8,128)(2,1)} %bitcast.148, bf16[128,1024]{1,0:T(8,128)(2,1)S(1)} %fusion.76, s32[]{:T(128)S(6)} %select_n.44), kind=kOutput, calls=%fused_computation.22 | convolution fusion | flops 403439616 | bytes 5636100 | tf_op jit(solution)/shard_map/tk,kphf->hpft/dot_general | solution.py:50
  78.2 0.9 copy.23
  79.1 5.1 %all-to-all-start = ((bf16[16,3,64,128]{3,2,1,0:T(8,128)(2,1)}), bf16[16,3,64,128]{3,2,1,0:T(8,128)(2,1)S(1)}, u32[]{:S(2)}, u32[]{:S(2)}) async-start(bf16[16,3,64,128]{3,2,1,0:T(8,128)(2,1)} %copy.23), calls=%async_computation | async-start | bytes 1572864 | tf_op jit(solution)/shard_map/all_to_all | solution.py:55
  84.9 13.1 %all-to-all-done = bf16[16,3,64,128]{3,2,1,0:T(8,128)(2,1)S(1)} async-done(((bf16[16,3,64,128]{3,2,1,0:T(8,128)(2,1)}), bf16[16,3,64,128]{3,2,1,0:T(8,128)(2,1)S(1)}, u32[]{:S(2)}, u32[]{:S(2)}) %all-to-all-start) | async-done | bytes 786464 | tf_op jit(solution)/shard_map/all_to_all | solution.py:55
  98.0 0.1 fusion.110
  98.1 0.2 copy.24
  98.2 0.2 copy.26
  98.4 0.2 copy.25
  98.6 2.8 %select_reduce_fusion.1 = (f32[2048]{0:T(1024)S(1)}, f32[2048,2048]{0,1:T(8,128)S(1)}) fusion(pred[2048]{0:T(1024)(128)(4,1)S(1)} %iota_compare_fusion, bf16[8,8,16,128]{3,2,1,0:T(8,128)(2,1)S(1)} %bitcast.153, bf16[8,8,16,128]{3,2,1,0:T(8,128)(2,1)S(1)} %bitcast.155), kind=kOutput, calls=%fused_computation.3 | convolution fusion | flops 549451776 | bytes 17311744 | tf_op jit(solution)/shard_map/dq,dk->qk/dot_general | solution.py:25
  101.4 0.0 copy-start.3
  101.4 0.0 copy-start.6
  101.4 0.0 copy-start.7
  101.4 4.8 %fusion = f32[2048]{0:T(1024)S(1)} fusion(f32[2048,2048]{0,1:T(8,128)S(1)} %get-tuple-element.12, f32[2048]{0:T(1024)S(1)} %get-tuple-element.11, pred[2048]{0:T(1024)(128)(4,1)S(1)} %iota_compare_fusion), kind=kLoop, calls=%fused_computation.4 | loop fusion | flops 16775168 | bytes 16795648 | tf_op jit(solution)/shard_map/reduce_sum | solution.py:31
  106.3 0.0 copy-start.4
  106.3 0.0 copy-start.5
  106.3 0.0 copy-start.1
  106.3 0.0 copy-start.2
  106.3 3.1 %fusion.61 = bf16[8,16,8,128]{3,2,1,0:T(8,128)(2,1)S(1)} fusion(f32[2048,2048]{0,1:T(8,128)S(1)} %get-tuple-element.12, f32[2048]{0:T(1024)S(1)} %get-tuple-element.11, pred[2048]{0:T(1024)(128)(4,1)S(1)} %iota_compare_fusion, bf16[8,8,16,128]{3,2,1,0:T(8,128)(2,1)S(1)} %bitcast.161, f32[2048]{0:T(1024)S(1)} %fusion), kind=kOutput, calls=%fused_computation.35 | convolution fusion | flops 553910272 | bytes 17319936 | tf_op jit(solution)/shard_map/qk,dk->dq/dot_general | solution.py:32
  109.4 0.1 copy.80
  109.5 10.6 %all_to_all.40 = bf16[16,64,128]{2,1,0:T(8,128)(2,1)S(1)} all-to-all(bf16[16,64,128]{2,1,0:T(8,128)(2,1)S(1)} %bitcast.157), channel_id=1, replica_groups=mesh['pipe'=2,'ctx'=16,'dp'=8] {'ctx'}, dimensions={0} | all-to-all | bytes 524288 | tf_op jit(solution)/shard_map/all_to_all | solution.py:58
  120.1 0.0 copy-done
  120.1 0.0 copy-done.3
  120.1 0.0 copy-done.6
  120.1 0.0 copy-done.7
  120.2 0.5 fusion.49
  120.6 1.3 collective-permute-start.1
  121.9 9.9 %collective-permute-done.1 = bf16[128,1024]{1,0:T(8,128)(2,1)S(1)} collective-permute-done((bf16[128,1024]{1,0:T(8,128)(2,1)S(1)}, bf16[128,1024]{1,0:T(8,128)(2,1)S(1)}, u32[]{:S(2)}, u32[]{:S(2)}) %collective-permute-start.1) | collective-permute-done | bytes 262176 | tf_op jit(solution)/shard_map/ppermute | solution.py:83
  131.8 0.1 convert_reduce_fusion
  131.9 0.2 fusion.69
  132.2 0.0 copy-done.4
  132.2 0.0 copy-done.5
  132.2 0.2 fusion.72
  132.4 0.0 copy-done.1
  132.4 1.0 fusion.92
  133.4 0.0 copy-done.2
  133.5 1.1 fusion.27
  134.5 0.1 copy.28
  134.6 16.5 %all_to_all.41 = bf16[16,3,64,128]{3,2,1,0:T(8,128)(2,1)S(1)} all-to-all(bf16[16,3,64,128]{3,2,1,0:T(8,128)(2,1)S(1)} %copy.28), channel_id=1, replica_groups=mesh['pipe'=2,'ctx'=16,'dp'=8] {'ctx'}, dimensions={0} | all-to-all | bytes 1572864 | tf_op jit(solution)/shard_map/all_to_all | solution.py:55
  151.1 0.1 fusion.109
  151.2 0.2 copy.29
  151.4 0.2 copy.31
  151.6 0.2 copy.30
  151.7 2.8 %select_reduce_fusion = (f32[2048]{0:T(1024)S(1)}, f32[2048,2048]{0,1:T(8,128)S(1)}) fusion(pred[2048]{0:T(1024)(128)(4,1)S(1)} %iota_compare_fusion, bf16[8,8,16,128]{3,2,1,0:T(8,128)(2,1)S(1)} %bitcast.154, bf16[8,8,16,128]{3,2,1,0:T(8,128)(2,1)S(1)} %bitcast.156), kind=kOutput, calls=%fused_computation.1 | convolution fusion | flops 549451776 | bytes 17311744 | tf_op jit(solution)/shard_map/dq,dk->qk/dot_general | solution.py:25
  154.5 4.8 %fusion.2 = f32[2048]{0:T(1024)S(1)} fusion(f32[2048,2048]{0,1:T(8,128)S(1)} %get-tuple-element.14, f32[2048]{0:T(1024)S(1)} %get-tuple-element.13, pred[2048]{0:T(1024)(128)(4,1)S(1)} %iota_compare_fusion), kind=kLoop, calls=%fused_computation.6 | loop fusion | flops 16775168 | bytes 16795648 | tf_op jit(solution)/shard_map/reduce_sum | solution.py:31
  159.4 3.1 %fusion.58 = bf16[8,16,8,128]{3,2,1,0:T(8,128)(2,1)S(1)} fusion(f32[2048,2048]{0,1:T(8,128)S(1)} %get-tuple-element.14, f32[2048]{0:T(1024)S(1)} %get-tuple-element.13, pred[2048]{0:T(1024)(128)(4,1)S(1)} %iota_compare_fusion, bf16[8,8,16,128]{3,2,1,0:T(8,128)(2,1)S(1)} %bitcast.160, f32[2048]{0:T(1024)S(1)} %fusion.2), kind=kOutput, calls=%fused_computation.34 | convolution fusion | flops 553910272 | bytes 17319936 | tf_op jit(solution)/shard_map/qk,dk->dq/dot_general | solution.py:32
  162.5 0.8 copy.79
  163.3 3.5 %all-to-all-start.3 = ((bf16[16,64,128]{2,1,0:T(8,128)(2,1)}), bf16[16,64,128]{2,1,0:T(8,128)(2,1)S(1)}, u32[]{:S(2)}, u32[]{:S(2)}) async-start(bf16[16,64,128]{2,1,0:T(8,128)(2,1)} %bitcast.142), calls=%async_computation.3 | async-start | bytes 524288 | tf_op jit(solution)/shard_map/all_to_all | solution.py:58
  166.8 8.0 %all-to-all-done.3 = bf16[16,64,128]{2,1,0:T(8,128)(2,1)S(1)} async-done(((bf16[16,64,128]{2,1,0:T(8,128)(2,1)}), bf16[16,64,128]{2,1,0:T(8,128)(2,1)S(1)}, u32[]{:S(2)}, u32[]{:S(2)}) %all-to-all-start.3) | async-done | bytes 262176 | tf_op jit(solution)/shard_map/all_to_all | solution.py:58
  174.8 1.2 fusion.55
  (5 shorter events, 0.0 us)
Async XLA Ops:
  6.5 113.6 %copy-start = (bf16[1,1024,1024]{2,1,0:T(8,128)(2,1)S(1)}, bf16[1,1024,1024]{2,1,0:T(8,128)(2,1)}, u32[]{:S(2)}) copy-start(bf16[1,1024,1024]{2,1,0:T(8,128)(2,1)} %param.13) | copy-start | bytes 6291460
  6.5 51.5 %all-gather.3.cloned.1.call-start = ((), (), s32[]{:S(2)}) async-start(), calls=%async_computation.4 | async-start | bytes 3538944 | tf_op jit(solution)/shard_map/all_gather | solution.py:71
  58.0 12.2 %collective-permute-start = (bf16[512,3072]{1,0:T(8,128)(2,1)}, bf16[512,3072]{1,0:T(8,128)(2,1)}, u32[]{:S(2)}, u32[]{:S(2)}) collective-permute-start(bf16[512,3072]{1,0:T(8,128)(2,1)} %bitcast.150), channel_id=1, source_target_pairs={{0,8},{8,0},{16,24},{24,16},{32,40},{40,32},{48,56},{56,48},{64,72... | collective-permute-start | bytes 9437192 | tf_op jit(solution)/shard_map/ppermute | solution.py:73
  79.1 18.8 %all-to-all-start = ((bf16[16,3,64,128]{3,2,1,0:T(8,128)(2,1)}), bf16[16,3,64,128]{3,2,1,0:T(8,128)(2,1)S(1)}, u32[]{:S(2)}, u32[]{:S(2)}) async-start(bf16[16,3,64,128]{3,2,1,0:T(8,128)(2,1)} %copy.23), calls=%async_computation | async-start | bytes 1572864 | tf_op jit(solution)/shard_map/all_to_all | solution.py:55
  101.4 18.7 %copy-start.3 = (bf16[1,1,128,1024]{3,2,1,0:T(8,128)(2,1)S(1)}, bf16[1,1,128,1024]{3,2,1,0:T(8,128)(2,1)}, u32[]{:S(2)}) copy-start(bf16[1,1,128,1024]{3,2,1,0:T(8,128)(2,1)} %param.8) | copy-start | bytes 786436
  101.4 18.7 %copy-start.6 = (f32[1,1024]{1,0:T(1,128)S(1)}, f32[1,1024]{1,0:T(1,128)}, u32[]{:S(2)}) copy-start(f32[1,1024]{1,0:T(1,128)} %param.14) | copy-start | bytes 12292
  101.4 18.7 %copy-start.7 = (f32[1,1024]{1,0:T(1,128)S(1)}, f32[1,1024]{1,0:T(1,128)}, u32[]{:S(2)}) copy-start(f32[1,1024]{1,0:T(1,128)} %param.15) | copy-start | bytes 12292
  106.3 25.9 %copy-start.4 = (f32[1,1024]{1,0:T(1,128)S(1)}, f32[1,1024]{1,0:T(1,128)}, u32[]{:S(2)}) copy-start(f32[1,1024]{1,0:T(1,128)} %param.11) | copy-start | bytes 12292
  106.3 25.9 %copy-start.5 = (f32[1,1024]{1,0:T(1,128)S(1)}, f32[1,1024]{1,0:T(1,128)}, u32[]{:S(2)}) copy-start(f32[1,1024]{1,0:T(1,128)} %param.10) | copy-start | bytes 12292
  106.3 26.1 %copy-start.1 = (bf16[1,512,3072]{1,2,0:T(8,128)(2,1)S(1)}, bf16[1,512,3072]{1,2,0:T(8,128)(2,1)}, u32[]{:S(2)}) copy-start(bf16[1,512,3072]{1,2,0:T(8,128)(2,1)} %copy.21) | copy-start | bytes 9437188
  106.3 27.1 %copy-start.2 = (bf16[512,3072]{0,1:T(8,128)(2,1)S(1)}, bf16[512,3072]{0,1:T(8,128)(2,1)}, u32[]{:S(2)}) copy-start(bf16[512,3072]{0,1:T(8,128)(2,1)} %copy.22) | copy-start | bytes 9437188
  120.6 11.2 %collective-permute-start.1 = (bf16[128,1024]{1,0:T(8,128)(2,1)S(1)}, bf16[128,1024]{1,0:T(8,128)(2,1)S(1)}, u32[]{:S(2)}, u32[]{:S(2)}) collective-permute-start(bf16[128,1024]{1,0:T(8,128)(2,1)S(1)} %fusion.49), channel_id=1, source_target_pairs={{0,128},{1,129},{2,130},{3,131},{4,132},{5,133},{6,134},{7,135},{8... | collective-permute-start | bytes 786440 | tf_op jit(solution)/shard_map/ppermute | solution.py:83
  163.3 11.5 %all-to-all-start.3 = ((bf16[16,64,128]{2,1,0:T(8,128)(2,1)}), bf16[16,64,128]{2,1,0:T(8,128)(2,1)S(1)}, u32[]{:S(2)}, u32[]{:S(2)}) async-start(bf16[16,64,128]{2,1,0:T(8,128)(2,1)} %bitcast.142), calls=%async_computation.3 | async-start | bytes 524288 | tf_op jit(solution)/shard_map/all_to_all | solution.py:58
Sparse Core Ops, SparseCore 0:
  9.1 48.8 all-gather.2
where the time goes:
time: 184 us; the launch traced here: 183 us
  waiting for transfers between devices  80.4 us (44%)
  blocking collectives  27.2 us (15%)
  matrix products  23 us (12%)
  local copies, waits for them, and re-layouts  14.3 us (8%)
  between operations  14.3 us (8%)
  other arithmetic  13.7 us (7%)
  starting transfers between devices  9.95 us (5%)
    all_gather x1, waiting for transfers between devices, per_device(): qkv_mine = lax.all_gather(rows_mine, 'dp', axis=1, tiled=True)  49.5 us
    all_to_all x1, blocking collectives, sublayer(): gathered = lax.all_to_all(projected, 'ctx', 0, 3, tiled=True)  16.5 us
    all_to_all x1, waiting for transfers between devices, sublayer(): gathered = lax.all_to_all(projected, 'ctx', 0, 3, tiled=True)  13.1 us
    all_to_all x1, blocking collectives, sublayer(): lax.all_to_all(context, 'ctx', 0, 0, tiled=True).reshape(width, tok_rows)  10.6 us
    ppermute x1, waiting for transfers between devices, per_device(): current = lax.ppermute(produced, 'pipe', pairs)  9.87 us
    reduce_sum x2, other arithmetic, head_attention(): totals = jnp.sum(weights, axis=-1)  9.64 us
    all_to_all x1, waiting for transfers between devices, sublayer(): lax.all_to_all(context, 'ctx', 0, 0, tiled=True).reshape(width, tok_rows)  7.98 us
    dot_general x2, matrix products, head_attention(): jnp.einsum('qk,dk->dq', weights.astype(jnp.bfloat16), value_rows, preferr...  6.26 us
  transfers between devices with their start and end apart: 5, of which 4 were waited for; matrix products, arithmetic and copies ran while one was open for 7% of the time, Pallas kernels for 0%

commit v1 on v0

--- a/solution.py
+++ b/solution.py
@@ -35,25 +35,51 @@
     return (context / totals[None, :]).astype(jnp.bfloat16)
 
 
-def sublayer(current, length, qkv_mine, qkv_other, out_full, gain, shift, out_shift, layer_scale):
+def chunk_tables(width, dp_count, chunks, head_width):
+    shard_width = 3 * width // dp_count
+    chunk_width = shard_width // chunks
+    per_segment = chunk_width // head_width
+    orders, parts = [], []
+    for j in range(chunks):
+        by_head = {}
+        for d in range(dp_count):
+            for i in range(per_segment):
+                column = d * shard_width + j * chunk_width + i * head_width
+                part, head = column // width, (column % width) // head_width
+                assert head not in by_head
+                by_head[head] = (d * per_segment + i, part)
+        assert sorted(by_head) == list(range(HEADS))
+        orders.append([by_head[h][0] for h in range(HEADS)])
+        parts.append([by_head[h][1] for h in range(HEADS)])
+    chunk_of_part = [[parts_h.index(p) for p in range(3)] for parts_h in zip(*parts)]
+    return orders, chunk_of_part
+
+
+def sublayer(current, length, weights_mine, weights_other, orders, chunk_of_part, out_full,
+             gain, shift, out_shift, layer_scale):
     tok_rows, width = current.shape
     head_width = width // HEADS
     ctx_count = lax.axis_size("ctx")
-    core = lax.axis_index("ctx") % 2
+    assert ctx_count == HEADS
+    head = lax.axis_index("ctx")
+    core = head % 2
     half = width // 2
     normed = normalize(current, gain, shift)
     normed_mine = lax.dynamic_slice_in_dim(normed, core * half, half, axis=1)
     normed_other = lax.dynamic_slice_in_dim(normed, (1 - core) * half, half, axis=1)
-    projected = jnp.einsum(
-        "tk,kphf->hpft", normed_mine, qkv_mine.reshape(half, 3, HEADS, head_width),
-        preferred_element_type=jnp.float32,
-    ) + jnp.einsum(
-        "tk,kphf->hpft", normed_other, qkv_other.reshape(half, 3, HEADS, head_width),
-        preferred_element_type=jnp.float32,
-    )
-    projected = projected.astype(jnp.bfloat16)
-    gathered = lax.all_to_all(projected, "ctx", 0, 3, tiled=True)
-    context = head_attention(gathered[0], length, head_width ** (-0.5))
+    received = []
+    for mine, other, order in zip(weights_mine, weights_other, orders):
+        projected = jnp.dot(normed_mine, mine, preferred_element_type=jnp.float32) + jnp.dot(
+            normed_other, other, preferred_element_type=jnp.float32
+        )
+        projected = projected.astype(jnp.bfloat16).reshape(tok_rows, -1, head_width)
+        projected = jnp.transpose(projected, (1, 2, 0))
+        by_head = jnp.concatenate([projected[k : k + 1] for k in order], axis=0)
+        received.append(lax.all_to_all(by_head, "ctx", 0, 2, tiled=True)[0])
+    received = jnp.stack(received)
+    pick = jnp.asarray(chunk_of_part, jnp.int32)[head]
+    qkv = jnp.take(received, pick, axis=0)
+    context = head_attention(qkv, length, head_width ** (-0.5))
     context = jnp.transpose(context.reshape(head_width, ctx_count, tok_rows), (1, 0, 2))
     spread = lax.all_to_all(context, "ctx", 0, 0, tiled=True).reshape(width, tok_rows)
     mixed = jnp.einsum("ft,fo->to", spread, out_full, preferred_element_type=jnp.float32)
@@ -64,14 +90,24 @@
 def per_device(patches, lengths, norm_gain, norm_bias, w_qkv, w_out, out_bias, scale_gain):
     section_index = lax.axis_index("pipe")
     section_count = lax.axis_size("pipe")
+    dp_count = lax.axis_size("dp")
     core = lax.axis_index("ctx") % 2
     width = w_qkv.shape[1]
     half = width // 2
+    head_width = width // HEADS
+    chunks = 3
+    orders, chunk_of_part = chunk_tables(width, dp_count, chunks, head_width)
     rows_mine = lax.dynamic_slice_in_dim(w_qkv[0], core * half, half, axis=0)
-    qkv_mine = lax.all_gather(rows_mine, "dp", axis=1, tiled=True)
+    chunk_width = rows_mine.shape[1] // chunks
     sibling = [(i, i ^ 1) for i in range(lax.axis_size("ctx"))]
-    qkv_other = lax.ppermute(qkv_mine, "ctx", sibling)
-    args = (qkv_mine, qkv_other, w_out[0], norm_gain[0], norm_bias[0], out_bias[0], scale_gain[0])
+    weights_mine, weights_other = [], []
+    for j in range(chunks):
+        piece = rows_mine[:, j * chunk_width : (j + 1) * chunk_width]
+        gathered = lax.all_gather(piece, "dp", axis=1, tiled=True)
+        weights_mine.append(gathered)
+        weights_other.append(lax.ppermute(gathered, "ctx", sibling))
+    args = (weights_mine, weights_other, orders, chunk_of_part, w_out[0], norm_gain[0],
+            norm_bias[0], out_bias[0], scale_gain[0])
     length = lengths[0, 0]
     current = patches[0, 0]
     outputs = []

time: 184 us -> 352 us (1.91)
  waiting for transfers between devices: 80.4 us -> 165 us
  local copies, waits for them, and re-layouts: 14.3 us -> 72.7 us
  starting transfers between devices: 9.95 us -> 33 us
  blocking collectives: 27.2 us -> 10.6 us
  matrix products: 23 us -> 33.8 us
  other arithmetic: 13.7 us -> 19.1 us
    all_gather x1 -> x3, waiting for transfers between devices: 49.5 us -> 117 us  [per_device(): gathered = lax.all_gather(piece, 'dp', axis=1, tiled=True)]
    unnamed x16 -> x68, local copies, waits for them, and re-layouts: 0.04 us -> 47.1 us
    all_to_all x1 -> x6, starting transfers between devices: 5.12 us -> 28.1 us  [sublayer(): received.append(lax.all_to_all(by_head, 'ctx', 0, 2, tiled=True)[0])]
    all_to_all x1 -> x0, blocking collectives: 16.5 us -> none  [sublayer(): gathered = lax.all_to_all(projected, 'ctx', 0, 3, tiled=True)]
    all_to_all x1 -> x6, waiting for transfers between devices: 13.1 us -> 29.1 us  [sublayer(): received.append(lax.all_to_all(by_head, 'ctx', 0, 2, tiled=True)[0])]
    dot_general x4 -> x12, matrix products: 9.42 us -> 20.2 us  [the longest x6 11.9 us: sublayer(): jnp.dot(normed_other, other, preferred_element_type=jnp.float32)]
    convert_element_type x2 -> x6, local copies, waits for them, and re-layouts: 0.99 us -> 8.49 us  [sublayer(): projected = projected.astype(jnp.bfloat16).reshape(tok_rows, -1, head_width)]
    concatenate x0 -> x6, local copies, waits for them, and re-layouts: none -> 6.73 us  [sublayer(): by_head = jnp.concatenate([projected[k:k + 1] for k in order], axis=0)]
  transfers between devices with their start and end apart: 5 -> 14, of which waited for: 4 -> 9; matrix products, arithmetic and copies ran while one was open for 7% -> 21% of each run, Pallas kernels for 0% -> 0%
where the time goes in v1:
time: 352 us; the launch traced here: 348 us
  waiting for transfers between devices  165 us (47%)
  local copies, waits for them, and re-layouts  72.7 us (21%)
  matrix products  33.8 us (10%)
  starting transfers between devices  33 us (9%)
  other arithmetic  19.1 us (5%)
  between operations  14.2 us (4%)
  blocking collectives  10.6 us (3%)
    all_gather x3, waiting for transfers between devices, per_device(): gathered = lax.all_gather(piece, 'dp', axis=1, tiled=True)  117 us
    unnamed x68, local copies, waits for them, and re-layouts  47.1 us
    all_to_all x6, waiting for transfers between devices, sublayer(): received.append(lax.all_to_all(by_head, 'ctx', 0, 2, tiled=True)[0])  29.1 us
    all_to_all x6, starting transfers between devices, sublayer(): received.append(lax.all_to_all(by_head, 'ctx', 0, 2, tiled=True)[0])  28.1 us
    dot_general x6, matrix products, sublayer(): jnp.dot(normed_other, other, preferred_element_type=jnp.float32)  11.9 us
    all_to_all x1, blocking collectives, sublayer(): lax.all_to_all(context, 'ctx', 0, 0, tiled=True).reshape(width, tok_rows)  10.6 us
    ppermute x1, waiting for transfers between devices, per_device(): current = lax.ppermute(produced, 'pipe', pairs)  9.87 us
    reduce_sum x2, other arithmetic, head_attention(): totals = jnp.sum(weights, axis=-1)  9.64 us
  transfers between devices with their start and end apart: 14, of which 9 were waited for; matrix products, arithmetic and copies ran while one was open for 21% of the time, Pallas kernels for 0%

profile of v1, /device:TPU:4, one launch (start us, length us, event | category | flops | bytes accessed | tf_op | source)
XLA Modules:
  0.0 348.5 jit_solution(4596958076334259962)
XLA Ops:
  13.6 37.7 %all-gather.6.cloned.1.call-done = bf16[512,1024]{1,0:T(8,128)(2,1)} async-done(((bf16[512,128]{1,0:T(8,128)(2,1)}), bf16[512,1024]{1,0:T(8,128)(2,1)}) %all-gather.6.cloned.1.call-update) | async-done | bytes 1048592 | tf_op jit(solution)/shard_map/all_gather | solution.py:106
  52.5 38.9 %all-gather.8.cloned.1.call-done = bf16[512,1024]{1,0:T(8,128)(2,1)} async-done(((bf16[512,128]{1,0:T(8,128)(2,1)}), bf16[512,1024]{1,0:T(8,128)(2,1)}) %all-gather.8.cloned.1.call-update) | async-done | bytes 1048592 | tf_op jit(solution)/shard_map/all_gather | solution.py:106
  91.4 40.1 %all-gather.4.cloned.1.call-done = bf16[512,1024]{1,0:T(8,128)(2,1)} async-done(((bf16[512,128]{1,0:T(8,128)(2,1)}), bf16[512,1024]{1,0:T(8,128)(2,1)}) %all-gather.4.cloned.1.call-update) | async-done | bytes 1048592 | tf_op jit(solution)/shard_map/all_gather | solution.py:106
  131.5 1.5 fusion.97
  133.0 2.3 fusion.95
  135.4 2.3 fusion.99
  138.8 1.8 copy.13
  141.9 1.4 constant_dynamic-update-slice_fusion.14
  143.3 1.4 constant_dynamic-update-slice_fusion.13
  144.7 1.4 constant_dynamic-update-slice_fusion.12
  147.4 1.4 constant_dynamic-update-slice_fusion.10
  148.8 1.4 constant_dynamic-update-slice_fusion.9
  151.5 5.2 %all-to-all-start.1 = ((bf16[16,64,128]{2,1,0:T(8,128)(2,1)}), bf16[16,64,128]{2,1,0:T(8,128)(2,1)}, u32[]{:S(2)}, u32[]{:S(2)}) async-start(bf16[16,64,128]{2,1,0:T(8,128)(2,1)} %constant_dynamic-update-slice_fusion.8), calls=%async_computation.1 | async-start | bytes 524288 | tf_op jit(solution)/shard_map/all_to_all | solution.py:78
  156.7 2.4 fusion.52
  159.1 1.8 copy.15
  160.9 1.4 constant_dynamic-update-slice_fusion.23
  162.2 1.4 constant_dynamic-update-slice_fusion.22
  163.6 1.4 constant_dynamic-update-slice_fusion.21
  165.0 1.4 constant_dynamic-update-slice_fusion.20
  166.4 1.4 constant_dynamic-update-slice_fusion.19
  167.7 1.4 constant_dynamic-update-slice_fusion.18
  169.1 1.4 constant_dynamic-update-slice_fusion.17
  170.5 1.4 constant_dynamic-update-slice_fusion.16
  171.9 2.4 fusion.50
  180.3 5.7 %all-to-all-start.2 = ((bf16[16,64,128]{2,1,0:T(8,128)(2,1)}), bf16[16,64,128]{2,1,0:T(8,128)(2,1)S(1)}, u32[]{:S(2)}, u32[]{:S(2)}) async-start(bf16[16,64,128]{2,1,0:T(8,128)(2,1)} %constant_dynamic-update-slice_fusion.16), calls=%async_computation.2 | async-start | bytes 524288 | tf_op jit(solution)/shard_map/all_to_all | solution.py:78
  185.9 1.7 copy_bitcast_fusion.4
  187.6 6.3 %all-to-all-done.2 = bf16[16,64,128]{2,1,0:T(8,128)(2,1)S(1)} async-done(((bf16[16,64,128]{2,1,0:T(8,128)(2,1)}), bf16[16,64,128]{2,1,0:T(8,128)(2,1)S(1)}, u32[]{:S(2)}, u32[]{:S(2)}) %all-to-all-start.2) | async-done | bytes 262176 | tf_op jit(solution)/shard_map/all_to_all | solution.py:78
  194.0 4.4 %all-to-all-start = ((bf16[16,64,128]{2,1,0:T(8,128)(2,1)}), bf16[16,64,128]{2,1,0:T(8,128)(2,1)}, u32[]{:S(2)}, u32[]{:S(2)}) async-start(bf16[16,64,128]{2,1,0:T(8,128)(2,1)} %constant_dynamic-update-slice_fusion), calls=%async_computation | async-start | bytes 524288 | tf_op jit(solution)/shard_map/all_to_all | solution.py:78
  199.1 7.1 %all-to-all-done = bf16[16,64,128]{2,1,0:T(8,128)(2,1)} async-done(((bf16[16,64,128]{2,1,0:T(8,128)(2,1)}), bf16[16,64,128]{2,1,0:T(8,128)(2,1)}, u32[]{:S(2)}, u32[]{:S(2)}) %all-to-all-start) | async-done | bytes 262176 | tf_op jit(solution)/shard_map/all_to_all | solution.py:78
  207.2 2.0 pad_maximum_fusion
  209.2 2.6 gather_fusion
  213.1 2.8 select_reduce_fusion.1
  216.0 4.8 %fusion = f32[2048]{0:T(1024)S(1)} fusion(f32[2048,2048]{0,1:T(8,128)S(1)} %get-tuple-element.12, f32[2048]{0:T(1024)S(1)} %get-tuple-element.11, pred[2048]{0:T(1024)(128)(4,1)S(1)} %iota_compare_fusion), kind=kLoop, calls=%fused_computation.6 | loop fusion | flops 16775168 | bytes 16795648 | tf_op jit(solution)/shard_map/reduce_sum | solution.py:31
  220.8 3.1 fusion.65
  224.1 10.6 %all_to_all.118 = bf16[16,64,128]{2,1,0:T(8,128)(2,1)S(1)} all-to-all(bf16[16,64,128]{2,1,0:T(8,128)(2,1)S(1)} %bitcast.230), channel_id=1, replica_groups=mesh['pipe'=2,'ctx'=16,'dp'=8] {'ctx'}, dimensions={0} | all-to-all | bytes 524288 | tf_op jit(solution)/shard_map/all_to_all | solution.py:84
  236.5 9.9 %collective-permute-done.3 = bf16[128,1024]{1,0:T(8,128)(2,1)S(1)} collective-permute-done((bf16[128,1024]{1,0:T(8,128)(2,1)S(1)}, bf16[128,1024]{1,0:T(8,128)(2,1)S(1)}, u32[]{:S(2)}, u32[]{:S(2)}) %collective-permute-start.3) | collective-permute-done | bytes 262176 | tf_op jit(solution)/shard_map/ppermute | solution.py:119
  247.4 2.3 fusion.53
  249.6 1.8 copy.18
  251.4 1.5 fusion.86
  253.0 2.3 fusion.55
  255.2 1.8 copy.22
  257.4 1.5 fusion.54
  264.0 3.5 %all-to-all-start.5 = ((bf16[16,64,128]{2,1,0:T(8,128)(2,1)}), bf16[16,64,128]{2,1,0:T(8,128)(2,1)S(1)}, u32[]{:S(2)}, u32[]{:S(2)}) async-start(bf16[16,64,128]{2,1,0:T(8,128)(2,1)} %constant_dynamic-update-slice_fusion.32), calls=%async_computation.5 | async-start | bytes 524288 | tf_op jit(solution)/shard_map/all_to_all | solution.py:78
  270.3 1.4 constant_dynamic-update-slice_fusion.45
  271.6 1.4 constant_dynamic-update-slice_fusion.44
  273.0 1.4 constant_dynamic-update-slice_fusion.43
  274.4 1.4 constant_dynamic-update-slice_fusion.42
  275.8 1.4 constant_dynamic-update-slice_fusion.41
  277.1 1.4 constant_dynamic-update-slice_fusion.40
  279.9 1.4 constant_dynamic-update-slice_fusion.30
  284.0 1.4 constant_dynamic-update-slice_fusion.27
  285.4 1.4 constant_dynamic-update-slice_fusion.26
  286.8 1.4 constant_dynamic-update-slice_fusion.25
  288.1 1.4 constant_dynamic-update-slice_fusion.24
  289.5 5.7 %all-to-all-start.6 = ((bf16[16,64,128]{2,1,0:T(8,128)(2,1)}), bf16[16,64,128]{2,1,0:T(8,128)(2,1)S(1)}, u32[]{:S(2)}, u32[]{:S(2)}) async-start(bf16[16,64,128]{2,1,0:T(8,128)(2,1)} %constant_dynamic-update-slice_fusion.40), calls=%async_computation.6 | async-start | bytes 524288 | tf_op jit(solution)/shard_map/all_to_all | solution.py:78
  295.2 8.0 %all-to-all-done.6 = bf16[16,64,128]{2,1,0:T(8,128)(2,1)S(1)} async-done(((bf16[16,64,128]{2,1,0:T(8,128)(2,1)}), bf16[16,64,128]{2,1,0:T(8,128)(2,1)S(1)}, u32[]{:S(2)}, u32[]{:S(2)}) %all-to-all-start.6) | async-done | bytes 262176 | tf_op jit(solution)/shard_map/all_to_all | solution.py:78
  303.2 3.8 %all-to-all-start.4 = ((bf16[16,64,128]{2,1,0:T(8,128)(2,1)}), bf16[16,64,128]{2,1,0:T(8,128)(2,1)S(1)}, u32[]{:S(2)}, u32[]{:S(2)}) async-start(bf16[16,64,128]{2,1,0:T(8,128)(2,1)} %constant_dynamic-update-slice_fusion.24), calls=%async_computation.4 | async-start | bytes 524288 | tf_op jit(solution)/shard_map/all_to_all | solution.py:78
  307.0 7.7 %all-to-all-done.4 = bf16[16,64,128]{2,1,0:T(8,128)(2,1)S(1)} async-done(((bf16[16,64,128]{2,1,0:T(8,128)(2,1)}), bf16[16,64,128]{2,1,0:T(8,128)(2,1)S(1)}, u32[]{:S(2)}, u32[]{:S(2)}) %all-to-all-start.4) | async-done | bytes 262176 | tf_op jit(solution)/shard_map/all_to_all | solution.py:78
  314.8 1.5 gather_fusion.1
  317.6 2.8 select_reduce_fusion
  320.4 4.8 %fusion.2 = f32[2048]{0:T(1024)S(1)} fusion(f32[2048,2048]{0,1:T(8,128)S(1)} %get-tuple-element.14, f32[2048]{0:T(1024)S(1)} %get-tuple-element.13, pred[2048]{0:T(1024)(128)(4,1)S(1)} %iota_compare_fusion), kind=kLoop, calls=%fused_computation.8 | loop fusion | flops 16775168 | bytes 16795648 | tf_op jit(solution)/shard_map/reduce_sum | solution.py:31
  325.3 3.2 fusion.62
  329.2 3.5 %all-to-all-start.7 = ((bf16[16,64,128]{2,1,0:T(8,128)(2,1)}), bf16[16,64,128]{2,1,0:T(8,128)(2,1)S(1)}, u32[]{:S(2)}, u32[]{:S(2)}) async-start(bf16[16,64,128]{2,1,0:T(8,128)(2,1)} %bitcast.178), calls=%async_computation.7 | async-start | bytes 524288 | tf_op jit(solution)/shard_map/all_to_all | solution.py:84
  332.7 8.0 %all-to-all-done.7 = bf16[16,64,128]{2,1,0:T(8,128)(2,1)S(1)} async-done(((bf16[16,64,128]{2,1,0:T(8,128)(2,1)}), bf16[16,64,128]{2,1,0:T(8,128)(2,1)S(1)}, u32[]{:S(2)}, u32[]{:S(2)}) %all-to-all-start.7) | async-done | bytes 262176 | tf_op jit(solution)/shard_map/all_to_all | solution.py:84
  (97 shorter events, 40.3 us)
Async XLA Ops:
  6.5 228.1 %copy-start = (bf16[1,1024,1024]{2,1,0:T(8,128)(2,1)S(1)}, bf16[1,1024,1024]{2,1,0:T(8,128)(2,1)}, u32[]{:S(2)}) copy-start(bf16[1,1024,1024]{2,1,0:T(8,128)(2,1)} %param.17) | copy-start | bytes 6291460
  6.5 44.8 %all-gather.6.cloned.1.call-start = ((), (), s32[]{:S(2)}) async-start(), calls=%async_computation.9 | async-start | bytes 1179648 | tf_op jit(solution)/shard_map/all_gather | solution.py:106
  8.5 82.9 %all-gather.8.cloned.1.call-start = ((), (), s32[]{:S(2)}) async-start(), calls=%async_computation.10 | async-start | bytes 1179648 | tf_op jit(solution)/shard_map/all_gather | solution.py:106
  9.3 122.2 %all-gather.4.cloned.1.call-start = ((), (), s32[]{:S(2)}) async-start(), calls=%async_computation.8 | async-start | bytes 1179648 | tf_op jit(solution)/shard_map/all_gather | solution.py:106
  51.3 86.4 %collective-permute-start.1 = (bf16[512,1024]{1,0:T(8,128)(2,1)}, bf16[512,1024]{1,0:T(8,128)(2,1)S(1)}, u32[]{:S(2)}, u32[]{:S(2)}) collective-permute-start(bf16[512,1024]{1,0:T(8,128)(2,1)} %all-gather.6.cloned.1.call-done), channel_id=1, source_target_pairs={{0,8},{8,0},{16,24},{24,16},{32,40},{40,32},{48,56},{56,48},{64,72... | collective-permute-start | bytes 3145736 | tf_op jit(solution)/shard_map/ppermute | solution.py:108
  91.4 65.3 %collective-permute-start.2 = (bf16[512,1024]{1,0:T(8,128)(2,1)}, bf16[512,1024]{1,0:T(8,128)(2,1)}, u32[]{:S(2)}, u32[]{:S(2)}) collective-permute-start(bf16[512,1024]{1,0:T(8,128)(2,1)} %all-gather.8.cloned.1.call-done), channel_id=1, source_target_pairs={{0,8},{8,0},{16,24},{24,16},{32,40},{40,32},{48,56},{56,48},{64,72... | collective-permute-start | bytes 3145736 | tf_op jit(solution)/shard_map/ppermute | solution.py:108
  131.5 40.4 %collective-permute-start = (bf16[512,1024]{1,0:T(8,128)(2,1)}, bf16[512,1024]{1,0:T(8,128)(2,1)}, u32[]{:S(2)}, u32[]{:S(2)}) collective-permute-start(bf16[512,1024]{1,0:T(8,128)(2,1)} %all-gather.4.cloned.1.call-done), channel_id=1, source_target_pairs={{0,8},{8,0},{16,24},{24,16},{32,40},{40,32},{48,56},{56,48},{64,72... | collective-permute-start | bytes 3145736 | tf_op jit(solution)/shard_map/ppermute | solution.py:108
  137.7 78.2 %copy-start.3 = (bf16[512,1024]{1,0:T(8,128)(2,1)}, bf16[512,1024]{1,0:T(8,128)(2,1)S(1)}, u32[]{:S(2)}) copy-start(bf16[512,1024]{1,0:T(8,128)(2,1)S(1)} %collective-permute-done.1) | copy-start | bytes 3145732
  151.5 28.8 %all-to-all-start.1 = ((bf16[16,64,128]{2,1,0:T(8,128)(2,1)}), bf16[16,64,128]{2,1,0:T(8,128)(2,1)}, u32[]{:S(2)}, u32[]{:S(2)}) async-start(bf16[16,64,128]{2,1,0:T(8,128)(2,1)} %constant_dynamic-update-slice_fusion.8), calls=%async_computation.1 | async-start | bytes 524288 | tf_op jit(solution)/shard_map/all_to_all | solution.py:78
  180.3 13.7 %all-to-all-start.2 = ((bf16[16,64,128]{2,1,0:T(8,128)(2,1)}), bf16[16,64,128]{2,1,0:T(8,128)(2,1)S(1)}, u32[]{:S(2)}, u32[]{:S(2)}) async-start(bf16[16,64,128]{2,1,0:T(8,128)(2,1)} %constant_dynamic-update-slice_fusion.16), calls=%async_computation.2 | async-start | bytes 524288 | tf_op jit(solution)/shard_map/all_to_all | solution.py:78
  194.0 12.2 %all-to-all-start = ((bf16[16,64,128]{2,1,0:T(8,128)(2,1)}), bf16[16,64,128]{2,1,0:T(8,128)(2,1)}, u32[]{:S(2)}, u32[]{:S(2)}) async-start(bf16[16,64,128]{2,1,0:T(8,128)(2,1)} %constant_dynamic-update-slice_fusion), calls=%async_computation | async-start | bytes 524288 | tf_op jit(solution)/shard_map/all_to_all | solution.py:78
  215.9 18.7 %copy-start.4 = (bf16[1,1,128,1024]{3,2,1,0:T(8,128)(2,1)S(1)}, bf16[1,1,128,1024]{3,2,1,0:T(8,128)(2,1)}, u32[]{:S(2)}) copy-start(bf16[1,1,128,1024]{3,2,1,0:T(8,128)(2,1)} %param.12) | copy-start | bytes 786436
  215.9 18.7 %copy-start.11 = (f32[1,1024]{1,0:T(1,128)S(1)}, f32[1,1024]{1,0:T(1,128)}, u32[]{:S(2)}) copy-start(f32[1,1024]{1,0:T(1,128)} %param.18) | copy-start | bytes 12292
  216.0 18.7 %copy-start.12 = (f32[1,1024]{1,0:T(1,128)S(1)}, f32[1,1024]{1,0:T(1,128)}, u32[]{:S(2)}) copy-start(f32[1,1024]{1,0:T(1,128)} %param.19) | copy-start | bytes 12292
  220.8 26.0 %copy-start.9 = (f32[1,1024]{1,0:T(1,128)S(1)}, f32[1,1024]{1,0:T(1,128)}, u32[]{:S(2)}) copy-start(f32[1,1024]{1,0:T(1,128)} %param.15) | copy-start | bytes 12292
  220.8 26.0 %copy-start.10 = (f32[1,1024]{1,0:T(1,128)S(1)}, f32[1,1024]{1,0:T(1,128)}, u32[]{:S(2)}) copy-start(f32[1,1024]{1,0:T(1,128)} %param.14) | copy-start | bytes 12292
  220.8 26.2 %copy-start.2 = (bf16[512,1024]{1,0:T(8,128)(2,1)S(1)}, bf16[512,1024]{1,0:T(8,128)(2,1)}, u32[]{:S(2)}) copy-start(bf16[512,1024]{1,0:T(8,128)(2,1)} %all-gather.4.cloned.1.call-done) | copy-start | bytes 3145732
  220.8 36.2 %copy-start.1 = (bf16[512,1024]{1,0:T(8,128)(2,1)S(1)}, bf16[512,1024]{1,0:T(8,128)(2,1)}, u32[]{:S(2)}) copy-start(bf16[512,1024]{1,0:T(8,128)(2,1)} %all-gather.6.cloned.1.call-done) | copy-start | bytes 3145732
  235.2 12.1 %copy-start.7 = (bf16[128,1024]{1,0:T(8,128)(2,1)}, bf16[128,1024]{1,0:T(8,128)(2,1)S(1)}, u32[]{:S(2)}) copy-start(bf16[128,1024]{1,0:T(8,128)(2,1)S(1)} %fusion.47) | copy-start | bytes 786436
  235.2 11.2 %collective-permute-start.3 = (bf16[128,1024]{1,0:T(8,128)(2,1)S(1)}, bf16[128,1024]{1,0:T(8,128)(2,1)S(1)}, u32[]{:S(2)}, u32[]{:S(2)}) collective-permute-start(bf16[128,1024]{1,0:T(8,128)(2,1)S(1)} %fusion.47), channel_id=1, source_target_pairs={{0,128},{1,129},{2,130},{3,131},{4,132},{5,133},{6,134},{7,135},{8... | collective-permute-start | bytes 786440 | tf_op jit(solution)/shard_map/ppermute | solution.py:119
  246.4 1.0 copy-start.5
  264.0 25.5 %all-to-all-start.5 = ((bf16[16,64,128]{2,1,0:T(8,128)(2,1)}), bf16[16,64,128]{2,1,0:T(8,128)(2,1)S(1)}, u32[]{:S(2)}, u32[]{:S(2)}) async-start(bf16[16,64,128]{2,1,0:T(8,128)(2,1)} %constant_dynamic-update-slice_fusion.32), calls=%async_computation.5 | async-start | bytes 524288 | tf_op jit(solution)/shard_map/all_to_all | solution.py:78
  289.5 13.7 %all-to-all-start.6 = ((bf16[16,64,128]{2,1,0:T(8,128)(2,1)}), bf16[16,64,128]{2,1,0:T(8,128)(2,1)S(1)}, u32[]{:S(2)}, u32[]{:S(2)}) async-start(bf16[16,64,128]{2,1,0:T(8,128)(2,1)} %constant_dynamic-update-slice_fusion.40), calls=%async_computation.6 | async-start | bytes 524288 | tf_op jit(solution)/shard_map/all_to_all | solution.py:78
  303.2 11.5 %all-to-all-start.4 = ((bf16[16,64,128]{2,1,0:T(8,128)(2,1)}), bf16[16,64,128]{2,1,0:T(8,128)(2,1)S(1)}, u32[]{:S(2)}, u32[]{:S(2)}) async-start(bf16[16,64,128]{2,1,0:T(8,128)(2,1)} %constant_dynamic-update-slice_fusion.24), calls=%async_computation.4 | async-start | bytes 524288 | tf_op jit(solution)/shard_map/all_to_all | solution.py:78
  320.4 20.3 %copy-start.6 = (bf16[128,1024]{1,0:T(8,128)(2,1)S(1)}, bf16[128,1024]{1,0:T(8,128)(2,1)}, u32[]{:S(2)}) copy-start(bf16[128,1024]{1,0:T(8,128)(2,1)} %copy-done.5) | copy-start | bytes 786436
  320.4 20.3 %copy-start.8 = (bf16[128,1024]{1,0:T(8,128)(2,1)S(1)}, bf16[128,1024]{1,0:T(8,128)(2,1)}, u32[]{:S(2)}) copy-start(bf16[128,1024]{1,0:T(8,128)(2,1)} %copy-done.7) | copy-start | bytes 786436
  329.2 11.5 %all-to-all-start.7 = ((bf16[16,64,128]{2,1,0:T(8,128)(2,1)}), bf16[16,64,128]{2,1,0:T(8,128)(2,1)S(1)}, u32[]{:S(2)}, u32[]{:S(2)}) async-start(bf16[16,64,128]{2,1,0:T(8,128)(2,1)} %bitcast.178), calls=%async_computation.7 | async-start | bytes 524288 | tf_op jit(solution)/shard_map/all_to_all | solution.py:84
Sparse Core Ops, SparseCore 0:
  9.0 42.2 all-gather.5
  53.0 38.3 all-gather.7
  93.1 38.3 all-gather.3

commit v2 on v0

--- a/solution.py
+++ b/solution.py
@@ -44,13 +44,10 @@
     normed = normalize(current, gain, shift)
     normed_mine = lax.dynamic_slice_in_dim(normed, core * half, half, axis=1)
     normed_other = lax.dynamic_slice_in_dim(normed, (1 - core) * half, half, axis=1)
-    projected = jnp.einsum(
-        "tk,kphf->hpft", normed_mine, qkv_mine.reshape(half, 3, HEADS, head_width),
-        preferred_element_type=jnp.float32,
-    ) + jnp.einsum(
-        "tk,kphf->hpft", normed_other, qkv_other.reshape(half, 3, HEADS, head_width),
-        preferred_element_type=jnp.float32,
+    projected = jnp.dot(normed_mine, qkv_mine, preferred_element_type=jnp.float32) + jnp.dot(
+        normed_other, qkv_other, preferred_element_type=jnp.float32
     )
+    projected = jnp.transpose(projected.reshape(tok_rows, 3, HEADS, head_width), (2, 1, 3, 0))
     projected = projected.astype(jnp.bfloat16)
     gathered = lax.all_to_all(projected, "ctx", 0, 3, tiled=True)
     context = head_attention(gathered[0], length, head_width ** (-0.5))

time: 184 us -> 178 us (0.967)
  local copies, waits for them, and re-layouts: 14.3 us -> 7.97 us
    ppermute x1 -> x0, local copies, waits for them, and re-layouts: 4.7 us -> none  [per_device(): qkv_other = lax.ppermute(qkv_mine, 'ctx', sibling)]
    all_gather x1 -> x0, local copies, waits for them, and re-layouts: 4.66 us -> none  [per_device(): qkv_mine = lax.all_gather(rows_mine, 'dp', axis=1, tiled=True)]
    convert_element_type x2 -> x4, local copies, waits for them, and re-layouts: 0.99 us -> 4 us  [sublayer(): projected = projected.astype(jnp.bfloat16)]
  transfers between devices with their start and end apart: 5 -> 5, of which waited for: 4 -> 4; matrix products, arithmetic and copies ran while one was open for 7% -> 3% of each run, Pallas kernels for 0% -> 0%
where the time goes in v2:
time: 178 us; the launch traced here: 177 us
  waiting for transfers between devices  80.3 us (45%)
  blocking collectives  27.2 us (15%)
  matrix products  23.5 us (13%)
  between operations  14.3 us (8%)
  other arithmetic  13.7 us (8%)
  starting transfers between devices  10.1 us (6%)
  local copies, waits for them, and re-layouts  7.97 us (4%)
    all_gather x1, waiting for transfers between devices, per_device(): qkv_mine = lax.all_gather(rows_mine, 'dp', axis=1, tiled=True)  49.5 us
    all_to_all x1, blocking collectives, sublayer(): gathered = lax.all_to_all(projected, 'ctx', 0, 3, tiled=True)  16.5 us
    all_to_all x1, waiting for transfers between devices, sublayer(): gathered = lax.all_to_all(projected, 'ctx', 0, 3, tiled=True)  13.1 us
    all_to_all x1, blocking collectives, sublayer(): lax.all_to_all(context, 'ctx', 0, 0, tiled=True).reshape(width, tok_rows)  10.6 us
    ppermute x1, waiting for transfers between devices, per_device(): current = lax.ppermute(produced, 'pipe', pairs)  9.68 us
    reduce_sum x2, other arithmetic, head_attention(): totals = jnp.sum(weights, axis=-1)  9.64 us
    all_to_all x1, waiting for transfers between devices, sublayer(): lax.all_to_all(context, 'ctx', 0, 0, tiled=True).reshape(width, tok_rows)  7.98 us
    dot_general x2, matrix products, sublayer(): jnp.dot(normed_other, qkv_other, preferred_element_type=jnp.float32)  6.83 us
  transfers between devices with their start and end apart: 5, of which 4 were waited for; matrix products, arithmetic and copies ran while one was open for 3% of the time, Pallas kernels for 0%

profile of v2, /device:TPU:4, one launch (start us, length us, event | category | flops | bytes accessed | tf_op | source)
XLA Modules:
  0.0 177.0 jit_solution(10619017852893557155)
XLA Ops:
  6.5 0.0 copy-start
  6.5 0.0 all-gather.3.cloned.1.call-start
  6.5 1.9 %constant_dynamic-slice_fusion = bf16[1,512,384]{2,1,0:T(8,128)(2,1)} fusion(bf16[1,1024,384]{2,1,0:T(8,128)(2,1)} %param.12, s32[]{:T(128)S(6)} %select_n.43), kind=kLoop, calls=%fused_computation.79 | loop fusion | bytes 786436 | tf_op jit(solution)/shard_map/dynamic_slice | solution.py:67
  8.5 0.0 all-gather.3.cloned.1.call-update
  8.5 49.5 %all-gather.3.cloned.1.call-done = bf16[1,512,3072]{2,1,0:T(8,128)(2,1)} async-done(((bf16[1,512,384]{2,1,0:T(8,128)(2,1)}), bf16[1,512,3072]{2,1,0:T(8,128)(2,1)}) %all-gather.3.cloned.1.call-update) | async-done | bytes 3145744 | tf_op jit(solution)/shard_map/all_gather | solution.py:68
  58.0 0.0 collective-permute-start
  58.0 1.1 convert_reduce_fusion.1
  59.1 1.2 fusion.73
  60.2 1.2 fusion.76
  61.5 2.5 %fusion.95 = f32[128,3072]{1,0:T(8,128)S(1)} fusion(bf16[128,1024]{1,0:T(8,128)(2,1)S(1)} %fusion.76, s32[]{:T(128)S(6)} %select_n.43, bf16[1,512,3072]{2,1,0:T(8,128)(2,1)} %all-gather.3.cloned.1.call-done), kind=kOutput, calls=%fused_computation.73 | convolution fusion | flops 402653184 | bytes 4849668 | tf_op jit(solution)/shard_map/dot_general | solution.py:47
  63.9 0.0 collective-permute-done
  64.0 3.4 %fusion.10 = bf16[128,3072]{1,0:T(8,128)(2,1)} fusion(f32[128,3072]{1,0:T(8,128)S(1)} %fusion.95, bf16[512,3072]{1,0:T(8,128)(2,1)} %collective-permute-done, bf16[128,1024]{1,0:T(8,128)(2,1)S(1)} %fusion.76, s32[]{:T(128)S(6)} %select_n.44), kind=kOutput, calls=%fused_computation.14 | convolution fusion | flops 403439616 | bytes 5636100 | tf_op jit(solution)/shard_map/dot_general | solution.py:47
  67.4 1.5 copy.19
  68.9 0.9 copy.20
  69.9 5.1 %all-to-all-start = ((bf16[16,3,64,128]{3,2,1,0:T(8,128)(2,1)}), bf16[16,3,64,128]{3,2,1,0:T(8,128)(2,1)S(1)}, u32[]{:S(2)}, u32[]{:S(2)}) async-start(bf16[16,3,64,128]{3,2,1,0:T(8,128)(2,1)} %copy.20), calls=%async_computation | async-start | bytes 1572864 | tf_op jit(solution)/shard_map/all_to_all | solution.py:52
  75.6 13.1 %all-to-all-done = bf16[16,3,64,128]{3,2,1,0:T(8,128)(2,1)S(1)} async-done(((bf16[16,3,64,128]{3,2,1,0:T(8,128)(2,1)}), bf16[16,3,64,128]{3,2,1,0:T(8,128)(2,1)S(1)}, u32[]{:S(2)}, u32[]{:S(2)}) %all-to-all-start) | async-done | bytes 786464 | tf_op jit(solution)/shard_map/all_to_all | solution.py:52
  88.7 0.1 fusion.108
  88.7 0.2 copy.21
  88.9 0.2 copy.23
  89.1 0.2 copy.22
  89.3 2.8 %select_reduce_fusion.1 = (f32[2048]{0:T(1024)S(1)}, f32[2048,2048]{0,1:T(8,128)S(1)}) fusion(pred[2048]{0:T(1024)(128)(4,1)S(1)} %iota_compare_fusion, bf16[8,8,16,128]{3,2,1,0:T(8,128)(2,1)S(1)} %bitcast.133, bf16[8,8,16,128]{3,2,1,0:T(8,128)(2,1)S(1)} %bitcast.135), kind=kOutput, calls=%fused_computation.3 | convolution fusion | flops 549451776 | bytes 17311744 | tf_op jit(solution)/shard_map/dq,dk->qk/dot_general | solution.py:25
  92.1 0.0 copy-start.2
  92.1 0.0 copy-start.5
  92.1 0.0 copy-start.6
  92.1 4.8 %fusion = f32[2048]{0:T(1024)S(1)} fusion(f32[2048,2048]{0,1:T(8,128)S(1)} %get-tuple-element.12, f32[2048]{0:T(1024)S(1)} %get-tuple-element.11, pred[2048]{0:T(1024)(128)(4,1)S(1)} %iota_compare_fusion), kind=kLoop, calls=%fused_computation.4 | loop fusion | flops 16775168 | bytes 16795648 | tf_op jit(solution)/shard_map/reduce_sum | solution.py:31
  96.9 0.0 copy-start.3
  97.0 0.0 copy-start.4
  97.0 0.0 copy-start.1
  97.0 3.1 %fusion.61 = bf16[8,16,8,128]{3,2,1,0:T(8,128)(2,1)S(1)} fusion(f32[2048,2048]{0,1:T(8,128)S(1)} %get-tuple-element.12, f32[2048]{0:T(1024)S(1)} %get-tuple-element.11, pred[2048]{0:T(1024)(128)(4,1)S(1)} %iota_compare_fusion, bf16[8,8,16,128]{3,2,1,0:T(8,128)(2,1)S(1)} %bitcast.141, f32[2048]{0:T(1024)S(1)} %fusion), kind=kOutput, calls=%fused_computation.35 | convolution fusion | flops 553910272 | bytes 17319936 | tf_op jit(solution)/shard_map/qk,dk->dq/dot_general | solution.py:32
  100.1 0.1 copy.74
  100.2 10.6 %all_to_all.40 = bf16[16,64,128]{2,1,0:T(8,128)(2,1)S(1)} all-to-all(bf16[16,64,128]{2,1,0:T(8,128)(2,1)S(1)} %bitcast.137), channel_id=1, replica_groups=mesh['pipe'=2,'ctx'=16,'dp'=8] {'ctx'}, dimensions={0} | all-to-all | bytes 524288 | tf_op jit(solution)/shard_map/all_to_all | solution.py:55
  110.8 0.0 copy-done
  110.8 0.0 copy-done.2
  110.8 0.0 copy-done.5
  110.8 0.0 copy-done.6
  110.8 0.5 fusion.49
  111.3 1.5 collective-permute-start.1
  112.8 9.7 %collective-permute-done.1 = bf16[128,1024]{1,0:T(8,128)(2,1)S(1)} collective-permute-done((bf16[128,1024]{1,0:T(8,128)(2,1)S(1)}, bf16[128,1024]{1,0:T(8,128)(2,1)S(1)}, u32[]{:S(2)}, u32[]{:S(2)}) %collective-permute-start.1) | collective-permute-done | bytes 262176 | tf_op jit(solution)/shard_map/ppermute | solution.py:80
  122.5 0.1 convert_reduce_fusion
  122.6 0.2 fusion.69
  122.8 0.0 copy-done.3
  122.9 0.0 copy-done.4
  122.9 0.2 fusion.72
  123.1 0.0 copy-done.1
  123.1 0.6 fusion.92
  123.7 3.4 %fusion.11 = bf16[128,3072]{1,0:T(8,128)(2,1)} fusion(f32[128,3072]{1,0:T(8,128)S(1)} %fusion.92, bf16[512,3072]{1,0:T(8,128)(2,1)} %collective-permute-done, bf16[128,1024]{1,0:T(8,128)(2,1)S(1)} %fusion.72, s32[]{:T(128)S(6)} %select_n.44), kind=kOutput, calls=%fused_computation.15 | convolution fusion | flops 403439616 | bytes 5636100 | tf_op jit(solution)/shard_map/dot_general | solution.py:47
  127.1 1.5 copy.25
  128.6 0.1 copy.26
  128.7 16.5 %all_to_all.41 = bf16[16,3,64,128]{3,2,1,0:T(8,128)(2,1)S(1)} all-to-all(bf16[16,3,64,128]{3,2,1,0:T(8,128)(2,1)S(1)} %copy.26), channel_id=1, replica_groups=mesh['pipe'=2,'ctx'=16,'dp'=8] {'ctx'}, dimensions={0} | all-to-all | bytes 1572864 | tf_op jit(solution)/shard_map/all_to_all | solution.py:52
  145.2 0.1 fusion.107
  145.3 0.2 copy.27
  145.5 0.2 copy.29
  145.7 0.2 copy.28
  145.8 2.8 %select_reduce_fusion = (f32[2048]{0:T(1024)S(1)}, f32[2048,2048]{0,1:T(8,128)S(1)}) fusion(pred[2048]{0:T(1024)(128)(4,1)S(1)} %iota_compare_fusion, bf16[8,8,16,128]{3,2,1,0:T(8,128)(2,1)S(1)} %bitcast.134, bf16[8,8,16,128]{3,2,1,0:T(8,128)(2,1)S(1)} %bitcast.136), kind=kOutput, calls=%fused_computation.1 | convolution fusion | flops 549451776 | bytes 17311744 | tf_op jit(solution)/shard_map/dq,dk->qk/dot_general | solution.py:25
  148.6 4.8 %fusion.2 = f32[2048]{0:T(1024)S(1)} fusion(f32[2048,2048]{0,1:T(8,128)S(1)} %get-tuple-element.14, f32[2048]{0:T(1024)S(1)} %get-tuple-element.13, pred[2048]{0:T(1024)(128)(4,1)S(1)} %iota_compare_fusion), kind=kLoop, calls=%fused_computation.6 | loop fusion | flops 16775168 | bytes 16795648 | tf_op jit(solution)/shard_map/reduce_sum | solution.py:31
  153.5 3.1 %fusion.58 = bf16[8,16,8,128]{3,2,1,0:T(8,128)(2,1)S(1)} fusion(f32[2048,2048]{0,1:T(8,128)S(1)} %get-tuple-element.14, f32[2048]{0:T(1024)S(1)} %get-tuple-element.13, pred[2048]{0:T(1024)(128)(4,1)S(1)} %iota_compare_fusion, bf16[8,8,16,128]{3,2,1,0:T(8,128)(2,1)S(1)} %bitcast.140, f32[2048]{0:T(1024)S(1)} %fusion.2), kind=kOutput, calls=%fused_computation.34 | convolution fusion | flops 553910272 | bytes 17319936 | tf_op jit(solution)/shard_map/qk,dk->dq/dot_general | solution.py:32
  156.6 0.8 copy.73
  157.4 3.5 %all-to-all-start.3 = ((bf16[16,64,128]{2,1,0:T(8,128)(2,1)}), bf16[16,64,128]{2,1,0:T(8,128)(2,1)S(1)}, u32[]{:S(2)}, u32[]{:S(2)}) async-start(bf16[16,64,128]{2,1,0:T(8,128)(2,1)} %bitcast.124), calls=%async_computation.3 | async-start | bytes 524288 | tf_op jit(solution)/shard_map/all_to_all | solution.py:55
  160.9 8.0 %all-to-all-done.3 = bf16[16,64,128]{2,1,0:T(8,128)(2,1)S(1)} async-done(((bf16[16,64,128]{2,1,0:T(8,128)(2,1)}), bf16[16,64,128]{2,1,0:T(8,128)(2,1)S(1)}, u32[]{:S(2)}, u32[]{:S(2)}) %all-to-all-start.3) | async-done | bytes 262176 | tf_op jit(solution)/shard_map/all_to_all | solution.py:55
  168.9 1.2 fusion.55
  (5 shorter events, 0.0 us)
Async XLA Ops:
  6.5 104.3 %copy-start = (bf16[1,1024,1024]{2,1,0:T(8,128)(2,1)S(1)}, bf16[1,1024,1024]{2,1,0:T(8,128)(2,1)}, u32[]{:S(2)}) copy-start(bf16[1,1024,1024]{2,1,0:T(8,128)(2,1)} %param.13) | copy-start | bytes 6291460
  6.5 51.5 %all-gather.3.cloned.1.call-start = ((), (), s32[]{:S(2)}) async-start(), calls=%async_computation.4 | async-start | bytes 3538944 | tf_op jit(solution)/shard_map/all_gather | solution.py:68
  58.0 6.0 %collective-permute-start = (bf16[512,3072]{1,0:T(8,128)(2,1)}, bf16[512,3072]{1,0:T(8,128)(2,1)}, u32[]{:S(2)}, u32[]{:S(2)}) collective-permute-start(bf16[512,3072]{1,0:T(8,128)(2,1)} %bitcast.128), channel_id=1, source_target_pairs={{0,8},{8,0},{16,24},{24,16},{32,40},{40,32},{48,56},{56,48},{64,72... | collective-permute-start | bytes 9437192 | tf_op jit(solution)/shard_map/ppermute | solution.py:70
  69.9 18.8 %all-to-all-start = ((bf16[16,3,64,128]{3,2,1,0:T(8,128)(2,1)}), bf16[16,3,64,128]{3,2,1,0:T(8,128)(2,1)S(1)}, u32[]{:S(2)}, u32[]{:S(2)}) async-start(bf16[16,3,64,128]{3,2,1,0:T(8,128)(2,1)} %copy.20), calls=%async_computation | async-start | bytes 1572864 | tf_op jit(solution)/shard_map/all_to_all | solution.py:52
  92.1 18.7 %copy-start.2 = (bf16[1,1,128,1024]{3,2,1,0:T(8,128)(2,1)S(1)}, bf16[1,1,128,1024]{3,2,1,0:T(8,128)(2,1)}, u32[]{:S(2)}) copy-start(bf16[1,1,128,1024]{3,2,1,0:T(8,128)(2,1)} %param.8) | copy-start | bytes 786436
  92.1 18.7 %copy-start.5 = (f32[1,1024]{1,0:T(1,128)S(1)}, f32[1,1024]{1,0:T(1,128)}, u32[]{:S(2)}) copy-start(f32[1,1024]{1,0:T(1,128)} %param.14) | copy-start | bytes 12292
  92.1 18.7 %copy-start.6 = (f32[1,1024]{1,0:T(1,128)S(1)}, f32[1,1024]{1,0:T(1,128)}, u32[]{:S(2)}) copy-start(f32[1,1024]{1,0:T(1,128)} %param.15) | copy-start | bytes 12292
  96.9 25.9 %copy-start.3 = (f32[1,1024]{1,0:T(1,128)S(1)}, f32[1,1024]{1,0:T(1,128)}, u32[]{:S(2)}) copy-start(f32[1,1024]{1,0:T(1,128)} %param.11) | copy-start | bytes 12292
  97.0 25.9 %copy-start.4 = (f32[1,1024]{1,0:T(1,128)S(1)}, f32[1,1024]{1,0:T(1,128)}, u32[]{:S(2)}) copy-start(f32[1,1024]{1,0:T(1,128)} %param.10) | copy-start | bytes 12292
  97.0 26.1 %copy-start.1 = (bf16[1,512,3072]{2,1,0:T(8,128)(2,1)S(1)}, bf16[1,512,3072]{2,1,0:T(8,128)(2,1)}, u32[]{:S(2)}) copy-start(bf16[1,512,3072]{2,1,0:T(8,128)(2,1)} %all-gather.3.cloned.1.call-done) | copy-start | bytes 9437188
  111.3 11.2 %collective-permute-start.1 = (bf16[128,1024]{1,0:T(8,128)(2,1)S(1)}, bf16[128,1024]{1,0:T(8,128)(2,1)S(1)}, u32[]{:S(2)}, u32[]{:S(2)}) collective-permute-start(bf16[128,1024]{1,0:T(8,128)(2,1)S(1)} %fusion.49), channel_id=1, source_target_pairs={{0,128},{1,129},{2,130},{3,131},{4,132},{5,133},{6,134},{7,135},{8... | collective-permute-start | bytes 786440 | tf_op jit(solution)/shard_map/ppermute | solution.py:80
  157.4 11.5 %all-to-all-start.3 = ((bf16[16,64,128]{2,1,0:T(8,128)(2,1)}), bf16[16,64,128]{2,1,0:T(8,128)(2,1)S(1)}, u32[]{:S(2)}, u32[]{:S(2)}) async-start(bf16[16,64,128]{2,1,0:T(8,128)(2,1)} %bitcast.124), calls=%async_computation.3 | async-start | bytes 524288 | tf_op jit(solution)/shard_map/all_to_all | solution.py:55
Sparse Core Ops, SparseCore 0:
  9.1 48.8 all-gather.2

commit v3 on v2

--- a/solution.py
+++ b/solution.py
@@ -58,6 +58,26 @@
     return (current.astype(jnp.float32) + layer_scale * mixed).astype(jnp.bfloat16)
 
 
+def ring_gather(piece, axis):
+    count = lax.axis_size(axis)
+    index = lax.axis_index(axis)
+    rows, cols = piece.shape
+    whole = jnp.zeros((rows, cols * count), piece.dtype)
+    whole = lax.dynamic_update_slice_in_dim(whole, piece, index * cols, axis=1)
+    right = [(i, (i + 1) % count) for i in range(count)]
+    left = [(i, (i - 1) % count) for i in range(count)]
+    forward, backward = piece, piece
+    for step in range(count // 2):
+        forward = lax.ppermute(forward, axis, right)
+        owner = (index - 1 - step) % count
+        whole = lax.dynamic_update_slice_in_dim(whole, forward, owner * cols, axis=1)
+        if step < (count - 1) // 2:
+            backward = lax.ppermute(backward, axis, left)
+            owner = (index + 1 + step) % count
+            whole = lax.dynamic_update_slice_in_dim(whole, backward, owner * cols, axis=1)
+    return whole
+
+
 def per_device(patches, lengths, norm_gain, norm_bias, w_qkv, w_out, out_bias, scale_gain):
     section_index = lax.axis_index("pipe")
     section_count = lax.axis_size("pipe")
@@ -65,7 +85,7 @@
     width = w_qkv.shape[1]
     half = width // 2
     rows_mine = lax.dynamic_slice_in_dim(w_qkv[0], core * half, half, axis=0)
-    qkv_mine = lax.all_gather(rows_mine, "dp", axis=1, tiled=True)
+    qkv_mine = ring_gather(rows_mine, "dp")
     sibling = [(i, i ^ 1) for i in range(lax.axis_size("ctx"))]
     qkv_other = lax.ppermute(qkv_mine, "ctx", sibling)
     args = (qkv_mine, qkv_other, w_out[0], norm_gain[0], norm_bias[0], out_bias[0], scale_gain[0])

time: 178 us -> 169 us (0.949)
  waiting for transfers between devices: 80.3 us -> 63.5 us
  between operations: 14.3 us -> 0.9 us
  starting transfers between devices: 10.1 us -> 22.5 us
  local copies, waits for them, and re-layouts: 7.97 us -> 18 us
  other arithmetic: 13.7 us -> 10.8 us
  matrix products: 23.5 us -> 25.3 us
    all_gather x1 -> x0, waiting for transfers between devices: 49.5 us -> none  [per_device(): qkv_mine = lax.all_gather(rows_mine, 'dp', axis=1, tiled=True)]
    ppermute x0 -> x7, waiting for transfers between devices: none -> 27.3 us  [the longest x4 27.3 us: ring_gather(): forward = lax.ppermute(forward, axis, right)]
    ppermute x0 -> x7, starting transfers between devices: none -> 12.4 us  [the longest x3 10.5 us: ring_gather(): backward = lax.ppermute(backward, axis, left)]
    dynamic_update_slice x0 -> x8, local copies, waits for them, and re-layouts: none -> 9.9 us  [the longest x4 4.47 us: ring_gather(): lax.dynamic_update_slice_in_dim(whole, forward, owner * cols, axis=1)]
    ppermute x1, waiting for transfers between devices: 0.05 us -> 5.37 us  [per_device(): qkv_other = lax.ppermute(qkv_mine, 'ctx', sibling)]
    dot_general x2, matrix products: 3.05 us -> 6.82 us  [sublayer(): jnp.dot(normed_mine, qkv_mine, preferred_element_type=jnp.float32)]
    broadcast_in_dim x0 -> x1, local copies, waits for them, and re-layouts: none -> 2.06 us  [ring_gather(): whole = jnp.zeros((rows, cols * count), piece.dtype)]
    dynamic_slice x1 -> x0, local copies, waits for them, and re-layouts: 1.93 us -> none  [per_device(): rows_mine = lax.dynamic_slice_in_dim(w_qkv[0], core * half, half, axis=0)]
  transfers between devices with their start and end apart: 5 -> 11, of which waited for: 4 -> 8; matrix products, arithmetic and copies ran while one was open for 3% -> 5% of each run, Pallas kernels for 0% -> 0%
where the time goes in v3:
time: 169 us; the launch traced here: 168 us
  waiting for transfers between devices  63.5 us (38%)
  blocking collectives  27.2 us (16%)
  matrix products  25.3 us (15%)
  starting transfers between devices  22.5 us (13%)
  local copies, waits for them, and re-layouts  18 us (11%)
  other arithmetic  10.8 us (6%)
    ppermute x4, waiting for transfers between devices, ring_gather(): forward = lax.ppermute(forward, axis, right)  27.3 us
    all_to_all x1, blocking collectives, sublayer(): gathered = lax.all_to_all(projected, 'ctx', 0, 3, tiled=True)  16.5 us
    all_to_all x1, waiting for transfers between devices, sublayer(): gathered = lax.all_to_all(projected, 'ctx', 0, 3, tiled=True)  13 us
    all_to_all x1, blocking collectives, sublayer(): lax.all_to_all(context, 'ctx', 0, 0, tiled=True).reshape(width, tok_rows)  10.6 us
    ppermute x3, starting transfers between devices, ring_gather(): backward = lax.ppermute(backward, axis, left)  10.5 us
    ppermute x1, waiting for transfers between devices, per_device(): current = lax.ppermute(produced, 'pipe', pairs)  9.87 us
    reduce_sum x2, other arithmetic, head_attention(): totals = jnp.sum(weights, axis=-1)  9.64 us
    all_to_all x1, waiting for transfers between devices, sublayer(): lax.all_to_all(context, 'ctx', 0, 0, tiled=True).reshape(width, tok_rows)  7.98 us
  transfers between devices with their start and end apart: 11, of which 8 were waited for; matrix products, arithmetic and copies ran while one was open for 5% of the time, Pallas kernels for 0%

profile of v3, /device:TPU:4, one launch (start us, length us, event | category | flops | bytes accessed | tf_op | source)
XLA Modules:
  0.0 168.2 jit_solution(14752410053374116237)
XLA Ops:
  0.0 2.1 %broadcast_in_dim.44 = bf16[512,3072]{1,0:T(8,128)(2,1)} broadcast(bf16[]{:T(256)} %constant.96.clone.1), dimensions={} | broadcast | bytes 3145730 | tf_op jit(solution)/shard_map/broadcast_in_dim | solution.py:65
  2.1 1.9 %constant_dynamic-update-slice_fusion.7 = (bf16[512,3072]{1,0:T(8,128)(2,1)}, bf16[512,384]{1,0:T(8,128)(2,1)S(1)}) fusion(bf16[512,3072]{1,0:T(8,128)(2,1)} %broadcast_in_dim.44, s32[]{:T(128)S(6)} %select_n.96, bf16[1,1024,384]{2,1,0:T(8,128)(2,1)} %param.12, s32[]{:T(128)S(6)} %select_n.95), kind=kLoop, calls=%fused_computation.87 | loop fusion | bytes 1179656 | tf_op jit(solution)/shard_map/dynamic_update_slice | solution.py:66
  4.0 1.9 %collective-permute-start = (bf16[512,384]{1,0:T(8,128)(2,1)S(1)}, bf16[512,384]{1,0:T(8,128)(2,1)S(1)}, u32[]{:S(2)}, u32[]{:S(2)}) collective-permute-start(bf16[512,384]{1,0:T(8,128)(2,1)S(1)} %get-tuple-element.6), channel_id=1, source_target_pairs={{0,1},{1,2},{2,3},{3,4},{4,5},{5,6},{6,7},{7,0},{8,9},{9,10},{10,1... | collective-permute-start | bytes 1179656 | tf_op jit(solution)/shard_map/ppermute | solution.py:71
  5.9 3.9 %collective-permute-start.1 = (bf16[512,384]{1,0:T(8,128)(2,1)S(1)}, bf16[512,384]{1,0:T(8,128)(2,1)}, u32[]{:S(2)}, u32[]{:S(2)}) collective-permute-start(bf16[512,384]{1,0:T(8,128)(2,1)S(1)} %get-tuple-element.6), channel_id=1, source_target_pairs={{0,7},{1,0},{2,1},{3,2},{4,3},{5,4},{6,5},{7,6},{8,15},{9,8},{10,9... | collective-permute-start | bytes 1179656 | tf_op jit(solution)/shard_map/ppermute | solution.py:75
  9.8 9.1 %collective-permute-done = bf16[512,384]{1,0:T(8,128)(2,1)S(1)} collective-permute-done((bf16[512,384]{1,0:T(8,128)(2,1)S(1)}, bf16[512,384]{1,0:T(8,128)(2,1)S(1)}, u32[]{:S(2)}, u32[]{:S(2)}) %collective-permute-start) | collective-permute-done | bytes 393248 | tf_op jit(solution)/shard_map/ppermute | solution.py:71
  18.9 0.0 collective-permute-start.2
  18.9 0.0 collective-permute-done.1
  18.9 3.2 %collective-permute-start.3 = (bf16[512,384]{1,0:T(8,128)(2,1)}, bf16[512,384]{1,0:T(8,128)(2,1)S(1)}, u32[]{:S(2)}, u32[]{:S(2)}) collective-permute-start(bf16[512,384]{1,0:T(8,128)(2,1)} %collective-permute-done.1), channel_id=1, source_target_pairs={{0,7},{1,0},{2,1},{3,2},{4,3},{5,4},{6,5},{7,6},{8,15},{9,8},{10,9... | collective-permute-start | bytes 1179656 | tf_op jit(solution)/shard_map/ppermute | solution.py:75
  22.2 8.2 %collective-permute-done.2 = bf16[512,384]{1,0:T(8,128)(2,1)S(1)} collective-permute-done((bf16[512,384]{1,0:T(8,128)(2,1)S(1)}, bf16[512,384]{1,0:T(8,128)(2,1)S(1)}, u32[]{:S(2)}, u32[]{:S(2)}) %collective-permute-start.2) | collective-permute-done | bytes 393248 | tf_op jit(solution)/shard_map/ppermute | solution.py:71
  30.4 1.8 %constant_dynamic-update-slice_fusion.6 = bf16[512,3072]{1,0:T(8,128)(2,1)} fusion(bf16[512,3072]{1,0:T(8,128)(2,1)} %get-tuple-element.5, bf16[512,384]{1,0:T(8,128)(2,1)} %copy-done.2, s32[]{:T(128)S(6)} %select_n.98), kind=kLoop, calls=%fused_computation.86 | loop fusion | bytes 786436 | tf_op jit(solution)/shard_map/dynamic_update_slice | solution.py:73
  32.3 0.0 collective-permute-done.3
  32.3 3.3 %collective-permute-start.5 = (bf16[512,384]{1,0:T(8,128)(2,1)S(1)}, bf16[512,384]{1,0:T(8,128)(2,1)S(1)}, u32[]{:S(2)}, u32[]{:S(2)}) collective-permute-start(bf16[512,384]{1,0:T(8,128)(2,1)S(1)} %collective-permute-done.3), channel_id=1, source_target_pairs={{0,7},{1,0},{2,1},{3,2},{4,3},{5,4},{6,5},{7,6},{8,15},{9,8},{10,9... | collective-permute-start | bytes 1179656 | tf_op jit(solution)/shard_map/ppermute | solution.py:75
  35.6 1.8 %constant_dynamic-update-slice_fusion.5 = bf16[512,3072]{1,0:T(8,128)(2,1)} fusion(bf16[512,3072]{1,0:T(8,128)(2,1)} %constant_dynamic-update-slice_fusion.6, bf16[512,384]{1,0:T(8,128)(2,1)} %collective-permute-done.1, s32[]{:T(128)S(6)} %select_n.100), kind=kLoop, calls=%fused_computation.85 | loop fusion | bytes 786436 | tf_op jit(solution)/shard_map/dynamic_update_slice | solution.py:77
  37.4 3.6 %collective-permute-done.4 = bf16[512,384]{1,0:T(8,128)(2,1)S(1)} collective-permute-done((bf16[512,384]{1,0:T(8,128)(2,1)S(1)}, bf16[512,384]{1,0:T(8,128)(2,1)S(1)}, u32[]{:S(2)}, u32[]{:S(2)}) %collective-permute-start.4) | collective-permute-done | bytes 393248 | tf_op jit(solution)/shard_map/ppermute | solution.py:71
  41.1 0.9 constant_dynamic-update-slice_fusion.4
  42.0 0.9 constant_dynamic-update-slice_fusion.3
  42.9 0.9 constant_dynamic-update-slice_fusion.2
  43.7 0.8 constant_dynamic-update-slice_fusion.1
  44.6 6.3 %collective-permute-done.6 = bf16[512,384]{1,0:T(8,128)(2,1)S(1)} collective-permute-done((bf16[512,384]{1,0:T(8,128)(2,1)S(1)}, bf16[512,384]{1,0:T(8,128)(2,1)S(1)}, u32[]{:S(2)}, u32[]{:S(2)}) %collective-permute-start.6) | collective-permute-done | bytes 393248 | tf_op jit(solution)/shard_map/ppermute | solution.py:71
  50.8 0.8 constant_dynamic-update-slice_fusion
  51.7 0.0 collective-permute-start.7
  51.7 0.1 convert_reduce_fusion.1
  51.8 0.2 fusion.73
  52.1 0.2 fusion.76
  52.3 5.4 %collective-permute-done.7 = bf16[512,3072]{1,0:T(8,128)(2,1)} collective-permute-done((bf16[512,3072]{1,0:T(8,128)(2,1)}, bf16[512,3072]{1,0:T(8,128)(2,1)}, u32[]{:S(2)}, u32[]{:S(2)}) %collective-permute-start.7) | collective-permute-done | bytes 3145760 | tf_op jit(solution)/shard_map/ppermute | solution.py:90
  57.7 2.5 %fusion.94 = f32[128,3072]{1,0:T(8,128)S(1)} fusion(bf16[512,3072]{1,0:T(8,128)(2,1)} %collective-permute-done.7, bf16[128,1024]{1,0:T(8,128)(2,1)S(1)} %fusion.76, s32[]{:T(128)S(6)} %select_n.111), kind=kOutput, calls=%fused_computation.73 | convolution fusion | flops 402653184 | bytes 4849668 | tf_op jit(solution)/shard_map/dot_general | solution.py:47
  60.2 3.4 %fusion.10 = bf16[128,3072]{1,0:T(8,128)(2,1)} fusion(f32[128,3072]{1,0:T(8,128)S(1)} %fusion.94, bf16[512,3072]{1,0:T(8,128)(2,1)} %constant_dynamic-update-slice_fusion, bf16[128,1024]{1,0:T(8,128)(2,1)S(1)} %fusion.76, s32[]{:T(128)S(6)} %select_n.95), kind=kOutput, calls=%fused_computation.14 | convolution fusion | flops 403439616 | bytes 5636100 | tf_op jit(solution)/shard_map/dot_general | solution.py:47
  63.6 1.5 copy.19
  65.1 0.9 copy.20
  66.0 5.2 %all-to-all-start = ((bf16[16,3,64,128]{3,2,1,0:T(8,128)(2,1)}), bf16[16,3,64,128]{3,2,1,0:T(8,128)(2,1)S(1)}, u32[]{:S(2)}, u32[]{:S(2)}) async-start(bf16[16,3,64,128]{3,2,1,0:T(8,128)(2,1)} %copy.20), calls=%async_computation | async-start | bytes 1572864 | tf_op jit(solution)/shard_map/all_to_all | solution.py:52
  71.9 13.0 %all-to-all-done = bf16[16,3,64,128]{3,2,1,0:T(8,128)(2,1)S(1)} async-done(((bf16[16,3,64,128]{3,2,1,0:T(8,128)(2,1)}), bf16[16,3,64,128]{3,2,1,0:T(8,128)(2,1)S(1)}, u32[]{:S(2)}, u32[]{:S(2)}) %all-to-all-start) | async-done | bytes 786464 | tf_op jit(solution)/shard_map/all_to_all | solution.py:52
  84.9 0.1 fusion.106
  85.0 0.2 copy.21
  85.2 0.2 copy.23
  85.4 0.2 copy.22
  85.6 2.8 %select_reduce_fusion.1 = (f32[2048]{0:T(1024)S(1)}, f32[2048,2048]{0,1:T(8,128)S(1)}) fusion(pred[2048]{0:T(1024)(128)(4,1)S(1)} %iota_compare_fusion, bf16[8,8,16,128]{3,2,1,0:T(8,128)(2,1)S(1)} %bitcast.132, bf16[8,8,16,128]{3,2,1,0:T(8,128)(2,1)S(1)} %bitcast.134), kind=kOutput, calls=%fused_computation.3 | convolution fusion | flops 549451776 | bytes 17311744 | tf_op jit(solution)/shard_map/dq,dk->qk/dot_general | solution.py:25
  88.4 4.8 %fusion = f32[2048]{0:T(1024)S(1)} fusion(f32[2048,2048]{0,1:T(8,128)S(1)} %get-tuple-element.14, f32[2048]{0:T(1024)S(1)} %get-tuple-element.13, pred[2048]{0:T(1024)(128)(4,1)S(1)} %iota_compare_fusion), kind=kLoop, calls=%fused_computation.4 | loop fusion | flops 16775168 | bytes 16795648 | tf_op jit(solution)/shard_map/reduce_sum | solution.py:31
  93.2 0.0 copy-start.5
  93.2 0.0 copy-start.6
  93.2 3.1 %fusion.61 = bf16[8,16,8,128]{3,2,1,0:T(8,128)(2,1)S(1)} fusion(f32[2048,2048]{0,1:T(8,128)S(1)} %get-tuple-element.14, f32[2048]{0:T(1024)S(1)} %get-tuple-element.13, pred[2048]{0:T(1024)(128)(4,1)S(1)} %iota_compare_fusion, bf16[8,8,16,128]{3,2,1,0:T(8,128)(2,1)S(1)} %bitcast.140, f32[2048]{0:T(1024)S(1)} %fusion), kind=kOutput, calls=%fused_computation.35 | convolution fusion | flops 553910272 | bytes 17319936 | tf_op jit(solution)/shard_map/qk,dk->dq/dot_general | solution.py:32
  96.3 0.1 copy.74
  96.4 10.6 %all_to_all.40 = bf16[16,64,128]{2,1,0:T(8,128)(2,1)S(1)} all-to-all(bf16[16,64,128]{2,1,0:T(8,128)(2,1)S(1)} %bitcast.136), channel_id=1, replica_groups=mesh['pipe'=2,'ctx'=16,'dp'=8] {'ctx'}, dimensions={0} | all-to-all | bytes 524288 | tf_op jit(solution)/shard_map/all_to_all | solution.py:55
  107.0 0.5 fusion.49
  107.5 1.3 collective-permute-start.8
  108.8 9.9 %collective-permute-done.8 = bf16[128,1024]{1,0:T(8,128)(2,1)S(1)} collective-permute-done((bf16[128,1024]{1,0:T(8,128)(2,1)S(1)}, bf16[128,1024]{1,0:T(8,128)(2,1)S(1)}, u32[]{:S(2)}, u32[]{:S(2)}) %collective-permute-start.8) | collective-permute-done | bytes 262176 | tf_op jit(solution)/shard_map/ppermute | solution.py:100
  118.7 0.1 convert_reduce_fusion
  118.8 0.2 fusion.69
  119.1 0.2 fusion.72
  119.3 2.5 %fusion.91 = f32[128,3072]{1,0:T(8,128)S(1)} fusion(bf16[512,3072]{1,0:T(8,128)(2,1)} %collective-permute-done.7, bf16[128,1024]{1,0:T(8,128)(2,1)S(1)} %fusion.72, s32[]{:T(128)S(6)} %select_n.111), kind=kOutput, calls=%fused_computation.70 | convolution fusion | flops 402653184 | bytes 4849668 | tf_op jit(solution)/shard_map/dot_general | solution.py:47
  121.8 3.4 %fusion.11 = bf16[128,3072]{1,0:T(8,128)(2,1)} fusion(f32[128,3072]{1,0:T(8,128)S(1)} %fusion.91, bf16[512,3072]{1,0:T(8,128)(2,1)} %constant_dynamic-update-slice_fusion, bf16[128,1024]{1,0:T(8,128)(2,1)S(1)} %fusion.72, s32[]{:T(128)S(6)} %select_n.95), kind=kOutput, calls=%fused_computation.15 | convolution fusion | flops 403439616 | bytes 5636100 | tf_op jit(solution)/shard_map/dot_general | solution.py:47
  125.2 1.5 copy.25
  126.7 0.1 copy.26
  126.8 16.5 %all_to_all.41 = bf16[16,3,64,128]{3,2,1,0:T(8,128)(2,1)S(1)} all-to-all(bf16[16,3,64,128]{3,2,1,0:T(8,128)(2,1)S(1)} %copy.26), channel_id=1, replica_groups=mesh['pipe'=2,'ctx'=16,'dp'=8] {'ctx'}, dimensions={0} | all-to-all | bytes 1572864 | tf_op jit(solution)/shard_map/all_to_all | solution.py:52
  143.3 0.1 fusion.105
  143.4 0.2 copy.27
  143.6 0.2 copy.29
  143.8 0.2 copy.28
  143.9 2.8 %select_reduce_fusion = (f32[2048]{0:T(1024)S(1)}, f32[2048,2048]{0,1:T(8,128)S(1)}) fusion(pred[2048]{0:T(1024)(128)(4,1)S(1)} %iota_compare_fusion, bf16[8,8,16,128]{3,2,1,0:T(8,128)(2,1)S(1)} %bitcast.133, bf16[8,8,16,128]{3,2,1,0:T(8,128)(2,1)S(1)} %bitcast.135), kind=kOutput, calls=%fused_computation.1 | convolution fusion | flops 549451776 | bytes 17311744 | tf_op jit(solution)/shard_map/dq,dk->qk/dot_general | solution.py:25
  146.7 4.8 %fusion.2 = f32[2048]{0:T(1024)S(1)} fusion(f32[2048,2048]{0,1:T(8,128)S(1)} %get-tuple-element.16, f32[2048]{0:T(1024)S(1)} %get-tuple-element.15, pred[2048]{0:T(1024)(128)(4,1)S(1)} %iota_compare_fusion), kind=kLoop, calls=%fused_computation.6 | loop fusion | flops 16775168 | bytes 16795648 | tf_op jit(solution)/shard_map/reduce_sum | solution.py:31
  151.6 3.1 %fusion.58 = bf16[8,16,8,128]{3,2,1,0:T(8,128)(2,1)S(1)} fusion(f32[2048,2048]{0,1:T(8,128)S(1)} %get-tuple-element.16, f32[2048]{0:T(1024)S(1)} %get-tuple-element.15, pred[2048]{0:T(1024)(128)(4,1)S(1)} %iota_compare_fusion, bf16[8,8,16,128]{3,2,1,0:T(8,128)(2,1)S(1)} %bitcast.139, f32[2048]{0:T(1024)S(1)} %fusion.2), kind=kOutput, calls=%fused_computation.34 | convolution fusion | flops 553910272 | bytes 17319936 | tf_op jit(solution)/shard_map/qk,dk->dq/dot_general | solution.py:32
  154.7 0.8 copy.73
  155.5 3.5 %all-to-all-start.3 = ((bf16[16,64,128]{2,1,0:T(8,128)(2,1)}), bf16[16,64,128]{2,1,0:T(8,128)(2,1)S(1)}, u32[]{:S(2)}, u32[]{:S(2)}) async-start(bf16[16,64,128]{2,1,0:T(8,128)(2,1)} %bitcast.124), calls=%async_computation.3 | async-start | bytes 524288 | tf_op jit(solution)/shard_map/all_to_all | solution.py:55
  159.0 8.0 %all-to-all-done.3 = bf16[16,64,128]{2,1,0:T(8,128)(2,1)S(1)} async-done(((bf16[16,64,128]{2,1,0:T(8,128)(2,1)}), bf16[16,64,128]{2,1,0:T(8,128)(2,1)S(1)}, u32[]{:S(2)}, u32[]{:S(2)}) %all-to-all-start.3) | async-done | bytes 262176 | tf_op jit(solution)/shard_map/all_to_all | solution.py:55
  167.0 1.2 fusion.55
  (20 shorter events, 0.1 us)
Async XLA Ops:
  0.0 107.0 %copy-start = (bf16[1,1024,1024]{2,1,0:T(8,128)(2,1)S(1)}, bf16[1,1024,1024]{2,1,0:T(8,128)(2,1)}, u32[]{:S(2)}) copy-start(bf16[1,1024,1024]{2,1,0:T(8,128)(2,1)} %param.13) | copy-start | bytes 6291460
  2.1 49.6 %copy-start.1 = (bf16[1,1,128,1024]{3,2,1,0:T(8,128)(2,1)S(1)}, bf16[1,1,128,1024]{3,2,1,0:T(8,128)(2,1)}, u32[]{:S(2)}) copy-start(bf16[1,1,128,1024]{3,2,1,0:T(8,128)(2,1)} %param.8) | copy-start | bytes 786436
  2.1 50.0 %copy-start.3 = (f32[1,1024]{1,0:T(1,128)S(1)}, f32[1,1024]{1,0:T(1,128)}, u32[]{:S(2)}) copy-start(f32[1,1024]{1,0:T(1,128)} %param.11) | copy-start | bytes 12292
  2.1 50.0 %copy-start.4 = (f32[1,1024]{1,0:T(1,128)S(1)}, f32[1,1024]{1,0:T(1,128)}, u32[]{:S(2)}) copy-start(f32[1,1024]{1,0:T(1,128)} %param.10) | copy-start | bytes 12292
  4.0 14.9 %collective-permute-start = (bf16[512,384]{1,0:T(8,128)(2,1)S(1)}, bf16[512,384]{1,0:T(8,128)(2,1)S(1)}, u32[]{:S(2)}, u32[]{:S(2)}) collective-permute-start(bf16[512,384]{1,0:T(8,128)(2,1)S(1)} %get-tuple-element.6), channel_id=1, source_target_pairs={{0,1},{1,2},{2,3},{3,4},{4,5},{5,6},{6,7},{7,0},{8,9},{9,10},{10,1... | collective-permute-start | bytes 1179656 | tf_op jit(solution)/shard_map/ppermute | solution.py:71
  5.9 13.1 %collective-permute-start.1 = (bf16[512,384]{1,0:T(8,128)(2,1)S(1)}, bf16[512,384]{1,0:T(8,128)(2,1)}, u32[]{:S(2)}, u32[]{:S(2)}) collective-permute-start(bf16[512,384]{1,0:T(8,128)(2,1)S(1)} %get-tuple-element.6), channel_id=1, source_target_pairs={{0,7},{1,0},{2,1},{3,2},{4,3},{5,4},{6,5},{7,6},{8,15},{9,8},{10,9... | collective-permute-start | bytes 1179656 | tf_op jit(solution)/shard_map/ppermute | solution.py:75
  18.9 11.5 %copy-start.2 = (bf16[512,384]{1,0:T(8,128)(2,1)}, bf16[512,384]{1,0:T(8,128)(2,1)S(1)}, u32[]{:S(2)}) copy-start(bf16[512,384]{1,0:T(8,128)(2,1)S(1)} %collective-permute-done) | copy-start | bytes 1179652
  18.9 11.5 %collective-permute-start.2 = (bf16[512,384]{1,0:T(8,128)(2,1)S(1)}, bf16[512,384]{1,0:T(8,128)(2,1)S(1)}, u32[]{:S(2)}, u32[]{:S(2)}) collective-permute-start(bf16[512,384]{1,0:T(8,128)(2,1)S(1)} %collective-permute-done), channel_id=1, source_target_pairs={{0,1},{1,2},{2,3},{3,4},{4,5},{5,6},{6,7},{7,0},{8,9},{9,10},{10,1... | collective-permute-start | bytes 1179656 | tf_op jit(solution)/shard_map/ppermute | solution.py:71
  18.9 13.3 %collective-permute-start.3 = (bf16[512,384]{1,0:T(8,128)(2,1)}, bf16[512,384]{1,0:T(8,128)(2,1)S(1)}, u32[]{:S(2)}, u32[]{:S(2)}) collective-permute-start(bf16[512,384]{1,0:T(8,128)(2,1)} %collective-permute-done.1), channel_id=1, source_target_pairs={{0,7},{1,0},{2,1},{3,2},{4,3},{5,4},{6,5},{7,6},{8,15},{9,8},{10,9... | collective-permute-start | bytes 1179656 | tf_op jit(solution)/shard_map/ppermute | solution.py:75
  30.4 10.6 %collective-permute-start.4 = (bf16[512,384]{1,0:T(8,128)(2,1)S(1)}, bf16[512,384]{1,0:T(8,128)(2,1)S(1)}, u32[]{:S(2)}, u32[]{:S(2)}) collective-permute-start(bf16[512,384]{1,0:T(8,128)(2,1)S(1)} %collective-permute-done.2), channel_id=1, source_target_pairs={{0,1},{1,2},{2,3},{3,4},{4,5},{5,6},{6,7},{7,0},{8,9},{9,10},{10,1... | collective-permute-start | bytes 1179656 | tf_op jit(solution)/shard_map/ppermute | solution.py:71
  32.3 11.5 %collective-permute-start.5 = (bf16[512,384]{1,0:T(8,128)(2,1)S(1)}, bf16[512,384]{1,0:T(8,128)(2,1)S(1)}, u32[]{:S(2)}, u32[]{:S(2)}) collective-permute-start(bf16[512,384]{1,0:T(8,128)(2,1)S(1)} %collective-permute-done.3), channel_id=1, source_target_pairs={{0,7},{1,0},{2,1},{3,2},{4,3},{5,4},{6,5},{7,6},{8,15},{9,8},{10,9... | collective-permute-start | bytes 1179656 | tf_op jit(solution)/shard_map/ppermute | solution.py:75
  41.1 9.8 %collective-permute-start.6 = (bf16[512,384]{1,0:T(8,128)(2,1)S(1)}, bf16[512,384]{1,0:T(8,128)(2,1)S(1)}, u32[]{:S(2)}, u32[]{:S(2)}) collective-permute-start(bf16[512,384]{1,0:T(8,128)(2,1)S(1)} %collective-permute-done.4), channel_id=1, source_target_pairs={{0,1},{1,2},{2,3},{3,4},{4,5},{5,6},{6,7},{7,0},{8,9},{9,10},{10,1... | collective-permute-start | bytes 1179656 | tf_op jit(solution)/shard_map/ppermute | solution.py:71
  51.7 6.0 %collective-permute-start.7 = (bf16[512,3072]{1,0:T(8,128)(2,1)}, bf16[512,3072]{1,0:T(8,128)(2,1)}, u32[]{:S(2)}, u32[]{:S(2)}) collective-permute-start(bf16[512,3072]{1,0:T(8,128)(2,1)} %constant_dynamic-update-slice_fusion), channel_id=1, source_target_pairs={{0,8},{8,0},{16,24},{24,16},{32,40},{40,32},{48,56},{56,48},{64,72... | collective-permute-start | bytes 9437192 | tf_op jit(solution)/shard_map/ppermute | solution.py:90
  66.0 18.9 %all-to-all-start = ((bf16[16,3,64,128]{3,2,1,0:T(8,128)(2,1)}), bf16[16,3,64,128]{3,2,1,0:T(8,128)(2,1)S(1)}, u32[]{:S(2)}, u32[]{:S(2)}) async-start(bf16[16,3,64,128]{3,2,1,0:T(8,128)(2,1)} %copy.20), calls=%async_computation | async-start | bytes 1572864 | tf_op jit(solution)/shard_map/all_to_all | solution.py:52
  93.2 13.9 %copy-start.5 = (f32[1,1024]{1,0:T(1,128)S(1)}, f32[1,1024]{1,0:T(1,128)}, u32[]{:S(2)}) copy-start(f32[1,1024]{1,0:T(1,128)} %param.14) | copy-start | bytes 12292
  93.2 13.8 %copy-start.6 = (f32[1,1024]{1,0:T(1,128)S(1)}, f32[1,1024]{1,0:T(1,128)}, u32[]{:S(2)}) copy-start(f32[1,1024]{1,0:T(1,128)} %param.15) | copy-start | bytes 12292
  107.5 11.2 %collective-permute-start.8 = (bf16[128,1024]{1,0:T(8,128)(2,1)S(1)}, bf16[128,1024]{1,0:T(8,128)(2,1)S(1)}, u32[]{:S(2)}, u32[]{:S(2)}) collective-permute-start(bf16[128,1024]{1,0:T(8,128)(2,1)S(1)} %fusion.49), channel_id=1, source_target_pairs={{0,128},{1,129},{2,130},{3,131},{4,132},{5,133},{6,134},{7,135},{8... | collective-permute-start | bytes 786440 | tf_op jit(solution)/shard_map/ppermute | solution.py:100
  155.5 11.5 %all-to-all-start.3 = ((bf16[16,64,128]{2,1,0:T(8,128)(2,1)}), bf16[16,64,128]{2,1,0:T(8,128)(2,1)S(1)}, u32[]{:S(2)}, u32[]{:S(2)}) async-start(bf16[16,64,128]{2,1,0:T(8,128)(2,1)} %bitcast.124), calls=%async_computation.3 | async-start | bytes 524288 | tf_op jit(solution)/shard_map/all_to_all | solution.py:55

commit v4 on v2

--- a/solution.py
+++ b/solution.py
@@ -35,20 +35,22 @@
     return (context / totals[None, :]).astype(jnp.bfloat16)
 
 
-def sublayer(current, length, qkv_mine, qkv_other, out_full, gain, shift, out_shift, layer_scale):
+def sublayer(current, length, qkv_mine, qkv_other, out_full, gain, shift, out_shift, layer_scale,
+             projected=None):
     tok_rows, width = current.shape
     head_width = width // HEADS
     ctx_count = lax.axis_size("ctx")
     core = lax.axis_index("ctx") % 2
     half = width // 2
-    normed = normalize(current, gain, shift)
-    normed_mine = lax.dynamic_slice_in_dim(normed, core * half, half, axis=1)
-    normed_other = lax.dynamic_slice_in_dim(normed, (1 - core) * half, half, axis=1)
-    projected = jnp.dot(normed_mine, qkv_mine, preferred_element_type=jnp.float32) + jnp.dot(
-        normed_other, qkv_other, preferred_element_type=jnp.float32
-    )
+    if projected is None:
+        normed = normalize(current, gain, shift)
+        normed_mine = lax.dynamic_slice_in_dim(normed, core * half, half, axis=1)
+        normed_other = lax.dynamic_slice_in_dim(normed, (1 - core) * half, half, axis=1)
+        projected = jnp.dot(normed_mine, qkv_mine, preferred_element_type=jnp.float32) + jnp.dot(
+            normed_other, qkv_other, preferred_element_type=jnp.float32
+        )
+        projected = unrotate(projected.astype(jnp.bfloat16), "dp")
     projected = jnp.transpose(projected.reshape(tok_rows, 3, HEADS, head_width), (2, 1, 3, 0))
-    projected = projected.astype(jnp.bfloat16)
     gathered = lax.all_to_all(projected, "ctx", 0, 3, tiled=True)
     context = head_attention(gathered[0], length, head_width ** (-0.5))
     context = jnp.transpose(context.reshape(head_width, ctx_count, tok_rows), (1, 0, 2))
@@ -58,6 +60,33 @@
     return (current.astype(jnp.float32) + layer_scale * mixed).astype(jnp.bfloat16)
 
 
+def ring_gather(piece, axis, on_block):
+    count = lax.axis_size(axis)
+    right = [(i, (i + 1) % count) for i in range(count)]
+    left = [(i, (i - 1) % count) for i in range(count)]
+    blocks = [None] * count
+    made = [None] * count
+    blocks[0], made[0] = piece, on_block(piece)
+    forward, backward = piece, piece
+    for step in range(count // 2):
+        forward = lax.ppermute(forward, axis, right)
+        k = count - 1 - step
+        blocks[k], made[k] = forward, on_block(forward)
+        if step < (count - 1) // 2:
+            backward = lax.ppermute(backward, axis, left)
+            k = 1 + step
+            blocks[k], made[k] = backward, on_block(backward)
+    return jnp.concatenate(blocks, axis=1), jnp.concatenate(made, axis=1)
+
+
+def unrotate(rotated, axis):
+    count = lax.axis_size(axis)
+    cols = rotated.shape[1]
+    shift = lax.axis_index(axis) * (cols // count)
+    doubled = jnp.concatenate([rotated, rotated], axis=1)
+    return lax.dynamic_slice_in_dim(doubled, cols - shift, cols, axis=1)
+
+
 def per_device(patches, lengths, norm_gain, norm_bias, w_qkv, w_out, out_bias, scale_gain):
     section_index = lax.axis_index("pipe")
     section_count = lax.axis_size("pipe")
@@ -65,15 +94,23 @@
     width = w_qkv.shape[1]
     half = width // 2
     rows_mine = lax.dynamic_slice_in_dim(w_qkv[0], core * half, half, axis=0)
-    qkv_mine = lax.all_gather(rows_mine, "dp", axis=1, tiled=True)
     sibling = [(i, i ^ 1) for i in range(lax.axis_size("ctx"))]
+    current = patches[0, 0]
+    normed = normalize(current, norm_gain[0], norm_bias[0])
+    both = jnp.concatenate([normed, lax.ppermute(normed, "ctx", sibling)], axis=0)
+    both = lax.dynamic_slice_in_dim(both, core * half, half, axis=1)
+    qkv_mine, partial = ring_gather(
+        rows_mine, "dp", lambda block: jnp.dot(both, block, preferred_element_type=jnp.float32)
+    )
+    tok_rows = current.shape[0]
+    partial_other = lax.ppermute(partial[tok_rows:], "ctx", sibling)
+    first = unrotate((partial[:tok_rows] + partial_other).astype(jnp.bfloat16), "dp")
     qkv_other = lax.ppermute(qkv_mine, "ctx", sibling)
     args = (qkv_mine, qkv_other, w_out[0], norm_gain[0], norm_bias[0], out_bias[0], scale_gain[0])
     length = lengths[0, 0]
-    current = patches[0, 0]
     outputs = []
     for turn_index in range(section_count):
-        produced = sublayer(current, length, *args)
+        produced = sublayer(current, length, *args, projected=first if turn_index == 0 else None)
         outputs.append(produced)
         if turn_index + 1 < section_count:
             pairs = [(i, i + 1) for i in range(section_count - 1)]

time: 178 us -> 165 us (0.927)
  waiting for transfers between devices: 80.3 us -> 54.5 us
  local copies, waits for them, and re-layouts: 7.97 us -> 22.6 us
  starting transfers between devices: 10.1 us -> 23.4 us
  between operations: 14.3 us -> 1.12 us
  matrix products: 23.5 us -> 19 us
  other arithmetic: 13.7 us -> 16.6 us
    all_gather x1 -> x0, waiting for transfers between devices: 49.5 us -> none  [per_device(): qkv_mine = lax.all_gather(rows_mine, 'dp', axis=1, tiled=True)]
    ppermute x0 -> x9, waiting for transfers between devices: none -> 33.3 us  [the longest x4 23.8 us: ring_gather(): forward = lax.ppermute(forward, axis, right)]
    ppermute x0 -> x9, starting transfers between devices: none -> 13 us  [the longest x3 12.9 us: ring_gather(): backward = lax.ppermute(backward, axis, left)]
    unnamed x14 -> x39, local copies, waits for them, and re-layouts: 0.04 us -> 12.8 us
    all_to_all x1, waiting for transfers between devices: 13.1 us -> 3.4 us  [sublayer(): gathered = lax.all_to_all(projected, 'ctx', 0, 3, tiled=True)]
    dot_general x2 -> x1, matrix products: 6.83 us -> 2.48 us  [sublayer(): jnp.dot(normed_other, qkv_other, preferred_element_type=jnp.float32)]
    convert_element_type x4 -> x0, local copies, waits for them, and re-layouts: 4 us -> none  [sublayer(): projected = projected.astype(jnp.bfloat16)]
    transpose x0 -> x2, local copies, waits for them, and re-layouts: none -> 3.27 us  [sublayer(): jnp.transpose(projected.reshape(tok_rows, 3, HEADS, head_width), (2, 1, 3...]
  transfers between devices with their start and end apart: 5 -> 13, of which waited for: 4 -> 10; matrix products, arithmetic and copies ran while one was open for 3% -> 16% of each run, Pallas kernels for 0% -> 0%
where the time goes in v4:
time: 165 us; the launch traced here: 164 us
  waiting for transfers between devices  54.5 us (33%)
  blocking collectives  27.2 us (16%)
  starting transfers between devices  23.4 us (14%)
  local copies, waits for them, and re-layouts  22.6 us (14%)
  matrix products  19 us (12%)
  other arithmetic  16.6 us (10%)
    ppermute x4, waiting for transfers between devices, ring_gather(): forward = lax.ppermute(forward, axis, right)  23.8 us
    all_to_all x1, blocking collectives, sublayer(): gathered = lax.all_to_all(projected, 'ctx', 0, 3, tiled=True)  16.5 us
    ppermute x3, starting transfers between devices, ring_gather(): backward = lax.ppermute(backward, axis, left)  12.9 us
    unnamed x39, local copies, waits for them, and re-layouts  12.8 us
    all_to_all x1, blocking collectives, sublayer(): lax.all_to_all(context, 'ctx', 0, 0, tiled=True).reshape(width, tok_rows)  10.6 us
    ppermute x1, waiting for transfers between devices, per_device(): current = lax.ppermute(produced, 'pipe', pairs)  9.86 us
    reduce_sum x2, other arithmetic, head_attention(): totals = jnp.sum(weights, axis=-1)  9.64 us
    all_to_all x1, waiting for transfers between devices, sublayer(): lax.all_to_all(context, 'ctx', 0, 0, tiled=True).reshape(width, tok_rows)  7.98 us
  transfers between devices with their start and end apart: 13, of which 10 were waited for; matrix products, arithmetic and copies ran while one was open for 16% of the time, Pallas kernels for 0%

profile of v4, /device:TPU:4, one launch (start us, length us, event | category | flops | bytes accessed | tf_op | source)
XLA Modules:
  0.0 164.3 jit_solution(10848570941880427701)
XLA Ops:
  0.0 2.0 %constant_dynamic-update-slice_fusion.7 = (bf16[512,3072]{1,0:T(8,128)(2,1)}, bf16[512,384]{1,0:T(8,128)(2,1)S(1)}) fusion(bf16[1,1024,384]{2,1,0:T(8,128)(2,1)} %param.12, s32[]{:T(128)S(6)} %select_n.44), kind=kLoop, calls=%fused_computation.97 | loop fusion | bytes 1179652
  2.0 5.9 %collective-permute-start.1 = (bf16[512,384]{1,0:T(8,128)(2,1)S(1)}, bf16[512,384]{1,0:T(8,128)(2,1)S(1)}, u32[]{:S(2)}, u32[]{:S(2)}) collective-permute-start(bf16[512,384]{1,0:T(8,128)(2,1)S(1)} %get-tuple-element.6), channel_id=1, source_target_pairs={{0,7},{1,0},{2,1},{3,2},{4,3},{5,4},{6,5},{7,6},{8,15},{9,8},{10,9... | collective-permute-start | bytes 1179656 | tf_op jit(solution)/shard_map/ppermute | solution.py:76
  7.9 1.1 convert_reduce_fusion.1
  8.9 1.2 fusion.75
  10.1 9.5 %collective-permute-done.4 = bf16[512,384]{1,0:T(8,128)(2,1)S(1)} collective-permute-done((bf16[512,384]{1,0:T(8,128)(2,1)S(1)}, bf16[512,384]{1,0:T(8,128)(2,1)S(1)}, u32[]{:S(2)}, u32[]{:S(2)}) %collective-permute-start.4) | collective-permute-done | bytes 393248 | tf_op jit(solution)/shard_map/ppermute | solution.py:72
  19.7 1.2 fusion.78
  21.0 3.3 %collective-permute-start.2 = (bf16[512,384]{1,0:T(8,128)(2,1)S(1)}, bf16[512,384]{1,0:T(8,128)(2,1)S(1)}, u32[]{:S(2)}, u32[]{:S(2)}) collective-permute-start(bf16[512,384]{1,0:T(8,128)(2,1)S(1)} %collective-permute-done.1), channel_id=1, source_target_pairs={{0,7},{1,0},{2,1},{3,2},{4,3},{5,4},{6,5},{7,6},{8,15},{9,8},{10,9... | collective-permute-start | bytes 1179656 | tf_op jit(solution)/shard_map/ppermute | solution.py:76
  24.3 6.3 %collective-permute-done.5 = bf16[512,384]{1,0:T(8,128)(2,1)S(1)} collective-permute-done((bf16[512,384]{1,0:T(8,128)(2,1)S(1)}, bf16[512,384]{1,0:T(8,128)(2,1)S(1)}, u32[]{:S(2)}, u32[]{:S(2)}) %collective-permute-start.5) | collective-permute-done | bytes 393248 | tf_op jit(solution)/shard_map/ppermute | solution.py:72
  30.6 0.3 convolution_dynamic-update-slice_fusion.7
  30.9 2.4 %collective-permute-done.2 = bf16[512,384]{1,0:T(8,128)(2,1)S(1)} collective-permute-done((bf16[512,384]{1,0:T(8,128)(2,1)S(1)}, bf16[512,384]{1,0:T(8,128)(2,1)S(1)}, u32[]{:S(2)}, u32[]{:S(2)}) %collective-permute-start.2) | collective-permute-done | bytes 393248 | tf_op jit(solution)/shard_map/ppermute | solution.py:76
  33.2 3.7 %collective-permute-start.3 = (bf16[512,384]{1,0:T(8,128)(2,1)S(1)}, bf16[512,384]{1,0:T(8,128)(2,1)S(1)}, u32[]{:S(2)}, u32[]{:S(2)}) collective-permute-start(bf16[512,384]{1,0:T(8,128)(2,1)S(1)} %collective-permute-done.2), channel_id=1, source_target_pairs={{0,7},{1,0},{2,1},{3,2},{4,3},{5,4},{6,5},{7,6},{8,15},{9,8},{10,9... | collective-permute-start | bytes 1179656 | tf_op jit(solution)/shard_map/ppermute | solution.py:76
  36.9 0.3 convolution_dynamic-update-slice_fusion.6
  37.2 3.4 %collective-permute-done.6 = bf16[512,384]{1,0:T(8,128)(2,1)S(1)} collective-permute-done((bf16[512,384]{1,0:T(8,128)(2,1)S(1)}, bf16[512,384]{1,0:T(8,128)(2,1)S(1)}, u32[]{:S(2)}, u32[]{:S(2)}) %collective-permute-start.6) | collective-permute-done | bytes 393248 | tf_op jit(solution)/shard_map/ppermute | solution.py:72
  40.7 0.3 convolution_dynamic-update-slice_fusion.5
  41.0 4.1 %collective-permute-done.3 = bf16[512,384]{1,0:T(8,128)(2,1)S(1)} collective-permute-done((bf16[512,384]{1,0:T(8,128)(2,1)S(1)}, bf16[512,384]{1,0:T(8,128)(2,1)S(1)}, u32[]{:S(2)}, u32[]{:S(2)}) %collective-permute-start.3) | collective-permute-done | bytes 393248 | tf_op jit(solution)/shard_map/ppermute | solution.py:76
  45.0 0.3 convolution_dynamic-update-slice_fusion.4
  45.3 4.6 %collective-permute-done.7 = bf16[512,384]{1,0:T(8,128)(2,1)S(1)} collective-permute-done((bf16[512,384]{1,0:T(8,128)(2,1)S(1)}, bf16[512,384]{1,0:T(8,128)(2,1)S(1)}, u32[]{:S(2)}, u32[]{:S(2)}) %collective-permute-start.7) | collective-permute-done | bytes 393248 | tf_op jit(solution)/shard_map/ppermute | solution.py:72
  49.9 0.3 convolution_dynamic-update-slice_fusion.3
  50.2 0.3 convolution_dynamic-update-slice_fusion.2
  50.5 0.3 convolution_dynamic-update-slice_fusion.1
  50.8 0.3 convolution_dynamic-update-slice_fusion
  51.1 1.7 %copy-done.3 = f32[256,3072]{1,0:T(8,128)} copy-done((f32[256,3072]{1,0:T(8,128)}, f32[256,3072]{1,0:T(8,128)S(1)}, u32[]{:S(2)}) %copy-start.3) | copy-done | bytes 3145752
  52.8 1.3 slice.39
  54.8 3.1 %collective-permute-done.8 = f32[128,3072]{1,0:T(8,128)} collective-permute-done((f32[128,3072]{1,0:T(8,128)}, f32[128,3072]{1,0:T(8,128)}, u32[]{:S(2)}, u32[]{:S(2)}) %collective-permute-start.8) | collective-permute-done | bytes 1572896 | tf_op jit(solution)/shard_map/ppermute | solution.py:106
  57.9 2.0 %fusion.27 = bf16[128,3072]{1,0:T(8,128)(2,1)S(1)} fusion(f32[128,3072]{1,0:T(8,128)} %collective-permute-done.8, f32[256,3072]{1,0:T(8,128)} %copy-done.3), kind=kLoop, calls=%fused_computation.23 | loop fusion | flops 786432 | bytes 3932160 | tf_op jit(solution)/shard_map/convert_element_type | solution.py:107
  60.0 0.4 fusion.65
  60.4 1.2 copy.19
  61.6 2.1 %copy.20 = bf16[16,3,64,128]{3,2,1,0:T(8,128)(2,1)} copy(bf16[16,3,64,128]{3,2,0,1:T(8,128)(2,1)} %bitcast.144) | data formatting | bytes 1572864 | tf_op jit(solution)/shard_map/transpose | solution.py:53
  63.7 5.2 %all-to-all-start = ((bf16[16,3,64,128]{3,2,1,0:T(8,128)(2,1)}), bf16[16,3,64,128]{3,2,1,0:T(8,128)(2,1)S(1)}, u32[]{:S(2)}, u32[]{:S(2)}) async-start(bf16[16,3,64,128]{3,2,1,0:T(8,128)(2,1)} %copy.20), calls=%async_computation | async-start | bytes 1572864 | tf_op jit(solution)/shard_map/all_to_all | solution.py:54
  68.9 1.9 %constant_dynamic-update-slice_fusion.6 = bf16[512,3072]{1,0:T(8,128)(2,1)} fusion(bf16[512,3072]{1,0:T(8,128)(2,1)} %get-tuple-element.5, bf16[512,384]{1,0:T(8,128)(2,1)} %copy-done.4), kind=kLoop, calls=%fused_computation.96 | loop fusion | bytes 786432
  70.8 1.8 %constant_dynamic-update-slice_fusion.5 = bf16[512,3072]{1,0:T(8,128)(2,1)} fusion(bf16[512,3072]{1,0:T(8,128)(2,1)} %constant_dynamic-update-slice_fusion.6, bf16[512,384]{1,0:T(8,128)(2,1)} %copy-done.7), kind=kLoop, calls=%fused_computation.95 | loop fusion | bytes 786432
  72.6 1.8 %constant_dynamic-update-slice_fusion.4 = bf16[512,3072]{1,0:T(8,128)(2,1)} fusion(bf16[512,3072]{1,0:T(8,128)(2,1)} %constant_dynamic-update-slice_fusion.5, bf16[512,384]{1,0:T(8,128)(2,1)} %copy-done.10), kind=kLoop, calls=%fused_computation.94 | loop fusion | bytes 786432
  74.4 1.8 %constant_dynamic-update-slice_fusion.3 = bf16[512,3072]{1,0:T(8,128)(2,1)} fusion(bf16[512,3072]{1,0:T(8,128)(2,1)} %constant_dynamic-update-slice_fusion.4, bf16[512,384]{1,0:T(8,128)(2,1)} %copy-done.11), kind=kLoop, calls=%fused_computation.93 | loop fusion | bytes 786432
  76.3 0.8 constant_dynamic-update-slice_fusion.2
  77.1 0.8 constant_dynamic-update-slice_fusion.1
  78.0 0.8 constant_dynamic-update-slice_fusion
  78.8 0.4 collective-permute-start.10
  79.2 3.4 %all-to-all-done = bf16[16,3,64,128]{3,2,1,0:T(8,128)(2,1)S(1)} async-done(((bf16[16,3,64,128]{3,2,1,0:T(8,128)(2,1)}), bf16[16,3,64,128]{3,2,1,0:T(8,128)(2,1)S(1)}, u32[]{:S(2)}, u32[]{:S(2)}) %all-to-all-start) | async-done | bytes 786464 | tf_op jit(solution)/shard_map/all_to_all | solution.py:54
  82.6 0.2 copy.22
  82.8 0.2 copy.23
  83.0 2.8 %select_reduce_fusion.1 = (f32[2048]{0:T(1024)S(1)}, f32[2048,2048]{0,1:T(8,128)S(1)}) fusion(pred[2048]{0:T(1024)(128)(4,1)S(1)} %iota_compare_fusion, bf16[8,8,16,128]{3,2,1,0:T(8,128)(2,1)S(1)} %bitcast.149, bf16[8,8,16,128]{3,2,1,0:T(8,128)(2,1)S(1)} %bitcast.148), kind=kOutput, calls=%fused_computation.3 | convolution fusion | flops 549451776 | bytes 17311744 | tf_op jit(solution)/shard_map/dq,dk->qk/dot_general | solution.py:25
  85.8 4.8 %fusion = f32[2048]{0:T(1024)S(1)} fusion(f32[2048,2048]{0,1:T(8,128)S(1)} %get-tuple-element.14, f32[2048]{0:T(1024)S(1)} %get-tuple-element.13, pred[2048]{0:T(1024)(128)(4,1)S(1)} %iota_compare_fusion), kind=kLoop, calls=%fused_computation.4 | loop fusion | flops 16775168 | bytes 16795648 | tf_op jit(solution)/shard_map/reduce_sum | solution.py:31
  90.6 0.2 copy.21
  90.9 3.1 %fusion.61 = bf16[8,16,8,128]{3,2,1,0:T(8,128)(2,1)S(1)} fusion(f32[2048,2048]{0,1:T(8,128)S(1)} %get-tuple-element.14, f32[2048]{0:T(1024)S(1)} %get-tuple-element.13, pred[2048]{0:T(1024)(128)(4,1)S(1)} %iota_compare_fusion, bf16[8,8,16,128]{3,2,1,0:T(8,128)(2,1)S(1)} %bitcast.154, f32[2048]{0:T(1024)S(1)} %fusion), kind=kOutput, calls=%fused_computation.47 | convolution fusion | flops 553910272 | bytes 17319936 | tf_op jit(solution)/shard_map/qk,dk->dq/dot_general | solution.py:32
  94.1 10.6 %all_to_all.40 = bf16[16,64,128]{2,1,0:T(8,128)(2,1)S(1)} all-to-all(bf16[16,64,128]{2,1,0:T(8,128)(2,1)S(1)} %bitcast.150), channel_id=1, replica_groups=mesh['pipe'=2,'ctx'=16,'dp'=8] {'ctx'}, dimensions={0} | all-to-all | bytes 524288 | tf_op jit(solution)/shard_map/all_to_all | solution.py:57
  104.7 0.5 fusion.49
  105.2 1.3 collective-permute-start.9
  106.5 9.9 %collective-permute-done.9 = bf16[128,1024]{1,0:T(8,128)(2,1)S(1)} collective-permute-done((bf16[128,1024]{1,0:T(8,128)(2,1)S(1)}, bf16[128,1024]{1,0:T(8,128)(2,1)S(1)}, u32[]{:S(2)}, u32[]{:S(2)}) %collective-permute-start.9) | collective-permute-done | bytes 262176 | tf_op jit(solution)/shard_map/ppermute | solution.py:117
  116.5 0.2 fusion.71
  116.8 0.2 fusion.74
  117.0 2.5 %fusion.94 = f32[128,3072]{1,0:T(8,128)S(1)} fusion(bf16[512,3072]{1,0:T(8,128)(2,1)} %collective-permute-done.10, bf16[128,1024]{1,0:T(8,128)(2,1)S(1)} %fusion.74, s32[]{:T(128)S(6)} %select_n.48), kind=kOutput, calls=%fused_computation.87 | convolution fusion | flops 402653184 | bytes 4849668 | tf_op jit(solution)/shard_map/dot_general | solution.py:49
  119.5 0.6 fusion.10
  120.1 0.4 fusion.64
  120.5 1.2 copy.25
  121.7 1.2 copy.26
  122.9 16.5 %all_to_all.41 = bf16[16,3,64,128]{3,2,1,0:T(8,128)(2,1)S(1)} all-to-all(bf16[16,3,64,128]{3,2,1,0:T(8,128)(2,1)S(1)} %copy.26), channel_id=1, replica_groups=mesh['pipe'=2,'ctx'=16,'dp'=8] {'ctx'}, dimensions={0} | all-to-all | bytes 1572864 | tf_op jit(solution)/shard_map/all_to_all | solution.py:54
  139.9 0.2 copy.27
  140.0 2.8 %select_reduce_fusion = (f32[2048]{0:T(1024)S(1)}, f32[2048,2048]{0,1:T(8,128)S(1)}) fusion(pred[2048]{0:T(1024)(128)(4,1)S(1)} %iota_compare_fusion, bf16[8,8,16,128]{3,2,1,0:T(8,128)(2,1)S(1)} %bitcast.147, bf16[8,8,16,128]{3,2,1,0:T(8,128)(2,1)S(1)} %bitcast.146), kind=kOutput, calls=%fused_computation.1 | convolution fusion | flops 549451776 | bytes 17311744 | tf_op jit(solution)/shard_map/dq,dk->qk/dot_general | solution.py:25
  142.8 4.8 %fusion.2 = f32[2048]{0:T(1024)S(1)} fusion(f32[2048,2048]{0,1:T(8,128)S(1)} %get-tuple-element.16, f32[2048]{0:T(1024)S(1)} %get-tuple-element.15, pred[2048]{0:T(1024)(128)(4,1)S(1)} %iota_compare_fusion), kind=kLoop, calls=%fused_computation.6 | loop fusion | flops 16775168 | bytes 16795648 | tf_op jit(solution)/shard_map/reduce_sum | solution.py:31
  147.7 3.1 %fusion.58 = bf16[8,16,8,128]{3,2,1,0:T(8,128)(2,1)S(1)} fusion(f32[2048,2048]{0,1:T(8,128)S(1)} %get-tuple-element.16, f32[2048]{0:T(1024)S(1)} %get-tuple-element.15, pred[2048]{0:T(1024)(128)(4,1)S(1)} %iota_compare_fusion, bf16[8,8,16,128]{3,2,1,0:T(8,128)(2,1)S(1)} %bitcast.153, f32[2048]{0:T(1024)S(1)} %fusion.2), kind=kOutput, calls=%fused_computation.46 | convolution fusion | flops 553910272 | bytes 17319936 | tf_op jit(solution)/shard_map/qk,dk->dq/dot_general | solution.py:32
  150.8 0.8 copy.73
  151.6 3.5 %all-to-all-start.3 = ((bf16[16,64,128]{2,1,0:T(8,128)(2,1)}), bf16[16,64,128]{2,1,0:T(8,128)(2,1)S(1)}, u32[]{:S(2)}, u32[]{:S(2)}) async-start(bf16[16,64,128]{2,1,0:T(8,128)(2,1)} %bitcast.138), calls=%async_computation.3 | async-start | bytes 524288 | tf_op jit(solution)/shard_map/all_to_all | solution.py:57
  155.1 8.0 %all-to-all-done.3 = bf16[16,64,128]{2,1,0:T(8,128)(2,1)S(1)} async-done(((bf16[16,64,128]{2,1,0:T(8,128)(2,1)}), bf16[16,64,128]{2,1,0:T(8,128)(2,1)S(1)}, u32[]{:S(2)}, u32[]{:S(2)}) %all-to-all-start.3) | async-done | bytes 262176 | tf_op jit(solution)/shard_map/all_to_all | solution.py:57
  163.1 1.2 fusion.55
  (52 shorter events, 0.9 us)
Async XLA Ops:
  0.0 104.7 %copy-start = (bf16[1,1024,1024]{2,1,0:T(8,128)(2,1)S(1)}, bf16[1,1024,1024]{2,1,0:T(8,128)(2,1)}, u32[]{:S(2)}) copy-start(bf16[1,1024,1024]{2,1,0:T(8,128)(2,1)} %param.13) | copy-start | bytes 6291460
  2.0 19.0 %collective-permute-start.1 = (bf16[512,384]{1,0:T(8,128)(2,1)S(1)}, bf16[512,384]{1,0:T(8,128)(2,1)S(1)}, u32[]{:S(2)}, u32[]{:S(2)}) collective-permute-start(bf16[512,384]{1,0:T(8,128)(2,1)S(1)} %get-tuple-element.6), channel_id=1, source_target_pairs={{0,7},{1,0},{2,1},{3,2},{4,3},{5,4},{6,5},{7,6},{8,15},{9,8},{10,9... | collective-permute-start | bytes 1179656 | tf_op jit(solution)/shard_map/ppermute | solution.py:76
  7.9 11.8 %collective-permute-start.4 = (bf16[512,384]{1,0:T(8,128)(2,1)S(1)}, bf16[512,384]{1,0:T(8,128)(2,1)S(1)}, u32[]{:S(2)}, u32[]{:S(2)}) collective-permute-start(bf16[512,384]{1,0:T(8,128)(2,1)S(1)} %get-tuple-element.6), channel_id=1, source_target_pairs={{0,1},{1,2},{2,3},{3,4},{4,5},{5,6},{6,7},{7,0},{8,9},{9,10},{10,1... | collective-permute-start | bytes 1179656 | tf_op jit(solution)/shard_map/ppermute | solution.py:72
  19.7 10.9 %collective-permute-start.5 = (bf16[512,384]{1,0:T(8,128)(2,1)S(1)}, bf16[512,384]{1,0:T(8,128)(2,1)S(1)}, u32[]{:S(2)}, u32[]{:S(2)}) collective-permute-start(bf16[512,384]{1,0:T(8,128)(2,1)S(1)} %collective-permute-done.4), channel_id=1, source_target_pairs={{0,1},{1,2},{2,3},{3,4},{4,5},{5,6},{6,7},{7,0},{8,9},{9,10},{10,1... | collective-permute-start | bytes 1179656 | tf_op jit(solution)/shard_map/ppermute | solution.py:72
  20.9 3.4 %collective-permute-start = (bf16[128,1024]{1,0:T(8,128)(2,1)S(1)}, bf16[128,1024]{1,0:T(8,128)(2,1)S(1)}, u32[]{:S(2)}, u32[]{:S(2)}) collective-permute-start(bf16[128,1024]{1,0:T(8,128)(2,1)S(1)} %fusion.78), channel_id=1, source_target_pairs={{0,8},{8,0},{16,24},{24,16},{32,40},{40,32},{48,56},{56,48},{64,72... | collective-permute-start | bytes 786440 | tf_op jit(solution)/shard_map/ppermute | solution.py:100
  21.0 29.5 %copy-start.4 = (bf16[512,384]{1,0:T(8,128)(2,1)}, bf16[512,384]{1,0:T(8,128)(2,1)S(1)}, u32[]{:S(2)}) copy-start(bf16[512,384]{1,0:T(8,128)(2,1)S(1)} %collective-permute-done.1) | copy-start | bytes 1179652
  21.0 12.3 %collective-permute-start.2 = (bf16[512,384]{1,0:T(8,128)(2,1)S(1)}, bf16[512,384]{1,0:T(8,128)(2,1)S(1)}, u32[]{:S(2)}, u32[]{:S(2)}) collective-permute-start(bf16[512,384]{1,0:T(8,128)(2,1)S(1)} %collective-permute-done.1), channel_id=1, source_target_pairs={{0,7},{1,0},{2,1},{3,2},{4,3},{5,4},{6,5},{7,6},{8,15},{9,8},{10,9... | collective-permute-start | bytes 1179656 | tf_op jit(solution)/shard_map/ppermute | solution.py:76
  30.6 19.9 %copy-start.5 = (bf16[512,384]{1,0:T(8,128)(2,1)}, bf16[512,384]{1,0:T(8,128)(2,1)S(1)}, u32[]{:S(2)}) copy-start(bf16[512,384]{1,0:T(8,128)(2,1)S(1)} %collective-permute-done.5) | copy-start | bytes 1179652
  30.6 10.1 %collective-permute-start.6 = (bf16[512,384]{1,0:T(8,128)(2,1)S(1)}, bf16[512,384]{1,0:T(8,128)(2,1)S(1)}, u32[]{:S(2)}, u32[]{:S(2)}) collective-permute-start(bf16[512,384]{1,0:T(8,128)(2,1)S(1)} %collective-permute-done.5), channel_id=1, source_target_pairs={{0,1},{1,2},{2,3},{3,4},{4,5},{5,6},{6,7},{7,0},{8,9},{9,10},{10,1... | collective-permute-start | bytes 1179656 | tf_op jit(solution)/shard_map/ppermute | solution.py:72
  33.2 17.6 %copy-start.7 = (bf16[512,384]{1,0:T(8,128)(2,1)}, bf16[512,384]{1,0:T(8,128)(2,1)S(1)}, u32[]{:S(2)}) copy-start(bf16[512,384]{1,0:T(8,128)(2,1)S(1)} %collective-permute-done.2) | copy-start | bytes 1179652
  33.2 11.8 %collective-permute-start.3 = (bf16[512,384]{1,0:T(8,128)(2,1)S(1)}, bf16[512,384]{1,0:T(8,128)(2,1)S(1)}, u32[]{:S(2)}, u32[]{:S(2)}) collective-permute-start(bf16[512,384]{1,0:T(8,128)(2,1)S(1)} %collective-permute-done.2), channel_id=1, source_target_pairs={{0,7},{1,0},{2,1},{3,2},{4,3},{5,4},{6,5},{7,6},{8,15},{9,8},{10,9... | collective-permute-start | bytes 1179656 | tf_op jit(solution)/shard_map/ppermute | solution.py:76
  40.7 10.1 %copy-start.8 = (bf16[512,384]{1,0:T(8,128)(2,1)}, bf16[512,384]{1,0:T(8,128)(2,1)S(1)}, u32[]{:S(2)}) copy-start(bf16[512,384]{1,0:T(8,128)(2,1)S(1)} %collective-permute-done.6) | copy-start | bytes 1179652
  40.7 9.2 %collective-permute-start.7 = (bf16[512,384]{1,0:T(8,128)(2,1)S(1)}, bf16[512,384]{1,0:T(8,128)(2,1)S(1)}, u32[]{:S(2)}, u32[]{:S(2)}) collective-permute-start(bf16[512,384]{1,0:T(8,128)(2,1)S(1)} %collective-permute-done.6), channel_id=1, source_target_pairs={{0,1},{1,2},{2,3},{3,4},{4,5},{5,6},{6,7},{7,0},{8,9},{9,10},{10,1... | collective-permute-start | bytes 1179656 | tf_op jit(solution)/shard_map/ppermute | solution.py:72
  45.0 5.8 %copy-start.10 = (bf16[512,384]{1,0:T(8,128)(2,1)}, bf16[512,384]{1,0:T(8,128)(2,1)S(1)}, u32[]{:S(2)}) copy-start(bf16[512,384]{1,0:T(8,128)(2,1)S(1)} %collective-permute-done.3) | copy-start | bytes 1179652
  49.9 0.9 copy-start.11
  51.1 1.7 %copy-start.3 = (f32[256,3072]{1,0:T(8,128)}, f32[256,3072]{1,0:T(8,128)S(1)}, u32[]{:S(2)}) copy-start(f32[256,3072]{1,0:T(8,128)S(1)} %convolution_dynamic-update-slice_fusion) | copy-start | bytes 9437188
  54.2 3.8 %collective-permute-start.8 = (f32[128,3072]{1,0:T(8,128)}, f32[128,3072]{1,0:T(8,128)}, u32[]{:S(2)}, u32[]{:S(2)}) collective-permute-start(f32[128,3072]{1,0:T(8,128)} %slice.39), channel_id=1, source_target_pairs={{0,8},{8,0},{16,24},{24,16},{32,40},{40,32},{48,56},{56,48},{64,72... | collective-permute-start | bytes 4718600 | tf_op jit(solution)/shard_map/ppermute | solution.py:106
  63.7 18.9 %all-to-all-start = ((bf16[16,3,64,128]{3,2,1,0:T(8,128)(2,1)}), bf16[16,3,64,128]{3,2,1,0:T(8,128)(2,1)S(1)}, u32[]{:S(2)}, u32[]{:S(2)}) async-start(bf16[16,3,64,128]{3,2,1,0:T(8,128)(2,1)} %copy.20), calls=%async_computation | async-start | bytes 1572864 | tf_op jit(solution)/shard_map/all_to_all | solution.py:54
  68.9 7.4 %copy-start.9 = (bf16[512,384]{1,0:T(8,128)(2,1)S(1)}, bf16[512,384]{1,0:T(8,128)(2,1)}, u32[]{:S(2)}) copy-start(bf16[512,384]{1,0:T(8,128)(2,1)} %copy-done.8) | copy-start | bytes 1179652
  68.9 8.2 %copy-start.6 = (bf16[512,384]{1,0:T(8,128)(2,1)S(1)}, bf16[512,384]{1,0:T(8,128)(2,1)}, u32[]{:S(2)}) copy-start(bf16[512,384]{1,0:T(8,128)(2,1)} %copy-done.5) | copy-start | bytes 1179652
  78.8 38.2 %collective-permute-start.10 = (bf16[512,3072]{1,0:T(8,128)(2,1)}, bf16[512,3072]{1,0:T(8,128)(2,1)}, u32[]{:S(2)}, u32[]{:S(2)}) collective-permute-start(bf16[512,3072]{1,0:T(8,128)(2,1)} %constant_dynamic-update-slice_fusion), channel_id=1, source_target_pairs={{0,8},{8,0},{16,24},{24,16},{32,40},{40,32},{48,56},{56,48},{64,72... | collective-permute-start | bytes 9437192 | tf_op jit(solution)/shard_map/ppermute | solution.py:108
  90.8 13.9 %copy-start.1 = (bf16[1,1,128,1024]{3,2,1,0:T(8,128)(2,1)S(1)}, bf16[1,1,128,1024]{3,2,1,0:T(8,128)(2,1)}, u32[]{:S(2)}) copy-start(bf16[1,1,128,1024]{3,2,1,0:T(8,128)(2,1)} %param.8) | copy-start | bytes 786436
  90.8 13.9 %copy-start.14 = (f32[1,1024]{1,0:T(1,128)S(1)}, f32[1,1024]{1,0:T(1,128)}, u32[]{:S(2)}) copy-start(f32[1,1024]{1,0:T(1,128)} %param.14) | copy-start | bytes 12292
  90.8 13.9 %copy-start.15 = (f32[1,1024]{1,0:T(1,128)S(1)}, f32[1,1024]{1,0:T(1,128)}, u32[]{:S(2)}) copy-start(f32[1,1024]{1,0:T(1,128)} %param.15) | copy-start | bytes 12292
  94.0 22.8 %copy-start.12 = (f32[1,1024]{1,0:T(1,128)S(1)}, f32[1,1024]{1,0:T(1,128)}, u32[]{:S(2)}) copy-start(f32[1,1024]{1,0:T(1,128)} %param.11) | copy-start | bytes 12292
  94.0 22.8 %copy-start.13 = (f32[1,1024]{1,0:T(1,128)S(1)}, f32[1,1024]{1,0:T(1,128)}, u32[]{:S(2)}) copy-start(f32[1,1024]{1,0:T(1,128)} %param.10) | copy-start | bytes 12292
  105.2 11.2 %collective-permute-start.9 = (bf16[128,1024]{1,0:T(8,128)(2,1)S(1)}, bf16[128,1024]{1,0:T(8,128)(2,1)S(1)}, u32[]{:S(2)}, u32[]{:S(2)}) collective-permute-start(bf16[128,1024]{1,0:T(8,128)(2,1)S(1)} %fusion.49), channel_id=1, source_target_pairs={{0,128},{1,129},{2,130},{3,131},{4,132},{5,133},{6,134},{7,135},{8... | collective-permute-start | bytes 786440 | tf_op jit(solution)/shard_map/ppermute | solution.py:117
  106.5 13.0 %copy-start.2 = (bf16[512,3072]{1,0:T(8,128)(2,1)S(1)}, bf16[512,3072]{1,0:T(8,128)(2,1)}, u32[]{:S(2)}) copy-start(bf16[512,3072]{1,0:T(8,128)(2,1)} %constant_dynamic-update-slice_fusion) | copy-start | bytes 9437188
  151.6 11.5 %all-to-all-start.3 = ((bf16[16,64,128]{2,1,0:T(8,128)(2,1)}), bf16[16,64,128]{2,1,0:T(8,128)(2,1)S(1)}, u32[]{:S(2)}, u32[]{:S(2)}) async-start(bf16[16,64,128]{2,1,0:T(8,128)(2,1)} %bitcast.138), calls=%async_computation.3 | async-start | bytes 524288 | tf_op jit(solution)/shard_map/all_to_all | solution.py:57

commit v5 on v4

--- a/solution.py
+++ b/solution.py
@@ -36,7 +36,7 @@
 
 
 def sublayer(current, length, qkv_mine, qkv_other, out_full, gain, shift, out_shift, layer_scale,
-             projected=None):
+             projected=None, to_both=False):
     tok_rows, width = current.shape
     head_width = width // HEADS
     ctx_count = lax.axis_size("ctx")
@@ -54,7 +54,12 @@
     gathered = lax.all_to_all(projected, "ctx", 0, 3, tiled=True)
     context = head_attention(gathered[0], length, head_width ** (-0.5))
     context = jnp.transpose(context.reshape(head_width, ctx_count, tok_rows), (1, 0, 2))
-    spread = lax.all_to_all(context, "ctx", 0, 0, tiled=True).reshape(width, tok_rows)
+    if to_both:
+        sent = jnp.concatenate([context] * lax.axis_size("pipe"), axis=0)
+        spread = lax.all_to_all(sent, ("pipe", "ctx"), 0, 0, tiled=True)[:ctx_count]
+    else:
+        spread = lax.all_to_all(context, "ctx", 0, 0, tiled=True)
+    spread = spread.reshape(width, tok_rows)
     mixed = jnp.einsum("ft,fo->to", spread, out_full, preferred_element_type=jnp.float32)
     mixed = mixed + out_shift
     return (current.astype(jnp.float32) + layer_scale * mixed).astype(jnp.bfloat16)
@@ -108,13 +113,17 @@
     qkv_other = lax.ppermute(qkv_mine, "ctx", sibling)
     args = (qkv_mine, qkv_other, w_out[0], norm_gain[0], norm_bias[0], out_bias[0], scale_gain[0])
     length = lengths[0, 0]
-    outputs = []
-    for turn_index in range(section_count):
-        produced = sublayer(current, length, *args, projected=first if turn_index == 0 else None)
-        outputs.append(produced)
-        if turn_index + 1 < section_count:
-            pairs = [(i, i + 1) for i in range(section_count - 1)]
-            current = lax.ppermute(produced, "pipe", pairs)
+    first_params = (w_out[0], out_bias[0], scale_gain[0])
+    onward = [(i, j) for i in range(1) for j in range(1, section_count)]
+    first_params = tuple(
+        jnp.where(section_index == 0, own, lax.ppermute(own, "pipe", onward))
+        for own in first_params
+    )
+    turn0_args = (qkv_mine, qkv_other, first_params[0], norm_gain[0], norm_bias[0],
+                  first_params[1], first_params[2])
+    assert section_count == 2
+    produced = sublayer(current, length, *turn0_args, projected=first, to_both=True)
+    outputs = [produced, sublayer(produced, length, *args)]
     result = outputs[0]
     for turn_index in range(1, section_count):
         result = jnp.where(section_index == turn_index, outputs[turn_index], result)

time: 165 us -> 198 us (1.20)
  starting transfers between devices: 23.4 us -> 63.2 us
  blocking collectives: 27.2 us -> 17.2 us
  local copies, waits for them, and re-layouts: 22.6 us -> 17.7 us
  matrix products: 19 us -> 23 us
    all_to_all x1 -> x2, starting transfers between devices: 3.53 us -> 40.4 us  [the longest x1 36.9 us: sublayer(): spread = lax.all_to_all(sent, ('pipe', 'ctx'), 0, 0, tiled=True)[:ctx_count]]
    all_to_all x1 -> x0, blocking collectives: 10.6 us -> none  [sublayer(): lax.all_to_all(context, 'ctx', 0, 0, tiled=True).reshape(width, tok_rows)]
    unnamed x39 -> x33, local copies, waits for them, and re-layouts: 12.8 us -> 7.34 us
    all_to_all x1, waiting for transfers between devices: 3.4 us -> 8.38 us  [sublayer(): gathered = lax.all_to_all(projected, 'ctx', 0, 3, tiled=True)]
    ppermute x1 -> x3, waiting for transfers between devices: 9.86 us -> 5.69 us  [per_device(): lax.ppermute(own, 'pipe', onward)]
    dot_general x2, matrix products: 1.71 us -> 5.75 us  [sublayer(): jnp.einsum('ft,fo->to', spread, out_full, preferred_element_type=jnp.floa...]
    ppermute x1 -> x3, starting transfers between devices: 1.29 us -> 3.86 us  [per_device(): lax.ppermute(own, 'pipe', onward)]
    all_to_all x1 -> x2, waiting for transfers between devices: 7.98 us -> 9.2 us  [the longest x1 7.99 us: sublayer(): spread = lax.all_to_all(context, 'ctx', 0, 0, tiled=True)]
  transfers between devices with their start and end apart: 13 -> 16, of which waited for: 10 -> 12; matrix products, arithmetic and copies ran while one was open for 16% -> 18% of each run, Pallas kernels for 0% -> 0%
where the time goes in v5:
time: 198 us; the launch traced here: 196 us
  starting transfers between devices  63.2 us (32%)
  waiting for transfers between devices  55.3 us (28%)
  matrix products  23 us (12%)
  other arithmetic  18.3 us (9%)
  local copies, waits for them, and re-layouts  17.7 us (9%)
  blocking collectives  17.2 us (9%)
    all_to_all x1, starting transfers between devices, sublayer(): spread = lax.all_to_all(sent, ('pipe', 'ctx'), 0, 0, tiled=True)[:ctx_count]  36.9 us
    ppermute x4, waiting for transfers between devices, ring_gather(): forward = lax.ppermute(forward, axis, right)  23.8 us
    all_to_all x1, blocking collectives, sublayer(): gathered = lax.all_to_all(projected, 'ctx', 0, 3, tiled=True)  17.2 us
    ppermute x3, starting transfers between devices, ring_gather(): backward = lax.ppermute(backward, axis, left)  12.9 us
    reduce_sum x2, other arithmetic, head_attention(): totals = jnp.sum(weights, axis=-1)  9.64 us
    all_to_all x1, waiting for transfers between devices, sublayer(): gathered = lax.all_to_all(projected, 'ctx', 0, 3, tiled=True)  8.38 us
    all_to_all x1, waiting for transfers between devices, sublayer(): spread = lax.all_to_all(context, 'ctx', 0, 0, tiled=True)  7.99 us
    unnamed x33, local copies, waits for them, and re-layouts  7.34 us
  transfers between devices with their start and end apart: 16, of which 12 were waited for; matrix products, arithmetic and copies ran while one was open for 18% of the time, Pallas kernels for 0%

profile of v5, /device:TPU:4, one launch (start us, length us, event | category | flops | bytes accessed | tf_op | source)
XLA Modules:
  0.0 195.9 jit_solution(13415832431012578743)
XLA Ops:
  0.0 1.1 constant_dynamic-update-slice_fusion.7
  1.1 5.9 %collective-permute-start.2 = (bf16[512,384]{1,0:T(8,128)(2,1)S(1)}, bf16[512,384]{1,0:T(8,128)(2,1)S(1)}, u32[]{:S(2)}, u32[]{:S(2)}) collective-permute-start(bf16[512,384]{1,0:T(8,128)(2,1)S(1)} %get-tuple-element.6), channel_id=1, source_target_pairs={{0,7},{1,0},{2,1},{3,2},{4,3},{5,4},{6,5},{7,6},{8,15},{9,8},{10,9... | collective-permute-start | bytes 1179656 | tf_op jit(solution)/shard_map/ppermute | solution.py:81
  7.0 1.1 convert_reduce_fusion.1
  8.1 1.2 fusion.53
  9.3 9.5 %collective-permute-done.5 = bf16[512,384]{1,0:T(8,128)(2,1)S(1)} collective-permute-done((bf16[512,384]{1,0:T(8,128)(2,1)S(1)}, bf16[512,384]{1,0:T(8,128)(2,1)S(1)}, u32[]{:S(2)}, u32[]{:S(2)}) %collective-permute-start.5) | collective-permute-done | bytes 393248 | tf_op jit(solution)/shard_map/ppermute | solution.py:77
  18.8 1.2 fusion.56
  20.1 3.3 %collective-permute-start.3 = (bf16[512,384]{1,0:T(8,128)(2,1)S(1)}, bf16[512,384]{1,0:T(8,128)(2,1)S(1)}, u32[]{:S(2)}, u32[]{:S(2)}) collective-permute-start(bf16[512,384]{1,0:T(8,128)(2,1)S(1)} %collective-permute-done.2), channel_id=1, source_target_pairs={{0,7},{1,0},{2,1},{3,2},{4,3},{5,4},{6,5},{7,6},{8,15},{9,8},{10,9... | collective-permute-start | bytes 1179656 | tf_op jit(solution)/shard_map/ppermute | solution.py:81
  23.5 6.3 %collective-permute-done.6 = bf16[512,384]{1,0:T(8,128)(2,1)S(1)} collective-permute-done((bf16[512,384]{1,0:T(8,128)(2,1)S(1)}, bf16[512,384]{1,0:T(8,128)(2,1)S(1)}, u32[]{:S(2)}, u32[]{:S(2)}) %collective-permute-start.6) | collective-permute-done | bytes 393248 | tf_op jit(solution)/shard_map/ppermute | solution.py:77
  29.7 0.3 convolution_dynamic-update-slice_fusion.7
  30.0 2.4 %collective-permute-done.3 = bf16[512,384]{1,0:T(8,128)(2,1)S(1)} collective-permute-done((bf16[512,384]{1,0:T(8,128)(2,1)S(1)}, bf16[512,384]{1,0:T(8,128)(2,1)S(1)}, u32[]{:S(2)}, u32[]{:S(2)}) %collective-permute-start.3) | collective-permute-done | bytes 393248 | tf_op jit(solution)/shard_map/ppermute | solution.py:81
  32.4 3.7 %collective-permute-start.4 = (bf16[512,384]{1,0:T(8,128)(2,1)S(1)}, bf16[512,384]{1,0:T(8,128)(2,1)S(1)}, u32[]{:S(2)}, u32[]{:S(2)}) collective-permute-start(bf16[512,384]{1,0:T(8,128)(2,1)S(1)} %collective-permute-done.3), channel_id=1, source_target_pairs={{0,7},{1,0},{2,1},{3,2},{4,3},{5,4},{6,5},{7,6},{8,15},{9,8},{10,9... | collective-permute-start | bytes 1179656 | tf_op jit(solution)/shard_map/ppermute | solution.py:81
  36.1 0.3 convolution_dynamic-update-slice_fusion.6
  36.4 3.4 %collective-permute-done.7 = bf16[512,384]{1,0:T(8,128)(2,1)S(1)} collective-permute-done((bf16[512,384]{1,0:T(8,128)(2,1)S(1)}, bf16[512,384]{1,0:T(8,128)(2,1)S(1)}, u32[]{:S(2)}, u32[]{:S(2)}) %collective-permute-start.7) | collective-permute-done | bytes 393248 | tf_op jit(solution)/shard_map/ppermute | solution.py:77
  39.8 0.3 convolution_dynamic-update-slice_fusion.5
  40.1 4.1 %collective-permute-done.4 = bf16[512,384]{1,0:T(8,128)(2,1)S(1)} collective-permute-done((bf16[512,384]{1,0:T(8,128)(2,1)S(1)}, bf16[512,384]{1,0:T(8,128)(2,1)S(1)}, u32[]{:S(2)}, u32[]{:S(2)}) %collective-permute-start.4) | collective-permute-done | bytes 393248 | tf_op jit(solution)/shard_map/ppermute | solution.py:81
  44.2 0.3 convolution_dynamic-update-slice_fusion.4
  44.5 4.6 %collective-permute-done.8 = bf16[512,384]{1,0:T(8,128)(2,1)S(1)} collective-permute-done((bf16[512,384]{1,0:T(8,128)(2,1)S(1)}, bf16[512,384]{1,0:T(8,128)(2,1)S(1)}, u32[]{:S(2)}, u32[]{:S(2)}) %collective-permute-start.8) | collective-permute-done | bytes 393248 | tf_op jit(solution)/shard_map/ppermute | solution.py:77
  49.0 0.3 convolution_dynamic-update-slice_fusion.3
  49.3 0.3 convolution_dynamic-update-slice_fusion.2
  49.7 0.3 convolution_dynamic-update-slice_fusion.1
  50.0 0.3 convolution_dynamic-update-slice_fusion
  50.3 1.6 copy-done
  51.9 1.3 slice.43
  53.2 1.3 collective-permute-start.10
  55.2 1.8 collective-permute-done.9
  57.0 2.0 %fusion.26 = bf16[128,3072]{1,0:T(8,128)(2,1)S(1)} fusion(f32[128,3072]{1,0:T(8,128)} %collective-permute-done.9, f32[256,3072]{1,0:T(8,128)} %copy-done), kind=kLoop, calls=%fused_computation.22 | loop fusion | flops 786432 | bytes 3932160 | tf_op jit(solution)/shard_map/convert_element_type | solution.py:112
  59.0 1.4 fusion.42
  60.4 2.3 %copy.19 = bf16[128,3072]{0,1:T(8,128)(2,1)} copy(bf16[128,3072]{1,0:T(8,128)(2,1)} %fusion.42) | data formatting | bytes 1572864 | tf_op jit(solution)/shard_map/dynamic_slice | solution.py:92
  62.7 2.1 %copy.20 = bf16[16,3,64,128]{3,2,1,0:T(8,128)(2,1)} copy(bf16[16,3,64,128]{3,2,0,1:T(8,128)(2,1)} %bitcast.131) | data formatting | bytes 1572864 | tf_op jit(solution)/shard_map/transpose | solution.py:53
  64.8 5.2 %all-to-all-start = ((bf16[16,3,64,128]{3,2,1,0:T(8,128)(2,1)}), bf16[16,3,64,128]{3,2,1,0:T(8,128)(2,1)}, u32[]{:S(2)}, u32[]{:S(2)}) async-start(bf16[16,3,64,128]{3,2,1,0:T(8,128)(2,1)} %copy.20), calls=%async_computation | async-start | bytes 1572864 | tf_op jit(solution)/shard_map/all_to_all | solution.py:54
  70.1 1.2 constant_dynamic-update-slice_fusion.6
  71.2 1.1 constant_dynamic-update-slice_fusion.5
  72.3 1.1 constant_dynamic-update-slice_fusion.4
  73.4 1.1 constant_dynamic-update-slice_fusion.3
  74.8 0.6 collective-permute-start.12
  75.5 8.4 %all-to-all-done = bf16[16,3,64,128]{3,2,1,0:T(8,128)(2,1)} async-done(((bf16[16,3,64,128]{3,2,1,0:T(8,128)(2,1)}), bf16[16,3,64,128]{3,2,1,0:T(8,128)(2,1)}, u32[]{:S(2)}, u32[]{:S(2)}) %all-to-all-start) | async-done | bytes 786464 | tf_op jit(solution)/shard_map/all_to_all | solution.py:54
  83.8 1.2 fusion.87
  85.0 0.2 copy.22
  85.4 2.8 %select_reduce_fusion.1 = (f32[2048]{0:T(1024)S(1)}, f32[2048,2048]{0,1:T(8,128)S(1)}) fusion(pred[2048]{0:T(1024)(128)(4,1)S(1)} %iota_compare_fusion, bf16[8,8,16,128]{3,2,1,0:T(8,128)(2,1)S(1)} %bitcast.136, bf16[8,8,16,128]{3,2,1,0:T(8,128)(2,1)S(1)} %bitcast.135), kind=kOutput, calls=%fused_computation.3 | convolution fusion | flops 549451776 | bytes 17311744 | tf_op jit(solution)/shard_map/dq,dk->qk/dot_general | solution.py:25
  88.2 4.8 %fusion = f32[2048]{0:T(1024)S(1)} fusion(f32[2048,2048]{0,1:T(8,128)S(1)} %get-tuple-element.14, f32[2048]{0:T(1024)S(1)} %get-tuple-element.13, pred[2048]{0:T(1024)(128)(4,1)S(1)} %iota_compare_fusion), kind=kLoop, calls=%fused_computation.4 | loop fusion | flops 16775168 | bytes 16795648 | tf_op jit(solution)/shard_map/reduce_sum | solution.py:31
  93.2 3.1 %fusion.38 = bf16[8,16,8,128]{3,2,1,0:T(8,128)(2,1)S(1)} fusion(f32[2048,2048]{0,1:T(8,128)S(1)} %get-tuple-element.14, f32[2048]{0:T(1024)S(1)} %get-tuple-element.13, pred[2048]{0:T(1024)(128)(4,1)S(1)} %iota_compare_fusion, bf16[8,8,16,128]{3,2,1,0:T(8,128)(2,1)S(1)} %bitcast.141, f32[2048]{0:T(1024)S(1)} %fusion), kind=kOutput, calls=%fused_computation.43 | convolution fusion | flops 553910272 | bytes 17319936 | tf_op jit(solution)/shard_map/qk,dk->dq/dot_general | solution.py:32
  96.4 0.8 pad_maximum_fusion
  97.3 36.9 %all-to-all-start.1 = ((bf16[32,64,128]{2,1,0:T(8,128)(2,1)}), bf16[32,64,128]{2,1,0:T(8,128)(2,1)}, u32[]{:S(2)}, u32[]{:S(2)}) async-start(bf16[32,64,128]{2,1,0:T(8,128)(2,1)} %pad_maximum_fusion), calls=%async_computation.1 | async-start | bytes 1048576 | tf_op jit(solution)/shard_map/all_to_all | solution.py:59
  134.2 1.3 collective-permute-start.11
  135.5 1.3 collective-permute-start
  136.8 4.4 %collective-permute-done.11 = f32[1024]{0:T(1024)S(1)} collective-permute-done((f32[1024]{0:T(1024)S(1)}, f32[1024]{0:T(1024)S(1)}, u32[]{:S(2)}, u32[]{:S(2)}) %collective-permute-start.11) | collective-permute-done | bytes 4128 | tf_op jit(solution)/shard_map/ppermute | solution.py:119
  141.2 1.3 collective-permute-done
  142.5 1.2 all-to-all-done.1
  143.7 1.0 slice.47
  144.7 2.9 %convert_reduce_fusion = (f32[128]{0:T(128)S(1)}, bf16[128,1024]{1,0:T(8,128)(2,1)S(1)}) fusion(f32[1024]{0:T(1024)S(1)} %broadcast_select_fusion, bf16[1024,128]{1,0:T(8,128)(2,1)S(1)} %bitcast.139, bf16[1024,1024]{1,0:T(8,128)(2,1)} %collective-permute-done.10, pred[]{:T(512)S(6)} %eq.12, bf16[1,1024,1024]{2,1,0:T(8,128)(2,1)} %param.13, ...), kind=kOutput, calls=%fused_computation.47 | convolution fusion | flops 270401408 | bytes 4989441 | tf_op jit(solution)/shard_map/ft,fo->to/dot_general | solution.py:63
  147.7 0.2 fusion.49
  147.9 0.2 fusion.52
  148.2 2.5 %fusion.73 = f32[128,3072]{1,0:T(8,128)S(1)} fusion(bf16[512,3072]{1,0:T(8,128)(2,1)} %collective-permute-done.12, bf16[128,1024]{1,0:T(8,128)(2,1)S(1)} %fusion.52, s32[]{:T(128)S(6)} %select_n.73), kind=kOutput, calls=%fused_computation.86 | convolution fusion | flops 402653184 | bytes 4849668 | tf_op jit(solution)/shard_map/dot_general | solution.py:49
  150.6 0.6 fusion.10
  151.3 0.4 fusion.41
  151.7 0.4 copy.25
  152.2 17.2 %all_to_all.40 = bf16[16,3,64,128]{3,2,1,0:T(8,128)(2,1)S(1)} all-to-all(bf16[16,3,64,128]{3,2,1,0:T(8,128)(2,1)S(1)} %copy.26), channel_id=1, replica_groups=mesh['pipe'=2,'ctx'=16,'dp'=8] {'ctx'}, dimensions={0} | all-to-all | bytes 1572864 | tf_op jit(solution)/shard_map/all_to_all | solution.py:54
  170.0 2.8 %select_reduce_fusion = (f32[2048]{0:T(1024)S(1)}, f32[2048,2048]{0,1:T(8,128)S(1)}) fusion(pred[2048]{0:T(1024)(128)(4,1)S(1)} %iota_compare_fusion, bf16[8,8,16,128]{3,2,1,0:T(8,128)(2,1)S(1)} %bitcast.134, bf16[8,8,16,128]{3,2,1,0:T(8,128)(2,1)S(1)} %bitcast.133), kind=kOutput, calls=%fused_computation.1 | convolution fusion | flops 549451776 | bytes 17311744 | tf_op jit(solution)/shard_map/dq,dk->qk/dot_general | solution.py:25
  172.8 4.8 %fusion.2 = f32[2048]{0:T(1024)S(1)} fusion(f32[2048,2048]{0,1:T(8,128)S(1)} %get-tuple-element.18, f32[2048]{0:T(1024)S(1)} %get-tuple-element.17, pred[2048]{0:T(1024)(128)(4,1)S(1)} %iota_compare_fusion), kind=kLoop, calls=%fused_computation.6 | loop fusion | flops 16775168 | bytes 16795648 | tf_op jit(solution)/shard_map/reduce_sum | solution.py:31
  177.6 3.1 %fusion.35 = bf16[8,16,8,128]{3,2,1,0:T(8,128)(2,1)S(1)} fusion(f32[2048,2048]{0,1:T(8,128)S(1)} %get-tuple-element.18, f32[2048]{0:T(1024)S(1)} %get-tuple-element.17, pred[2048]{0:T(1024)(128)(4,1)S(1)} %iota_compare_fusion, bf16[8,8,16,128]{3,2,1,0:T(8,128)(2,1)S(1)} %bitcast.140, f32[2048]{0:T(1024)S(1)} %fusion.2), kind=kOutput, calls=%fused_computation.42 | convolution fusion | flops 553910272 | bytes 17319936 | tf_op jit(solution)/shard_map/qk,dk->dq/dot_general | solution.py:32
  180.8 0.8 copy.73
  181.6 3.5 %all-to-all-start.3 = ((bf16[16,64,128]{2,1,0:T(8,128)(2,1)}), bf16[16,64,128]{2,1,0:T(8,128)(2,1)S(1)}, u32[]{:S(2)}, u32[]{:S(2)}) async-start(bf16[16,64,128]{2,1,0:T(8,128)(2,1)} %bitcast.126), calls=%async_computation.3 | async-start | bytes 524288 | tf_op jit(solution)/shard_map/all_to_all | solution.py:61
  185.1 8.0 %all-to-all-done.3 = bf16[16,64,128]{2,1,0:T(8,128)(2,1)S(1)} async-done(((bf16[16,64,128]{2,1,0:T(8,128)(2,1)}), bf16[16,64,128]{2,1,0:T(8,128)(2,1)S(1)}, u32[]{:S(2)}, u32[]{:S(2)}) %all-to-all-start.3) | async-done | bytes 262176 | tf_op jit(solution)/shard_map/all_to_all | solution.py:61
  193.1 2.8 %fusion.34 = bf16[1,1,1,128,1024]{4,3,2,1,0:T(8,128)(2,1)} fusion(bf16[128,1024]{1,0:T(8,128)(2,1)S(1)} %get-tuple-element.16, bf16[1024,128]{1,0:T(8,128)(2,1)S(1)} %bitcast.137, f32[1024]{0:T(1024)S(1)} %bitcast.148, f32[1024]{0:T(1024)S(1)} %bitcast.151, pred[]{:T(512)S(6)} %eq.11, bf16[1,1024,1024]{2,1,0:T(8,128)(2,1)} %param.13), kind=kOutput, calls=%fused_computation.41 | convolution fusion | flops 269221888 | bytes 2891777 | tf_op jit(solution)/shard_map/ft,fo->to/dot_general | solution.py:63
  (54 shorter events, 1.5 us)
Async XLA Ops:
  1.1 19.0 %collective-permute-start.2 = (bf16[512,384]{1,0:T(8,128)(2,1)S(1)}, bf16[512,384]{1,0:T(8,128)(2,1)S(1)}, u32[]{:S(2)}, u32[]{:S(2)}) collective-permute-start(bf16[512,384]{1,0:T(8,128)(2,1)S(1)} %get-tuple-element.6), channel_id=1, source_target_pairs={{0,7},{1,0},{2,1},{3,2},{4,3},{5,4},{6,5},{7,6},{8,15},{9,8},{10,9... | collective-permute-start | bytes 1179656 | tf_op jit(solution)/shard_map/ppermute | solution.py:81
  7.0 11.8 %collective-permute-start.5 = (bf16[512,384]{1,0:T(8,128)(2,1)S(1)}, bf16[512,384]{1,0:T(8,128)(2,1)S(1)}, u32[]{:S(2)}, u32[]{:S(2)}) collective-permute-start(bf16[512,384]{1,0:T(8,128)(2,1)S(1)} %get-tuple-element.6), channel_id=1, source_target_pairs={{0,1},{1,2},{2,3},{3,4},{4,5},{5,6},{6,7},{7,0},{8,9},{9,10},{10,1... | collective-permute-start | bytes 1179656 | tf_op jit(solution)/shard_map/ppermute | solution.py:77
  18.8 10.9 %collective-permute-start.6 = (bf16[512,384]{1,0:T(8,128)(2,1)S(1)}, bf16[512,384]{1,0:T(8,128)(2,1)S(1)}, u32[]{:S(2)}, u32[]{:S(2)}) collective-permute-start(bf16[512,384]{1,0:T(8,128)(2,1)S(1)} %collective-permute-done.5), channel_id=1, source_target_pairs={{0,1},{1,2},{2,3},{3,4},{4,5},{5,6},{6,7},{7,0},{8,9},{9,10},{10,1... | collective-permute-start | bytes 1179656 | tf_op jit(solution)/shard_map/ppermute | solution.py:77
  20.0 3.4 %collective-permute-start.1 = (bf16[128,1024]{1,0:T(8,128)(2,1)S(1)}, bf16[128,1024]{1,0:T(8,128)(2,1)S(1)}, u32[]{:S(2)}, u32[]{:S(2)}) collective-permute-start(bf16[128,1024]{1,0:T(8,128)(2,1)S(1)} %fusion.56), channel_id=1, source_target_pairs={{0,8},{8,0},{16,24},{24,16},{32,40},{40,32},{48,56},{56,48},{64,72... | collective-permute-start | bytes 786440 | tf_op jit(solution)/shard_map/ppermute | solution.py:105
  20.1 29.5 %copy-start.1 = (bf16[512,384]{1,0:T(8,128)(2,1)}, bf16[512,384]{1,0:T(8,128)(2,1)S(1)}, u32[]{:S(2)}) copy-start(bf16[512,384]{1,0:T(8,128)(2,1)S(1)} %collective-permute-done.2) | copy-start | bytes 1179652
  20.1 12.3 %collective-permute-start.3 = (bf16[512,384]{1,0:T(8,128)(2,1)S(1)}, bf16[512,384]{1,0:T(8,128)(2,1)S(1)}, u32[]{:S(2)}, u32[]{:S(2)}) collective-permute-start(bf16[512,384]{1,0:T(8,128)(2,1)S(1)} %collective-permute-done.2), channel_id=1, source_target_pairs={{0,7},{1,0},{2,1},{3,2},{4,3},{5,4},{6,5},{7,6},{8,15},{9,8},{10,9... | collective-permute-start | bytes 1179656 | tf_op jit(solution)/shard_map/ppermute | solution.py:81
  29.7 19.9 %copy-start.2 = (bf16[512,384]{1,0:T(8,128)(2,1)}, bf16[512,384]{1,0:T(8,128)(2,1)S(1)}, u32[]{:S(2)}) copy-start(bf16[512,384]{1,0:T(8,128)(2,1)S(1)} %collective-permute-done.6) | copy-start | bytes 1179652
  29.7 10.1 %collective-permute-start.7 = (bf16[512,384]{1,0:T(8,128)(2,1)S(1)}, bf16[512,384]{1,0:T(8,128)(2,1)S(1)}, u32[]{:S(2)}, u32[]{:S(2)}) collective-permute-start(bf16[512,384]{1,0:T(8,128)(2,1)S(1)} %collective-permute-done.6), channel_id=1, source_target_pairs={{0,1},{1,2},{2,3},{3,4},{4,5},{5,6},{6,7},{7,0},{8,9},{9,10},{10,1... | collective-permute-start | bytes 1179656 | tf_op jit(solution)/shard_map/ppermute | solution.py:77
  32.4 17.6 %copy-start.4 = (bf16[512,384]{1,0:T(8,128)(2,1)}, bf16[512,384]{1,0:T(8,128)(2,1)S(1)}, u32[]{:S(2)}) copy-start(bf16[512,384]{1,0:T(8,128)(2,1)S(1)} %collective-permute-done.3) | copy-start | bytes 1179652
  32.4 11.8 %collective-permute-start.4 = (bf16[512,384]{1,0:T(8,128)(2,1)S(1)}, bf16[512,384]{1,0:T(8,128)(2,1)S(1)}, u32[]{:S(2)}, u32[]{:S(2)}) collective-permute-start(bf16[512,384]{1,0:T(8,128)(2,1)S(1)} %collective-permute-done.3), channel_id=1, source_target_pairs={{0,7},{1,0},{2,1},{3,2},{4,3},{5,4},{6,5},{7,6},{8,15},{9,8},{10,9... | collective-permute-start | bytes 1179656 | tf_op jit(solution)/shard_map/ppermute | solution.py:81
  39.8 10.1 %copy-start.5 = (bf16[512,384]{1,0:T(8,128)(2,1)}, bf16[512,384]{1,0:T(8,128)(2,1)S(1)}, u32[]{:S(2)}) copy-start(bf16[512,384]{1,0:T(8,128)(2,1)S(1)} %collective-permute-done.7) | copy-start | bytes 1179652
  39.8 9.2 %collective-permute-start.8 = (bf16[512,384]{1,0:T(8,128)(2,1)S(1)}, bf16[512,384]{1,0:T(8,128)(2,1)S(1)}, u32[]{:S(2)}, u32[]{:S(2)}) collective-permute-start(bf16[512,384]{1,0:T(8,128)(2,1)S(1)} %collective-permute-done.7), channel_id=1, source_target_pairs={{0,1},{1,2},{2,3},{3,4},{4,5},{5,6},{6,7},{7,0},{8,9},{9,10},{10,1... | collective-permute-start | bytes 1179656 | tf_op jit(solution)/shard_map/ppermute | solution.py:77
  44.2 5.8 %copy-start.7 = (bf16[512,384]{1,0:T(8,128)(2,1)}, bf16[512,384]{1,0:T(8,128)(2,1)S(1)}, u32[]{:S(2)}) copy-start(bf16[512,384]{1,0:T(8,128)(2,1)S(1)} %collective-permute-done.4) | copy-start | bytes 1179652
  49.0 0.9 copy-start.8
  50.3 1.6 copy-start
  53.2 3.8 %collective-permute-start.9 = (f32[128,3072]{1,0:T(8,128)}, f32[128,3072]{1,0:T(8,128)}, u32[]{:S(2)}, u32[]{:S(2)}) collective-permute-start(f32[128,3072]{1,0:T(8,128)} %slice.43), channel_id=1, source_target_pairs={{0,8},{8,0},{16,24},{24,16},{32,40},{40,32},{48,56},{56,48},{64,72... | collective-permute-start | bytes 4718600 | tf_op jit(solution)/shard_map/ppermute | solution.py:111
  53.2 91.5 %collective-permute-start.10 = (bf16[1024,1024]{1,0:T(8,128)(2,1)}, bf16[1024,1024]{1,0:T(8,128)(2,1)}, u32[]{:S(2)}, u32[]{:S(2)}) collective-permute-start(bf16[1024,1024]{1,0:T(8,128)(2,1)} %bitcast.13), channel_id=1, source_target_pairs={{0,128},{1,129},{2,130},{3,131},{4,132},{5,133},{6,134},{7,135},{8... | collective-permute-start | bytes 6291464 | tf_op jit(solution)/shard_map/ppermute | solution.py:119
  64.8 19.0 %all-to-all-start = ((bf16[16,3,64,128]{3,2,1,0:T(8,128)(2,1)}), bf16[16,3,64,128]{3,2,1,0:T(8,128)(2,1)}, u32[]{:S(2)}, u32[]{:S(2)}) async-start(bf16[16,3,64,128]{3,2,1,0:T(8,128)(2,1)} %copy.20), calls=%async_computation | async-start | bytes 1572864 | tf_op jit(solution)/shard_map/all_to_all | solution.py:54
  70.1 4.5 %copy-start.6 = (bf16[512,384]{1,0:T(8,128)(2,1)S(1)}, bf16[512,384]{1,0:T(8,128)(2,1)}, u32[]{:S(2)}) copy-start(bf16[512,384]{1,0:T(8,128)(2,1)} %copy-done.5) | copy-start | bytes 1179652
  70.1 4.6 %copy-start.3 = (bf16[512,384]{1,0:T(8,128)(2,1)S(1)}, bf16[512,384]{1,0:T(8,128)(2,1)}, u32[]{:S(2)}) copy-start(bf16[512,384]{1,0:T(8,128)(2,1)} %copy-done.2) | copy-start | bytes 1179652
  74.8 73.3 %collective-permute-start.12 = (bf16[512,3072]{1,0:T(8,128)(2,1)S(1)}, bf16[512,3072]{1,0:T(8,128)(2,1)}, u32[]{:S(2)}, u32[]{:S(2)}) collective-permute-start(bf16[512,3072]{1,0:T(8,128)(2,1)S(1)} %constant_dynamic-update-slice_fusion), channel_id=1, source_target_pairs={{0,8},{8,0},{16,24},{24,16},{32,40},{40,32},{48,56},{56,48},{64,72... | collective-permute-start | bytes 9437192 | tf_op jit(solution)/shard_map/ppermute | solution.py:113
  93.2 41.0 %copy-start.11 = (f32[1,1024]{1,0:T(1,128)S(1)}, f32[1,1024]{1,0:T(1,128)}, u32[]{:S(2)}) copy-start(f32[1,1024]{1,0:T(1,128)} %param.14) | copy-start | bytes 12292
  93.2 42.3 %copy-start.12 = (f32[1,1024]{1,0:T(1,128)S(1)}, f32[1,1024]{1,0:T(1,128)}, u32[]{:S(2)}) copy-start(f32[1,1024]{1,0:T(1,128)} %param.15) | copy-start | bytes 12292
  97.3 46.5 %all-to-all-start.1 = ((bf16[32,64,128]{2,1,0:T(8,128)(2,1)}), bf16[32,64,128]{2,1,0:T(8,128)(2,1)}, u32[]{:S(2)}, u32[]{:S(2)}) async-start(bf16[32,64,128]{2,1,0:T(8,128)(2,1)} %pad_maximum_fusion), calls=%async_computation.1 | async-start | bytes 1048576 | tf_op jit(solution)/shard_map/all_to_all | solution.py:59
  134.2 13.7 %copy-start.9 = (f32[1,1024]{1,0:T(1,128)S(1)}, f32[1,1024]{1,0:T(1,128)}, u32[]{:S(2)}) copy-start(f32[1,1024]{1,0:T(1,128)} %param.11) | copy-start | bytes 12292
  134.2 13.7 %copy-start.10 = (f32[1,1024]{1,0:T(1,128)S(1)}, f32[1,1024]{1,0:T(1,128)}, u32[]{:S(2)}) copy-start(f32[1,1024]{1,0:T(1,128)} %param.10) | copy-start | bytes 12292
  134.2 7.0 %collective-permute-start.11 = (f32[1024]{0:T(1024)S(1)}, f32[1024]{0:T(1024)S(1)}, u32[]{:S(2)}, u32[]{:S(2)}) collective-permute-start(f32[1024]{0:T(1024)S(1)} %bitcast.146), channel_id=1, source_target_pairs={{0,128},{1,129},{2,130},{3,131},{4,132},{5,133},{6,134},{7,135},{8... | collective-permute-start | bytes 12296 | tf_op jit(solution)/shard_map/ppermute | solution.py:119
  135.5 7.0 %collective-permute-start = (f32[1024]{0:T(1024)S(1)}, f32[1024]{0:T(1024)S(1)}, u32[]{:S(2)}, u32[]{:S(2)}) collective-permute-start(f32[1024]{0:T(1024)S(1)} %bitcast.149), channel_id=1, source_target_pairs={{0,128},{1,129},{2,130},{3,131},{4,132},{5,133},{6,134},{7,135},{8... | collective-permute-start | bytes 12296 | tf_op jit(solution)/shard_map/ppermute | solution.py:119
  181.6 11.5 %all-to-all-start.3 = ((bf16[16,64,128]{2,1,0:T(8,128)(2,1)}), bf16[16,64,128]{2,1,0:T(8,128)(2,1)S(1)}, u32[]{:S(2)}, u32[]{:S(2)}) async-start(bf16[16,64,128]{2,1,0:T(8,128)(2,1)} %bitcast.126), calls=%async_computation.3 | async-start | bytes 524288 | tf_op jit(solution)/shard_map/all_to_all | solution.py:61

commit v6 on v4

--- a/solution.py
+++ b/solution.py
@@ -1,6 +1,8 @@
 import jax
 import jax.numpy as jnp
 from jax import lax
+from jax.experimental import pallas as pl
+from jax.experimental.pallas import tpu as pltpu
 from jax.sharding import PartitionSpec as P
 
 HEADS = 16
@@ -18,21 +20,41 @@
     return (centered * lax.rsqrt(variance + epsilon) * gain + shift).astype(jnp.bfloat16)
 
 
+def attention_kernel(score_scale, length_ref, qkv_ref, out_ref):
+    block = out_ref.shape[1]
+    start = pl.multiple_of(pl.program_id(0) * block, block)
+    queries = qkv_ref[0, :, pl.ds(start, block)]
+    key_rows = qkv_ref[1]
+    value_rows = qkv_ref[2]
+    scores = lax.dot_general(
+        key_rows, queries, (((0,), (0,)), ((), ())), preferred_element_type=jnp.float32
+    ) * score_scale
+    valid = lax.broadcasted_iota(jnp.int32, scores.shape, 0) < length_ref[0]
+    top = jnp.max(jnp.where(valid, scores, masked_score), axis=0, keepdims=True)
+    weights = jnp.where(valid, jnp.exp(scores - top), 0.0)
+    totals = jnp.sum(weights, axis=0, keepdims=True)
+    context = jnp.dot(value_rows, weights.astype(jnp.bfloat16), preferred_element_type=jnp.float32)
+    out_ref[...] = (context / totals).astype(out_ref.dtype)
+
+
 def head_attention(qkv, length, score_scale):
-    queries, key_rows, value_rows = qkv[0], qkv[1], qkv[2]
-    count = qkv.shape[-1]
-    scores = (
-        jnp.einsum("dq,dk->qk", queries, key_rows, preferred_element_type=jnp.float32)
-        * score_scale
-    )
-    valid = jnp.arange(count, dtype=jnp.int32) < length
-    top = jnp.max(jnp.where(valid[None, :], scores, masked_score), axis=-1)
-    weights = jnp.where(valid[None, :], jnp.exp(scores - top[:, None]), 0.0)
-    totals = jnp.sum(weights, axis=-1)
-    context = jnp.einsum(
-        "qk,dk->dq", weights.astype(jnp.bfloat16), value_rows, preferred_element_type=jnp.float32
-    )
-    return (context / totals[None, :]).astype(jnp.bfloat16)
+    _, head_width, count = qkv.shape
+    block = 256
+    return pl.pallas_call(
+        lambda *refs: attention_kernel(score_scale, *refs),
+        out_shape=jax.ShapeDtypeStruct((head_width, count), jnp.bfloat16),
+        grid_spec=pltpu.PrefetchScalarGridSpec(
+            num_scalar_prefetch=1,
+            grid=(count // block,),
+            in_specs=[pl.BlockSpec(qkv.shape, lambda i, n: (0, 0, 0))],
+            out_specs=pl.BlockSpec((head_width, block), lambda i, n: (0, i)),
+        ),
+        cost_estimate=pl.CostEstimate(
+            flops=4 * count * count * head_width,
+            transcendentals=count * count,
+            bytes_accessed=4 * head_width * count * 2,
+        ),
+    )(jnp.reshape(length, (1,)).astype(jnp.int32), qkv)
 
 
 def sublayer(current, length, qkv_mine, qkv_other, out_full, gain, shift, out_shift, layer_scale,

time: 165 us -> 182 us (1.10)
  Pallas kernels: 0 us -> 25.7 us
  matrix products: 19 us -> 7.11 us
  other arithmetic: 16.6 us -> 6.55 us
  waiting for transfers between devices: 54.5 us -> 61.1 us
  local copies, waits for them, and re-layouts: 22.6 us -> 28.9 us
    pallas_call x0 -> x2, Pallas kernels: none -> 25.7 us  [head_attention(): pl.pallas_call(lambda *refs: attention_kernel(score_scale, *refs), out_sh...]
    dot_general x4 -> x0, matrix products: 11.9 us -> none  [the longest x2 6.27 us: head_attention(): jnp.einsum('qk,dk->dq', weights.astype(jnp.bfloat16), value_rows, preferr...]
    all_to_all x1, waiting for transfers between devices: 3.4 us -> 13.1 us  [sublayer(): gathered = lax.all_to_all(projected, 'ctx', 0, 3, tiled=True)]
    reduce_sum x2 -> x0, other arithmetic: 9.64 us -> none  [head_attention(): totals = jnp.sum(weights, axis=-1)]
    squeeze x0 -> x2, local copies, waits for them, and re-layouts: none -> 3.42 us  [sublayer(): context = head_attention(gathered[0], length, head_width ** (-0.5))]
    ppermute x1, waiting for transfers between devices: 3.08 us -> 0.01 us  [per_device(): partial_other = lax.ppermute(partial[tok_rows:], 'ctx', sibling)]
    transpose x0 -> x2, local copies, waits for them, and re-layouts: none -> 2.74 us  [sublayer(): jnp.transpose(context.reshape(head_width, ctx_count, tok_rows), (1, 0, 2))]
    all_to_all x0 -> x2, local copies, waits for them, and re-layouts: none -> 1.92 us  [sublayer(): gathered = lax.all_to_all(projected, 'ctx', 0, 3, tiled=True)]
  transfers between devices with their start and end apart: 13 -> 13, of which waited for: 10 -> 9; matrix products, arithmetic and copies ran while one was open for 16% -> 14% of each run, Pallas kernels for 0% -> 7%
where the time goes in v6:
time: 182 us; the launch traced here: 181 us
  waiting for transfers between devices  61.1 us (34%)
  local copies, waits for them, and re-layouts  28.9 us (16%)
  blocking collectives  27.2 us (15%)
  Pallas kernels  25.7 us (14%)
  starting transfers between devices  23.5 us (13%)
  matrix products  7.11 us (4%)
  other arithmetic  6.55 us (4%)
    pallas_call x2, Pallas kernels, head_attention(): pl.pallas_call(lambda *refs: attention_kernel(score_scale, *refs), out_sh...  25.7 us
    ppermute x4, waiting for transfers between devices, ring_gather(): forward = lax.ppermute(forward, axis, right)  23.8 us
    all_to_all x1, blocking collectives, sublayer(): gathered = lax.all_to_all(projected, 'ctx', 0, 3, tiled=True)  16.5 us
    all_to_all x1, waiting for transfers between devices, sublayer(): gathered = lax.all_to_all(projected, 'ctx', 0, 3, tiled=True)  13.1 us
    unnamed x33, local copies, waits for them, and re-layouts  13 us
    ppermute x3, starting transfers between devices, ring_gather(): backward = lax.ppermute(backward, axis, left)  12.9 us
    all_to_all x1, blocking collectives, sublayer(): lax.all_to_all(context, 'ctx', 0, 0, tiled=True).reshape(width, tok_rows)  10.6 us
    ppermute x1, waiting for transfers between devices, per_device(): current = lax.ppermute(produced, 'pipe', pairs)  9.85 us
  transfers between devices with their start and end apart: 13, of which 9 were waited for; matrix products, arithmetic and copies ran while one was open for 14% of the time, Pallas kernels for 7%

profile of v6, /device:TPU:4, one launch (start us, length us, event | category | flops | bytes accessed | tf_op | source)
XLA Modules:
  0.0 181.0 jit_solution(13114693235574279753)
XLA Ops:
  0.0 2.1 %constant_dynamic-update-slice_fusion.7 = (bf16[512,3072]{1,0:T(8,128)(2,1)}, bf16[512,384]{1,0:T(8,128)(2,1)S(1)}) fusion(bf16[1,1024,384]{2,1,0:T(8,128)(2,1)} %param.12, s32[]{:T(128)S(6)} %select_n.31), kind=kLoop, calls=%fused_computation.65 | loop fusion | bytes 1179652
  2.1 5.9 %collective-permute-start.1 = (bf16[512,384]{1,0:T(8,128)(2,1)S(1)}, bf16[512,384]{1,0:T(8,128)(2,1)S(1)}, u32[]{:S(2)}, u32[]{:S(2)}) collective-permute-start(bf16[512,384]{1,0:T(8,128)(2,1)S(1)} %get-tuple-element.6), channel_id=1, source_target_pairs={{0,7},{1,0},{2,1},{3,2},{4,3},{5,4},{6,5},{7,6},{8,15},{9,8},{10,9... | collective-permute-start | bytes 1179656 | tf_op jit(solution)/shard_map/ppermute | solution.py:98
  7.9 1.1 convert_reduce_fusion.1
  9.0 1.2 fusion.47
  10.2 9.5 %collective-permute-done.4 = bf16[512,384]{1,0:T(8,128)(2,1)S(1)} collective-permute-done((bf16[512,384]{1,0:T(8,128)(2,1)S(1)}, bf16[512,384]{1,0:T(8,128)(2,1)S(1)}, u32[]{:S(2)}, u32[]{:S(2)}) %collective-permute-start.4) | collective-permute-done | bytes 393248 | tf_op jit(solution)/shard_map/ppermute | solution.py:94
  19.7 0.0 collective-permute-start.5
  19.7 1.2 fusion.50
  20.9 0.1 collective-permute-start
  21.0 0.0 collective-permute-done.1
  21.0 3.3 %collective-permute-start.2 = (bf16[512,384]{1,0:T(8,128)(2,1)S(1)}, bf16[512,384]{1,0:T(8,128)(2,1)S(1)}, u32[]{:S(2)}, u32[]{:S(2)}) collective-permute-start(bf16[512,384]{1,0:T(8,128)(2,1)S(1)} %collective-permute-done.1), channel_id=1, source_target_pairs={{0,7},{1,0},{2,1},{3,2},{4,3},{5,4},{6,5},{7,6},{8,15},{9,8},{10,9... | collective-permute-start | bytes 1179656 | tf_op jit(solution)/shard_map/ppermute | solution.py:98
  24.4 6.3 %collective-permute-done.5 = bf16[512,384]{1,0:T(8,128)(2,1)S(1)} collective-permute-done((bf16[512,384]{1,0:T(8,128)(2,1)S(1)}, bf16[512,384]{1,0:T(8,128)(2,1)S(1)}, u32[]{:S(2)}, u32[]{:S(2)}) %collective-permute-start.5) | collective-permute-done | bytes 393248 | tf_op jit(solution)/shard_map/ppermute | solution.py:94
  30.6 0.3 convolution_dynamic-update-slice_fusion.7
  30.9 2.4 %collective-permute-done.2 = bf16[512,384]{1,0:T(8,128)(2,1)S(1)} collective-permute-done((bf16[512,384]{1,0:T(8,128)(2,1)S(1)}, bf16[512,384]{1,0:T(8,128)(2,1)S(1)}, u32[]{:S(2)}, u32[]{:S(2)}) %collective-permute-start.2) | collective-permute-done | bytes 393248 | tf_op jit(solution)/shard_map/ppermute | solution.py:98
  33.3 3.7 %collective-permute-start.3 = (bf16[512,384]{1,0:T(8,128)(2,1)S(1)}, bf16[512,384]{1,0:T(8,128)(2,1)S(1)}, u32[]{:S(2)}, u32[]{:S(2)}) collective-permute-start(bf16[512,384]{1,0:T(8,128)(2,1)S(1)} %collective-permute-done.2), channel_id=1, source_target_pairs={{0,7},{1,0},{2,1},{3,2},{4,3},{5,4},{6,5},{7,6},{8,15},{9,8},{10,9... | collective-permute-start | bytes 1179656 | tf_op jit(solution)/shard_map/ppermute | solution.py:98
  37.0 0.3 convolution_dynamic-update-slice_fusion.6
  37.3 3.4 %collective-permute-done.6 = bf16[512,384]{1,0:T(8,128)(2,1)S(1)} collective-permute-done((bf16[512,384]{1,0:T(8,128)(2,1)S(1)}, bf16[512,384]{1,0:T(8,128)(2,1)S(1)}, u32[]{:S(2)}, u32[]{:S(2)}) %collective-permute-start.6) | collective-permute-done | bytes 393248 | tf_op jit(solution)/shard_map/ppermute | solution.py:94
  40.7 0.3 convolution_dynamic-update-slice_fusion.5
  41.0 4.1 %collective-permute-done.3 = bf16[512,384]{1,0:T(8,128)(2,1)S(1)} collective-permute-done((bf16[512,384]{1,0:T(8,128)(2,1)S(1)}, bf16[512,384]{1,0:T(8,128)(2,1)S(1)}, u32[]{:S(2)}, u32[]{:S(2)}) %collective-permute-start.3) | collective-permute-done | bytes 393248 | tf_op jit(solution)/shard_map/ppermute | solution.py:98
  45.1 0.3 convolution_dynamic-update-slice_fusion.4
  45.4 4.6 %collective-permute-done.7 = bf16[512,384]{1,0:T(8,128)(2,1)S(1)} collective-permute-done((bf16[512,384]{1,0:T(8,128)(2,1)S(1)}, bf16[512,384]{1,0:T(8,128)(2,1)S(1)}, u32[]{:S(2)}, u32[]{:S(2)}) %collective-permute-start.7) | collective-permute-done | bytes 393248 | tf_op jit(solution)/shard_map/ppermute | solution.py:94
  49.9 0.3 convolution_dynamic-update-slice_fusion.3
  50.2 0.3 convolution_dynamic-update-slice_fusion.2
  50.5 0.3 convolution_dynamic-update-slice_fusion.1
  50.9 0.3 convolution_dynamic-update-slice_fusion
  51.2 1.6 copy-done.3
  52.8 1.3 slice.9
  54.1 0.9 constant_dynamic-update-slice_fusion.6
  55.0 2.0 %constant_dynamic-update-slice_fusion.5 = bf16[512,3072]{1,0:T(8,128)(2,1)} fusion(bf16[512,3072]{1,0:T(8,128)(2,1)} %constant_dynamic-update-slice_fusion.6, bf16[512,384]{1,0:T(8,128)(2,1)} %copy-done.5), kind=kLoop, calls=%fused_computation.63 | loop fusion | bytes 786432
  57.0 1.8 %constant_dynamic-update-slice_fusion.4 = bf16[512,3072]{1,0:T(8,128)(2,1)} fusion(bf16[512,3072]{1,0:T(8,128)(2,1)} %constant_dynamic-update-slice_fusion.5, bf16[512,384]{1,0:T(8,128)(2,1)} %copy-done.7), kind=kLoop, calls=%fused_computation.62 | loop fusion | bytes 786432
  58.9 1.8 %constant_dynamic-update-slice_fusion.3 = bf16[512,3072]{1,0:T(8,128)(2,1)} fusion(bf16[512,3072]{1,0:T(8,128)(2,1)} %constant_dynamic-update-slice_fusion.4, bf16[512,384]{1,0:T(8,128)(2,1)} %copy-done.8), kind=kLoop, calls=%fused_computation.61 | loop fusion | bytes 786432
  60.7 1.8 %constant_dynamic-update-slice_fusion.2 = bf16[512,3072]{1,0:T(8,128)(2,1)} fusion(bf16[512,3072]{1,0:T(8,128)(2,1)} %constant_dynamic-update-slice_fusion.3, bf16[512,384]{1,0:T(8,128)(2,1)} %copy-done.6), kind=kLoop, calls=%fused_computation.60 | loop fusion | bytes 786432
  62.5 0.8 constant_dynamic-update-slice_fusion.1
  63.4 0.9 constant_dynamic-update-slice_fusion
  64.2 0.5 collective-permute-start.10
  64.8 1.6 fusion.5
  66.4 0.4 fusion.37
  66.8 1.2 copy.15
  68.0 2.1 %copy.16 = bf16[16,3,64,128]{3,2,1,0:T(8,128)(2,1)} copy(bf16[16,3,64,128]{3,2,0,1:T(8,128)(2,1)} %bitcast.108) | data formatting | bytes 1572864 | tf_op jit(solution)/shard_map/transpose | solution.py:75
  70.1 5.2 %all-to-all-start = ((bf16[16,3,64,128]{3,2,1,0:T(8,128)(2,1)}), bf16[16,3,64,128]{3,2,1,0:T(8,128)(2,1)S(1)}, u32[]{:S(2)}, u32[]{:S(2)}) async-start(bf16[16,3,64,128]{3,2,1,0:T(8,128)(2,1)} %copy.16), calls=%async_computation | async-start | bytes 1572864 | tf_op jit(solution)/shard_map/all_to_all | solution.py:76
  76.0 13.1 %all-to-all-done = bf16[16,3,64,128]{3,2,1,0:T(8,128)(2,1)S(1)} async-done(((bf16[16,3,64,128]{3,2,1,0:T(8,128)(2,1)}), bf16[16,3,64,128]{3,2,1,0:T(8,128)(2,1)S(1)}, u32[]{:S(2)}, u32[]{:S(2)}) %all-to-all-start) | async-done | bytes 786464 | tf_op jit(solution)/shard_map/all_to_all | solution.py:76
  89.0 1.4 copy.17
  90.4 2.2 %squeeze.11.refs_1_ = bf16[3,64,2048]{2,1,0:T(8,128)(2,1)} reshape(bf16[1,3,64,16,128]{4,3,2,1,0:T(8,128)(2,1)} %copy.17) | data formatting | bytes 1572864 | tf_op jit(solution)/shard_map/squeeze | solution.py:77
  92.6 12.9 %shard_map.82 = bf16[64,2048]{1,0:T(8,128)(2,1)} custom-call(s32[1]{0:T(128)} %bitcast.105.refs_0_, bf16[3,64,2048]{2,1,0:T(8,128)(2,1)} %squeeze.11.refs_1_), custom_call_target="tpu_custom_call" | custom-call | flops 1073741824 | bytes 1048576 | tf_op jit(solution)/shard_map/pallas_call | solution.py:43
  105.5 1.0 bitcast_bitcast_fusion.1
  106.6 10.6 %all_to_all.40 = bf16[16,64,128]{2,1,0:T(8,128)(2,1)S(1)} all-to-all(bf16[16,64,128]{2,1,0:T(8,128)(2,1)S(1)} %bitcast_bitcast_fusion.1), channel_id=1, replica_groups=mesh['pipe'=2,'ctx'=16,'dp'=8] {'ctx'}, dimensions={0} | all-to-all | bytes 524288 | tf_op jit(solution)/shard_map/all_to_all | solution.py:79
  117.2 0.5 fusion.27
  117.7 1.3 collective-permute-start.9
  119.0 9.8 %collective-permute-done.9 = bf16[128,1024]{1,0:T(8,128)(2,1)S(1)} collective-permute-done((bf16[128,1024]{1,0:T(8,128)(2,1)S(1)}, bf16[128,1024]{1,0:T(8,128)(2,1)S(1)}, u32[]{:S(2)}, u32[]{:S(2)}) %collective-permute-start.9) | collective-permute-done | bytes 262176 | tf_op jit(solution)/shard_map/ppermute | solution.py:139
  128.9 0.1 convert_reduce_fusion
  129.0 0.2 fusion.43
  129.3 0.2 fusion.46
  129.5 2.5 %fusion.52 = f32[128,3072]{1,0:T(8,128)S(1)} fusion(bf16[512,3072]{1,0:T(8,128)(2,1)} %collective-permute-done.10, bf16[128,1024]{1,0:T(8,128)(2,1)S(1)} %fusion.46, s32[]{:T(128)S(6)} %select_n.33), kind=kOutput, calls=%fused_computation.55 | convolution fusion | flops 402653184 | bytes 4849668 | tf_op jit(solution)/shard_map/dot_general | solution.py:71
  132.0 0.6 fusion
  132.6 0.4 fusion.36
  133.0 1.2 copy.19
  134.2 1.2 copy.20
  135.4 16.5 %all_to_all.41 = bf16[16,3,64,128]{3,2,1,0:T(8,128)(2,1)S(1)} all-to-all(bf16[16,3,64,128]{3,2,1,0:T(8,128)(2,1)S(1)} %copy.20), channel_id=1, replica_groups=mesh['pipe'=2,'ctx'=16,'dp'=8] {'ctx'}, dimensions={0} | all-to-all | bytes 1572864 | tf_op jit(solution)/shard_map/all_to_all | solution.py:76
  151.9 0.5 copy.21
  152.5 1.2 squeeze.13.refs_1_
  153.7 12.8 %shard_map.83 = bf16[64,2048]{1,0:T(8,128)(2,1)} custom-call(s32[1]{0:T(128)} %bitcast.106.refs_0_, bf16[3,64,2048]{2,1,0:T(8,128)(2,1)} %squeeze.13.refs_1_), custom_call_target="tpu_custom_call" | custom-call | flops 1073741824 | bytes 1048576 | tf_op jit(solution)/shard_map/pallas_call | solution.py:43
  166.5 1.7 bitcast_bitcast_fusion
  168.2 3.5 %all-to-all-start.3 = ((bf16[16,64,128]{2,1,0:T(8,128)(2,1)}), bf16[16,64,128]{2,1,0:T(8,128)(2,1)S(1)}, u32[]{:S(2)}, u32[]{:S(2)}) async-start(bf16[16,64,128]{2,1,0:T(8,128)(2,1)} %bitcast_bitcast_fusion), calls=%async_computation.3 | async-start | bytes 524288 | tf_op jit(solution)/shard_map/all_to_all | solution.py:79
  171.8 8.0 %all-to-all-done.3 = bf16[16,64,128]{2,1,0:T(8,128)(2,1)S(1)} async-done(((bf16[16,64,128]{2,1,0:T(8,128)(2,1)}), bf16[16,64,128]{2,1,0:T(8,128)(2,1)S(1)}, u32[]{:S(2)}, u32[]{:S(2)}) %all-to-all-start.3) | async-done | bytes 262176 | tf_op jit(solution)/shard_map/all_to_all | solution.py:79
  179.8 1.2 fusion.33
  (37 shorter events, 0.1 us)
Async XLA Ops:
  0.0 117.2 %copy-start = (bf16[1,1024,1024]{2,1,0:T(8,128)(2,1)S(1)}, bf16[1,1024,1024]{2,1,0:T(8,128)(2,1)}, u32[]{:S(2)}) copy-start(bf16[1,1024,1024]{2,1,0:T(8,128)(2,1)} %param.13) | copy-start | bytes 6291460
  2.1 19.0 %collective-permute-start.1 = (bf16[512,384]{1,0:T(8,128)(2,1)S(1)}, bf16[512,384]{1,0:T(8,128)(2,1)S(1)}, u32[]{:S(2)}, u32[]{:S(2)}) collective-permute-start(bf16[512,384]{1,0:T(8,128)(2,1)S(1)} %get-tuple-element.6), channel_id=1, source_target_pairs={{0,7},{1,0},{2,1},{3,2},{4,3},{5,4},{6,5},{7,6},{8,15},{9,8},{10,9... | collective-permute-start | bytes 1179656 | tf_op jit(solution)/shard_map/ppermute | solution.py:98
  7.9 11.8 %collective-permute-start.4 = (bf16[512,384]{1,0:T(8,128)(2,1)S(1)}, bf16[512,384]{1,0:T(8,128)(2,1)S(1)}, u32[]{:S(2)}, u32[]{:S(2)}) collective-permute-start(bf16[512,384]{1,0:T(8,128)(2,1)S(1)} %get-tuple-element.6), channel_id=1, source_target_pairs={{0,1},{1,2},{2,3},{3,4},{4,5},{5,6},{6,7},{7,0},{8,9},{9,10},{10,1... | collective-permute-start | bytes 1179656 | tf_op jit(solution)/shard_map/ppermute | solution.py:94
  19.7 10.9 %collective-permute-start.5 = (bf16[512,384]{1,0:T(8,128)(2,1)S(1)}, bf16[512,384]{1,0:T(8,128)(2,1)S(1)}, u32[]{:S(2)}, u32[]{:S(2)}) collective-permute-start(bf16[512,384]{1,0:T(8,128)(2,1)S(1)} %collective-permute-done.4), channel_id=1, source_target_pairs={{0,1},{1,2},{2,3},{3,4},{4,5},{5,6},{6,7},{7,0},{8,9},{9,10},{10,1... | collective-permute-start | bytes 1179656 | tf_op jit(solution)/shard_map/ppermute | solution.py:94
  20.9 3.4 %collective-permute-start = (bf16[128,1024]{1,0:T(8,128)(2,1)S(1)}, bf16[128,1024]{1,0:T(8,128)(2,1)S(1)}, u32[]{:S(2)}, u32[]{:S(2)}) collective-permute-start(bf16[128,1024]{1,0:T(8,128)(2,1)S(1)} %fusion.50), channel_id=1, source_target_pairs={{0,8},{8,0},{16,24},{24,16},{32,40},{40,32},{48,56},{56,48},{64,72... | collective-permute-start | bytes 786440 | tf_op jit(solution)/shard_map/ppermute | solution.py:122
  21.0 12.3 %collective-permute-start.2 = (bf16[512,384]{1,0:T(8,128)(2,1)S(1)}, bf16[512,384]{1,0:T(8,128)(2,1)S(1)}, u32[]{:S(2)}, u32[]{:S(2)}) collective-permute-start(bf16[512,384]{1,0:T(8,128)(2,1)S(1)} %collective-permute-done.1), channel_id=1, source_target_pairs={{0,7},{1,0},{2,1},{3,2},{4,3},{5,4},{6,5},{7,6},{8,15},{9,8},{10,9... | collective-permute-start | bytes 1179656 | tf_op jit(solution)/shard_map/ppermute | solution.py:98
  30.6 10.1 %collective-permute-start.6 = (bf16[512,384]{1,0:T(8,128)(2,1)S(1)}, bf16[512,384]{1,0:T(8,128)(2,1)S(1)}, u32[]{:S(2)}, u32[]{:S(2)}) collective-permute-start(bf16[512,384]{1,0:T(8,128)(2,1)S(1)} %collective-permute-done.5), channel_id=1, source_target_pairs={{0,1},{1,2},{2,3},{3,4},{4,5},{5,6},{6,7},{7,0},{8,9},{9,10},{10,1... | collective-permute-start | bytes 1179656 | tf_op jit(solution)/shard_map/ppermute | solution.py:94
  33.3 17.5 %copy-start.5 = (bf16[512,384]{1,0:T(8,128)(2,1)}, bf16[512,384]{1,0:T(8,128)(2,1)S(1)}, u32[]{:S(2)}) copy-start(bf16[512,384]{1,0:T(8,128)(2,1)S(1)} %collective-permute-done.2) | copy-start | bytes 1179652
  33.3 11.8 %collective-permute-start.3 = (bf16[512,384]{1,0:T(8,128)(2,1)S(1)}, bf16[512,384]{1,0:T(8,128)(2,1)S(1)}, u32[]{:S(2)}, u32[]{:S(2)}) collective-permute-start(bf16[512,384]{1,0:T(8,128)(2,1)S(1)} %collective-permute-done.2), channel_id=1, source_target_pairs={{0,7},{1,0},{2,1},{3,2},{4,3},{5,4},{6,5},{7,6},{8,15},{9,8},{10,9... | collective-permute-start | bytes 1179656 | tf_op jit(solution)/shard_map/ppermute | solution.py:98
  40.7 10.1 %copy-start.6 = (bf16[512,384]{1,0:T(8,128)(2,1)}, bf16[512,384]{1,0:T(8,128)(2,1)S(1)}, u32[]{:S(2)}) copy-start(bf16[512,384]{1,0:T(8,128)(2,1)S(1)} %collective-permute-done.6) | copy-start | bytes 1179652
  40.7 9.2 %collective-permute-start.7 = (bf16[512,384]{1,0:T(8,128)(2,1)S(1)}, bf16[512,384]{1,0:T(8,128)(2,1)S(1)}, u32[]{:S(2)}, u32[]{:S(2)}) collective-permute-start(bf16[512,384]{1,0:T(8,128)(2,1)S(1)} %collective-permute-done.6), channel_id=1, source_target_pairs={{0,1},{1,2},{2,3},{3,4},{4,5},{5,6},{6,7},{7,0},{8,9},{9,10},{10,1... | collective-permute-start | bytes 1179656 | tf_op jit(solution)/shard_map/ppermute | solution.py:94
  45.1 5.8 %copy-start.7 = (bf16[512,384]{1,0:T(8,128)(2,1)}, bf16[512,384]{1,0:T(8,128)(2,1)S(1)}, u32[]{:S(2)}) copy-start(bf16[512,384]{1,0:T(8,128)(2,1)S(1)} %collective-permute-done.3) | copy-start | bytes 1179652
  49.9 0.9 copy-start.8
  51.2 1.7 copy-start.3
  54.1 10.6 %collective-permute-start.8 = (f32[128,3072]{1,0:T(8,128)}, f32[128,3072]{1,0:T(8,128)}, u32[]{:S(2)}, u32[]{:S(2)}) collective-permute-start(f32[128,3072]{1,0:T(8,128)} %slice.9), channel_id=1, source_target_pairs={{0,8},{8,0},{16,24},{24,16},{32,40},{40,32},{48,56},{56,48},{64,72... | collective-permute-start | bytes 4718600 | tf_op jit(solution)/shard_map/ppermute | solution.py:128
  54.1 10.6 %copy-start.4 = (f32[256,3072]{1,0:T(8,128)S(1)}, f32[256,3072]{1,0:T(8,128)}, u32[]{:S(2)}) copy-start(f32[256,3072]{1,0:T(8,128)} %copy-done.3) | copy-start | bytes 9437188
  64.2 65.3 %collective-permute-start.10 = (bf16[512,3072]{1,0:T(8,128)(2,1)}, bf16[512,3072]{1,0:T(8,128)(2,1)}, u32[]{:S(2)}, u32[]{:S(2)}) collective-permute-start(bf16[512,3072]{1,0:T(8,128)(2,1)} %constant_dynamic-update-slice_fusion), channel_id=1, source_target_pairs={{0,8},{8,0},{16,24},{24,16},{32,40},{40,32},{48,56},{56,48},{64,72... | collective-permute-start | bytes 9437192 | tf_op jit(solution)/shard_map/ppermute | solution.py:130
  70.1 18.9 %all-to-all-start = ((bf16[16,3,64,128]{3,2,1,0:T(8,128)(2,1)}), bf16[16,3,64,128]{3,2,1,0:T(8,128)(2,1)S(1)}, u32[]{:S(2)}, u32[]{:S(2)}) async-start(bf16[16,3,64,128]{3,2,1,0:T(8,128)(2,1)} %copy.16), calls=%async_computation | async-start | bytes 1572864 | tf_op jit(solution)/shard_map/all_to_all | solution.py:76
  92.6 24.6 %copy-start.1 = (bf16[1,1,128,1024]{3,2,1,0:T(8,128)(2,1)S(1)}, bf16[1,1,128,1024]{3,2,1,0:T(8,128)(2,1)}, u32[]{:S(2)}) copy-start(bf16[1,1,128,1024]{3,2,1,0:T(8,128)(2,1)} %param.8) | copy-start | bytes 786436
  92.6 24.6 %copy-start.11 = (f32[1,1024]{1,0:T(1,128)S(1)}, f32[1,1024]{1,0:T(1,128)}, u32[]{:S(2)}) copy-start(f32[1,1024]{1,0:T(1,128)} %param.14) | copy-start | bytes 12292
  92.6 24.6 %copy-start.12 = (f32[1,1024]{1,0:T(1,128)S(1)}, f32[1,1024]{1,0:T(1,128)}, u32[]{:S(2)}) copy-start(f32[1,1024]{1,0:T(1,128)} %param.15) | copy-start | bytes 12292
  105.5 23.7 %copy-start.9 = (f32[1,1024]{1,0:T(1,128)S(1)}, f32[1,1024]{1,0:T(1,128)}, u32[]{:S(2)}) copy-start(f32[1,1024]{1,0:T(1,128)} %param.11) | copy-start | bytes 12292
  105.5 23.7 %copy-start.10 = (f32[1,1024]{1,0:T(1,128)S(1)}, f32[1,1024]{1,0:T(1,128)}, u32[]{:S(2)}) copy-start(f32[1,1024]{1,0:T(1,128)} %param.10) | copy-start | bytes 12292
  117.7 11.2 %collective-permute-start.9 = (bf16[128,1024]{1,0:T(8,128)(2,1)S(1)}, bf16[128,1024]{1,0:T(8,128)(2,1)S(1)}, u32[]{:S(2)}, u32[]{:S(2)}) collective-permute-start(bf16[128,1024]{1,0:T(8,128)(2,1)S(1)} %fusion.27), channel_id=1, source_target_pairs={{0,128},{1,129},{2,130},{3,131},{4,132},{5,133},{6,134},{7,135},{8... | collective-permute-start | bytes 786440 | tf_op jit(solution)/shard_map/ppermute | solution.py:139
  119.0 13.0 %copy-start.2 = (bf16[512,3072]{1,0:T(8,128)(2,1)S(1)}, bf16[512,3072]{1,0:T(8,128)(2,1)}, u32[]{:S(2)}) copy-start(bf16[512,3072]{1,0:T(8,128)(2,1)} %constant_dynamic-update-slice_fusion) | copy-start | bytes 9437188
  168.2 11.5 %all-to-all-start.3 = ((bf16[16,64,128]{2,1,0:T(8,128)(2,1)}), bf16[16,64,128]{2,1,0:T(8,128)(2,1)S(1)}, u32[]{:S(2)}, u32[]{:S(2)}) async-start(bf16[16,64,128]{2,1,0:T(8,128)(2,1)} %bitcast_bitcast_fusion), calls=%async_computation.3 | async-start | bytes 524288 | tf_op jit(solution)/shard_map/all_to_all | solution.py:79

commit v7 on v4

--- a/solution.py
+++ b/solution.py
@@ -50,7 +50,9 @@
             normed_other, qkv_other, preferred_element_type=jnp.float32
         )
         projected = unrotate(projected.astype(jnp.bfloat16), "dp")
-    projected = jnp.transpose(projected.reshape(tok_rows, 3, HEADS, head_width), (2, 1, 3, 0))
+        projected = jnp.transpose(
+            projected.reshape(tok_rows, 3, HEADS, head_width), (2, 1, 3, 0)
+        )
     gathered = lax.all_to_all(projected, "ctx", 0, 3, tiled=True)
     context = head_attention(gathered[0], length, head_width ** (-0.5))
     context = jnp.transpose(context.reshape(head_width, ctx_count, tok_rows), (1, 0, 2))
@@ -60,7 +62,7 @@
     return (current.astype(jnp.float32) + layer_scale * mixed).astype(jnp.bfloat16)
 
 
-def ring_gather(piece, axis, on_block):
+def ring_gather(piece, axis, on_block, made_axis=1):
     count = lax.axis_size(axis)
     right = [(i, (i + 1) % count) for i in range(count)]
     left = [(i, (i - 1) % count) for i in range(count)]
@@ -76,15 +78,15 @@
             backward = lax.ppermute(backward, axis, left)
             k = 1 + step
             blocks[k], made[k] = backward, on_block(backward)
-    return jnp.concatenate(blocks, axis=1), jnp.concatenate(made, axis=1)
+    return jnp.concatenate(blocks, axis=1), jnp.concatenate(made, axis=made_axis)
 
 
-def unrotate(rotated, axis):
+def unrotate(rotated, axis, along=1):
     count = lax.axis_size(axis)
-    cols = rotated.shape[1]
+    cols = rotated.shape[along]
     shift = lax.axis_index(axis) * (cols // count)
-    doubled = jnp.concatenate([rotated, rotated], axis=1)
-    return lax.dynamic_slice_in_dim(doubled, cols - shift, cols, axis=1)
+    doubled = jnp.concatenate([rotated, rotated], axis=along)
+    return lax.dynamic_slice_in_dim(doubled, cols - shift, cols, axis=along)
 
 
 def per_device(patches, lengths, norm_gain, norm_bias, w_qkv, w_out, out_bias, scale_gain):
@@ -97,14 +99,20 @@
     sibling = [(i, i ^ 1) for i in range(lax.axis_size("ctx"))]
     current = patches[0, 0]
     normed = normalize(current, norm_gain[0], norm_bias[0])
-    both = jnp.concatenate([normed, lax.ppermute(normed, "ctx", sibling)], axis=0)
-    both = lax.dynamic_slice_in_dim(both, core * half, half, axis=1)
-    qkv_mine, partial = ring_gather(
-        rows_mine, "dp", lambda block: jnp.dot(both, block, preferred_element_type=jnp.float32)
-    )
+    normed_sibling = lax.ppermute(normed, "ctx", sibling)
+    mine_rows = lax.dynamic_slice_in_dim(normed, core * half, half, axis=1)
+    sibling_rows = lax.dynamic_slice_in_dim(normed_sibling, core * half, half, axis=1)
+
+    both = jnp.stack([mine_rows, sibling_rows])
+
+    def on_block(block):
+        return jnp.einsum("kc,stk->sct", block, both, preferred_element_type=jnp.float32)
+
+    qkv_mine, partial = ring_gather(rows_mine, "dp", on_block, made_axis=1)
     tok_rows = current.shape[0]
-    partial_other = lax.ppermute(partial[tok_rows:], "ctx", sibling)
-    first = unrotate((partial[:tok_rows] + partial_other).astype(jnp.bfloat16), "dp")
+    partial_other = lax.ppermute(partial[1], "ctx", sibling)
+    first = unrotate((partial[0] + partial_other).astype(jnp.bfloat16), "dp", along=0)
+    first = jnp.transpose(first.reshape(3, HEADS, width // HEADS, tok_rows), (1, 0, 2, 3))
     qkv_other = lax.ppermute(qkv_mine, "ctx", sibling)
     args = (qkv_mine, qkv_other, w_out[0], norm_gain[0], norm_bias[0], out_bias[0], scale_gain[0])
     length = lengths[0, 0]

time: 165 us -> 165 us (level)
    transpose x2 -> x1, local copies, waits for them, and re-layouts: 3.27 us -> 1.18 us  [sublayer(): jnp.transpose(projected.reshape(tok_rows, 3, HEADS, head_width), (2, 1, 3...]
    transpose x0 -> x1, local copies, waits for them, and re-layouts: none -> 2.08 us  [per_device(): jnp.transpose(first.reshape(3, HEADS, width // HEADS, tok_rows), (1, 0, 2...]
  transfers between devices with their start and end apart: 13 -> 13, of which waited for: 10 -> 10; matrix products, arithmetic and copies ran while one was open for 16% -> 17% of each run, Pallas kernels for 0% -> 0%
where the time goes in v7:
time: 165 us; the launch traced here: 164 us
  waiting for transfers between devices  53.4 us (32%)
  blocking collectives  27.2 us (16%)
  starting transfers between devices  23.4 us (14%)
  local copies, waits for them, and re-layouts  22.6 us (14%)
  matrix products  20.1 us (12%)
  other arithmetic  16.6 us (10%)
    ppermute x4, waiting for transfers between devices, ring_gather(): forward = lax.ppermute(forward, axis, right)  23.8 us
    all_to_all x1, blocking collectives, sublayer(): gathered = lax.all_to_all(projected, 'ctx', 0, 3, tiled=True)  16.5 us
    ppermute x3, starting transfers between devices, ring_gather(): backward = lax.ppermute(backward, axis, left)  12.9 us
    unnamed x39, local copies, waits for them, and re-layouts  12.8 us
    all_to_all x1, blocking collectives, sublayer(): lax.all_to_all(context, 'ctx', 0, 0, tiled=True).reshape(width, tok_rows)  10.6 us
    ppermute x1, waiting for transfers between devices, per_device(): current = lax.ppermute(produced, 'pipe', pairs)  9.86 us
    reduce_sum x2, other arithmetic, head_attention(): totals = jnp.sum(weights, axis=-1)  9.64 us
    all_to_all x1, waiting for transfers between devices, sublayer(): lax.all_to_all(context, 'ctx', 0, 0, tiled=True).reshape(width, tok_rows)  7.98 us
  transfers between devices with their start and end apart: 13, of which 10 were waited for; matrix products, arithmetic and copies ran while one was open for 17% of the time, Pallas kernels for 0%

profile of v7, /device:TPU:4, one launch (start us, length us, event | category | flops | bytes accessed | tf_op | source)
XLA Modules:
  0.0 164.3 jit_solution(8226910666279071028)
XLA Ops:
  0.0 2.0 %constant_dynamic-update-slice_fusion.7 = (bf16[512,3072]{1,0:T(8,128)(2,1)}, bf16[512,384]{1,0:T(8,128)(2,1)S(1)}) fusion(bf16[1,1024,384]{2,1,0:T(8,128)(2,1)} %param.12, s32[]{:T(128)S(6)} %select_n.45), kind=kLoop, calls=%fused_computation.116 | loop fusion | bytes 1179652
  2.0 5.9 %collective-permute-start.1 = (bf16[512,384]{1,0:T(8,128)(2,1)S(1)}, bf16[512,384]{1,0:T(8,128)(2,1)S(1)}, u32[]{:S(2)}, u32[]{:S(2)}) collective-permute-start(bf16[512,384]{1,0:T(8,128)(2,1)S(1)} %get-tuple-element.6), channel_id=1, source_target_pairs={{0,7},{1,0},{2,1},{3,2},{4,3},{5,4},{6,5},{7,6},{8,15},{9,8},{10,9... | collective-permute-start | bytes 1179656 | tf_op jit(solution)/shard_map/ppermute | solution.py:78
  7.9 1.1 convert_reduce_fusion.1
  8.9 1.2 fusion.84
  10.1 9.5 %collective-permute-done.4 = bf16[512,384]{1,0:T(8,128)(2,1)S(1)} collective-permute-done((bf16[512,384]{1,0:T(8,128)(2,1)S(1)}, bf16[512,384]{1,0:T(8,128)(2,1)S(1)}, u32[]{:S(2)}, u32[]{:S(2)}) %collective-permute-start.4) | collective-permute-done | bytes 393248 | tf_op jit(solution)/shard_map/ppermute | solution.py:74
  19.7 1.2 fusion.87
  21.0 3.3 %collective-permute-start.2 = (bf16[512,384]{1,0:T(8,128)(2,1)S(1)}, bf16[512,384]{1,0:T(8,128)(2,1)S(1)}, u32[]{:S(2)}, u32[]{:S(2)}) collective-permute-start(bf16[512,384]{1,0:T(8,128)(2,1)S(1)} %collective-permute-done.1), channel_id=1, source_target_pairs={{0,7},{1,0},{2,1},{3,2},{4,3},{5,4},{6,5},{7,6},{8,15},{9,8},{10,9... | collective-permute-start | bytes 1179656 | tf_op jit(solution)/shard_map/ppermute | solution.py:78
  24.3 6.3 %collective-permute-done.5 = bf16[512,384]{1,0:T(8,128)(2,1)S(1)} collective-permute-done((bf16[512,384]{1,0:T(8,128)(2,1)S(1)}, bf16[512,384]{1,0:T(8,128)(2,1)S(1)}, u32[]{:S(2)}, u32[]{:S(2)}) %collective-permute-start.5) | collective-permute-done | bytes 393248 | tf_op jit(solution)/shard_map/ppermute | solution.py:74
  30.6 1.4 fusion.60
  32.0 1.2 collective-permute-done.2
  33.2 3.7 %collective-permute-start.3 = (bf16[512,384]{1,0:T(8,128)(2,1)S(1)}, bf16[512,384]{1,0:T(8,128)(2,1)S(1)}, u32[]{:S(2)}, u32[]{:S(2)}) collective-permute-start(bf16[512,384]{1,0:T(8,128)(2,1)S(1)} %collective-permute-done.2), channel_id=1, source_target_pairs={{0,7},{1,0},{2,1},{3,2},{4,3},{5,4},{6,5},{7,6},{8,15},{9,8},{10,9... | collective-permute-start | bytes 1179656 | tf_op jit(solution)/shard_map/ppermute | solution.py:78
  36.9 0.3 fusion.59
  37.2 3.4 %collective-permute-done.6 = bf16[512,384]{1,0:T(8,128)(2,1)S(1)} collective-permute-done((bf16[512,384]{1,0:T(8,128)(2,1)S(1)}, bf16[512,384]{1,0:T(8,128)(2,1)S(1)}, u32[]{:S(2)}, u32[]{:S(2)}) %collective-permute-start.6) | collective-permute-done | bytes 393248 | tf_op jit(solution)/shard_map/ppermute | solution.py:74
  40.7 0.3 fusion.58
  41.0 4.1 %collective-permute-done.3 = bf16[512,384]{1,0:T(8,128)(2,1)S(1)} collective-permute-done((bf16[512,384]{1,0:T(8,128)(2,1)S(1)}, bf16[512,384]{1,0:T(8,128)(2,1)S(1)}, u32[]{:S(2)}, u32[]{:S(2)}) %collective-permute-start.3) | collective-permute-done | bytes 393248 | tf_op jit(solution)/shard_map/ppermute | solution.py:78
  45.0 0.3 fusion.57
  45.3 4.6 %collective-permute-done.7 = bf16[512,384]{1,0:T(8,128)(2,1)S(1)} collective-permute-done((bf16[512,384]{1,0:T(8,128)(2,1)S(1)}, bf16[512,384]{1,0:T(8,128)(2,1)S(1)}, u32[]{:S(2)}, u32[]{:S(2)}) %collective-permute-start.7) | collective-permute-done | bytes 393248 | tf_op jit(solution)/shard_map/ppermute | solution.py:74
  49.9 0.3 fusion.56
  50.2 0.3 fusion.55
  50.5 0.3 fusion.54
  50.8 0.3 fusion.53
  51.1 1.7 %copy-done.3 = f32[2,3072,128]{1,2,0:T(8,128)} copy-done((f32[2,3072,128]{1,2,0:T(8,128)}, f32[2,3072,128]{1,2,0:T(8,128)S(1)}, u32[]{:S(2)}) %copy-start.3) | copy-done | bytes 3145752
  52.8 1.3 slice_bitcast_fusion
  54.8 3.1 %collective-permute-done.8 = f32[3072,128]{0,1:T(8,128)} collective-permute-done((f32[3072,128]{0,1:T(8,128)}, f32[3072,128]{0,1:T(8,128)}, u32[]{:S(2)}, u32[]{:S(2)}) %collective-permute-start.8) | collective-permute-done | bytes 1572896 | tf_op jit(solution)/shard_map/ppermute | solution.py:113
  57.9 2.0 %fusion.28 = bf16[3072,128]{0,1:T(8,128)(2,1)S(1)} fusion(f32[3072,128]{0,1:T(8,128)} %collective-permute-done.8, f32[2,3072,128]{1,2,0:T(8,128)} %copy-done.3), kind=kLoop, calls=%fused_computation.25 | loop fusion | flops 786432 | bytes 3932160 | tf_op jit(solution)/shard_map/convert_element_type | solution.py:114
  60.0 0.4 fusion.74
  60.4 1.2 copy.19
  61.6 2.1 %copy.20 = bf16[16,3,64,128]{3,2,1,0:T(8,128)(2,1)} copy(bf16[16,3,64,128]{3,2,0,1:T(8,128)(2,1)} %bitcast.196) | data formatting | bytes 1572864 | tf_op jit(solution)/shard_map/transpose | solution.py:115
  63.7 5.2 %all-to-all-start = ((bf16[16,3,64,128]{3,2,1,0:T(8,128)(2,1)}), bf16[16,3,64,128]{3,2,1,0:T(8,128)(2,1)S(1)}, u32[]{:S(2)}, u32[]{:S(2)}) async-start(bf16[16,3,64,128]{3,2,1,0:T(8,128)(2,1)} %copy.20), calls=%async_computation | async-start | bytes 1572864 | tf_op jit(solution)/shard_map/all_to_all | solution.py:56
  68.9 1.9 %constant_dynamic-update-slice_fusion.6 = bf16[512,3072]{1,0:T(8,128)(2,1)} fusion(bf16[512,3072]{1,0:T(8,128)(2,1)} %get-tuple-element.5, bf16[512,384]{1,0:T(8,128)(2,1)} %copy-done.4), kind=kLoop, calls=%fused_computation.115 | loop fusion | bytes 786432
  70.8 1.8 %constant_dynamic-update-slice_fusion.5 = bf16[512,3072]{1,0:T(8,128)(2,1)} fusion(bf16[512,3072]{1,0:T(8,128)(2,1)} %constant_dynamic-update-slice_fusion.6, bf16[512,384]{1,0:T(8,128)(2,1)} %copy-done.9), kind=kLoop, calls=%fused_computation.114 | loop fusion | bytes 786432
  72.6 1.8 %constant_dynamic-update-slice_fusion.4 = bf16[512,3072]{1,0:T(8,128)(2,1)} fusion(bf16[512,3072]{1,0:T(8,128)(2,1)} %constant_dynamic-update-slice_fusion.5, bf16[512,384]{1,0:T(8,128)(2,1)} %copy-done.10), kind=kLoop, calls=%fused_computation.113 | loop fusion | bytes 786432
  74.4 1.8 %constant_dynamic-update-slice_fusion.3 = bf16[512,3072]{1,0:T(8,128)(2,1)} fusion(bf16[512,3072]{1,0:T(8,128)(2,1)} %constant_dynamic-update-slice_fusion.4, bf16[512,384]{1,0:T(8,128)(2,1)} %copy-done.11), kind=kLoop, calls=%fused_computation.112 | loop fusion | bytes 786432
  76.3 0.8 constant_dynamic-update-slice_fusion.2
  77.1 0.8 constant_dynamic-update-slice_fusion.1
  78.0 0.8 constant_dynamic-update-slice_fusion
  78.8 0.4 collective-permute-start.10
  79.2 3.4 %all-to-all-done = bf16[16,3,64,128]{3,2,1,0:T(8,128)(2,1)S(1)} async-done(((bf16[16,3,64,128]{3,2,1,0:T(8,128)(2,1)}), bf16[16,3,64,128]{3,2,1,0:T(8,128)(2,1)S(1)}, u32[]{:S(2)}, u32[]{:S(2)}) %all-to-all-start) | async-done | bytes 786464 | tf_op jit(solution)/shard_map/all_to_all | solution.py:56
  82.7 0.2 copy.22
  82.8 0.2 copy.23
  83.0 2.8 %select_reduce_fusion.1 = (f32[2048]{0:T(1024)S(1)}, f32[2048,2048]{0,1:T(8,128)S(1)}) fusion(pred[2048]{0:T(1024)(128)(4,1)S(1)} %iota_compare_fusion, bf16[8,8,16,128]{3,2,1,0:T(8,128)(2,1)S(1)} %bitcast.201, bf16[8,8,16,128]{3,2,1,0:T(8,128)(2,1)S(1)} %bitcast.200), kind=kOutput, calls=%fused_computation.3 | convolution fusion | flops 549451776 | bytes 17311744 | tf_op jit(solution)/shard_map/dq,dk->qk/dot_general | solution.py:25
  85.8 4.8 %fusion = f32[2048]{0:T(1024)S(1)} fusion(f32[2048,2048]{0,1:T(8,128)S(1)} %get-tuple-element.14, f32[2048]{0:T(1024)S(1)} %get-tuple-element.13, pred[2048]{0:T(1024)(128)(4,1)S(1)} %iota_compare_fusion), kind=kLoop, calls=%fused_computation.4 | loop fusion | flops 16775168 | bytes 16795648 | tf_op jit(solution)/shard_map/reduce_sum | solution.py:31
  90.6 0.2 copy.21
  90.9 3.1 %fusion.70 = bf16[8,16,8,128]{3,2,1,0:T(8,128)(2,1)S(1)} fusion(f32[2048,2048]{0,1:T(8,128)S(1)} %get-tuple-element.14, f32[2048]{0:T(1024)S(1)} %get-tuple-element.13, pred[2048]{0:T(1024)(128)(4,1)S(1)} %iota_compare_fusion, bf16[8,8,16,128]{3,2,1,0:T(8,128)(2,1)S(1)} %bitcast.206, f32[2048]{0:T(1024)S(1)} %fusion), kind=kOutput, calls=%fused_computation.57 | convolution fusion | flops 553910272 | bytes 17319936 | tf_op jit(solution)/shard_map/qk,dk->dq/dot_general | solution.py:32
  94.1 10.6 %all_to_all.40 = bf16[16,64,128]{2,1,0:T(8,128)(2,1)S(1)} all-to-all(bf16[16,64,128]{2,1,0:T(8,128)(2,1)S(1)} %bitcast.202), channel_id=1, replica_groups=mesh['pipe'=2,'ctx'=16,'dp'=8] {'ctx'}, dimensions={0} | all-to-all | bytes 524288 | tf_op jit(solution)/shard_map/all_to_all | solution.py:59
  104.7 0.5 fusion.50
  105.2 1.3 collective-permute-start.9
  106.5 9.9 %collective-permute-done.9 = bf16[128,1024]{1,0:T(8,128)(2,1)S(1)} collective-permute-done((bf16[128,1024]{1,0:T(8,128)(2,1)S(1)}, bf16[128,1024]{1,0:T(8,128)(2,1)S(1)}, u32[]{:S(2)}, u32[]{:S(2)}) %collective-permute-start.9) | collective-permute-done | bytes 262176 | tf_op jit(solution)/shard_map/ppermute | solution.py:125
  116.5 0.2 fusion.80
  116.8 0.2 fusion.83
  117.0 2.5 %fusion.111 = f32[128,3072]{1,0:T(8,128)S(1)} fusion(bf16[512,3072]{1,0:T(8,128)(2,1)} %collective-permute-done.10, bf16[128,1024]{1,0:T(8,128)(2,1)S(1)} %fusion.83, s32[]{:T(128)S(6)} %select_n.49), kind=kOutput, calls=%fused_computation.104 | convolution fusion | flops 402653184 | bytes 4849668 | tf_op jit(solution)/shard_map/dot_general | solution.py:49
  119.5 0.6 fusion.10
  120.1 0.4 fusion.73
  120.5 1.2 copy.25
  121.7 1.2 copy.26
  122.9 16.5 %all_to_all.41 = bf16[16,3,64,128]{3,2,1,0:T(8,128)(2,1)S(1)} all-to-all(bf16[16,3,64,128]{3,2,1,0:T(8,128)(2,1)S(1)} %copy.26), channel_id=1, replica_groups=mesh['pipe'=2,'ctx'=16,'dp'=8] {'ctx'}, dimensions={0} | all-to-all | bytes 1572864 | tf_op jit(solution)/shard_map/all_to_all | solution.py:56
  139.5 0.2 copy.28
  140.0 2.8 %select_reduce_fusion = (f32[2048]{0:T(1024)S(1)}, f32[2048,2048]{0,1:T(8,128)S(1)}) fusion(pred[2048]{0:T(1024)(128)(4,1)S(1)} %iota_compare_fusion, bf16[8,8,16,128]{3,2,1,0:T(8,128)(2,1)S(1)} %bitcast.199, bf16[8,8,16,128]{3,2,1,0:T(8,128)(2,1)S(1)} %bitcast.198), kind=kOutput, calls=%fused_computation.1 | convolution fusion | flops 549451776 | bytes 17311744 | tf_op jit(solution)/shard_map/dq,dk->qk/dot_general | solution.py:25
  142.9 4.8 %fusion.2 = f32[2048]{0:T(1024)S(1)} fusion(f32[2048,2048]{0,1:T(8,128)S(1)} %get-tuple-element.16, f32[2048]{0:T(1024)S(1)} %get-tuple-element.15, pred[2048]{0:T(1024)(128)(4,1)S(1)} %iota_compare_fusion), kind=kLoop, calls=%fused_computation.6 | loop fusion | flops 16775168 | bytes 16795648 | tf_op jit(solution)/shard_map/reduce_sum | solution.py:31
  147.7 3.1 %fusion.67 = bf16[8,16,8,128]{3,2,1,0:T(8,128)(2,1)S(1)} fusion(f32[2048,2048]{0,1:T(8,128)S(1)} %get-tuple-element.16, f32[2048]{0:T(1024)S(1)} %get-tuple-element.15, pred[2048]{0:T(1024)(128)(4,1)S(1)} %iota_compare_fusion, bf16[8,8,16,128]{3,2,1,0:T(8,128)(2,1)S(1)} %bitcast.205, f32[2048]{0:T(1024)S(1)} %fusion.2), kind=kOutput, calls=%fused_computation.56 | convolution fusion | flops 553910272 | bytes 17319936 | tf_op jit(solution)/shard_map/qk,dk->dq/dot_general | solution.py:32
  150.8 0.8 copy.73
  151.6 3.5 %all-to-all-start.3 = ((bf16[16,64,128]{2,1,0:T(8,128)(2,1)}), bf16[16,64,128]{2,1,0:T(8,128)(2,1)S(1)}, u32[]{:S(2)}, u32[]{:S(2)}) async-start(bf16[16,64,128]{2,1,0:T(8,128)(2,1)} %bitcast.190), calls=%async_computation.3 | async-start | bytes 524288 | tf_op jit(solution)/shard_map/all_to_all | solution.py:59
  155.1 8.0 %all-to-all-done.3 = bf16[16,64,128]{2,1,0:T(8,128)(2,1)S(1)} async-done(((bf16[16,64,128]{2,1,0:T(8,128)(2,1)}), bf16[16,64,128]{2,1,0:T(8,128)(2,1)S(1)}, u32[]{:S(2)}, u32[]{:S(2)}) %all-to-all-start.3) | async-done | bytes 262176 | tf_op jit(solution)/shard_map/all_to_all | solution.py:59
  163.1 1.2 fusion.64
  (53 shorter events, 0.9 us)
Async XLA Ops:
  0.0 104.7 %copy-start = (bf16[1,1024,1024]{2,1,0:T(8,128)(2,1)S(1)}, bf16[1,1024,1024]{2,1,0:T(8,128)(2,1)}, u32[]{:S(2)}) copy-start(bf16[1,1024,1024]{2,1,0:T(8,128)(2,1)} %param.13) | copy-start | bytes 6291460
  2.0 19.0 %collective-permute-start.1 = (bf16[512,384]{1,0:T(8,128)(2,1)S(1)}, bf16[512,384]{1,0:T(8,128)(2,1)S(1)}, u32[]{:S(2)}, u32[]{:S(2)}) collective-permute-start(bf16[512,384]{1,0:T(8,128)(2,1)S(1)} %get-tuple-element.6), channel_id=1, source_target_pairs={{0,7},{1,0},{2,1},{3,2},{4,3},{5,4},{6,5},{7,6},{8,15},{9,8},{10,9... | collective-permute-start | bytes 1179656 | tf_op jit(solution)/shard_map/ppermute | solution.py:78
  7.9 11.8 %collective-permute-start.4 = (bf16[512,384]{1,0:T(8,128)(2,1)S(1)}, bf16[512,384]{1,0:T(8,128)(2,1)S(1)}, u32[]{:S(2)}, u32[]{:S(2)}) collective-permute-start(bf16[512,384]{1,0:T(8,128)(2,1)S(1)} %get-tuple-element.6), channel_id=1, source_target_pairs={{0,1},{1,2},{2,3},{3,4},{4,5},{5,6},{6,7},{7,0},{8,9},{9,10},{10,1... | collective-permute-start | bytes 1179656 | tf_op jit(solution)/shard_map/ppermute | solution.py:74
  19.7 10.9 %collective-permute-start.5 = (bf16[512,384]{1,0:T(8,128)(2,1)S(1)}, bf16[512,384]{1,0:T(8,128)(2,1)S(1)}, u32[]{:S(2)}, u32[]{:S(2)}) collective-permute-start(bf16[512,384]{1,0:T(8,128)(2,1)S(1)} %collective-permute-done.4), channel_id=1, source_target_pairs={{0,1},{1,2},{2,3},{3,4},{4,5},{5,6},{6,7},{7,0},{8,9},{9,10},{10,1... | collective-permute-start | bytes 1179656 | tf_op jit(solution)/shard_map/ppermute | solution.py:74
  20.9 9.7 %collective-permute-start = (bf16[128,1024]{1,0:T(8,128)(2,1)S(1)}, bf16[128,1024]{1,0:T(8,128)(2,1)S(1)}, u32[]{:S(2)}, u32[]{:S(2)}) collective-permute-start(bf16[128,1024]{1,0:T(8,128)(2,1)S(1)} %fusion.87), channel_id=1, source_target_pairs={{0,8},{8,0},{16,24},{24,16},{32,40},{40,32},{48,56},{56,48},{64,72... | collective-permute-start | bytes 786440 | tf_op jit(solution)/shard_map/ppermute | solution.py:102
  21.0 29.5 %copy-start.4 = (bf16[512,384]{1,0:T(8,128)(2,1)}, bf16[512,384]{1,0:T(8,128)(2,1)S(1)}, u32[]{:S(2)}) copy-start(bf16[512,384]{1,0:T(8,128)(2,1)S(1)} %collective-permute-done.1) | copy-start | bytes 1179652
  21.0 12.3 %collective-permute-start.2 = (bf16[512,384]{1,0:T(8,128)(2,1)S(1)}, bf16[512,384]{1,0:T(8,128)(2,1)S(1)}, u32[]{:S(2)}, u32[]{:S(2)}) collective-permute-start(bf16[512,384]{1,0:T(8,128)(2,1)S(1)} %collective-permute-done.1), channel_id=1, source_target_pairs={{0,7},{1,0},{2,1},{3,2},{4,3},{5,4},{6,5},{7,6},{8,15},{9,8},{10,9... | collective-permute-start | bytes 1179656 | tf_op jit(solution)/shard_map/ppermute | solution.py:78
  30.6 19.9 %copy-start.5 = (bf16[512,384]{1,0:T(8,128)(2,1)}, bf16[512,384]{1,0:T(8,128)(2,1)S(1)}, u32[]{:S(2)}) copy-start(bf16[512,384]{1,0:T(8,128)(2,1)S(1)} %collective-permute-done.5) | copy-start | bytes 1179652
  30.6 10.1 %collective-permute-start.6 = (bf16[512,384]{1,0:T(8,128)(2,1)S(1)}, bf16[512,384]{1,0:T(8,128)(2,1)S(1)}, u32[]{:S(2)}, u32[]{:S(2)}) collective-permute-start(bf16[512,384]{1,0:T(8,128)(2,1)S(1)} %collective-permute-done.5), channel_id=1, source_target_pairs={{0,1},{1,2},{2,3},{3,4},{4,5},{5,6},{6,7},{7,0},{8,9},{9,10},{10,1... | collective-permute-start | bytes 1179656 | tf_op jit(solution)/shard_map/ppermute | solution.py:74
  33.2 17.6 %copy-start.9 = (bf16[512,384]{1,0:T(8,128)(2,1)}, bf16[512,384]{1,0:T(8,128)(2,1)S(1)}, u32[]{:S(2)}) copy-start(bf16[512,384]{1,0:T(8,128)(2,1)S(1)} %collective-permute-done.2) | copy-start | bytes 1179652
  33.2 11.8 %collective-permute-start.3 = (bf16[512,384]{1,0:T(8,128)(2,1)S(1)}, bf16[512,384]{1,0:T(8,128)(2,1)S(1)}, u32[]{:S(2)}, u32[]{:S(2)}) collective-permute-start(bf16[512,384]{1,0:T(8,128)(2,1)S(1)} %collective-permute-done.2), channel_id=1, source_target_pairs={{0,7},{1,0},{2,1},{3,2},{4,3},{5,4},{6,5},{7,6},{8,15},{9,8},{10,9... | collective-permute-start | bytes 1179656 | tf_op jit(solution)/shard_map/ppermute | solution.py:78
  40.7 10.1 %copy-start.7 = (bf16[512,384]{1,0:T(8,128)(2,1)}, bf16[512,384]{1,0:T(8,128)(2,1)S(1)}, u32[]{:S(2)}) copy-start(bf16[512,384]{1,0:T(8,128)(2,1)S(1)} %collective-permute-done.6) | copy-start | bytes 1179652
  40.7 9.2 %collective-permute-start.7 = (bf16[512,384]{1,0:T(8,128)(2,1)S(1)}, bf16[512,384]{1,0:T(8,128)(2,1)S(1)}, u32[]{:S(2)}, u32[]{:S(2)}) collective-permute-start(bf16[512,384]{1,0:T(8,128)(2,1)S(1)} %collective-permute-done.6), channel_id=1, source_target_pairs={{0,1},{1,2},{2,3},{3,4},{4,5},{5,6},{6,7},{7,0},{8,9},{9,10},{10,1... | collective-permute-start | bytes 1179656 | tf_op jit(solution)/shard_map/ppermute | solution.py:74
  45.0 5.8 %copy-start.10 = (bf16[512,384]{1,0:T(8,128)(2,1)}, bf16[512,384]{1,0:T(8,128)(2,1)S(1)}, u32[]{:S(2)}) copy-start(bf16[512,384]{1,0:T(8,128)(2,1)S(1)} %collective-permute-done.3) | copy-start | bytes 1179652
  49.9 0.9 copy-start.11
  51.1 1.7 %copy-start.3 = (f32[2,3072,128]{1,2,0:T(8,128)}, f32[2,3072,128]{1,2,0:T(8,128)S(1)}, u32[]{:S(2)}) copy-start(f32[2,3072,128]{1,2,0:T(8,128)S(1)} %fusion.53) | copy-start | bytes 9437188
  54.2 3.8 %collective-permute-start.8 = (f32[3072,128]{0,1:T(8,128)}, f32[3072,128]{0,1:T(8,128)}, u32[]{:S(2)}, u32[]{:S(2)}) collective-permute-start(f32[3072,128]{0,1:T(8,128)} %slice_bitcast_fusion), channel_id=1, source_target_pairs={{0,8},{8,0},{16,24},{24,16},{32,40},{40,32},{48,56},{56,48},{64,72... | collective-permute-start | bytes 4718600 | tf_op jit(solution)/shard_map/ppermute | solution.py:113
  63.7 18.9 %all-to-all-start = ((bf16[16,3,64,128]{3,2,1,0:T(8,128)(2,1)}), bf16[16,3,64,128]{3,2,1,0:T(8,128)(2,1)S(1)}, u32[]{:S(2)}, u32[]{:S(2)}) async-start(bf16[16,3,64,128]{3,2,1,0:T(8,128)(2,1)} %copy.20), calls=%async_computation | async-start | bytes 1572864 | tf_op jit(solution)/shard_map/all_to_all | solution.py:56
  68.9 7.4 %copy-start.8 = (bf16[512,384]{1,0:T(8,128)(2,1)S(1)}, bf16[512,384]{1,0:T(8,128)(2,1)}, u32[]{:S(2)}) copy-start(bf16[512,384]{1,0:T(8,128)(2,1)} %copy-done.7) | copy-start | bytes 1179652
  68.9 8.2 %copy-start.6 = (bf16[512,384]{1,0:T(8,128)(2,1)S(1)}, bf16[512,384]{1,0:T(8,128)(2,1)}, u32[]{:S(2)}) copy-start(bf16[512,384]{1,0:T(8,128)(2,1)} %copy-done.5) | copy-start | bytes 1179652
  78.8 38.2 %collective-permute-start.10 = (bf16[512,3072]{1,0:T(8,128)(2,1)}, bf16[512,3072]{1,0:T(8,128)(2,1)}, u32[]{:S(2)}, u32[]{:S(2)}) collective-permute-start(bf16[512,3072]{1,0:T(8,128)(2,1)} %constant_dynamic-update-slice_fusion), channel_id=1, source_target_pairs={{0,8},{8,0},{16,24},{24,16},{32,40},{40,32},{48,56},{56,48},{64,72... | collective-permute-start | bytes 9437192 | tf_op jit(solution)/shard_map/ppermute | solution.py:116
  90.8 13.9 %copy-start.1 = (bf16[1,1,128,1024]{3,2,1,0:T(8,128)(2,1)S(1)}, bf16[1,1,128,1024]{3,2,1,0:T(8,128)(2,1)}, u32[]{:S(2)}) copy-start(bf16[1,1,128,1024]{3,2,1,0:T(8,128)(2,1)} %param.8) | copy-start | bytes 786436
  90.8 13.9 %copy-start.14 = (f32[1,1024]{1,0:T(1,128)S(1)}, f32[1,1024]{1,0:T(1,128)}, u32[]{:S(2)}) copy-start(f32[1,1024]{1,0:T(1,128)} %param.14) | copy-start | bytes 12292
  90.9 13.9 %copy-start.15 = (f32[1,1024]{1,0:T(1,128)S(1)}, f32[1,1024]{1,0:T(1,128)}, u32[]{:S(2)}) copy-start(f32[1,1024]{1,0:T(1,128)} %param.15) | copy-start | bytes 12292
  94.0 22.8 %copy-start.12 = (f32[1,1024]{1,0:T(1,128)S(1)}, f32[1,1024]{1,0:T(1,128)}, u32[]{:S(2)}) copy-start(f32[1,1024]{1,0:T(1,128)} %param.11) | copy-start | bytes 12292
  94.0 22.8 %copy-start.13 = (f32[1,1024]{1,0:T(1,128)S(1)}, f32[1,1024]{1,0:T(1,128)}, u32[]{:S(2)}) copy-start(f32[1,1024]{1,0:T(1,128)} %param.10) | copy-start | bytes 12292
  105.2 11.2 %collective-permute-start.9 = (bf16[128,1024]{1,0:T(8,128)(2,1)S(1)}, bf16[128,1024]{1,0:T(8,128)(2,1)S(1)}, u32[]{:S(2)}, u32[]{:S(2)}) collective-permute-start(bf16[128,1024]{1,0:T(8,128)(2,1)S(1)} %fusion.50), channel_id=1, source_target_pairs={{0,128},{1,129},{2,130},{3,131},{4,132},{5,133},{6,134},{7,135},{8... | collective-permute-start | bytes 786440 | tf_op jit(solution)/shard_map/ppermute | solution.py:125
  106.5 13.0 %copy-start.2 = (bf16[512,3072]{1,0:T(8,128)(2,1)S(1)}, bf16[512,3072]{1,0:T(8,128)(2,1)}, u32[]{:S(2)}) copy-start(bf16[512,3072]{1,0:T(8,128)(2,1)} %constant_dynamic-update-slice_fusion) | copy-start | bytes 9437188
  151.6 11.5 %all-to-all-start.3 = ((bf16[16,64,128]{2,1,0:T(8,128)(2,1)}), bf16[16,64,128]{2,1,0:T(8,128)(2,1)S(1)}, u32[]{:S(2)}, u32[]{:S(2)}) async-start(bf16[16,64,128]{2,1,0:T(8,128)(2,1)} %bitcast.190), calls=%async_computation.3 | async-start | bytes 524288 | tf_op jit(solution)/shard_map/all_to_all | solution.py:59

commit v8 on v7

--- a/solution.py
+++ b/solution.py
@@ -62,7 +62,7 @@
     return (current.astype(jnp.float32) + layer_scale * mixed).astype(jnp.bfloat16)
 
 
-def ring_gather(piece, axis, on_block, made_axis=1):
+def ring_gather(piece, axis, on_block, made_axis):
     count = lax.axis_size(axis)
     right = [(i, (i + 1) % count) for i in range(count)]
     left = [(i, (i - 1) % count) for i in range(count)]
@@ -78,7 +78,9 @@
             backward = lax.ppermute(backward, axis, left)
             k = 1 + step
             blocks[k], made[k] = backward, on_block(backward)
-    return jnp.concatenate(blocks, axis=1), jnp.concatenate(made, axis=made_axis)
+    blocks = lax.optimization_barrier(blocks)
+    made = [jnp.concatenate(parts, axis=made_axis) for parts in zip(*made)]
+    return jnp.concatenate(blocks, axis=1), made
 
 
 def unrotate(rotated, axis, along=1):
@@ -103,12 +105,13 @@
     mine_rows = lax.dynamic_slice_in_dim(normed, core * half, half, axis=1)
     sibling_rows = lax.dynamic_slice_in_dim(normed_sibling, core * half, half, axis=1)
 
-    both = jnp.stack([mine_rows, sibling_rows])
+    def on_block(block):
+        return tuple(
+            jnp.einsum("kc,tk->ct", block, rows, preferred_element_type=jnp.float32)
+            for rows in (mine_rows, sibling_rows)
+        )
 
-    def on_block(block):
-        return jnp.einsum("kc,stk->sct", block, both, preferred_element_type=jnp.float32)
-
-    qkv_mine, partial = ring_gather(rows_mine, "dp", on_block, made_axis=1)
+    qkv_mine, partial = ring_gather(rows_mine, "dp", on_block, made_axis=0)
     tok_rows = current.shape[0]
     partial_other = lax.ppermute(partial[1], "ctx", sibling)
     first = unrotate((partial[0] + partial_other).astype(jnp.bfloat16), "dp", along=0)

time: 165 us -> 166 us (level)
  matrix products: 20.1 us -> 30.3 us
  waiting for transfers between devices: 53.4 us -> 47.8 us
  local copies, waits for them, and re-layouts: 22.6 us -> 18.4 us
    dot_general x8 -> x16, matrix products: 3.44 us -> 13.7 us  [on_block(): jnp.einsum('kc,tk->ct', block, rows, preferred_element_type=jnp.float32)]
    ppermute x3, waiting for transfers between devices: 5.27 us -> 0.01 us  [ring_gather(): backward = lax.ppermute(backward, axis, left)]
    ppermute x1, waiting for transfers between devices: 3.08 us -> 0.01 us  [per_device(): partial_other = lax.ppermute(partial[1], 'ctx', sibling)]
    unnamed x39 -> x33, local copies, waits for them, and re-layouts: 12.8 us -> 9.99 us
    ppermute x4, waiting for transfers between devices: 23.8 us -> 26.5 us  [ring_gather(): forward = lax.ppermute(forward, axis, right)]
    concatenate x2, other arithmetic: 0.85 us -> 3.17 us  [unrotate(): doubled = jnp.concatenate([rotated, rotated], axis=along)]
    convert_element_type x1, other arithmetic: 2.04 us -> 0.16 us  [per_device(): (partial[0] + partial_other).astype(jnp.bfloat16)]
  transfers between devices with their start and end apart: 13 -> 13, of which waited for: 10 -> 7; matrix products, arithmetic and copies ran while one was open for 17% -> 23% of each run, Pallas kernels for 0% -> 0%
where the time goes in v8:
time: 166 us; the launch traced here: 165 us
  waiting for transfers between devices  47.8 us (29%)
  matrix products  30.3 us (18%)
  blocking collectives  27.2 us (16%)
  starting transfers between devices  23.4 us (14%)
  local copies, waits for them, and re-layouts  18.4 us (11%)
  other arithmetic  17 us (10%)
    ppermute x4, waiting for transfers between devices, ring_gather(): forward = lax.ppermute(forward, axis, right)  26.5 us
    all_to_all x1, blocking collectives, sublayer(): gathered = lax.all_to_all(projected, 'ctx', 0, 3, tiled=True)  16.5 us
    dot_general x16, matrix products, on_block(): jnp.einsum('kc,tk->ct', block, rows, preferred_element_type=jnp.float32)  13.7 us
    ppermute x3, starting transfers between devices, ring_gather(): backward = lax.ppermute(backward, axis, left)  12.5 us
    all_to_all x1, blocking collectives, sublayer(): lax.all_to_all(context, 'ctx', 0, 0, tiled=True).reshape(width, tok_rows)  10.6 us
    unnamed x33, local copies, waits for them, and re-layouts  9.99 us
    ppermute x1, waiting for transfers between devices, per_device(): current = lax.ppermute(produced, 'pipe', pairs)  9.86 us
    reduce_sum x2, other arithmetic, head_attention(): totals = jnp.sum(weights, axis=-1)  9.64 us
  transfers between devices with their start and end apart: 13, of which 7 were waited for; matrix products, arithmetic and copies ran while one was open for 23% of the time, Pallas kernels for 0%

profile of v8, /device:TPU:4, one launch (start us, length us, event | category | flops | bytes accessed | tf_op | source)
XLA Modules:
  0.0 165.3 jit_solution(13975363779195929846)
XLA Ops:
  0.0 1.2 dynamic-slice_bitcast_fusion
  1.2 5.9 %collective-permute-start = (bf16[512,384]{1,0:T(8,128)(2,1)S(1)}, bf16[512,384]{1,0:T(8,128)(2,1)S(1)}, u32[]{:S(2)}, u32[]{:S(2)}) collective-permute-start(bf16[512,384]{1,0:T(8,128)(2,1)S(1)} %dynamic-slice_bitcast_fusion), channel_id=1, source_target_pairs={{0,7},{1,0},{2,1},{3,2},{4,3},{5,4},{6,5},{7,6},{8,15},{9,8},{10,9... | collective-permute-start | bytes 1179656 | tf_op jit(solution)/shard_map/ppermute | solution.py:78
  7.1 1.1 convert_reduce_fusion.1
  8.2 1.2 fusion.74
  9.4 9.5 %collective-permute-done.3 = bf16[512,384]{1,0:T(8,128)(2,1)S(1)} collective-permute-done((bf16[512,384]{1,0:T(8,128)(2,1)S(1)}, bf16[512,384]{1,0:T(8,128)(2,1)S(1)}, u32[]{:S(2)}, u32[]{:S(2)}) %collective-permute-start.3) | collective-permute-done | bytes 393248 | tf_op jit(solution)/shard_map/ppermute | solution.py:74
  18.9 3.2 %collective-permute-start.1 = (bf16[512,384]{1,0:T(8,128)(2,1)S(1)}, bf16[512,384]{1,0:T(8,128)(2,1)}, u32[]{:S(2)}, u32[]{:S(2)}) collective-permute-start(bf16[512,384]{1,0:T(8,128)(2,1)S(1)} %collective-permute-done), channel_id=1, source_target_pairs={{0,7},{1,0},{2,1},{3,2},{4,3},{5,4},{6,5},{7,6},{8,15},{9,8},{10,9... | collective-permute-start | bytes 1179656 | tf_op jit(solution)/shard_map/ppermute | solution.py:78
  22.2 1.2 fusion.77
  24.1 2.0 %convolution_dynamic-update-slice_fusion.15 = f32[3072,128]{1,0:T(8,128)} fusion(bf16[128,1024]{1,0:T(8,128)(2,1)S(1)} %fusion.77, s32[]{:T(128)S(6)} %select_n.45, bf16[1,1024,384]{2,1,0:T(8,128)(2,1)} %param.12), kind=kOutput, calls=%fused_computation.50 | convolution fusion | flops 50331648 | bytes 721920 | tf_op jit(solution)/shard_map/kc,tk->ct/dot_general | solution.py:110
  26.1 3.8 %collective-permute-done.4 = bf16[512,384]{1,0:T(8,128)(2,1)} collective-permute-done((bf16[512,384]{1,0:T(8,128)(2,1)S(1)}, bf16[512,384]{1,0:T(8,128)(2,1)}, u32[]{:S(2)}, u32[]{:S(2)}) %collective-permute-start.4) | collective-permute-done | bytes 393248 | tf_op jit(solution)/shard_map/ppermute | solution.py:74
  30.0 1.4 convolution_dynamic-update-slice_fusion.7
  31.4 3.3 %collective-permute-start.2 = (bf16[512,384]{1,0:T(8,128)(2,1)}, bf16[512,384]{1,0:T(8,128)(2,1)S(1)}, u32[]{:S(2)}, u32[]{:S(2)}) collective-permute-start(bf16[512,384]{1,0:T(8,128)(2,1)} %collective-permute-done.1), channel_id=1, source_target_pairs={{0,7},{1,0},{2,1},{3,2},{4,3},{5,4},{6,5},{7,6},{8,15},{9,8},{10,9... | collective-permute-start | bytes 1179656 | tf_op jit(solution)/shard_map/ppermute | solution.py:78
  34.7 0.3 convolution_dynamic-update-slice_fusion.6
  35.0 5.3 %collective-permute-done.5 = bf16[512,384]{1,0:T(8,128)(2,1)} collective-permute-done((bf16[512,384]{1,0:T(8,128)(2,1)}, bf16[512,384]{1,0:T(8,128)(2,1)}, u32[]{:S(2)}, u32[]{:S(2)}) %collective-permute-start.5) | collective-permute-done | bytes 393248 | tf_op jit(solution)/shard_map/ppermute | solution.py:74
  40.4 1.3 convolution_dynamic-update-slice_fusion.5
  41.7 0.3 convolution_dynamic-update-slice_fusion.4
  42.0 7.8 %collective-permute-done.6 = bf16[512,384]{1,0:T(8,128)(2,1)S(1)} collective-permute-done((bf16[512,384]{1,0:T(8,128)(2,1)}, bf16[512,384]{1,0:T(8,128)(2,1)S(1)}, u32[]{:S(2)}, u32[]{:S(2)}) %collective-permute-start.6) | collective-permute-done | bytes 393248 | tf_op jit(solution)/shard_map/ppermute | solution.py:74
  49.8 0.3 convolution_dynamic-update-slice_fusion.3
  50.1 1.3 convolution_dynamic-update-slice_fusion.2
  51.4 1.3 convolution_dynamic-update-slice_fusion.1
  52.7 0.3 convolution_dynamic-update-slice_fusion
  53.0 0.3 collective-permute-start.8
  53.3 0.3 convolution_dynamic-update-slice_fusion.14
  53.6 1.3 convolution_dynamic-update-slice_fusion.13
  55.0 0.3 convolution_dynamic-update-slice_fusion.12
  55.3 0.9 constant_dynamic-update-slice_fusion.7
  56.2 0.3 convolution_dynamic-update-slice_fusion.11
  56.5 1.3 convolution_dynamic-update-slice_fusion.10
  57.8 1.3 convolution_dynamic-update-slice_fusion.9
  59.1 0.3 convolution_dynamic-update-slice_fusion.8
  59.6 2.7 %fusion.64 = bf16[3072,128]{1,0:T(8,128)(2,1)S(1)} fusion(s32[]{:T(128)S(6)} %select_n.46, bf16[3072,128]{1,0:T(8,128)(2,1)S(1)} %add_convert_fusion), kind=kLoop, calls=%fused_computation.56 | loop fusion | flops 1572864 | bytes 1572868 | tf_op jit(solution)/shard_map/concatenate | solution.py:90
  62.4 0.9 copy.24
  63.3 5.4 %all-to-all-start = ((bf16[16,3,64,128]{3,2,1,0:T(8,128)(2,1)}), bf16[16,3,64,128]{3,2,1,0:T(8,128)(2,1)}, u32[]{:S(2)}, u32[]{:S(2)}) async-start(bf16[16,3,64,128]{3,2,1,0:T(8,128)(2,1)} %copy.24), calls=%async_computation | async-start | bytes 1572864 | tf_op jit(solution)/shard_map/all_to_all | solution.py:56
  68.7 0.8 constant_dynamic-update-slice_fusion.6
  69.5 1.8 %constant_dynamic-update-slice_fusion.5 = bf16[512,3072]{1,0:T(8,128)(2,1)} fusion(bf16[512,3072]{1,0:T(8,128)(2,1)} %constant_dynamic-update-slice_fusion.6, bf16[512,384]{1,0:T(8,128)(2,1)} %collective-permute-done.1), kind=kLoop, calls=%fused_computation.99 | loop fusion | bytes 786432
  71.3 0.9 constant_dynamic-update-slice_fusion.4
  72.2 1.8 %constant_dynamic-update-slice_fusion.3 = bf16[512,3072]{1,0:T(8,128)(2,1)} fusion(bf16[512,3072]{1,0:T(8,128)(2,1)} %constant_dynamic-update-slice_fusion.4, bf16[512,384]{1,0:T(8,128)(2,1)} %copy-done.5), kind=kLoop, calls=%fused_computation.97 | loop fusion | bytes 786432
  74.1 1.8 %constant_dynamic-update-slice_fusion.2 = bf16[512,3072]{1,0:T(8,128)(2,1)} fusion(bf16[512,3072]{1,0:T(8,128)(2,1)} %constant_dynamic-update-slice_fusion.3, bf16[512,384]{1,0:T(8,128)(2,1)} %collective-permute-done.5), kind=kLoop, calls=%fused_computation.96 | loop fusion | bytes 786432
  75.9 1.8 %constant_dynamic-update-slice_fusion.1 = bf16[512,3072]{1,0:T(8,128)(2,1)} fusion(bf16[512,3072]{1,0:T(8,128)(2,1)} %constant_dynamic-update-slice_fusion.2, bf16[512,384]{1,0:T(8,128)(2,1)} %collective-permute-done.4), kind=kLoop, calls=%fused_computation.95 | loop fusion | bytes 786432
  77.7 0.9 constant_dynamic-update-slice_fusion
  78.6 0.4 collective-permute-start.10
  79.0 3.5 %all-to-all-done = bf16[16,3,64,128]{3,2,1,0:T(8,128)(2,1)} async-done(((bf16[16,3,64,128]{3,2,1,0:T(8,128)(2,1)}), bf16[16,3,64,128]{3,2,1,0:T(8,128)(2,1)}, u32[]{:S(2)}, u32[]{:S(2)}) %all-to-all-start) | async-done | bytes 786464 | tf_op jit(solution)/shard_map/all_to_all | solution.py:56
  82.5 1.2 fusion.134
  84.0 2.8 %select_reduce_fusion.1 = (f32[2048]{0:T(1024)S(1)}, f32[2048,2048]{0,1:T(8,128)S(1)}) fusion(pred[2048]{0:T(1024)(128)(4,1)S(1)} %iota_compare_fusion, bf16[8,8,16,128]{3,2,1,0:T(8,128)(2,1)S(1)} %bitcast.147, bf16[8,8,16,128]{3,2,1,0:T(8,128)(2,1)S(1)} %bitcast.146), kind=kOutput, calls=%fused_computation.3 | convolution fusion | flops 549451776 | bytes 17311744 | tf_op jit(solution)/shard_map/dq,dk->qk/dot_general | solution.py:25
  86.8 4.8 %fusion = f32[2048]{0:T(1024)S(1)} fusion(f32[2048,2048]{0,1:T(8,128)S(1)} %get-tuple-element.28, f32[2048]{0:T(1024)S(1)} %get-tuple-element.27, pred[2048]{0:T(1024)(128)(4,1)S(1)} %iota_compare_fusion), kind=kLoop, calls=%fused_computation.4 | loop fusion | flops 16775168 | bytes 16795648 | tf_op jit(solution)/shard_map/reduce_sum | solution.py:31
  91.8 3.1 %fusion.60 = bf16[8,16,8,128]{3,2,1,0:T(8,128)(2,1)S(1)} fusion(f32[2048,2048]{0,1:T(8,128)S(1)} %get-tuple-element.28, f32[2048]{0:T(1024)S(1)} %get-tuple-element.27, pred[2048]{0:T(1024)(128)(4,1)S(1)} %iota_compare_fusion, bf16[8,8,16,128]{3,2,1,0:T(8,128)(2,1)S(1)} %bitcast.152, f32[2048]{0:T(1024)S(1)} %fusion), kind=kOutput, calls=%fused_computation.54 | convolution fusion | flops 553910272 | bytes 17319936 | tf_op jit(solution)/shard_map/qk,dk->dq/dot_general | solution.py:32
  95.1 10.6 %all_to_all.40 = bf16[16,64,128]{2,1,0:T(8,128)(2,1)S(1)} all-to-all(bf16[16,64,128]{2,1,0:T(8,128)(2,1)S(1)} %bitcast.148), channel_id=1, replica_groups=mesh['pipe'=2,'ctx'=16,'dp'=8] {'ctx'}, dimensions={0} | all-to-all | bytes 524288 | tf_op jit(solution)/shard_map/all_to_all | solution.py:59
  105.7 0.5 fusion.48
  106.2 1.3 collective-permute-start.9
  107.5 9.9 %collective-permute-done.9 = bf16[128,1024]{1,0:T(8,128)(2,1)S(1)} collective-permute-done((bf16[128,1024]{1,0:T(8,128)(2,1)S(1)}, bf16[128,1024]{1,0:T(8,128)(2,1)S(1)}, u32[]{:S(2)}, u32[]{:S(2)}) %collective-permute-start.9) | collective-permute-done | bytes 262176 | tf_op jit(solution)/shard_map/ppermute | solution.py:128
  117.5 0.2 fusion.70
  117.7 0.2 fusion.73
  118.0 2.5 %fusion.92 = f32[128,3072]{1,0:T(8,128)S(1)} fusion(bf16[512,3072]{1,0:T(8,128)(2,1)} %collective-permute-done.10, bf16[128,1024]{1,0:T(8,128)(2,1)S(1)} %fusion.73, s32[]{:T(128)S(6)} %select_n.49), kind=kOutput, calls=%fused_computation.91 | convolution fusion | flops 402653184 | bytes 4849668 | tf_op jit(solution)/shard_map/dot_general | solution.py:49
  120.5 0.6 fusion.10
  121.1 0.4 fusion.63
  121.5 1.2 copy.29
  122.7 1.2 copy.30
  123.9 16.5 %all_to_all.41 = bf16[16,3,64,128]{3,2,1,0:T(8,128)(2,1)S(1)} all-to-all(bf16[16,3,64,128]{3,2,1,0:T(8,128)(2,1)S(1)} %copy.30), channel_id=1, replica_groups=mesh['pipe'=2,'ctx'=16,'dp'=8] {'ctx'}, dimensions={0} | all-to-all | bytes 1572864 | tf_op jit(solution)/shard_map/all_to_all | solution.py:56
  141.0 2.8 %select_reduce_fusion = (f32[2048]{0:T(1024)S(1)}, f32[2048,2048]{0,1:T(8,128)S(1)}) fusion(pred[2048]{0:T(1024)(128)(4,1)S(1)} %iota_compare_fusion, bf16[8,8,16,128]{3,2,1,0:T(8,128)(2,1)S(1)} %bitcast.145, bf16[8,8,16,128]{3,2,1,0:T(8,128)(2,1)S(1)} %bitcast.144), kind=kOutput, calls=%fused_computation.1 | convolution fusion | flops 549451776 | bytes 17311744 | tf_op jit(solution)/shard_map/dq,dk->qk/dot_general | solution.py:25
  143.8 4.8 %fusion.2 = f32[2048]{0:T(1024)S(1)} fusion(f32[2048,2048]{0,1:T(8,128)S(1)} %get-tuple-element.30, f32[2048]{0:T(1024)S(1)} %get-tuple-element.29, pred[2048]{0:T(1024)(128)(4,1)S(1)} %iota_compare_fusion), kind=kLoop, calls=%fused_computation.6 | loop fusion | flops 16775168 | bytes 16795648 | tf_op jit(solution)/shard_map/reduce_sum | solution.py:31
  148.6 3.1 %fusion.57 = bf16[8,16,8,128]{3,2,1,0:T(8,128)(2,1)S(1)} fusion(f32[2048,2048]{0,1:T(8,128)S(1)} %get-tuple-element.30, f32[2048]{0:T(1024)S(1)} %get-tuple-element.29, pred[2048]{0:T(1024)(128)(4,1)S(1)} %iota_compare_fusion, bf16[8,8,16,128]{3,2,1,0:T(8,128)(2,1)S(1)} %bitcast.151, f32[2048]{0:T(1024)S(1)} %fusion.2), kind=kOutput, calls=%fused_computation.53 | convolution fusion | flops 553910272 | bytes 17319936 | tf_op jit(solution)/shard_map/qk,dk->dq/dot_general | solution.py:32
  151.8 0.8 copy.77
  152.6 3.5 %all-to-all-start.3 = ((bf16[16,64,128]{2,1,0:T(8,128)(2,1)}), bf16[16,64,128]{2,1,0:T(8,128)(2,1)S(1)}, u32[]{:S(2)}, u32[]{:S(2)}) async-start(bf16[16,64,128]{2,1,0:T(8,128)(2,1)} %bitcast.137), calls=%async_computation.3 | async-start | bytes 524288 | tf_op jit(solution)/shard_map/all_to_all | solution.py:59
  156.1 8.0 %all-to-all-done.3 = bf16[16,64,128]{2,1,0:T(8,128)(2,1)S(1)} async-done(((bf16[16,64,128]{2,1,0:T(8,128)(2,1)}), bf16[16,64,128]{2,1,0:T(8,128)(2,1)S(1)}, u32[]{:S(2)}, u32[]{:S(2)}) %all-to-all-start.3) | async-done | bytes 262176 | tf_op jit(solution)/shard_map/all_to_all | solution.py:59
  164.1 1.2 fusion.54
  (52 shorter events, 1.7 us)
Async XLA Ops:
  0.0 105.7 %copy-start = (bf16[1,1024,1024]{2,1,0:T(8,128)(2,1)S(1)}, bf16[1,1024,1024]{2,1,0:T(8,128)(2,1)}, u32[]{:S(2)}) copy-start(bf16[1,1024,1024]{2,1,0:T(8,128)(2,1)} %param.13) | copy-start | bytes 6291460
  1.2 28.8 %copy-start.7 = (bf16[512,384]{1,0:T(8,128)(2,1)}, bf16[512,384]{1,0:T(8,128)(2,1)S(1)}, u32[]{:S(2)}) copy-start(bf16[512,384]{1,0:T(8,128)(2,1)S(1)} %dynamic-slice_bitcast_fusion) | copy-start | bytes 1179652
  1.2 17.7 %collective-permute-start = (bf16[512,384]{1,0:T(8,128)(2,1)S(1)}, bf16[512,384]{1,0:T(8,128)(2,1)S(1)}, u32[]{:S(2)}, u32[]{:S(2)}) collective-permute-start(bf16[512,384]{1,0:T(8,128)(2,1)S(1)} %dynamic-slice_bitcast_fusion), channel_id=1, source_target_pairs={{0,7},{1,0},{2,1},{3,2},{4,3},{5,4},{6,5},{7,6},{8,15},{9,8},{10,9... | collective-permute-start | bytes 1179656 | tf_op jit(solution)/shard_map/ppermute | solution.py:78
  7.1 11.8 %collective-permute-start.3 = (bf16[512,384]{1,0:T(8,128)(2,1)S(1)}, bf16[512,384]{1,0:T(8,128)(2,1)S(1)}, u32[]{:S(2)}, u32[]{:S(2)}) collective-permute-start(bf16[512,384]{1,0:T(8,128)(2,1)S(1)} %dynamic-slice_bitcast_fusion), channel_id=1, source_target_pairs={{0,1},{1,2},{2,3},{3,4},{4,5},{5,6},{6,7},{7,0},{8,9},{9,10},{10,1... | collective-permute-start | bytes 1179656 | tf_op jit(solution)/shard_map/ppermute | solution.py:74
  18.9 11.0 %collective-permute-start.4 = (bf16[512,384]{1,0:T(8,128)(2,1)S(1)}, bf16[512,384]{1,0:T(8,128)(2,1)}, u32[]{:S(2)}, u32[]{:S(2)}) collective-permute-start(bf16[512,384]{1,0:T(8,128)(2,1)S(1)} %collective-permute-done.3), channel_id=1, source_target_pairs={{0,1},{1,2},{2,3},{3,4},{4,5},{5,6},{6,7},{7,0},{8,9},{9,10},{10,1... | collective-permute-start | bytes 1179656 | tf_op jit(solution)/shard_map/ppermute | solution.py:74
  18.9 12.5 %collective-permute-start.1 = (bf16[512,384]{1,0:T(8,128)(2,1)S(1)}, bf16[512,384]{1,0:T(8,128)(2,1)}, u32[]{:S(2)}, u32[]{:S(2)}) collective-permute-start(bf16[512,384]{1,0:T(8,128)(2,1)S(1)} %collective-permute-done), channel_id=1, source_target_pairs={{0,7},{1,0},{2,1},{3,2},{4,3},{5,4},{6,5},{7,6},{8,15},{9,8},{10,9... | collective-permute-start | bytes 1179656 | tf_op jit(solution)/shard_map/ppermute | solution.py:78
  23.4 6.6 %collective-permute-start.7 = (bf16[128,1024]{1,0:T(8,128)(2,1)S(1)}, bf16[128,1024]{1,0:T(8,128)(2,1)S(1)}, u32[]{:S(2)}, u32[]{:S(2)}) collective-permute-start(bf16[128,1024]{1,0:T(8,128)(2,1)S(1)} %fusion.77), channel_id=1, source_target_pairs={{0,8},{8,0},{16,24},{24,16},{32,40},{40,32},{48,56},{56,48},{64,72... | collective-permute-start | bytes 786440 | tf_op jit(solution)/shard_map/ppermute | solution.py:104
  30.0 10.4 %collective-permute-start.5 = (bf16[512,384]{1,0:T(8,128)(2,1)}, bf16[512,384]{1,0:T(8,128)(2,1)}, u32[]{:S(2)}, u32[]{:S(2)}) collective-permute-start(bf16[512,384]{1,0:T(8,128)(2,1)} %collective-permute-done.4), channel_id=1, source_target_pairs={{0,1},{1,2},{2,3},{3,4},{4,5},{5,6},{6,7},{7,0},{8,9},{9,10},{10,1... | collective-permute-start | bytes 1179656 | tf_op jit(solution)/shard_map/ppermute | solution.py:74
  30.0 23.3 %copy-start.6 = (f32[3072,128]{1,0:T(8,128)S(1)}, f32[3072,128]{1,0:T(8,128)}, u32[]{:S(2)}) copy-start(f32[3072,128]{1,0:T(8,128)} %convolution_dynamic-update-slice_fusion.15) | copy-start | bytes 4718596
  31.4 10.2 %collective-permute-start.2 = (bf16[512,384]{1,0:T(8,128)(2,1)}, bf16[512,384]{1,0:T(8,128)(2,1)S(1)}, u32[]{:S(2)}, u32[]{:S(2)}) collective-permute-start(bf16[512,384]{1,0:T(8,128)(2,1)} %collective-permute-done.1), channel_id=1, source_target_pairs={{0,7},{1,0},{2,1},{3,2},{4,3},{5,4},{6,5},{7,6},{8,15},{9,8},{10,9... | collective-permute-start | bytes 1179656 | tf_op jit(solution)/shard_map/ppermute | solution.py:78
  35.0 20.3 %copy-start.8 = (bf16[512,384]{1,0:T(8,128)(2,1)S(1)}, bf16[512,384]{1,0:T(8,128)(2,1)}, u32[]{:S(2)}) copy-start(bf16[512,384]{1,0:T(8,128)(2,1)} %copy-done.7) | copy-start | bytes 1179652
  40.4 9.4 %collective-permute-start.6 = (bf16[512,384]{1,0:T(8,128)(2,1)}, bf16[512,384]{1,0:T(8,128)(2,1)S(1)}, u32[]{:S(2)}, u32[]{:S(2)}) collective-permute-start(bf16[512,384]{1,0:T(8,128)(2,1)} %collective-permute-done.5), channel_id=1, source_target_pairs={{0,1},{1,2},{2,3},{3,4},{4,5},{5,6},{6,7},{7,0},{8,9},{9,10},{10,1... | collective-permute-start | bytes 1179656 | tf_op jit(solution)/shard_map/ppermute | solution.py:74
  41.7 13.3 %copy-start.3 = (bf16[512,384]{1,0:T(8,128)(2,1)}, bf16[512,384]{1,0:T(8,128)(2,1)S(1)}, u32[]{:S(2)}) copy-start(bf16[512,384]{1,0:T(8,128)(2,1)S(1)} %collective-permute-done.2) | copy-start | bytes 1179652
  49.8 6.7 %copy-start.5 = (bf16[512,384]{1,0:T(8,128)(2,1)}, bf16[512,384]{1,0:T(8,128)(2,1)S(1)}, u32[]{:S(2)}) copy-start(bf16[512,384]{1,0:T(8,128)(2,1)S(1)} %collective-permute-done.6) | copy-start | bytes 1179652
  53.0 6.4 %collective-permute-start.8 = (f32[3072,128]{1,0:T(8,128)S(1)}, f32[3072,128]{1,0:T(8,128)S(1)}, u32[]{:S(2)}, u32[]{:S(2)}) collective-permute-start(f32[3072,128]{1,0:T(8,128)S(1)} %convolution_dynamic-update-slice_fusion), channel_id=1, source_target_pairs={{0,8},{8,0},{16,24},{24,16},{32,40},{40,32},{48,56},{56,48},{64,72... | collective-permute-start | bytes 4718600 | tf_op jit(solution)/shard_map/ppermute | solution.py:116
  59.6 11.7 %copy-start.4 = (bf16[512,384]{1,0:T(8,128)(2,1)S(1)}, bf16[512,384]{1,0:T(8,128)(2,1)}, u32[]{:S(2)}) copy-start(bf16[512,384]{1,0:T(8,128)(2,1)} %copy-done.3) | copy-start | bytes 1179652
  63.3 19.2 %all-to-all-start = ((bf16[16,3,64,128]{3,2,1,0:T(8,128)(2,1)}), bf16[16,3,64,128]{3,2,1,0:T(8,128)(2,1)}, u32[]{:S(2)}, u32[]{:S(2)}) async-start(bf16[16,3,64,128]{3,2,1,0:T(8,128)(2,1)} %copy.24), calls=%async_computation | async-start | bytes 1572864 | tf_op jit(solution)/shard_map/all_to_all | solution.py:56
  78.6 39.4 %collective-permute-start.10 = (bf16[512,3072]{1,0:T(8,128)(2,1)}, bf16[512,3072]{1,0:T(8,128)(2,1)}, u32[]{:S(2)}, u32[]{:S(2)}) collective-permute-start(bf16[512,3072]{1,0:T(8,128)(2,1)} %constant_dynamic-update-slice_fusion), channel_id=1, source_target_pairs={{0,8},{8,0},{16,24},{24,16},{32,40},{40,32},{48,56},{56,48},{64,72... | collective-permute-start | bytes 9437192 | tf_op jit(solution)/shard_map/ppermute | solution.py:119
  91.8 13.9 %copy-start.1 = (bf16[1,1,128,1024]{3,2,1,0:T(8,128)(2,1)S(1)}, bf16[1,1,128,1024]{3,2,1,0:T(8,128)(2,1)}, u32[]{:S(2)}) copy-start(bf16[1,1,128,1024]{3,2,1,0:T(8,128)(2,1)} %param.8) | copy-start | bytes 786436
  91.8 13.9 %copy-start.11 = (f32[1,1024]{1,0:T(1,128)S(1)}, f32[1,1024]{1,0:T(1,128)}, u32[]{:S(2)}) copy-start(f32[1,1024]{1,0:T(1,128)} %param.14) | copy-start | bytes 12292
  91.8 13.9 %copy-start.12 = (f32[1,1024]{1,0:T(1,128)S(1)}, f32[1,1024]{1,0:T(1,128)}, u32[]{:S(2)}) copy-start(f32[1,1024]{1,0:T(1,128)} %param.15) | copy-start | bytes 12292
  95.0 22.8 %copy-start.9 = (f32[1,1024]{1,0:T(1,128)S(1)}, f32[1,1024]{1,0:T(1,128)}, u32[]{:S(2)}) copy-start(f32[1,1024]{1,0:T(1,128)} %param.11) | copy-start | bytes 12292
  95.0 22.8 %copy-start.10 = (f32[1,1024]{1,0:T(1,128)S(1)}, f32[1,1024]{1,0:T(1,128)}, u32[]{:S(2)}) copy-start(f32[1,1024]{1,0:T(1,128)} %param.10) | copy-start | bytes 12292
  106.2 11.2 %collective-permute-start.9 = (bf16[128,1024]{1,0:T(8,128)(2,1)S(1)}, bf16[128,1024]{1,0:T(8,128)(2,1)S(1)}, u32[]{:S(2)}, u32[]{:S(2)}) collective-permute-start(bf16[128,1024]{1,0:T(8,128)(2,1)S(1)} %fusion.48), channel_id=1, source_target_pairs={{0,128},{1,129},{2,130},{3,131},{4,132},{5,133},{6,134},{7,135},{8... | collective-permute-start | bytes 786440 | tf_op jit(solution)/shard_map/ppermute | solution.py:128
  107.5 13.0 %copy-start.2 = (bf16[512,3072]{1,0:T(8,128)(2,1)S(1)}, bf16[512,3072]{1,0:T(8,128)(2,1)}, u32[]{:S(2)}) copy-start(bf16[512,3072]{1,0:T(8,128)(2,1)} %constant_dynamic-update-slice_fusion) | copy-start | bytes 9437188
  152.6 11.5 %all-to-all-start.3 = ((bf16[16,64,128]{2,1,0:T(8,128)(2,1)}), bf16[16,64,128]{2,1,0:T(8,128)(2,1)S(1)}, u32[]{:S(2)}, u32[]{:S(2)}) async-start(bf16[16,64,128]{2,1,0:T(8,128)(2,1)} %bitcast.137), calls=%async_computation.3 | async-start | bytes 524288 | tf_op jit(solution)/shard_map/all_to_all | solution.py:59

commit v9 on v7

--- a/solution.py
+++ b/solution.py
@@ -1,4 +1,5 @@
 import jax
+import numpy as np
 import jax.numpy as jnp
 from jax import lax
 from jax.sharding import PartitionSpec as P
@@ -18,14 +19,14 @@
     return (centered * lax.rsqrt(variance + epsilon) * gain + shift).astype(jnp.bfloat16)
 
 
-def head_attention(qkv, length, score_scale):
+def head_attention(qkv, length, score_scale, positions):
     queries, key_rows, value_rows = qkv[0], qkv[1], qkv[2]
     count = qkv.shape[-1]
     scores = (
         jnp.einsum("dq,dk->qk", queries, key_rows, preferred_element_type=jnp.float32)
         * score_scale
     )
-    valid = jnp.arange(count, dtype=jnp.int32) < length
+    valid = positions < length
     top = jnp.max(jnp.where(valid[None, :], scores, masked_score), axis=-1)
     weights = jnp.where(valid[None, :], jnp.exp(scores - top[:, None]), 0.0)
     totals = jnp.sum(weights, axis=-1)
@@ -36,7 +37,7 @@
 
 
 def sublayer(current, length, qkv_mine, qkv_other, out_full, gain, shift, out_shift, layer_scale,
-             projected=None):
+             projected=None, chunk_of=None, residual=None):
     tok_rows, width = current.shape
     head_width = width // HEADS
     ctx_count = lax.axis_size("ctx")
@@ -54,12 +55,20 @@
             projected.reshape(tok_rows, 3, HEADS, head_width), (2, 1, 3, 0)
         )
     gathered = lax.all_to_all(projected, "ctx", 0, 3, tiled=True)
-    context = head_attention(gathered[0], length, head_width ** (-0.5))
+    chunk_of = list(range(ctx_count)) if chunk_of is None else chunk_of
+    positions = np.arange(ctx_count * tok_rows).reshape(ctx_count, tok_rows)[chunk_of]
+    context = head_attention(
+        gathered[0], length, head_width ** (-0.5), jnp.asarray(positions.reshape(-1), jnp.int32)
+    )
     context = jnp.transpose(context.reshape(head_width, ctx_count, tok_rows), (1, 0, 2))
+    if chunk_of != list(range(ctx_count)):
+        held_at = [chunk_of.index(t) for t in range(ctx_count)]
+        context = jnp.concatenate([context[k : k + 1] for k in held_at], axis=0)
     spread = lax.all_to_all(context, "ctx", 0, 0, tiled=True).reshape(width, tok_rows)
     mixed = jnp.einsum("ft,fo->to", spread, out_full, preferred_element_type=jnp.float32)
     mixed = mixed + out_shift
-    return (current.astype(jnp.float32) + layer_scale * mixed).astype(jnp.bfloat16)
+    residual = current if residual is None else residual
+    return (residual.astype(jnp.float32) + layer_scale * mixed).astype(jnp.bfloat16)
 
 
 def ring_gather(piece, axis, on_block, made_axis=1):
@@ -116,13 +125,15 @@
     qkv_other = lax.ppermute(qkv_mine, "ctx", sibling)
     args = (qkv_mine, qkv_other, w_out[0], norm_gain[0], norm_bias[0], out_bias[0], scale_gain[0])
     length = lengths[0, 0]
-    outputs = []
-    for turn_index in range(section_count):
-        produced = sublayer(current, length, *args, projected=first if turn_index == 0 else None)
-        outputs.append(produced)
-        if turn_index + 1 < section_count:
-            pairs = [(i, i + 1) for i in range(section_count - 1)]
-            current = lax.ppermute(produced, "pipe", pairs)
+    assert section_count == 2
+    ctx_count = lax.axis_size("ctx")
+    produced = sublayer(current, length, *args, projected=first)
+    flip = 2
+    onward = [(c, ctx_count + (c ^ flip)) for c in range(ctx_count)]
+    handed = lax.ppermute(produced, ("pipe", "ctx"), onward)
+    residual = lax.ppermute(handed, "ctx", [(c, c ^ flip) for c in range(ctx_count)])
+    chunk_of = [c ^ flip for c in range(ctx_count)]
+    outputs = [produced, sublayer(handed, length, *args, chunk_of=chunk_of, residual=residual)]
     result = outputs[0]
     for turn_index in range(1, section_count):
         result = jnp.where(section_index == turn_index, outputs[turn_index], result)

time: 165 us -> 172 us (1.042)
  local copies, waits for them, and re-layouts: 22.6 us -> 26.9 us
  starting transfers between devices: 23.4 us -> 25.2 us
    unnamed x39 -> x48, local copies, waits for them, and re-layouts: 12.8 us -> 17.1 us
    ppermute x1 -> x2, starting transfers between devices: 1.29 us -> 3.1 us  [the longest x1 1.81 us: per_device(): lax.ppermute(handed, 'ctx', [(c, c ^ flip) for c in range(ctx_count)])]
    ppermute x1 -> x2, waiting for transfers between devices: 9.86 us -> 10.7 us  [the longest x1 8.35 us: per_device(): handed = lax.ppermute(produced, ('pipe', 'ctx'), onward)]
  transfers between devices with their start and end apart: 13 -> 14, of which waited for: 10 -> 11; matrix products, arithmetic and copies ran while one was open for 17% -> 17% of each run, Pallas kernels for 0% -> 0%
where the time goes in v9:
time: 172 us; the launch traced here: 171 us
  waiting for transfers between devices  53 us (31%)
  blocking collectives  28.4 us (17%)
  local copies, waits for them, and re-layouts  26.9 us (16%)
  starting transfers between devices  25.2 us (15%)
  matrix products  19.3 us (11%)
  other arithmetic  17.4 us (10%)
    ppermute x4, waiting for transfers between devices, ring_gather(): forward = lax.ppermute(forward, axis, right)  23.8 us
    all_to_all x1, blocking collectives, sublayer(): gathered = lax.all_to_all(projected, 'ctx', 0, 3, tiled=True)  17.8 us
    unnamed x48, local copies, waits for them, and re-layouts  17.1 us
    ppermute x3, starting transfers between devices, ring_gather(): backward = lax.ppermute(backward, axis, left)  12.9 us
    all_to_all x1, blocking collectives, sublayer(): lax.all_to_all(context, 'ctx', 0, 0, tiled=True).reshape(width, tok_rows)  10.6 us
    reduce_sum x2, other arithmetic, head_attention(): totals = jnp.sum(weights, axis=-1)  9.64 us
    ppermute x1, waiting for transfers between devices, per_device(): handed = lax.ppermute(produced, ('pipe', 'ctx'), onward)  8.35 us
    all_to_all x1, waiting for transfers between devices, sublayer(): lax.all_to_all(context, 'ctx', 0, 0, tiled=True).reshape(width, tok_rows)  6.74 us
  transfers between devices with their start and end apart: 14, of which 11 were waited for; matrix products, arithmetic and copies ran while one was open for 17% of the time, Pallas kernels for 0%

profile of v9, /device:TPU:4, one launch (start us, length us, event | category | flops | bytes accessed | tf_op | source)
XLA Modules:
  0.0 171.3 jit_solution(17664650772063878742)
XLA Ops:
  0.0 2.0 %constant_dynamic-update-slice_fusion.7 = (bf16[512,3072]{1,0:T(8,128)(2,1)}, bf16[512,384]{1,0:T(8,128)(2,1)S(1)}) fusion(bf16[1,1024,384]{2,1,0:T(8,128)(2,1)} %param.14, s32[]{:T(128)S(6)} %select_n.45), kind=kLoop, calls=%fused_computation.115 | loop fusion | bytes 1179652
  2.0 5.9 %collective-permute-start.1 = (bf16[512,384]{1,0:T(8,128)(2,1)S(1)}, bf16[512,384]{1,0:T(8,128)(2,1)S(1)}, u32[]{:S(2)}, u32[]{:S(2)}) collective-permute-start(bf16[512,384]{1,0:T(8,128)(2,1)S(1)} %get-tuple-element.6), channel_id=1, source_target_pairs={{0,7},{1,0},{2,1},{3,2},{4,3},{5,4},{6,5},{7,6},{8,15},{9,8},{10,9... | collective-permute-start | bytes 1179656 | tf_op jit(solution)/shard_map/ppermute | solution.py:87
  7.9 1.1 convert_reduce_fusion.1
  8.9 1.2 fusion.72
  10.1 9.5 %collective-permute-done.4 = bf16[512,384]{1,0:T(8,128)(2,1)S(1)} collective-permute-done((bf16[512,384]{1,0:T(8,128)(2,1)S(1)}, bf16[512,384]{1,0:T(8,128)(2,1)S(1)}, u32[]{:S(2)}, u32[]{:S(2)}) %collective-permute-start.4) | collective-permute-done | bytes 393248 | tf_op jit(solution)/shard_map/ppermute | solution.py:83
  19.7 1.2 fusion.75
  21.0 3.3 %collective-permute-start.2 = (bf16[512,384]{1,0:T(8,128)(2,1)S(1)}, bf16[512,384]{1,0:T(8,128)(2,1)S(1)}, u32[]{:S(2)}, u32[]{:S(2)}) collective-permute-start(bf16[512,384]{1,0:T(8,128)(2,1)S(1)} %collective-permute-done.1), channel_id=1, source_target_pairs={{0,7},{1,0},{2,1},{3,2},{4,3},{5,4},{6,5},{7,6},{8,15},{9,8},{10,9... | collective-permute-start | bytes 1179656 | tf_op jit(solution)/shard_map/ppermute | solution.py:87
  24.3 6.3 %collective-permute-done.5 = bf16[512,384]{1,0:T(8,128)(2,1)S(1)} collective-permute-done((bf16[512,384]{1,0:T(8,128)(2,1)S(1)}, bf16[512,384]{1,0:T(8,128)(2,1)S(1)}, u32[]{:S(2)}, u32[]{:S(2)}) %collective-permute-start.5) | collective-permute-done | bytes 393248 | tf_op jit(solution)/shard_map/ppermute | solution.py:83
  30.6 1.4 fusion.54
  32.0 1.2 collective-permute-done.2
  33.2 3.7 %collective-permute-start.3 = (bf16[512,384]{1,0:T(8,128)(2,1)S(1)}, bf16[512,384]{1,0:T(8,128)(2,1)S(1)}, u32[]{:S(2)}, u32[]{:S(2)}) collective-permute-start(bf16[512,384]{1,0:T(8,128)(2,1)S(1)} %collective-permute-done.2), channel_id=1, source_target_pairs={{0,7},{1,0},{2,1},{3,2},{4,3},{5,4},{6,5},{7,6},{8,15},{9,8},{10,9... | collective-permute-start | bytes 1179656 | tf_op jit(solution)/shard_map/ppermute | solution.py:87
  37.2 3.4 %collective-permute-done.6 = bf16[512,384]{1,0:T(8,128)(2,1)S(1)} collective-permute-done((bf16[512,384]{1,0:T(8,128)(2,1)S(1)}, bf16[512,384]{1,0:T(8,128)(2,1)S(1)}, u32[]{:S(2)}, u32[]{:S(2)}) %collective-permute-start.6) | collective-permute-done | bytes 393248 | tf_op jit(solution)/shard_map/ppermute | solution.py:83
  41.0 4.1 %collective-permute-done.3 = bf16[512,384]{1,0:T(8,128)(2,1)S(1)} collective-permute-done((bf16[512,384]{1,0:T(8,128)(2,1)S(1)}, bf16[512,384]{1,0:T(8,128)(2,1)S(1)}, u32[]{:S(2)}, u32[]{:S(2)}) %collective-permute-start.3) | collective-permute-done | bytes 393248 | tf_op jit(solution)/shard_map/ppermute | solution.py:87
  45.3 4.6 %collective-permute-done.7 = bf16[512,384]{1,0:T(8,128)(2,1)S(1)} collective-permute-done((bf16[512,384]{1,0:T(8,128)(2,1)S(1)}, bf16[512,384]{1,0:T(8,128)(2,1)S(1)}, u32[]{:S(2)}, u32[]{:S(2)}) %collective-permute-start.7) | collective-permute-done | bytes 393248 | tf_op jit(solution)/shard_map/ppermute | solution.py:83
  50.2 0.3 fusion.49
  50.5 0.3 fusion.48
  50.8 0.3 fusion.47
  51.2 1.7 copy-done.3
  52.8 1.3 slice_bitcast_fusion
  54.9 3.1 %collective-permute-done.8 = f32[3072,128]{0,1:T(8,128)} collective-permute-done((f32[3072,128]{0,1:T(8,128)}, f32[3072,128]{0,1:T(8,128)}, u32[]{:S(2)}, u32[]{:S(2)}) %collective-permute-start.8) | collective-permute-done | bytes 1572896 | tf_op jit(solution)/shard_map/ppermute | solution.py:122
  57.9 2.0 %fusion.28 = bf16[3072,128]{0,1:T(8,128)(2,1)S(1)} fusion(f32[3072,128]{0,1:T(8,128)} %collective-permute-done.8, f32[2,3072,128]{1,2,0:T(8,128)} %copy-done.3), kind=kLoop, calls=%fused_computation.25 | loop fusion | flops 786432 | bytes 3932160 | tf_op jit(solution)/shard_map/convert_element_type | solution.py:123
  60.0 0.4 fusion.62
  60.4 1.2 copy.21
  61.6 2.1 %copy.22 = bf16[16,3,64,128]{3,2,1,0:T(8,128)(2,1)} copy(bf16[16,3,64,128]{3,2,0,1:T(8,128)(2,1)} %bitcast.188) | data formatting | bytes 1572864 | tf_op jit(solution)/shard_map/transpose | solution.py:124
  63.7 5.2 %all-to-all-start = ((bf16[16,3,64,128]{3,2,1,0:T(8,128)(2,1)}), bf16[16,3,64,128]{3,2,1,0:T(8,128)(2,1)S(1)}, u32[]{:S(2)}, u32[]{:S(2)}) async-start(bf16[16,3,64,128]{3,2,1,0:T(8,128)(2,1)} %copy.22), calls=%async_computation | async-start | bytes 1572864 | tf_op jit(solution)/shard_map/all_to_all | solution.py:57
  68.9 1.9 %constant_dynamic-update-slice_fusion.6 = bf16[512,3072]{1,0:T(8,128)(2,1)} fusion(bf16[512,3072]{1,0:T(8,128)(2,1)} %get-tuple-element.5, bf16[512,384]{1,0:T(8,128)(2,1)} %copy-done.4), kind=kLoop, calls=%fused_computation.114 | loop fusion | bytes 786432
  70.8 1.8 %constant_dynamic-update-slice_fusion.5 = bf16[512,3072]{1,0:T(8,128)(2,1)} fusion(bf16[512,3072]{1,0:T(8,128)(2,1)} %constant_dynamic-update-slice_fusion.6, bf16[512,384]{1,0:T(8,128)(2,1)} %copy-done.9), kind=kLoop, calls=%fused_computation.113 | loop fusion | bytes 786432
  72.6 1.8 %constant_dynamic-update-slice_fusion.4 = bf16[512,3072]{1,0:T(8,128)(2,1)} fusion(bf16[512,3072]{1,0:T(8,128)(2,1)} %constant_dynamic-update-slice_fusion.5, bf16[512,384]{1,0:T(8,128)(2,1)} %copy-done.10), kind=kLoop, calls=%fused_computation.112 | loop fusion | bytes 786432
  74.4 1.8 %constant_dynamic-update-slice_fusion.3 = bf16[512,3072]{1,0:T(8,128)(2,1)} fusion(bf16[512,3072]{1,0:T(8,128)(2,1)} %constant_dynamic-update-slice_fusion.4, bf16[512,384]{1,0:T(8,128)(2,1)} %copy-done.11), kind=kLoop, calls=%fused_computation.111 | loop fusion | bytes 786432
  76.3 0.8 constant_dynamic-update-slice_fusion.2
  77.1 0.8 constant_dynamic-update-slice_fusion.1
  78.0 0.8 constant_dynamic-update-slice_fusion
  78.8 0.4 collective-permute-start.11
  79.2 3.4 %all-to-all-done = bf16[16,3,64,128]{3,2,1,0:T(8,128)(2,1)S(1)} async-done(((bf16[16,3,64,128]{3,2,1,0:T(8,128)(2,1)}), bf16[16,3,64,128]{3,2,1,0:T(8,128)(2,1)S(1)}, u32[]{:S(2)}, u32[]{:S(2)}) %all-to-all-start) | async-done | bytes 786464 | tf_op jit(solution)/shard_map/all_to_all | solution.py:57
  83.0 2.8 %select_reduce_fusion.1 = (f32[2048]{0:T(1024)S(1)}, f32[2048,2048]{0,1:T(8,128)S(1)}) fusion(pred[2048]{0:T(1024)(128)(4,1)S(1)} %get-tuple-element.17, bf16[8,8,16,128]{3,2,1,0:T(8,128)(2,1)S(1)} %bitcast.193, bf16[8,8,16,128]{3,2,1,0:T(8,128)(2,1)S(1)} %bitcast.192), kind=kOutput, calls=%fused_computation.3 | convolution fusion | flops 549451776 | bytes 17311744 | tf_op jit(solution)/shard_map/dq,dk->qk/dot_general | solution.py:26
  85.8 4.8 %fusion = f32[2048]{0:T(1024)S(1)} fusion(f32[2048,2048]{0,1:T(8,128)S(1)} %get-tuple-element.14, f32[2048]{0:T(1024)S(1)} %get-tuple-element.13, pred[2048]{0:T(1024)(128)(4,1)S(1)} %get-tuple-element.17), kind=kLoop, calls=%fused_computation.4 | loop fusion | flops 16775168 | bytes 16795648 | tf_op jit(solution)/shard_map/reduce_sum | solution.py:32
  90.9 3.1 %fusion.58 = bf16[8,16,8,128]{3,2,1,0:T(8,128)(2,1)S(1)} fusion(f32[2048,2048]{0,1:T(8,128)S(1)} %get-tuple-element.14, f32[2048]{0:T(1024)S(1)} %get-tuple-element.13, pred[2048]{0:T(1024)(128)(4,1)S(1)} %get-tuple-element.17, bf16[8,8,16,128]{3,2,1,0:T(8,128)(2,1)S(1)} %bitcast.206, f32[2048]{0:T(1024)S(1)} %fusion), kind=kOutput, calls=%fused_computation.53 | convolution fusion | flops 553910272 | bytes 17319936 | tf_op jit(solution)/shard_map/qk,dk->dq/dot_general | solution.py:33
  94.1 10.6 %all_to_all.40 = bf16[16,64,128]{2,1,0:T(8,128)(2,1)S(1)} all-to-all(bf16[16,64,128]{2,1,0:T(8,128)(2,1)S(1)} %bitcast.202), channel_id=1, replica_groups=mesh['pipe'=2,'ctx'=16,'dp'=8] {'ctx'}, dimensions={0} | all-to-all | bytes 524288 | tf_op jit(solution)/shard_map/all_to_all | solution.py:67
  104.8 0.5 fusion.44
  105.2 1.3 collective-permute-start.9
  106.6 8.4 %collective-permute-done.9 = bf16[128,1024]{1,0:T(8,128)(2,1)S(1)} collective-permute-done((bf16[128,1024]{1,0:T(8,128)(2,1)S(1)}, bf16[128,1024]{1,0:T(8,128)(2,1)S(1)}, u32[]{:S(2)}, u32[]{:S(2)}) %collective-permute-start.9) | collective-permute-done | bytes 262176 | tf_op jit(solution)/shard_map/ppermute | solution.py:133
  115.5 2.5 %fusion.101 = f32[128,3072]{1,0:T(8,128)S(1)} fusion(bf16[512,3072]{1,0:T(8,128)(2,1)} %collective-permute-done.11, bf16[128,1024]{1,0:T(8,128)(2,1)S(1)} %fusion.71, s32[]{:T(128)S(6)} %select_n.49), kind=kOutput, calls=%fused_computation.103 | convolution fusion | flops 402653184 | bytes 4849668 | tf_op jit(solution)/shard_map/dot_general | solution.py:50
  118.0 0.6 fusion.10
  118.6 0.4 fusion.61
  119.1 1.2 copy.27
  120.2 1.2 copy.28
  121.4 17.8 %all_to_all.41 = bf16[16,3,64,128]{3,2,1,0:T(8,128)(2,1)S(1)} all-to-all(bf16[16,3,64,128]{3,2,1,0:T(8,128)(2,1)S(1)} %copy.28), channel_id=1, replica_groups=mesh['pipe'=2,'ctx'=16,'dp'=8] {'ctx'}, dimensions={0} | all-to-all | bytes 1572864 | tf_op jit(solution)/shard_map/all_to_all | solution.py:57
  139.8 2.8 %select_reduce_fusion = (f32[2048]{0:T(1024)S(1)}, f32[2048,2048]{0,1:T(8,128)S(1)}) fusion(pred[2048]{0:T(1024)(128)(4,1)S(1)} %get-tuple-element.18, bf16[8,8,16,128]{3,2,1,0:T(8,128)(2,1)S(1)} %bitcast.191, bf16[8,8,16,128]{3,2,1,0:T(8,128)(2,1)S(1)} %bitcast.190), kind=kOutput, calls=%fused_computation.1 | convolution fusion | flops 549451776 | bytes 17311744 | tf_op jit(solution)/shard_map/dq,dk->qk/dot_general | solution.py:26
  142.6 4.8 %fusion.2 = f32[2048]{0:T(1024)S(1)} fusion(f32[2048,2048]{0,1:T(8,128)S(1)} %get-tuple-element.16, f32[2048]{0:T(1024)S(1)} %get-tuple-element.15, pred[2048]{0:T(1024)(128)(4,1)S(1)} %get-tuple-element.18), kind=kLoop, calls=%fused_computation.6 | loop fusion | flops 16775168 | bytes 16795648 | tf_op jit(solution)/shard_map/reduce_sum | solution.py:32
  147.4 3.1 %fusion.55 = bf16[8,16,8,128]{3,2,1,0:T(8,128)(2,1)S(1)} fusion(f32[2048,2048]{0,1:T(8,128)S(1)} %get-tuple-element.16, f32[2048]{0:T(1024)S(1)} %get-tuple-element.15, pred[2048]{0:T(1024)(128)(4,1)S(1)} %get-tuple-element.18, bf16[8,8,16,128]{3,2,1,0:T(8,128)(2,1)S(1)} %bitcast.205, f32[2048]{0:T(1024)S(1)} %fusion.2), kind=kOutput, calls=%fused_computation.52 | convolution fusion | flops 553910272 | bytes 17319936 | tf_op jit(solution)/shard_map/qk,dk->dq/dot_general | solution.py:33
  150.6 0.6 constant_dynamic-update-slice_fusion.15
  151.2 0.6 constant_dynamic-update-slice_fusion.14
  151.9 0.6 constant_dynamic-update-slice_fusion.13
  152.5 0.6 constant_dynamic-update-slice_fusion.12
  153.1 0.6 constant_dynamic-update-slice_fusion.11
  153.7 0.6 constant_dynamic-update-slice_fusion.10
  154.3 0.6 constant_dynamic-update-slice_fusion.9
  155.0 0.6 constant_dynamic-update-slice_fusion.8
  155.6 3.5 %all-to-all-start.3 = ((bf16[16,64,128]{2,1,0:T(8,128)(2,1)}), bf16[16,64,128]{2,1,0:T(8,128)(2,1)S(1)}, u32[]{:S(2)}, u32[]{:S(2)}) async-start(bf16[16,64,128]{2,1,0:T(8,128)(2,1)} %constant_dynamic-update-slice_fusion.8), calls=%async_computation.3 | async-start | bytes 524288 | tf_op jit(solution)/shard_map/all_to_all | solution.py:67
  159.1 1.8 %collective-permute-start.10 = (bf16[128,1024]{1,0:T(8,128)(2,1)S(1)}, bf16[128,1024]{1,0:T(8,128)(2,1)S(1)}, u32[]{:S(2)}, u32[]{:S(2)}) collective-permute-start(bf16[128,1024]{1,0:T(8,128)(2,1)S(1)} %collective-permute-done.9), channel_id=1, source_target_pairs={{0,16},{8,24},{16,0},{24,8},{32,48},{40,56},{48,32},{56,40},{64,80... | collective-permute-start | bytes 786440 | tf_op jit(solution)/shard_map/ppermute | solution.py:134
  160.9 6.7 %all-to-all-done.3 = bf16[16,64,128]{2,1,0:T(8,128)(2,1)S(1)} async-done(((bf16[16,64,128]{2,1,0:T(8,128)(2,1)}), bf16[16,64,128]{2,1,0:T(8,128)(2,1)S(1)}, u32[]{:S(2)}, u32[]{:S(2)}) %all-to-all-start.3) | async-done | bytes 262176 | tf_op jit(solution)/shard_map/all_to_all | solution.py:67
  167.7 0.5 fusion.41
  168.1 2.4 %collective-permute-done.10 = bf16[128,1024]{1,0:T(8,128)(2,1)S(1)} collective-permute-done((bf16[128,1024]{1,0:T(8,128)(2,1)S(1)}, bf16[128,1024]{1,0:T(8,128)(2,1)S(1)}, u32[]{:S(2)}, u32[]{:S(2)}) %collective-permute-start.10) | collective-permute-done | bytes 262176 | tf_op jit(solution)/shard_map/ppermute | solution.py:134
  170.5 0.8 fusion.86
  (66 shorter events, 3.3 us)
Async XLA Ops:
  0.0 104.7 %copy-start = (bf16[1,1024,1024]{2,1,0:T(8,128)(2,1)S(1)}, bf16[1,1024,1024]{2,1,0:T(8,128)(2,1)}, u32[]{:S(2)}) copy-start(bf16[1,1024,1024]{2,1,0:T(8,128)(2,1)} %param.15) | copy-start | bytes 6291460
  2.0 19.0 %collective-permute-start.1 = (bf16[512,384]{1,0:T(8,128)(2,1)S(1)}, bf16[512,384]{1,0:T(8,128)(2,1)S(1)}, u32[]{:S(2)}, u32[]{:S(2)}) collective-permute-start(bf16[512,384]{1,0:T(8,128)(2,1)S(1)} %get-tuple-element.6), channel_id=1, source_target_pairs={{0,7},{1,0},{2,1},{3,2},{4,3},{5,4},{6,5},{7,6},{8,15},{9,8},{10,9... | collective-permute-start | bytes 1179656 | tf_op jit(solution)/shard_map/ppermute | solution.py:87
  7.9 11.8 %collective-permute-start.4 = (bf16[512,384]{1,0:T(8,128)(2,1)S(1)}, bf16[512,384]{1,0:T(8,128)(2,1)S(1)}, u32[]{:S(2)}, u32[]{:S(2)}) collective-permute-start(bf16[512,384]{1,0:T(8,128)(2,1)S(1)} %get-tuple-element.6), channel_id=1, source_target_pairs={{0,1},{1,2},{2,3},{3,4},{4,5},{5,6},{6,7},{7,0},{8,9},{9,10},{10,1... | collective-permute-start | bytes 1179656 | tf_op jit(solution)/shard_map/ppermute | solution.py:83
  19.6 10.9 %collective-permute-start.5 = (bf16[512,384]{1,0:T(8,128)(2,1)S(1)}, bf16[512,384]{1,0:T(8,128)(2,1)S(1)}, u32[]{:S(2)}, u32[]{:S(2)}) collective-permute-start(bf16[512,384]{1,0:T(8,128)(2,1)S(1)} %collective-permute-done.4), channel_id=1, source_target_pairs={{0,1},{1,2},{2,3},{3,4},{4,5},{5,6},{6,7},{7,0},{8,9},{9,10},{10,1... | collective-permute-start | bytes 1179656 | tf_op jit(solution)/shard_map/ppermute | solution.py:83
  20.9 9.7 %collective-permute-start = (bf16[128,1024]{1,0:T(8,128)(2,1)S(1)}, bf16[128,1024]{1,0:T(8,128)(2,1)S(1)}, u32[]{:S(2)}, u32[]{:S(2)}) collective-permute-start(bf16[128,1024]{1,0:T(8,128)(2,1)S(1)} %fusion.75), channel_id=1, source_target_pairs={{0,8},{8,0},{16,24},{24,16},{32,40},{40,32},{48,56},{56,48},{64,72... | collective-permute-start | bytes 786440 | tf_op jit(solution)/shard_map/ppermute | solution.py:111
  21.0 29.5 %copy-start.4 = (bf16[512,384]{1,0:T(8,128)(2,1)}, bf16[512,384]{1,0:T(8,128)(2,1)S(1)}, u32[]{:S(2)}) copy-start(bf16[512,384]{1,0:T(8,128)(2,1)S(1)} %collective-permute-done.1) | copy-start | bytes 1179652
  21.0 12.3 %collective-permute-start.2 = (bf16[512,384]{1,0:T(8,128)(2,1)S(1)}, bf16[512,384]{1,0:T(8,128)(2,1)S(1)}, u32[]{:S(2)}, u32[]{:S(2)}) collective-permute-start(bf16[512,384]{1,0:T(8,128)(2,1)S(1)} %collective-permute-done.1), channel_id=1, source_target_pairs={{0,7},{1,0},{2,1},{3,2},{4,3},{5,4},{6,5},{7,6},{8,15},{9,8},{10,9... | collective-permute-start | bytes 1179656 | tf_op jit(solution)/shard_map/ppermute | solution.py:87
  30.6 19.9 %copy-start.5 = (bf16[512,384]{1,0:T(8,128)(2,1)}, bf16[512,384]{1,0:T(8,128)(2,1)S(1)}, u32[]{:S(2)}) copy-start(bf16[512,384]{1,0:T(8,128)(2,1)S(1)} %collective-permute-done.5) | copy-start | bytes 1179652
  30.6 10.1 %collective-permute-start.6 = (bf16[512,384]{1,0:T(8,128)(2,1)S(1)}, bf16[512,384]{1,0:T(8,128)(2,1)S(1)}, u32[]{:S(2)}, u32[]{:S(2)}) collective-permute-start(bf16[512,384]{1,0:T(8,128)(2,1)S(1)} %collective-permute-done.5), channel_id=1, source_target_pairs={{0,1},{1,2},{2,3},{3,4},{4,5},{5,6},{6,7},{7,0},{8,9},{9,10},{10,1... | collective-permute-start | bytes 1179656 | tf_op jit(solution)/shard_map/ppermute | solution.py:83
  33.2 17.6 %copy-start.9 = (bf16[512,384]{1,0:T(8,128)(2,1)}, bf16[512,384]{1,0:T(8,128)(2,1)S(1)}, u32[]{:S(2)}) copy-start(bf16[512,384]{1,0:T(8,128)(2,1)S(1)} %collective-permute-done.2) | copy-start | bytes 1179652
  33.2 11.8 %collective-permute-start.3 = (bf16[512,384]{1,0:T(8,128)(2,1)S(1)}, bf16[512,384]{1,0:T(8,128)(2,1)S(1)}, u32[]{:S(2)}, u32[]{:S(2)}) collective-permute-start(bf16[512,384]{1,0:T(8,128)(2,1)S(1)} %collective-permute-done.2), channel_id=1, source_target_pairs={{0,7},{1,0},{2,1},{3,2},{4,3},{5,4},{6,5},{7,6},{8,15},{9,8},{10,9... | collective-permute-start | bytes 1179656 | tf_op jit(solution)/shard_map/ppermute | solution.py:87
  40.7 10.2 %copy-start.7 = (bf16[512,384]{1,0:T(8,128)(2,1)}, bf16[512,384]{1,0:T(8,128)(2,1)S(1)}, u32[]{:S(2)}) copy-start(bf16[512,384]{1,0:T(8,128)(2,1)S(1)} %collective-permute-done.6) | copy-start | bytes 1179652
  40.7 9.2 %collective-permute-start.7 = (bf16[512,384]{1,0:T(8,128)(2,1)S(1)}, bf16[512,384]{1,0:T(8,128)(2,1)S(1)}, u32[]{:S(2)}, u32[]{:S(2)}) collective-permute-start(bf16[512,384]{1,0:T(8,128)(2,1)S(1)} %collective-permute-done.6), channel_id=1, source_target_pairs={{0,1},{1,2},{2,3},{3,4},{4,5},{5,6},{6,7},{7,0},{8,9},{9,10},{10,1... | collective-permute-start | bytes 1179656 | tf_op jit(solution)/shard_map/ppermute | solution.py:83
  45.0 5.8 %copy-start.10 = (bf16[512,384]{1,0:T(8,128)(2,1)}, bf16[512,384]{1,0:T(8,128)(2,1)S(1)}, u32[]{:S(2)}) copy-start(bf16[512,384]{1,0:T(8,128)(2,1)S(1)} %collective-permute-done.3) | copy-start | bytes 1179652
  49.9 1.0 copy-start.11
  50.2 4.7 %copy-start.16 = (s32[2048]{0:T(1024)S(1)}, s32[2048]{0:T(1024)}, u32[]{:S(2)}) copy-start(s32[2048]{0:T(1024)} %constant.63.clone) | copy-start | bytes 24580
  51.1 1.7 copy-start.3
  54.2 3.8 %collective-permute-start.8 = (f32[3072,128]{0,1:T(8,128)}, f32[3072,128]{0,1:T(8,128)}, u32[]{:S(2)}, u32[]{:S(2)}) collective-permute-start(f32[3072,128]{0,1:T(8,128)} %slice_bitcast_fusion), channel_id=1, source_target_pairs={{0,8},{8,0},{16,24},{24,16},{32,40},{40,32},{48,56},{56,48},{64,72... | collective-permute-start | bytes 4718600 | tf_op jit(solution)/shard_map/ppermute | solution.py:122
  63.7 18.9 %all-to-all-start = ((bf16[16,3,64,128]{3,2,1,0:T(8,128)(2,1)}), bf16[16,3,64,128]{3,2,1,0:T(8,128)(2,1)S(1)}, u32[]{:S(2)}, u32[]{:S(2)}) async-start(bf16[16,3,64,128]{3,2,1,0:T(8,128)(2,1)} %copy.22), calls=%async_computation | async-start | bytes 1572864 | tf_op jit(solution)/shard_map/all_to_all | solution.py:57
  68.9 7.4 %copy-start.8 = (bf16[512,384]{1,0:T(8,128)(2,1)S(1)}, bf16[512,384]{1,0:T(8,128)(2,1)}, u32[]{:S(2)}) copy-start(bf16[512,384]{1,0:T(8,128)(2,1)} %copy-done.7) | copy-start | bytes 1179652
  68.9 8.2 %copy-start.6 = (bf16[512,384]{1,0:T(8,128)(2,1)S(1)}, bf16[512,384]{1,0:T(8,128)(2,1)}, u32[]{:S(2)}) copy-start(bf16[512,384]{1,0:T(8,128)(2,1)} %copy-done.5) | copy-start | bytes 1179652
  78.8 36.7 %collective-permute-start.11 = (bf16[512,3072]{1,0:T(8,128)(2,1)}, bf16[512,3072]{1,0:T(8,128)(2,1)}, u32[]{:S(2)}, u32[]{:S(2)}) collective-permute-start(bf16[512,3072]{1,0:T(8,128)(2,1)} %constant_dynamic-update-slice_fusion), channel_id=1, source_target_pairs={{0,8},{8,0},{16,24},{24,16},{32,40},{40,32},{48,56},{56,48},{64,72... | collective-permute-start | bytes 9437192 | tf_op jit(solution)/shard_map/ppermute | solution.py:125
  90.8 13.9 %copy-start.1 = (bf16[1,1,128,1024]{3,2,1,0:T(8,128)(2,1)S(1)}, bf16[1,1,128,1024]{3,2,1,0:T(8,128)(2,1)}, u32[]{:S(2)}) copy-start(bf16[1,1,128,1024]{3,2,1,0:T(8,128)(2,1)} %param.10) | copy-start | bytes 786436
  90.9 13.9 %copy-start.14 = (f32[1,1024]{1,0:T(1,128)S(1)}, f32[1,1024]{1,0:T(1,128)}, u32[]{:S(2)}) copy-start(f32[1,1024]{1,0:T(1,128)} %param.16) | copy-start | bytes 12292
  90.9 13.9 %copy-start.15 = (f32[1,1024]{1,0:T(1,128)S(1)}, f32[1,1024]{1,0:T(1,128)}, u32[]{:S(2)}) copy-start(f32[1,1024]{1,0:T(1,128)} %param.17) | copy-start | bytes 12292
  94.0 21.2 %copy-start.12 = (f32[1,1024]{1,0:T(1,128)S(1)}, f32[1,1024]{1,0:T(1,128)}, u32[]{:S(2)}) copy-start(f32[1,1024]{1,0:T(1,128)} %param.13) | copy-start | bytes 12292
  94.0 21.2 %copy-start.13 = (f32[1,1024]{1,0:T(1,128)S(1)}, f32[1,1024]{1,0:T(1,128)}, u32[]{:S(2)}) copy-start(f32[1,1024]{1,0:T(1,128)} %param.12) | copy-start | bytes 12292
  105.2 9.7 %collective-permute-start.9 = (bf16[128,1024]{1,0:T(8,128)(2,1)S(1)}, bf16[128,1024]{1,0:T(8,128)(2,1)S(1)}, u32[]{:S(2)}, u32[]{:S(2)}) collective-permute-start(bf16[128,1024]{1,0:T(8,128)(2,1)S(1)} %fusion.44), channel_id=1, source_target_pairs={{0,144},{8,152},{16,128},{24,136},{32,176},{40,184},{48,160},{56,1... | collective-permute-start | bytes 786440 | tf_op jit(solution)/shard_map/ppermute | solution.py:133
  106.5 11.5 %copy-start.2 = (bf16[512,3072]{1,0:T(8,128)(2,1)S(1)}, bf16[512,3072]{1,0:T(8,128)(2,1)}, u32[]{:S(2)}) copy-start(bf16[512,3072]{1,0:T(8,128)(2,1)} %constant_dynamic-update-slice_fusion) | copy-start | bytes 9437188
  155.6 12.1 %all-to-all-start.3 = ((bf16[16,64,128]{2,1,0:T(8,128)(2,1)}), bf16[16,64,128]{2,1,0:T(8,128)(2,1)S(1)}, u32[]{:S(2)}, u32[]{:S(2)}) async-start(bf16[16,64,128]{2,1,0:T(8,128)(2,1)} %constant_dynamic-update-slice_fusion.8), calls=%async_computation.3 | async-start | bytes 524288 | tf_op jit(solution)/shard_map/all_to_all | solution.py:67
  159.1 11.4 %collective-permute-start.10 = (bf16[128,1024]{1,0:T(8,128)(2,1)S(1)}, bf16[128,1024]{1,0:T(8,128)(2,1)S(1)}, u32[]{:S(2)}, u32[]{:S(2)}) collective-permute-start(bf16[128,1024]{1,0:T(8,128)(2,1)S(1)} %collective-permute-done.9), channel_id=1, source_target_pairs={{0,16},{8,24},{16,0},{24,8},{32,48},{40,56},{48,32},{56,40},{64,80... | collective-permute-start | bytes 786440 | tf_op jit(solution)/shard_map/ppermute | solution.py:134

commit v10 on v7

--- a/solution.py
+++ b/solution.py
@@ -28,10 +28,10 @@
     valid = jnp.arange(count, dtype=jnp.int32) < length
     top = jnp.max(jnp.where(valid[None, :], scores, masked_score), axis=-1)
     weights = jnp.where(valid[None, :], jnp.exp(scores - top[:, None]), 0.0)
-    totals = jnp.sum(weights, axis=-1)
-    context = jnp.einsum(
-        "qk,dk->dq", weights.astype(jnp.bfloat16), value_rows, preferred_element_type=jnp.float32
+    totals, rounded = lax.optimization_barrier(
+        (jnp.sum(weights, axis=-1), weights.astype(jnp.bfloat16))
     )
+    context = jnp.einsum("qk,dk->dq", rounded, value_rows, preferred_element_type=jnp.float32)
     return (context / totals[None, :]).astype(jnp.bfloat16)
 
 

time: 165 us -> 163 us (0.988)
  matrix products: 20.1 us -> 16.9 us
    convert_element_type x0 -> x2, other arithmetic: none -> 10.2 us  [head_attention(): weights.astype(jnp.bfloat16)]
    reduce_sum x2 -> x0, other arithmetic: 9.64 us -> none  [head_attention(): totals = jnp.sum(weights, axis=-1)]
    dot_general x2, matrix products: 6.28 us -> 3.14 us  [head_attention(): jnp.einsum('qk,dk->dq', rounded, value_rows, preferred_element_type=jnp.f...]
where the time goes in v10:
time: 163 us; the launch traced here: 162 us
  waiting for transfers between devices  53.3 us (33%)
  blocking collectives  27.2 us (17%)
  starting transfers between devices  23.4 us (14%)
  local copies, waits for them, and re-layouts  22.7 us (14%)
  other arithmetic  17.2 us (11%)
  matrix products  16.9 us (10%)
    ppermute x4, waiting for transfers between devices, ring_gather(): forward = lax.ppermute(forward, axis, right)  23.8 us
    all_to_all x1, blocking collectives, sublayer(): gathered = lax.all_to_all(projected, 'ctx', 0, 3, tiled=True)  16.5 us
    unnamed x39, local copies, waits for them, and re-layouts  12.9 us
    ppermute x3, starting transfers between devices, ring_gather(): backward = lax.ppermute(backward, axis, left)  12.9 us
    all_to_all x1, blocking collectives, sublayer(): lax.all_to_all(context, 'ctx', 0, 0, tiled=True).reshape(width, tok_rows)  10.6 us
    convert_element_type x2, other arithmetic, head_attention(): weights.astype(jnp.bfloat16)  10.2 us
    ppermute x1, waiting for transfers between devices, per_device(): current = lax.ppermute(produced, 'pipe', pairs)  9.85 us
    all_to_all x1, waiting for transfers between devices, sublayer(): lax.all_to_all(context, 'ctx', 0, 0, tiled=True).reshape(width, tok_rows)  7.98 us
  transfers between devices with their start and end apart: 13, of which 10 were waited for; matrix products, arithmetic and copies ran while one was open for 17% of the time, Pallas kernels for 0%

profile of v10, /device:TPU:4, one launch (start us, length us, event | category | flops | bytes accessed | tf_op | source)
XLA Modules:
  0.0 161.8 jit_solution(8121881345600657781)
XLA Ops:
  0.0 2.0 %constant_dynamic-update-slice_fusion.7 = (bf16[512,3072]{1,0:T(8,128)(2,1)}, bf16[512,384]{1,0:T(8,128)(2,1)S(1)}) fusion(bf16[1,1024,384]{2,1,0:T(8,128)(2,1)} %param.12, s32[]{:T(128)S(6)} %select_n.45), kind=kLoop, calls=%fused_computation.112 | loop fusion | bytes 1179652
  2.0 5.9 %collective-permute-start.1 = (bf16[512,384]{1,0:T(8,128)(2,1)S(1)}, bf16[512,384]{1,0:T(8,128)(2,1)S(1)}, u32[]{:S(2)}, u32[]{:S(2)}) collective-permute-start(bf16[512,384]{1,0:T(8,128)(2,1)S(1)} %get-tuple-element.14), channel_id=1, source_target_pairs={{0,7},{1,0},{2,1},{3,2},{4,3},{5,4},{6,5},{7,6},{8,15},{9,8},{10,9... | collective-permute-start | bytes 1179656 | tf_op jit(solution)/shard_map/ppermute | solution.py:78
  7.9 1.1 convert_reduce_fusion.1
  9.0 1.2 fusion.64
  10.2 9.5 %collective-permute-done.4 = bf16[512,384]{1,0:T(8,128)(2,1)S(1)} collective-permute-done((bf16[512,384]{1,0:T(8,128)(2,1)S(1)}, bf16[512,384]{1,0:T(8,128)(2,1)S(1)}, u32[]{:S(2)}, u32[]{:S(2)}) %collective-permute-start.4) | collective-permute-done | bytes 393248 | tf_op jit(solution)/shard_map/ppermute | solution.py:74
  19.7 1.2 fusion.67
  21.0 3.3 %collective-permute-start.2 = (bf16[512,384]{1,0:T(8,128)(2,1)S(1)}, bf16[512,384]{1,0:T(8,128)(2,1)S(1)}, u32[]{:S(2)}, u32[]{:S(2)}) collective-permute-start(bf16[512,384]{1,0:T(8,128)(2,1)S(1)} %collective-permute-done.1), channel_id=1, source_target_pairs={{0,7},{1,0},{2,1},{3,2},{4,3},{5,4},{6,5},{7,6},{8,15},{9,8},{10,9... | collective-permute-start | bytes 1179656 | tf_op jit(solution)/shard_map/ppermute | solution.py:78
  24.3 6.3 %collective-permute-done.5 = bf16[512,384]{1,0:T(8,128)(2,1)S(1)} collective-permute-done((bf16[512,384]{1,0:T(8,128)(2,1)S(1)}, bf16[512,384]{1,0:T(8,128)(2,1)S(1)}, u32[]{:S(2)}, u32[]{:S(2)}) %collective-permute-start.5) | collective-permute-done | bytes 393248 | tf_op jit(solution)/shard_map/ppermute | solution.py:74
  30.6 1.4 fusion.44
  32.1 1.2 collective-permute-done.2
  33.3 3.7 %collective-permute-start.3 = (bf16[512,384]{1,0:T(8,128)(2,1)S(1)}, bf16[512,384]{1,0:T(8,128)(2,1)S(1)}, u32[]{:S(2)}, u32[]{:S(2)}) collective-permute-start(bf16[512,384]{1,0:T(8,128)(2,1)S(1)} %collective-permute-done.2), channel_id=1, source_target_pairs={{0,7},{1,0},{2,1},{3,2},{4,3},{5,4},{6,5},{7,6},{8,15},{9,8},{10,9... | collective-permute-start | bytes 1179656 | tf_op jit(solution)/shard_map/ppermute | solution.py:78
  37.0 0.3 fusion.43
  37.3 3.4 %collective-permute-done.6 = bf16[512,384]{1,0:T(8,128)(2,1)S(1)} collective-permute-done((bf16[512,384]{1,0:T(8,128)(2,1)S(1)}, bf16[512,384]{1,0:T(8,128)(2,1)S(1)}, u32[]{:S(2)}, u32[]{:S(2)}) %collective-permute-start.6) | collective-permute-done | bytes 393248 | tf_op jit(solution)/shard_map/ppermute | solution.py:74
  40.7 0.3 fusion.42
  41.0 4.1 %collective-permute-done.3 = bf16[512,384]{1,0:T(8,128)(2,1)S(1)} collective-permute-done((bf16[512,384]{1,0:T(8,128)(2,1)S(1)}, bf16[512,384]{1,0:T(8,128)(2,1)S(1)}, u32[]{:S(2)}, u32[]{:S(2)}) %collective-permute-start.3) | collective-permute-done | bytes 393248 | tf_op jit(solution)/shard_map/ppermute | solution.py:78
  45.1 0.3 fusion.41
  45.4 4.6 %collective-permute-done.7 = bf16[512,384]{1,0:T(8,128)(2,1)S(1)} collective-permute-done((bf16[512,384]{1,0:T(8,128)(2,1)S(1)}, bf16[512,384]{1,0:T(8,128)(2,1)S(1)}, u32[]{:S(2)}, u32[]{:S(2)}) %collective-permute-start.7) | collective-permute-done | bytes 393248 | tf_op jit(solution)/shard_map/ppermute | solution.py:74
  49.9 0.3 fusion.40
  50.2 0.3 fusion.39
  50.5 0.3 fusion.38
  50.9 0.3 fusion.37
  51.2 1.7 %copy-done.3 = f32[2,3072,128]{1,2,0:T(8,128)} copy-done((f32[2,3072,128]{1,2,0:T(8,128)}, f32[2,3072,128]{1,2,0:T(8,128)S(1)}, u32[]{:S(2)}) %copy-start.3) | copy-done | bytes 3145752
  52.8 1.4 slice_bitcast_fusion
  54.9 3.1 %collective-permute-done.8 = f32[3072,128]{0,1:T(8,128)} collective-permute-done((f32[3072,128]{0,1:T(8,128)}, f32[3072,128]{0,1:T(8,128)}, u32[]{:S(2)}, u32[]{:S(2)}) %collective-permute-start.8) | collective-permute-done | bytes 1572896 | tf_op jit(solution)/shard_map/ppermute | solution.py:113
  57.9 2.0 %fusion.12 = bf16[3072,128]{0,1:T(8,128)(2,1)S(1)} fusion(f32[3072,128]{0,1:T(8,128)} %collective-permute-done.8, f32[2,3072,128]{1,2,0:T(8,128)} %copy-done.3), kind=kLoop, calls=%fused_computation.21 | loop fusion | flops 786432 | bytes 3932160 | tf_op jit(solution)/shard_map/convert_element_type | solution.py:114
  60.0 0.4 fusion.54
  60.4 1.2 copy.19
  61.6 2.1 %copy.20 = bf16[16,3,64,128]{3,2,1,0:T(8,128)(2,1)} copy(bf16[16,3,64,128]{3,2,0,1:T(8,128)(2,1)} %bitcast.198) | data formatting | bytes 1572864 | tf_op jit(solution)/shard_map/transpose | solution.py:115
  63.7 5.2 %all-to-all-start = ((bf16[16,3,64,128]{3,2,1,0:T(8,128)(2,1)}), bf16[16,3,64,128]{3,2,1,0:T(8,128)(2,1)S(1)}, u32[]{:S(2)}, u32[]{:S(2)}) async-start(bf16[16,3,64,128]{3,2,1,0:T(8,128)(2,1)} %copy.20), calls=%async_computation | async-start | bytes 1572864 | tf_op jit(solution)/shard_map/all_to_all | solution.py:56
  68.9 1.9 %constant_dynamic-update-slice_fusion.6 = bf16[512,3072]{1,0:T(8,128)(2,1)} fusion(bf16[512,3072]{1,0:T(8,128)(2,1)} %get-tuple-element.13, bf16[512,384]{1,0:T(8,128)(2,1)} %copy-done.4), kind=kLoop, calls=%fused_computation.111 | loop fusion | bytes 786432
  70.8 1.8 %constant_dynamic-update-slice_fusion.5 = bf16[512,3072]{1,0:T(8,128)(2,1)} fusion(bf16[512,3072]{1,0:T(8,128)(2,1)} %constant_dynamic-update-slice_fusion.6, bf16[512,384]{1,0:T(8,128)(2,1)} %copy-done.9), kind=kLoop, calls=%fused_computation.110 | loop fusion | bytes 786432
  72.7 1.8 %constant_dynamic-update-slice_fusion.4 = bf16[512,3072]{1,0:T(8,128)(2,1)} fusion(bf16[512,3072]{1,0:T(8,128)(2,1)} %constant_dynamic-update-slice_fusion.5, bf16[512,384]{1,0:T(8,128)(2,1)} %copy-done.10), kind=kLoop, calls=%fused_computation.109 | loop fusion | bytes 786432
  74.5 1.8 %constant_dynamic-update-slice_fusion.3 = bf16[512,3072]{1,0:T(8,128)(2,1)} fusion(bf16[512,3072]{1,0:T(8,128)(2,1)} %constant_dynamic-update-slice_fusion.4, bf16[512,384]{1,0:T(8,128)(2,1)} %copy-done.11), kind=kLoop, calls=%fused_computation.108 | loop fusion | bytes 786432
  76.3 0.8 constant_dynamic-update-slice_fusion.2
  77.2 0.8 constant_dynamic-update-slice_fusion.1
  78.0 0.9 constant_dynamic-update-slice_fusion
  78.9 0.4 collective-permute-start.10
  79.3 3.3 %all-to-all-done = bf16[16,3,64,128]{3,2,1,0:T(8,128)(2,1)S(1)} async-done(((bf16[16,3,64,128]{3,2,1,0:T(8,128)(2,1)}), bf16[16,3,64,128]{3,2,1,0:T(8,128)(2,1)S(1)}, u32[]{:S(2)}, u32[]{:S(2)}) %all-to-all-start) | async-done | bytes 786464 | tf_op jit(solution)/shard_map/all_to_all | solution.py:56
  82.7 0.2 copy.22
  82.9 0.2 copy.23
  83.1 2.8 %select_reduce_fusion.1 = (f32[2048]{0:T(1024)S(1)}, f32[2048,2048]{0,1:T(8,128)S(1)}) fusion(pred[2048]{0:T(1024)(128)(4,1)S(1)} %iota_compare_fusion, bf16[8,8,16,128]{3,2,1,0:T(8,128)(2,1)S(1)} %bitcast.204, bf16[8,8,16,128]{3,2,1,0:T(8,128)(2,1)S(1)} %bitcast.202), kind=kOutput, calls=%fused_computation.3 | convolution fusion | flops 549451776 | bytes 17311744 | tf_op jit(solution)/shard_map/dq,dk->qk/dot_general | solution.py:25
  85.8 5.1 %fusion = (bf16[2048,2048]{0,1:T(8,128)(2,1)S(1)}, f32[2048]{0:T(1024)S(1)}) fusion(f32[2048,2048]{0,1:T(8,128)S(1)} %get-tuple-element.26, f32[2048]{0:T(1024)S(1)} %get-tuple-element.25, pred[2048]{0:T(1024)(128)(4,1)S(1)} %iota_compare_fusion), kind=kLoop, calls=%fused_computation.4 | loop fusion | flops 20969472 | bytes 25184256 | tf_op jit(solution)/shard_map/convert_element_type | solution.py:32
  91.0 0.2 copy.21
  91.2 1.6 fusion.52
  92.8 10.6 %all_to_all.40 = bf16[16,64,128]{2,1,0:T(8,128)(2,1)S(1)} all-to-all(bf16[16,64,128]{2,1,0:T(8,128)(2,1)S(1)} %bitcast.206), channel_id=1, replica_groups=mesh['pipe'=2,'ctx'=16,'dp'=8] {'ctx'}, dimensions={0} | all-to-all | bytes 524288 | tf_op jit(solution)/shard_map/all_to_all | solution.py:59
  103.5 0.5 fusion.34
  104.0 1.3 collective-permute-start.9
  105.3 9.8 %collective-permute-done.9 = bf16[128,1024]{1,0:T(8,128)(2,1)S(1)} collective-permute-done((bf16[128,1024]{1,0:T(8,128)(2,1)S(1)}, bf16[128,1024]{1,0:T(8,128)(2,1)S(1)}, u32[]{:S(2)}, u32[]{:S(2)}) %collective-permute-start.9) | collective-permute-done | bytes 262176 | tf_op jit(solution)/shard_map/ppermute | solution.py:125
  115.3 0.2 fusion.60
  115.5 0.2 fusion.63
  115.8 2.5 %fusion.91 = f32[128,3072]{1,0:T(8,128)S(1)} fusion(bf16[512,3072]{1,0:T(8,128)(2,1)} %collective-permute-done.10, bf16[128,1024]{1,0:T(8,128)(2,1)S(1)} %fusion.63, s32[]{:T(128)S(6)} %select_n.49), kind=kOutput, calls=%fused_computation.100 | convolution fusion | flops 402653184 | bytes 4849668 | tf_op jit(solution)/shard_map/dot_general | solution.py:49
  118.3 0.6 fusion.4
  118.9 0.4 fusion.53
  119.3 1.2 copy.25
  120.5 1.2 copy.26
  121.7 16.5 %all_to_all.41 = bf16[16,3,64,128]{3,2,1,0:T(8,128)(2,1)S(1)} all-to-all(bf16[16,3,64,128]{3,2,1,0:T(8,128)(2,1)S(1)} %copy.26), channel_id=1, replica_groups=mesh['pipe'=2,'ctx'=16,'dp'=8] {'ctx'}, dimensions={0} | all-to-all | bytes 1572864 | tf_op jit(solution)/shard_map/all_to_all | solution.py:56
  138.6 2.8 %select_reduce_fusion = (f32[2048]{0:T(1024)S(1)}, f32[2048,2048]{0,1:T(8,128)S(1)}) fusion(pred[2048]{0:T(1024)(128)(4,1)S(1)} %iota_compare_fusion, bf16[8,8,16,128]{3,2,1,0:T(8,128)(2,1)S(1)} %bitcast.205, bf16[8,8,16,128]{3,2,1,0:T(8,128)(2,1)S(1)} %bitcast.203), kind=kOutput, calls=%fused_computation.1 | convolution fusion | flops 549451776 | bytes 17311744 | tf_op jit(solution)/shard_map/dq,dk->qk/dot_general | solution.py:25
  141.4 5.1 %fusion.2 = (bf16[2048,2048]{0,1:T(8,128)(2,1)S(1)}, f32[2048]{0:T(1024)S(1)}) fusion(f32[2048,2048]{0,1:T(8,128)S(1)} %get-tuple-element.28, f32[2048]{0:T(1024)S(1)} %get-tuple-element.27, pred[2048]{0:T(1024)(128)(4,1)S(1)} %iota_compare_fusion), kind=kLoop, calls=%fused_computation.6 | loop fusion | flops 20969472 | bytes 25184256 | tf_op jit(solution)/shard_map/convert_element_type | solution.py:32
  146.6 0.2 copy.27
  146.7 1.6 fusion.51
  148.3 0.8 copy.73
  149.1 3.5 %all-to-all-start.3 = ((bf16[16,64,128]{2,1,0:T(8,128)(2,1)}), bf16[16,64,128]{2,1,0:T(8,128)(2,1)S(1)}, u32[]{:S(2)}, u32[]{:S(2)}) async-start(bf16[16,64,128]{2,1,0:T(8,128)(2,1)} %bitcast.192), calls=%async_computation.3 | async-start | bytes 524288 | tf_op jit(solution)/shard_map/all_to_all | solution.py:59
  152.6 8.0 %all-to-all-done.3 = bf16[16,64,128]{2,1,0:T(8,128)(2,1)S(1)} async-done(((bf16[16,64,128]{2,1,0:T(8,128)(2,1)}), bf16[16,64,128]{2,1,0:T(8,128)(2,1)S(1)}, u32[]{:S(2)}, u32[]{:S(2)}) %all-to-all-start.3) | async-done | bytes 262176 | tf_op jit(solution)/shard_map/all_to_all | solution.py:59
  160.6 1.2 fusion.48
  (53 shorter events, 0.9 us)
Async XLA Ops:
  0.0 103.5 %copy-start = (bf16[1,1024,1024]{2,1,0:T(8,128)(2,1)S(1)}, bf16[1,1024,1024]{2,1,0:T(8,128)(2,1)}, u32[]{:S(2)}) copy-start(bf16[1,1024,1024]{2,1,0:T(8,128)(2,1)} %param.13) | copy-start | bytes 6291460
  2.0 19.0 %collective-permute-start.1 = (bf16[512,384]{1,0:T(8,128)(2,1)S(1)}, bf16[512,384]{1,0:T(8,128)(2,1)S(1)}, u32[]{:S(2)}, u32[]{:S(2)}) collective-permute-start(bf16[512,384]{1,0:T(8,128)(2,1)S(1)} %get-tuple-element.14), channel_id=1, source_target_pairs={{0,7},{1,0},{2,1},{3,2},{4,3},{5,4},{6,5},{7,6},{8,15},{9,8},{10,9... | collective-permute-start | bytes 1179656 | tf_op jit(solution)/shard_map/ppermute | solution.py:78
  7.9 11.8 %collective-permute-start.4 = (bf16[512,384]{1,0:T(8,128)(2,1)S(1)}, bf16[512,384]{1,0:T(8,128)(2,1)S(1)}, u32[]{:S(2)}, u32[]{:S(2)}) collective-permute-start(bf16[512,384]{1,0:T(8,128)(2,1)S(1)} %get-tuple-element.14), channel_id=1, source_target_pairs={{0,1},{1,2},{2,3},{3,4},{4,5},{5,6},{6,7},{7,0},{8,9},{9,10},{10,1... | collective-permute-start | bytes 1179656 | tf_op jit(solution)/shard_map/ppermute | solution.py:74
  19.7 10.9 %collective-permute-start.5 = (bf16[512,384]{1,0:T(8,128)(2,1)S(1)}, bf16[512,384]{1,0:T(8,128)(2,1)S(1)}, u32[]{:S(2)}, u32[]{:S(2)}) collective-permute-start(bf16[512,384]{1,0:T(8,128)(2,1)S(1)} %collective-permute-done.4), channel_id=1, source_target_pairs={{0,1},{1,2},{2,3},{3,4},{4,5},{5,6},{6,7},{7,0},{8,9},{9,10},{10,1... | collective-permute-start | bytes 1179656 | tf_op jit(solution)/shard_map/ppermute | solution.py:74
  20.9 9.7 %collective-permute-start = (bf16[128,1024]{1,0:T(8,128)(2,1)S(1)}, bf16[128,1024]{1,0:T(8,128)(2,1)S(1)}, u32[]{:S(2)}, u32[]{:S(2)}) collective-permute-start(bf16[128,1024]{1,0:T(8,128)(2,1)S(1)} %fusion.67), channel_id=1, source_target_pairs={{0,8},{8,0},{16,24},{24,16},{32,40},{40,32},{48,56},{56,48},{64,72... | collective-permute-start | bytes 786440 | tf_op jit(solution)/shard_map/ppermute | solution.py:102
  21.0 29.5 %copy-start.4 = (bf16[512,384]{1,0:T(8,128)(2,1)}, bf16[512,384]{1,0:T(8,128)(2,1)S(1)}, u32[]{:S(2)}) copy-start(bf16[512,384]{1,0:T(8,128)(2,1)S(1)} %collective-permute-done.1) | copy-start | bytes 1179652
  21.0 12.3 %collective-permute-start.2 = (bf16[512,384]{1,0:T(8,128)(2,1)S(1)}, bf16[512,384]{1,0:T(8,128)(2,1)S(1)}, u32[]{:S(2)}, u32[]{:S(2)}) collective-permute-start(bf16[512,384]{1,0:T(8,128)(2,1)S(1)} %collective-permute-done.1), channel_id=1, source_target_pairs={{0,7},{1,0},{2,1},{3,2},{4,3},{5,4},{6,5},{7,6},{8,15},{9,8},{10,9... | collective-permute-start | bytes 1179656 | tf_op jit(solution)/shard_map/ppermute | solution.py:78
  30.6 19.9 %copy-start.5 = (bf16[512,384]{1,0:T(8,128)(2,1)}, bf16[512,384]{1,0:T(8,128)(2,1)S(1)}, u32[]{:S(2)}) copy-start(bf16[512,384]{1,0:T(8,128)(2,1)S(1)} %collective-permute-done.5) | copy-start | bytes 1179652
  30.6 10.1 %collective-permute-start.6 = (bf16[512,384]{1,0:T(8,128)(2,1)S(1)}, bf16[512,384]{1,0:T(8,128)(2,1)S(1)}, u32[]{:S(2)}, u32[]{:S(2)}) collective-permute-start(bf16[512,384]{1,0:T(8,128)(2,1)S(1)} %collective-permute-done.5), channel_id=1, source_target_pairs={{0,1},{1,2},{2,3},{3,4},{4,5},{5,6},{6,7},{7,0},{8,9},{9,10},{10,1... | collective-permute-start | bytes 1179656 | tf_op jit(solution)/shard_map/ppermute | solution.py:74
  33.3 17.6 %copy-start.9 = (bf16[512,384]{1,0:T(8,128)(2,1)}, bf16[512,384]{1,0:T(8,128)(2,1)S(1)}, u32[]{:S(2)}) copy-start(bf16[512,384]{1,0:T(8,128)(2,1)S(1)} %collective-permute-done.2) | copy-start | bytes 1179652
  33.3 11.8 %collective-permute-start.3 = (bf16[512,384]{1,0:T(8,128)(2,1)S(1)}, bf16[512,384]{1,0:T(8,128)(2,1)S(1)}, u32[]{:S(2)}, u32[]{:S(2)}) collective-permute-start(bf16[512,384]{1,0:T(8,128)(2,1)S(1)} %collective-permute-done.2), channel_id=1, source_target_pairs={{0,7},{1,0},{2,1},{3,2},{4,3},{5,4},{6,5},{7,6},{8,15},{9,8},{10,9... | collective-permute-start | bytes 1179656 | tf_op jit(solution)/shard_map/ppermute | solution.py:78
  40.7 10.2 %copy-start.7 = (bf16[512,384]{1,0:T(8,128)(2,1)}, bf16[512,384]{1,0:T(8,128)(2,1)S(1)}, u32[]{:S(2)}) copy-start(bf16[512,384]{1,0:T(8,128)(2,1)S(1)} %collective-permute-done.6) | copy-start | bytes 1179652
  40.7 9.2 %collective-permute-start.7 = (bf16[512,384]{1,0:T(8,128)(2,1)S(1)}, bf16[512,384]{1,0:T(8,128)(2,1)S(1)}, u32[]{:S(2)}, u32[]{:S(2)}) collective-permute-start(bf16[512,384]{1,0:T(8,128)(2,1)S(1)} %collective-permute-done.6), channel_id=1, source_target_pairs={{0,1},{1,2},{2,3},{3,4},{4,5},{5,6},{6,7},{7,0},{8,9},{9,10},{10,1... | collective-permute-start | bytes 1179656 | tf_op jit(solution)/shard_map/ppermute | solution.py:74
  45.1 5.8 %copy-start.10 = (bf16[512,384]{1,0:T(8,128)(2,1)}, bf16[512,384]{1,0:T(8,128)(2,1)S(1)}, u32[]{:S(2)}) copy-start(bf16[512,384]{1,0:T(8,128)(2,1)S(1)} %collective-permute-done.3) | copy-start | bytes 1179652
  49.9 0.9 copy-start.11
  51.2 1.7 %copy-start.3 = (f32[2,3072,128]{1,2,0:T(8,128)}, f32[2,3072,128]{1,2,0:T(8,128)S(1)}, u32[]{:S(2)}) copy-start(f32[2,3072,128]{1,2,0:T(8,128)S(1)} %fusion.37) | copy-start | bytes 9437188
  54.2 3.8 %collective-permute-start.8 = (f32[3072,128]{0,1:T(8,128)}, f32[3072,128]{0,1:T(8,128)}, u32[]{:S(2)}, u32[]{:S(2)}) collective-permute-start(f32[3072,128]{0,1:T(8,128)} %slice_bitcast_fusion), channel_id=1, source_target_pairs={{0,8},{8,0},{16,24},{24,16},{32,40},{40,32},{48,56},{56,48},{64,72... | collective-permute-start | bytes 4718600 | tf_op jit(solution)/shard_map/ppermute | solution.py:113
  63.7 18.9 %all-to-all-start = ((bf16[16,3,64,128]{3,2,1,0:T(8,128)(2,1)}), bf16[16,3,64,128]{3,2,1,0:T(8,128)(2,1)S(1)}, u32[]{:S(2)}, u32[]{:S(2)}) async-start(bf16[16,3,64,128]{3,2,1,0:T(8,128)(2,1)} %copy.20), calls=%async_computation | async-start | bytes 1572864 | tf_op jit(solution)/shard_map/all_to_all | solution.py:56
  68.9 7.4 %copy-start.8 = (bf16[512,384]{1,0:T(8,128)(2,1)S(1)}, bf16[512,384]{1,0:T(8,128)(2,1)}, u32[]{:S(2)}) copy-start(bf16[512,384]{1,0:T(8,128)(2,1)} %copy-done.7) | copy-start | bytes 1179652
  68.9 8.3 %copy-start.6 = (bf16[512,384]{1,0:T(8,128)(2,1)S(1)}, bf16[512,384]{1,0:T(8,128)(2,1)}, u32[]{:S(2)}) copy-start(bf16[512,384]{1,0:T(8,128)(2,1)} %copy-done.5) | copy-start | bytes 1179652
  78.9 36.9 %collective-permute-start.10 = (bf16[512,3072]{1,0:T(8,128)(2,1)}, bf16[512,3072]{1,0:T(8,128)(2,1)}, u32[]{:S(2)}, u32[]{:S(2)}) collective-permute-start(bf16[512,3072]{1,0:T(8,128)(2,1)} %constant_dynamic-update-slice_fusion), channel_id=1, source_target_pairs={{0,8},{8,0},{16,24},{24,16},{32,40},{40,32},{48,56},{56,48},{64,72... | collective-permute-start | bytes 9437192 | tf_op jit(solution)/shard_map/ppermute | solution.py:116
  91.1 12.3 %copy-start.1 = (bf16[1,1,128,1024]{3,2,1,0:T(8,128)(2,1)S(1)}, bf16[1,1,128,1024]{3,2,1,0:T(8,128)(2,1)}, u32[]{:S(2)}) copy-start(bf16[1,1,128,1024]{3,2,1,0:T(8,128)(2,1)} %param.8) | copy-start | bytes 786436
  91.2 12.3 %copy-start.14 = (f32[1,1024]{1,0:T(1,128)S(1)}, f32[1,1024]{1,0:T(1,128)}, u32[]{:S(2)}) copy-start(f32[1,1024]{1,0:T(1,128)} %param.14) | copy-start | bytes 12292
  91.2 12.3 %copy-start.15 = (f32[1,1024]{1,0:T(1,128)S(1)}, f32[1,1024]{1,0:T(1,128)}, u32[]{:S(2)}) copy-start(f32[1,1024]{1,0:T(1,128)} %param.15) | copy-start | bytes 12292
  92.8 22.8 %copy-start.12 = (f32[1,1024]{1,0:T(1,128)S(1)}, f32[1,1024]{1,0:T(1,128)}, u32[]{:S(2)}) copy-start(f32[1,1024]{1,0:T(1,128)} %param.11) | copy-start | bytes 12292
  92.8 22.8 %copy-start.13 = (f32[1,1024]{1,0:T(1,128)S(1)}, f32[1,1024]{1,0:T(1,128)}, u32[]{:S(2)}) copy-start(f32[1,1024]{1,0:T(1,128)} %param.10) | copy-start | bytes 12292
  104.0 11.2 %collective-permute-start.9 = (bf16[128,1024]{1,0:T(8,128)(2,1)S(1)}, bf16[128,1024]{1,0:T(8,128)(2,1)S(1)}, u32[]{:S(2)}, u32[]{:S(2)}) collective-permute-start(bf16[128,1024]{1,0:T(8,128)(2,1)S(1)} %fusion.34), channel_id=1, source_target_pairs={{0,128},{1,129},{2,130},{3,131},{4,132},{5,133},{6,134},{7,135},{8... | collective-permute-start | bytes 786440 | tf_op jit(solution)/shard_map/ppermute | solution.py:125
  105.3 13.0 %copy-start.2 = (bf16[512,3072]{1,0:T(8,128)(2,1)S(1)}, bf16[512,3072]{1,0:T(8,128)(2,1)}, u32[]{:S(2)}) copy-start(bf16[512,3072]{1,0:T(8,128)(2,1)} %constant_dynamic-update-slice_fusion) | copy-start | bytes 9437188
  149.1 11.5 %all-to-all-start.3 = ((bf16[16,64,128]{2,1,0:T(8,128)(2,1)}), bf16[16,64,128]{2,1,0:T(8,128)(2,1)S(1)}, u32[]{:S(2)}, u32[]{:S(2)}) async-start(bf16[16,64,128]{2,1,0:T(8,128)(2,1)} %bitcast.192), calls=%async_computation.3 | async-start | bytes 524288 | tf_op jit(solution)/shard_map/all_to_all | solution.py:59

commit v11 on v10

--- a/solution.py
+++ b/solution.py
@@ -49,9 +49,8 @@
         projected = jnp.dot(normed_mine, qkv_mine, preferred_element_type=jnp.float32) + jnp.dot(
             normed_other, qkv_other, preferred_element_type=jnp.float32
         )
-        projected = unrotate(projected.astype(jnp.bfloat16), "dp")
         projected = jnp.transpose(
-            projected.reshape(tok_rows, 3, HEADS, head_width), (2, 1, 3, 0)
+            projected.astype(jnp.bfloat16).reshape(tok_rows, HEADS, 3, head_width), (1, 2, 3, 0)
         )
     gathered = lax.all_to_all(projected, "ctx", 0, 3, tiled=True)
     context = head_attention(gathered[0], length, head_width ** (-0.5))
@@ -113,6 +112,8 @@
     partial_other = lax.ppermute(partial[1], "ctx", sibling)
     first = unrotate((partial[0] + partial_other).astype(jnp.bfloat16), "dp", along=0)
     first = jnp.transpose(first.reshape(3, HEADS, width // HEADS, tok_rows), (1, 0, 2, 3))
+    qkv_mine = unrotate(qkv_mine, "dp").reshape(half, 3, HEADS, width // HEADS)
+    qkv_mine = jnp.transpose(qkv_mine, (0, 2, 1, 3)).reshape(half, 3 * width)
     qkv_other = lax.ppermute(qkv_mine, "ctx", sibling)
     args = (qkv_mine, qkv_other, w_out[0], norm_gain[0], norm_bias[0], out_bias[0], scale_gain[0])
     length = lengths[0, 0]

time: 163 us -> 175 us (1.074)
  local copies, waits for them, and re-layouts: 22.7 us -> 38.9 us
  waiting for transfers between devices: 53.3 us -> 43.4 us
  matrix products: 16.9 us -> 21.9 us
  blocking collectives: 27.2 us -> 29.8 us
    dynamic_slice x2 -> x3, local copies, waits for them, and re-layouts: 2.36 us -> 10.8 us  [unrotate(): return lax.dynamic_slice_in_dim(doubled, cols - shift, cols, axis=along)]
    all_to_all x1, waiting for transfers between devices: 3.34 us -> 0.01 us  [sublayer(): gathered = lax.all_to_all(projected, 'ctx', 0, 3, tiled=True)]
    ppermute x1, waiting for transfers between devices: 3.08 us -> 0.01 us  [per_device(): partial_other = lax.ppermute(partial[1], 'ctx', sibling)]
    ppermute x3, waiting for transfers between devices: 5.27 us -> 2.23 us  [ring_gather(): backward = lax.ppermute(backward, axis, left)]
    unnamed x39 -> x35, local copies, waits for them, and re-layouts: 12.9 us -> 15.7 us
    transpose x1, local copies, waits for them, and re-layouts: 1.18 us -> 3.88 us  [per_device(): qkv_mine = jnp.transpose(qkv_mine, (0, 2, 1, 3)).reshape(half, 3 * width)]
    all_to_all x1, blocking collectives: 10.6 us -> 13.2 us  [sublayer(): lax.all_to_all(context, 'ctx', 0, 0, tiled=True).reshape(width, tok_rows)]
    dot_general x1, matrix products: 0.58 us -> 3.03 us  [sublayer(): jnp.dot(normed_mine, qkv_mine, preferred_element_type=jnp.float32)]
  transfers between devices with their start and end apart: 13 -> 13, of which waited for: 10 -> 7; matrix products, arithmetic and copies ran while one was open for 17% -> 29% of each run, Pallas kernels for 0% -> 0%
where the time goes in v11:
time: 175 us; the launch traced here: 174 us
  waiting for transfers between devices  43.4 us (25%)
  local copies, waits for them, and re-layouts  38.9 us (22%)
  blocking collectives  29.8 us (17%)
  starting transfers between devices  23.6 us (13%)
  matrix products  21.9 us (13%)
  other arithmetic  15.7 us (9%)
    ppermute x4, waiting for transfers between devices, ring_gather(): forward = lax.ppermute(forward, axis, right)  23.3 us
    all_to_all x1, blocking collectives, sublayer(): gathered = lax.all_to_all(projected, 'ctx', 0, 3, tiled=True)  16.5 us
    unnamed x35, local copies, waits for them, and re-layouts  15.7 us
    all_to_all x1, blocking collectives, sublayer(): lax.all_to_all(context, 'ctx', 0, 0, tiled=True).reshape(width, tok_rows)  13.2 us
    ppermute x3, starting transfers between devices, ring_gather(): backward = lax.ppermute(backward, axis, left)  10.9 us
    dynamic_slice x3, local copies, waits for them, and re-layouts, unrotate(): return lax.dynamic_slice_in_dim(doubled, cols - shift, cols, axis=along)  10.8 us
    convert_element_type x2, other arithmetic, head_attention(): weights.astype(jnp.bfloat16)  10.2 us
    ppermute x1, waiting for transfers between devices, per_device(): current = lax.ppermute(produced, 'pipe', pairs)  9.89 us
  transfers between devices with their start and end apart: 13, of which 7 were waited for; matrix products, arithmetic and copies ran while one was open for 29% of the time, Pallas kernels for 0%

profile of v11, /device:TPU:4, one launch (start us, length us, event | category | flops | bytes accessed | tf_op | source)
XLA Modules:
  0.0 174.3 jit_solution(13067268690692166228)
XLA Ops:
  0.0 2.0 %constant_dynamic-update-slice_fusion.15 = (bf16[512,6144]{1,0:T(8,128)(2,1)}, bf16[512,384]{1,0:T(8,128)(2,1)S(1)}) fusion(bf16[1,1024,384]{2,1,0:T(8,128)(2,1)} %param.12, s32[]{:T(128)S(6)} %select_n.45), kind=kLoop, calls=%fused_computation.117 | loop fusion | bytes 1179652
  2.0 1.9 %collective-permute-start.4 = (bf16[512,384]{1,0:T(8,128)(2,1)S(1)}, bf16[512,384]{1,0:T(8,128)(2,1)S(1)}, u32[]{:S(2)}, u32[]{:S(2)}) collective-permute-start(bf16[512,384]{1,0:T(8,128)(2,1)S(1)} %get-tuple-element.14), channel_id=1, source_target_pairs={{0,1},{1,2},{2,3},{3,4},{4,5},{5,6},{6,7},{7,0},{8,9},{9,10},{10,1... | collective-permute-start | bytes 1179656 | tf_op jit(solution)/shard_map/ppermute | solution.py:73
  3.9 3.9 %collective-permute-start.1 = (bf16[512,384]{1,0:T(8,128)(2,1)S(1)}, bf16[512,384]{1,0:T(8,128)(2,1)S(1)}, u32[]{:S(2)}, u32[]{:S(2)}) collective-permute-start(bf16[512,384]{1,0:T(8,128)(2,1)S(1)} %get-tuple-element.14), channel_id=1, source_target_pairs={{0,7},{1,0},{2,1},{3,2},{4,3},{5,4},{6,5},{7,6},{8,15},{9,8},{10,9... | collective-permute-start | bytes 1179656 | tf_op jit(solution)/shard_map/ppermute | solution.py:77
  7.9 1.1 convert_reduce_fusion.1
  8.9 1.2 fusion.63
  10.1 6.9 %collective-permute-done.4 = bf16[512,384]{1,0:T(8,128)(2,1)S(1)} collective-permute-done((bf16[512,384]{1,0:T(8,128)(2,1)S(1)}, bf16[512,384]{1,0:T(8,128)(2,1)S(1)}, u32[]{:S(2)}, u32[]{:S(2)}) %collective-permute-start.4) | collective-permute-done | bytes 393248 | tf_op jit(solution)/shard_map/ppermute | solution.py:73
  17.0 1.2 fusion.66
  18.3 3.3 %collective-permute-start.2 = (bf16[512,384]{1,0:T(8,128)(2,1)S(1)}, bf16[512,384]{1,0:T(8,128)(2,1)}, u32[]{:S(2)}, u32[]{:S(2)}) collective-permute-start(bf16[512,384]{1,0:T(8,128)(2,1)S(1)} %collective-permute-done.1), channel_id=1, source_target_pairs={{0,7},{1,0},{2,1},{3,2},{4,3},{5,4},{6,5},{7,6},{8,15},{9,8},{10,9... | collective-permute-start | bytes 1179656 | tf_op jit(solution)/shard_map/ppermute | solution.py:77
  22.3 6.2 %collective-permute-done.5 = bf16[512,384]{1,0:T(8,128)(2,1)S(1)} collective-permute-done((bf16[512,384]{1,0:T(8,128)(2,1)S(1)}, bf16[512,384]{1,0:T(8,128)(2,1)S(1)}, u32[]{:S(2)}, u32[]{:S(2)}) %collective-permute-start.5) | collective-permute-done | bytes 393248 | tf_op jit(solution)/shard_map/ppermute | solution.py:73
  28.5 0.9 dynamic-slice_bitcast_fusion.1
  29.4 1.3 fusion.44
  30.7 3.7 %collective-permute-start.3 = (bf16[512,384]{1,0:T(8,128)(2,1)}, bf16[512,384]{1,0:T(8,128)(2,1)S(1)}, u32[]{:S(2)}, u32[]{:S(2)}) collective-permute-start(bf16[512,384]{1,0:T(8,128)(2,1)} %collective-permute-done.2), channel_id=1, source_target_pairs={{0,7},{1,0},{2,1},{3,2},{4,3},{5,4},{6,5},{7,6},{8,15},{9,8},{10,9... | collective-permute-start | bytes 1179656 | tf_op jit(solution)/shard_map/ppermute | solution.py:77
  34.4 0.3 fusion.43
  34.7 4.4 %collective-permute-done.6 = bf16[512,384]{1,0:T(8,128)(2,1)S(1)} collective-permute-done((bf16[512,384]{1,0:T(8,128)(2,1)S(1)}, bf16[512,384]{1,0:T(8,128)(2,1)S(1)}, u32[]{:S(2)}, u32[]{:S(2)}) %collective-permute-start.6) | collective-permute-done | bytes 393248 | tf_op jit(solution)/shard_map/ppermute | solution.py:73
  39.1 1.4 fusion.42
  40.5 2.2 %collective-permute-done.3 = bf16[512,384]{1,0:T(8,128)(2,1)S(1)} collective-permute-done((bf16[512,384]{1,0:T(8,128)(2,1)}, bf16[512,384]{1,0:T(8,128)(2,1)S(1)}, u32[]{:S(2)}, u32[]{:S(2)}) %collective-permute-start.3) | collective-permute-done | bytes 393248 | tf_op jit(solution)/shard_map/ppermute | solution.py:77
  42.8 0.3 fusion.41
  43.1 5.8 %collective-permute-done.7 = bf16[512,384]{1,0:T(8,128)(2,1)S(1)} collective-permute-done((bf16[512,384]{1,0:T(8,128)(2,1)S(1)}, bf16[512,384]{1,0:T(8,128)(2,1)S(1)}, u32[]{:S(2)}, u32[]{:S(2)}) %collective-permute-start.7) | collective-permute-done | bytes 393248 | tf_op jit(solution)/shard_map/ppermute | solution.py:73
  48.9 0.3 fusion.40
  49.2 0.3 fusion.39
  49.5 0.3 fusion.38
  49.8 0.3 fusion.37
  50.4 0.8 constant_dynamic-update-slice_fusion.14
  51.2 1.8 %constant_dynamic-update-slice_fusion.13 = bf16[512,6144]{1,0:T(8,128)(2,1)} fusion(bf16[512,6144]{1,0:T(8,128)(2,1)} %constant_dynamic-update-slice_fusion.14, bf16[512,384]{1,0:T(8,128)(2,1)} %collective-permute-done.2), kind=kLoop, calls=%fused_computation.115 | loop fusion | bytes 786432
  53.0 0.8 constant_dynamic-update-slice_fusion.12
  53.8 0.9 constant_dynamic-update-slice_fusion.11
  54.7 0.8 constant_dynamic-update-slice_fusion.10
  55.5 0.8 constant_dynamic-update-slice_fusion.9
  56.3 0.8 constant_dynamic-update-slice_fusion.8
  57.2 0.8 constant_dynamic-update-slice_fusion.7
  58.0 0.8 constant_dynamic-update-slice_fusion.6
  58.8 1.8 %constant_dynamic-update-slice_fusion.5 = bf16[512,6144]{1,0:T(8,128)(2,1)} fusion(bf16[512,6144]{1,0:T(8,128)(2,1)} %constant_dynamic-update-slice_fusion.6, bf16[512,384]{1,0:T(8,128)(2,1)} %collective-permute-done.2), kind=kLoop, calls=%fused_computation.107 | loop fusion | bytes 786432
  60.6 0.9 constant_dynamic-update-slice_fusion.4
  61.5 0.8 constant_dynamic-update-slice_fusion.3
  62.5 1.3 fusion.53
  63.8 2.3 %copy.21 = bf16[3072,128]{1,0:T(8,128)(2,1)} copy(bf16[3072,128]{0,1:T(8,128)(2,1)} %fusion.53) | data formatting | bytes 1572864 | tf_op jit(solution)/shard_map/dynamic_slice | solution.py:88
  66.1 2.1 %copy.22 = bf16[16,3,64,128]{3,2,1,0:T(8,128)(2,1)} copy(bf16[16,3,64,128]{3,2,0,1:T(8,128)(2,1)} %bitcast.202) | data formatting | bytes 1572864 | tf_op jit(solution)/shard_map/transpose | solution.py:114
  68.2 5.3 %all-to-all-start = ((bf16[16,3,64,128]{3,2,1,0:T(8,128)(2,1)}), bf16[16,3,64,128]{3,2,1,0:T(8,128)(2,1)}, u32[]{:S(2)}, u32[]{:S(2)}) async-start(bf16[16,3,64,128]{3,2,1,0:T(8,128)(2,1)} %copy.22), calls=%async_computation | async-start | bytes 1572864 | tf_op jit(solution)/shard_map/all_to_all | solution.py:55
  73.6 0.8 constant_dynamic-update-slice_fusion.2
  74.4 0.8 constant_dynamic-update-slice_fusion.1
  75.2 0.8 constant_dynamic-update-slice_fusion
  76.0 3.8 %constant_dynamic-slice_fusion = bf16[512,3072]{1,0:T(8,128)(2,1)} fusion(bf16[512,6144]{1,0:T(8,128)(2,1)} %constant_dynamic-update-slice_fusion, s32[]{:T(128)S(6)} %select_n.46), kind=kLoop, calls=%fused_computation.121 | loop fusion | bytes 6291460 | tf_op jit(solution)/shard_map/dynamic_slice | solution.py:88
  79.8 4.7 %copy.27 = bf16[512,3072]{0,1:T(8,128)(2,1)} copy(bf16[512,3072]{1,0:T(8,128)(2,1)} %constant_dynamic-slice_fusion) | data formatting | bytes 6291456 | tf_op jit(solution)/shard_map/dynamic_slice | solution.py:88
  84.5 3.9 %copy.28 = bf16[512,16,3,64]{0,3,2,1:T(8,128)(2,1)} copy(bf16[512,16,3,64]{0,3,1,2:T(8,128)(2,1)} %bitcast.200) | data formatting | bytes 6291456 | tf_op jit(solution)/shard_map/transpose | solution.py:116
  88.4 0.4 collective-permute-start.10
  88.7 1.2 fusion.97
  90.3 2.8 %select_reduce_fusion.1 = (f32[2048]{0:T(1024)S(1)}, f32[2048,2048]{0,1:T(8,128)S(1)}) fusion(pred[2048]{0:T(1024)(128)(4,1)S(1)} %iota_compare_fusion, bf16[8,8,16,128]{3,2,1,0:T(8,128)(2,1)S(1)} %bitcast.207, bf16[8,8,16,128]{3,2,1,0:T(8,128)(2,1)S(1)} %bitcast.208), kind=kOutput, calls=%fused_computation.3 | convolution fusion | flops 549451776 | bytes 17311744 | tf_op jit(solution)/shard_map/dq,dk->qk/dot_general | solution.py:25
  93.1 5.1 %fusion = (bf16[2048,2048]{0,1:T(8,128)(2,1)S(1)}, f32[2048]{0:T(1024)S(1)}) fusion(f32[2048,2048]{0,1:T(8,128)S(1)} %get-tuple-element.26, f32[2048]{0:T(1024)S(1)} %get-tuple-element.25, pred[2048]{0:T(1024)(128)(4,1)S(1)} %iota_compare_fusion), kind=kLoop, calls=%fused_computation.4 | loop fusion | flops 20969472 | bytes 25184256 | tf_op jit(solution)/shard_map/convert_element_type | solution.py:32
  98.4 1.6 fusion.52
  100.1 13.2 %all_to_all.40 = bf16[16,64,128]{2,1,0:T(8,128)(2,1)S(1)} all-to-all(bf16[16,64,128]{2,1,0:T(8,128)(2,1)S(1)} %bitcast.210), channel_id=1, replica_groups=mesh['pipe'=2,'ctx'=16,'dp'=8] {'ctx'}, dimensions={0} | all-to-all | bytes 524288 | tf_op jit(solution)/shard_map/all_to_all | solution.py:58
  113.3 0.5 fusion.34
  113.8 1.3 collective-permute-start.9
  115.1 9.9 %collective-permute-done.9 = bf16[128,1024]{1,0:T(8,128)(2,1)S(1)} collective-permute-done((bf16[128,1024]{1,0:T(8,128)(2,1)S(1)}, bf16[128,1024]{1,0:T(8,128)(2,1)S(1)}, u32[]{:S(2)}, u32[]{:S(2)}) %collective-permute-start.9) | collective-permute-done | bytes 262176 | tf_op jit(solution)/shard_map/ppermute | solution.py:126
  125.6 3.0 %fusion.91 = f32[128,3072]{1,0:T(8,128)S(1)} fusion(bf16[512,3072]{0,1:T(8,128)(2,1)} %bitcast.37, bf16[128,1024]{1,0:T(8,128)(2,1)S(1)} %fusion.62, s32[]{:T(128)S(6)} %select_n.45), kind=kOutput, calls=%fused_computation.98 | convolution fusion | flops 402653184 | bytes 4849668 | tf_op jit(solution)/shard_map/dot_general | solution.py:49
  128.7 3.9 %fusion.4 = bf16[128,3072]{1,0:T(8,128)(2,1)} fusion(f32[128,3072]{1,0:T(8,128)S(1)} %fusion.91, bf16[512,3072]{0,1:T(8,128)(2,1)} %collective-permute-done.10, bf16[128,1024]{1,0:T(8,128)(2,1)S(1)} %fusion.62, s32[]{:T(128)S(6)} %select_n.49), kind=kOutput, calls=%fused_computation.9 | convolution fusion | flops 403439616 | bytes 5636100 | tf_op jit(solution)/shard_map/dot_general | solution.py:49
  132.6 1.5 copy.29
  134.1 16.5 %all_to_all.41 = bf16[16,3,64,128]{3,2,1,0:T(8,128)(2,1)S(1)} all-to-all(bf16[16,3,64,128]{3,2,1,0:T(8,128)(2,1)S(1)} %bitcast.203), channel_id=1, replica_groups=mesh['pipe'=2,'ctx'=16,'dp'=8] {'ctx'}, dimensions={0} | all-to-all | bytes 1572864 | tf_op jit(solution)/shard_map/all_to_all | solution.py:55
  151.3 2.8 %select_reduce_fusion = (f32[2048]{0:T(1024)S(1)}, f32[2048,2048]{0,1:T(8,128)S(1)}) fusion(pred[2048]{0:T(1024)(128)(4,1)S(1)} %iota_compare_fusion, bf16[8,8,16,128]{3,2,1,0:T(8,128)(2,1)S(1)} %bitcast.206, bf16[8,8,16,128]{3,2,1,0:T(8,128)(2,1)S(1)} %bitcast.209), kind=kOutput, calls=%fused_computation.1 | convolution fusion | flops 549451776 | bytes 17311744 | tf_op jit(solution)/shard_map/dq,dk->qk/dot_general | solution.py:25
  154.1 5.1 %fusion.2 = (bf16[2048,2048]{0,1:T(8,128)(2,1)S(1)}, f32[2048]{0:T(1024)S(1)}) fusion(f32[2048,2048]{0,1:T(8,128)S(1)} %get-tuple-element.28, f32[2048]{0:T(1024)S(1)} %get-tuple-element.27, pred[2048]{0:T(1024)(128)(4,1)S(1)} %iota_compare_fusion), kind=kLoop, calls=%fused_computation.6 | loop fusion | flops 20969472 | bytes 25184256 | tf_op jit(solution)/shard_map/convert_element_type | solution.py:32
  159.2 1.6 fusion.51
  160.8 0.8 copy.76
  161.5 3.5 %all-to-all-start.3 = ((bf16[16,64,128]{2,1,0:T(8,128)(2,1)}), bf16[16,64,128]{2,1,0:T(8,128)(2,1)S(1)}, u32[]{:S(2)}, u32[]{:S(2)}) async-start(bf16[16,64,128]{2,1,0:T(8,128)(2,1)} %bitcast.196), calls=%async_computation.3 | async-start | bytes 524288 | tf_op jit(solution)/shard_map/all_to_all | solution.py:58
  165.1 8.0 %all-to-all-done.3 = bf16[16,64,128]{2,1,0:T(8,128)(2,1)S(1)} async-done(((bf16[16,64,128]{2,1,0:T(8,128)(2,1)}), bf16[16,64,128]{2,1,0:T(8,128)(2,1)S(1)}, u32[]{:S(2)}, u32[]{:S(2)}) %all-to-all-start.3) | async-done | bytes 262176 | tf_op jit(solution)/shard_map/all_to_all | solution.py:58
  173.1 1.2 fusion.48
  (50 shorter events, 2.3 us)
Async XLA Ops:
  0.0 113.3 %copy-start = (bf16[1,1024,1024]{2,1,0:T(8,128)(2,1)S(1)}, bf16[1,1024,1024]{2,1,0:T(8,128)(2,1)}, u32[]{:S(2)}) copy-start(bf16[1,1024,1024]{2,1,0:T(8,128)(2,1)} %param.13) | copy-start | bytes 6291460
  2.0 16.3 %copy-start.4 = (bf16[512,384]{1,0:T(8,128)(2,1)}, bf16[512,384]{1,0:T(8,128)(2,1)S(1)}, u32[]{:S(2)}) copy-start(bf16[512,384]{1,0:T(8,128)(2,1)S(1)} %get-tuple-element.14) | copy-start | bytes 1179652
  2.0 15.0 %collective-permute-start.4 = (bf16[512,384]{1,0:T(8,128)(2,1)S(1)}, bf16[512,384]{1,0:T(8,128)(2,1)S(1)}, u32[]{:S(2)}, u32[]{:S(2)}) collective-permute-start(bf16[512,384]{1,0:T(8,128)(2,1)S(1)} %get-tuple-element.14), channel_id=1, source_target_pairs={{0,1},{1,2},{2,3},{3,4},{4,5},{5,6},{6,7},{7,0},{8,9},{9,10},{10,1... | collective-permute-start | bytes 1179656 | tf_op jit(solution)/shard_map/ppermute | solution.py:73
  3.9 14.4 %collective-permute-start.1 = (bf16[512,384]{1,0:T(8,128)(2,1)S(1)}, bf16[512,384]{1,0:T(8,128)(2,1)S(1)}, u32[]{:S(2)}, u32[]{:S(2)}) collective-permute-start(bf16[512,384]{1,0:T(8,128)(2,1)S(1)} %get-tuple-element.14), channel_id=1, source_target_pairs={{0,7},{1,0},{2,1},{3,2},{4,3},{5,4},{6,5},{7,6},{8,15},{9,8},{10,9... | collective-permute-start | bytes 1179656 | tf_op jit(solution)/shard_map/ppermute | solution.py:77
  17.0 11.5 %collective-permute-start.5 = (bf16[512,384]{1,0:T(8,128)(2,1)S(1)}, bf16[512,384]{1,0:T(8,128)(2,1)S(1)}, u32[]{:S(2)}, u32[]{:S(2)}) collective-permute-start(bf16[512,384]{1,0:T(8,128)(2,1)S(1)} %collective-permute-done.4), channel_id=1, source_target_pairs={{0,1},{1,2},{2,3},{3,4},{4,5},{5,6},{6,7},{7,0},{8,9},{9,10},{10,1... | collective-permute-start | bytes 1179656 | tf_op jit(solution)/shard_map/ppermute | solution.py:73
  18.2 10.3 %collective-permute-start = (bf16[128,1024]{1,0:T(8,128)(2,1)S(1)}, bf16[128,1024]{1,0:T(8,128)(2,1)}, u32[]{:S(2)}, u32[]{:S(2)}) collective-permute-start(bf16[128,1024]{1,0:T(8,128)(2,1)S(1)} %fusion.66), channel_id=1, source_target_pairs={{0,8},{8,0},{16,24},{24,16},{32,40},{40,32},{48,56},{56,48},{64,72... | collective-permute-start | bytes 786440 | tf_op jit(solution)/shard_map/ppermute | solution.py:101
  18.3 12.4 %collective-permute-start.2 = (bf16[512,384]{1,0:T(8,128)(2,1)S(1)}, bf16[512,384]{1,0:T(8,128)(2,1)}, u32[]{:S(2)}, u32[]{:S(2)}) collective-permute-start(bf16[512,384]{1,0:T(8,128)(2,1)S(1)} %collective-permute-done.1), channel_id=1, source_target_pairs={{0,7},{1,0},{2,1},{3,2},{4,3},{5,4},{6,5},{7,6},{8,15},{9,8},{10,9... | collective-permute-start | bytes 1179656 | tf_op jit(solution)/shard_map/ppermute | solution.py:77
  28.5 10.6 %collective-permute-start.6 = (bf16[512,384]{1,0:T(8,128)(2,1)S(1)}, bf16[512,384]{1,0:T(8,128)(2,1)S(1)}, u32[]{:S(2)}, u32[]{:S(2)}) collective-permute-start(bf16[512,384]{1,0:T(8,128)(2,1)S(1)} %collective-permute-done.5), channel_id=1, source_target_pairs={{0,1},{1,2},{2,3},{3,4},{4,5},{5,6},{6,7},{7,0},{8,9},{9,10},{10,1... | collective-permute-start | bytes 1179656 | tf_op jit(solution)/shard_map/ppermute | solution.py:73
  30.7 12.1 %collective-permute-start.3 = (bf16[512,384]{1,0:T(8,128)(2,1)}, bf16[512,384]{1,0:T(8,128)(2,1)S(1)}, u32[]{:S(2)}, u32[]{:S(2)}) collective-permute-start(bf16[512,384]{1,0:T(8,128)(2,1)} %collective-permute-done.2), channel_id=1, source_target_pairs={{0,7},{1,0},{2,1},{3,2},{4,3},{5,4},{6,5},{7,6},{8,15},{9,8},{10,9... | collective-permute-start | bytes 1179656 | tf_op jit(solution)/shard_map/ppermute | solution.py:77
  39.1 15.6 %copy-start.2 = (bf16[512,384]{1,0:T(8,128)(2,1)}, bf16[512,384]{1,0:T(8,128)(2,1)S(1)}, u32[]{:S(2)}) copy-start(bf16[512,384]{1,0:T(8,128)(2,1)S(1)} %collective-permute-done.6) | copy-start | bytes 1179652
  39.1 9.8 %collective-permute-start.7 = (bf16[512,384]{1,0:T(8,128)(2,1)S(1)}, bf16[512,384]{1,0:T(8,128)(2,1)S(1)}, u32[]{:S(2)}, u32[]{:S(2)}) collective-permute-start(bf16[512,384]{1,0:T(8,128)(2,1)S(1)} %collective-permute-done.6), channel_id=1, source_target_pairs={{0,1},{1,2},{2,3},{3,4},{4,5},{5,6},{6,7},{7,0},{8,9},{9,10},{10,1... | collective-permute-start | bytes 1179656 | tf_op jit(solution)/shard_map/ppermute | solution.py:73
  43.1 14.1 %copy-start.5 = (bf16[512,384]{1,0:T(8,128)(2,1)S(1)}, bf16[512,384]{1,0:T(8,128)(2,1)}, u32[]{:S(2)}) copy-start(bf16[512,384]{1,0:T(8,128)(2,1)} %copy-done.4) | copy-start | bytes 1179652
  50.2 12.1 %collective-permute-start.8 = (f32[3072,128]{0,1:T(8,128)S(1)}, f32[3072,128]{0,1:T(8,128)S(1)}, u32[]{:S(2)}, u32[]{:S(2)}) collective-permute-start(f32[3072,128]{0,1:T(8,128)S(1)} %slice_bitcast_fusion), channel_id=1, source_target_pairs={{0,8},{8,0},{16,24},{24,16},{32,40},{40,32},{48,56},{56,48},{64,72... | collective-permute-start | bytes 4718600 | tf_op jit(solution)/shard_map/ppermute | solution.py:112
  58.8 14.7 %copy-start.3 = (bf16[512,384]{1,0:T(8,128)(2,1)S(1)}, bf16[512,384]{1,0:T(8,128)(2,1)}, u32[]{:S(2)}) copy-start(bf16[512,384]{1,0:T(8,128)(2,1)} %copy-done.2) | copy-start | bytes 1179652
  68.2 20.6 %all-to-all-start = ((bf16[16,3,64,128]{3,2,1,0:T(8,128)(2,1)}), bf16[16,3,64,128]{3,2,1,0:T(8,128)(2,1)}, u32[]{:S(2)}, u32[]{:S(2)}) async-start(bf16[16,3,64,128]{3,2,1,0:T(8,128)(2,1)} %copy.22), calls=%async_computation | async-start | bytes 1572864 | tf_op jit(solution)/shard_map/all_to_all | solution.py:55
  88.4 40.3 %collective-permute-start.10 = (bf16[512,3072]{0,1:T(8,128)(2,1)}, bf16[512,3072]{0,1:T(8,128)(2,1)}, u32[]{:S(2)}, u32[]{:S(2)}) collective-permute-start(bf16[512,3072]{0,1:T(8,128)(2,1)} %bitcast.37), channel_id=1, source_target_pairs={{0,8},{8,0},{16,24},{24,16},{32,40},{40,32},{48,56},{56,48},{64,72... | collective-permute-start | bytes 9437192 | tf_op jit(solution)/shard_map/ppermute | solution.py:117
  98.4 15.0 %copy-start.1 = (bf16[1,1,128,1024]{3,2,1,0:T(8,128)(2,1)S(1)}, bf16[1,1,128,1024]{3,2,1,0:T(8,128)(2,1)}, u32[]{:S(2)}) copy-start(bf16[1,1,128,1024]{3,2,1,0:T(8,128)(2,1)} %param.8) | copy-start | bytes 786436
  98.4 14.9 %copy-start.8 = (f32[1,1024]{1,0:T(1,128)S(1)}, f32[1,1024]{1,0:T(1,128)}, u32[]{:S(2)}) copy-start(f32[1,1024]{1,0:T(1,128)} %param.14) | copy-start | bytes 12292
  98.4 14.9 %copy-start.9 = (f32[1,1024]{1,0:T(1,128)S(1)}, f32[1,1024]{1,0:T(1,128)}, u32[]{:S(2)}) copy-start(f32[1,1024]{1,0:T(1,128)} %param.15) | copy-start | bytes 12292
  98.4 27.0 %copy-start.6 = (f32[1,1024]{1,0:T(1,128)S(1)}, f32[1,1024]{1,0:T(1,128)}, u32[]{:S(2)}) copy-start(f32[1,1024]{1,0:T(1,128)} %param.11) | copy-start | bytes 12292
  98.4 27.0 %copy-start.7 = (f32[1,1024]{1,0:T(1,128)S(1)}, f32[1,1024]{1,0:T(1,128)}, u32[]{:S(2)}) copy-start(f32[1,1024]{1,0:T(1,128)} %param.10) | copy-start | bytes 12292
  113.8 11.2 %collective-permute-start.9 = (bf16[128,1024]{1,0:T(8,128)(2,1)S(1)}, bf16[128,1024]{1,0:T(8,128)(2,1)S(1)}, u32[]{:S(2)}, u32[]{:S(2)}) collective-permute-start(bf16[128,1024]{1,0:T(8,128)(2,1)S(1)} %fusion.34), channel_id=1, source_target_pairs={{0,128},{1,129},{2,130},{3,131},{4,132},{5,133},{6,134},{7,135},{8... | collective-permute-start | bytes 786440 | tf_op jit(solution)/shard_map/ppermute | solution.py:126
  161.5 11.5 %all-to-all-start.3 = ((bf16[16,64,128]{2,1,0:T(8,128)(2,1)}), bf16[16,64,128]{2,1,0:T(8,128)(2,1)S(1)}, u32[]{:S(2)}, u32[]{:S(2)}) async-start(bf16[16,64,128]{2,1,0:T(8,128)(2,1)} %bitcast.196), calls=%async_computation.3 | async-start | bytes 524288 | tf_op jit(solution)/shard_map/all_to_all | solution.py:58

commit v12 on v10

--- a/solution.py
+++ b/solution.py
@@ -78,6 +78,8 @@
             backward = lax.ppermute(backward, axis, left)
             k = 1 + step
             blocks[k], made[k] = backward, on_block(backward)
+    if made_axis is None:
+        return jnp.concatenate(blocks, axis=1), made
     return jnp.concatenate(blocks, axis=1), jnp.concatenate(made, axis=made_axis)
 
 
@@ -103,16 +105,24 @@
     mine_rows = lax.dynamic_slice_in_dim(normed, core * half, half, axis=1)
     sibling_rows = lax.dynamic_slice_in_dim(normed_sibling, core * half, half, axis=1)
 
-    both = jnp.stack([mine_rows, sibling_rows])
+    tok_rows = current.shape[0]
+    head_width = width // HEADS
+    dp_count = lax.axis_size("dp")
+    shard_segments = 3 * HEADS // dp_count
 
     def on_block(block):
-        return jnp.einsum("kc,stk->sct", block, both, preferred_element_type=jnp.float32)
+        own = jnp.dot(mine_rows, block, preferred_element_type=jnp.float32)
+        theirs = jnp.dot(sibling_rows, block, preferred_element_type=jnp.float32)
+        summed = (own + lax.ppermute(theirs, "ctx", sibling)).astype(jnp.bfloat16)
+        return (jnp.transpose(summed.reshape(tok_rows, shard_segments, head_width), (1, 2, 0)),)
 
-    qkv_mine, partial = ring_gather(rows_mine, "dp", on_block, made_axis=1)
-    tok_rows = current.shape[0]
-    partial_other = lax.ppermute(partial[1], "ctx", sibling)
-    first = unrotate((partial[0] + partial_other).astype(jnp.bfloat16), "dp", along=0)
-    first = jnp.transpose(first.reshape(3, HEADS, width // HEADS, tok_rows), (1, 0, 2, 3))
+    qkv_mine, made = ring_gather(rows_mine, "dp", on_block, made_axis=None)
+    dp_index = lax.axis_index("dp")
+    flat = jnp.zeros((3 * HEADS, head_width, tok_rows), jnp.bfloat16)
+    for k, (segments,) in enumerate(made):
+        owner = (dp_index + k) % dp_count
+        flat = lax.dynamic_update_slice_in_dim(flat, segments, owner * shard_segments, axis=0)
+    first = jnp.transpose(flat.reshape(3, HEADS, head_width, tok_rows), (1, 0, 2, 3))
     qkv_other = lax.ppermute(qkv_mine, "ctx", sibling)
     args = (qkv_mine, qkv_other, w_out[0], norm_gain[0], norm_bias[0], out_bias[0], scale_gain[0])
     length = lengths[0, 0]

time: 163 us -> 178 us (1.092)
  waiting for transfers between devices: 53.3 us -> 30.5 us
  matrix products: 16.9 us -> 36 us
  local copies, waits for them, and re-layouts: 22.7 us -> 38.2 us
  starting transfers between devices: 23.4 us -> 27.5 us
    dot_general x8 -> x16, matrix products: 3.46 us -> 22.5 us  [the longest x8 13.6 us: on_block(): own = jnp.dot(mine_rows, block, preferred_element_type=jnp.float32)]
    ppermute x4, waiting for transfers between devices: 23.8 us -> 7.82 us  [ring_gather(): forward = lax.ppermute(forward, axis, right)]
    convert_element_type x0 -> x8, local copies, waits for them, and re-layouts: none -> 8.82 us  [on_block(): summed = (own + lax.ppermute(theirs, 'ctx', sibling)).astype(jnp.bfloat16)]
    dynamic_update_slice x0 -> x8, local copies, waits for them, and re-layouts: none -> 8.79 us  [per_device(): lax.dynamic_update_slice_in_dim(flat, segments, owner * shard_segments, a...]
    ppermute x4, starting transfers between devices: 0.01 us -> 5.28 us  [ring_gather(): forward = lax.ppermute(forward, axis, right)]
    ppermute x3, waiting for transfers between devices: 5.27 us -> 1.2 us  [ring_gather(): backward = lax.ppermute(backward, axis, left)]
    ppermute x3, starting transfers between devices: 12.9 us -> 9.31 us  [ring_gather(): backward = lax.ppermute(backward, axis, left)]
    ppermute x1 -> x8, waiting for transfers between devices: 3.08 us -> 0.02 us  [on_block(): summed = (own + lax.ppermute(theirs, 'ctx', sibling)).astype(jnp.bfloat16)]
  transfers between devices with their start and end apart: 13 -> 20, of which waited for: 10 -> 6; matrix products, arithmetic and copies ran while one was open for 17% -> 35% of each run, Pallas kernels for 0% -> 0%
where the time goes in v12:
time: 178 us; the launch traced here: 177 us
  local copies, waits for them, and re-layouts  38.2 us (21%)
  matrix products  36 us (20%)
  waiting for transfers between devices  30.5 us (17%)
  starting transfers between devices  27.5 us (15%)
  blocking collectives  27.2 us (15%)
  other arithmetic  16.3 us (9%)
    all_to_all x1, blocking collectives, sublayer(): gathered = lax.all_to_all(projected, 'ctx', 0, 3, tiled=True)  16.5 us
    dot_general x8, matrix products, on_block(): own = jnp.dot(mine_rows, block, preferred_element_type=jnp.float32)  13.6 us
    unnamed x29, local copies, waits for them, and re-layouts  11.2 us
    all_to_all x1, blocking collectives, sublayer(): lax.all_to_all(context, 'ctx', 0, 0, tiled=True).reshape(width, tok_rows)  10.6 us
    convert_element_type x2, other arithmetic, head_attention(): weights.astype(jnp.bfloat16)  10.2 us
    ppermute x1, waiting for transfers between devices, per_device(): current = lax.ppermute(produced, 'pipe', pairs)  9.84 us
    ppermute x3, starting transfers between devices, ring_gather(): backward = lax.ppermute(backward, axis, left)  9.31 us
    dot_general x8, matrix products, on_block(): theirs = jnp.dot(sibling_rows, block, preferred_element_type=jnp.float32)  8.86 us
  transfers between devices with their start and end apart: 20, of which 6 were waited for; matrix products, arithmetic and copies ran while one was open for 35% of the time, Pallas kernels for 0%

profile of v12, /device:TPU:4, one launch (start us, length us, event | category | flops | bytes accessed | tf_op | source)
XLA Modules:
  0.0 176.8 jit_solution(13194150839443622347)
XLA Ops:
  0.0 2.1 %constant_dynamic-update-slice_fusion.7 = (bf16[512,3072]{1,0:T(8,128)(2,1)}, bf16[512,384]{1,0:T(8,128)(2,1)}) fusion(bf16[1,1024,384]{2,1,0:T(8,128)(2,1)} %param.12, s32[]{:T(128)S(6)} %select_n.100), kind=kLoop, calls=%fused_computation.117 | loop fusion | bytes 1179652
  2.1 1.9 %collective-permute-start.8 = (bf16[512,384]{1,0:T(8,128)(2,1)}, bf16[512,384]{1,0:T(8,128)(2,1)S(1)}, u32[]{:S(2)}, u32[]{:S(2)}) collective-permute-start(bf16[512,384]{1,0:T(8,128)(2,1)} %get-tuple-element.14), channel_id=1, source_target_pairs={{0,1},{1,2},{2,3},{3,4},{4,5},{5,6},{6,7},{7,0},{8,9},{9,10},{10,1... | collective-permute-start | bytes 1179656 | tf_op jit(solution)/shard_map/ppermute | solution.py:74
  4.0 3.9 %collective-permute-start.2 = (bf16[512,384]{1,0:T(8,128)(2,1)}, bf16[512,384]{1,0:T(8,128)(2,1)S(1)}, u32[]{:S(2)}, u32[]{:S(2)}) collective-permute-start(bf16[512,384]{1,0:T(8,128)(2,1)} %get-tuple-element.14), channel_id=1, source_target_pairs={{0,7},{1,0},{2,1},{3,2},{4,3},{5,4},{6,5},{7,6},{8,15},{9,8},{10,9... | collective-permute-start | bytes 1179656 | tf_op jit(solution)/shard_map/ppermute | solution.py:78
  8.0 1.1 convert_reduce_fusion.1
  9.1 1.2 fusion.60
  10.2 1.2 fusion.63
  11.6 1.9 %fusion.104 = f32[128,384]{1,0:T(8,128)} fusion(bf16[512,384]{1,0:T(8,128)(2,1)} %get-tuple-element.14, bf16[128,1024]{1,0:T(8,128)(2,1)S(1)} %fusion.63, s32[]{:T(128)S(6)} %select_n.100), kind=kOutput, calls=%fused_computation.108 | convolution fusion | flops 50331648 | bytes 720900 | tf_op jit(solution)/shard_map/dot_general | solution.py:114
  14.2 1.2 fusion.95
  16.7 0.9 fusion.93
  17.6 0.9 fusion.81
  19.3 3.3 %collective-permute-start.4 = (bf16[512,384]{1,0:T(8,128)(2,1)S(1)}, bf16[512,384]{1,0:T(8,128)(2,1)}, u32[]{:S(2)}, u32[]{:S(2)}) collective-permute-start(bf16[512,384]{1,0:T(8,128)(2,1)S(1)} %collective-permute-done.2), channel_id=1, source_target_pairs={{0,7},{1,0},{2,1},{3,2},{4,3},{5,4},{6,5},{7,6},{8,15},{9,8},{10,9... | collective-permute-start | bytes 1179656 | tf_op jit(solution)/shard_map/ppermute | solution.py:78
  22.6 1.6 add_convert_fusion
  24.2 1.0 copy.40
  25.2 1.1 broadcast_in_dim.44
  27.0 1.1 fusion.43
  28.1 1.8 %fusion.49 = bf16[128,384]{1,0:T(8,128)(2,1)} fusion(f32[128,384]{1,0:T(8,128)} %collective-permute-done.15, bf16[512,384]{1,0:T(8,128)(2,1)S(1)} %collective-permute-done.8, bf16[128,1024]{1,0:T(8,128)(2,1)S(1)} %fusion.63, s32[]{:T(128)S(6)} %select_n.100), kind=kOutput, calls=%fused_computation.45 | convolution fusion | flops 50429952 | bytes 819204 | tf_op jit(solution)/shard_map/dot_general | solution.py:114
  30.7 1.0 copy.47
  31.7 1.5 constant_dynamic-update-slice_fusion.14
  33.3 1.2 fusion.91
  34.6 1.2 fusion.83
  36.4 1.2 collective-permute-start.10
  37.6 2.1 %collective-permute-start.6 = (bf16[512,384]{1,0:T(8,128)(2,1)}, bf16[512,384]{1,0:T(8,128)(2,1)}, u32[]{:S(2)}, u32[]{:S(2)}) collective-permute-start(bf16[512,384]{1,0:T(8,128)(2,1)} %collective-permute-done.4), channel_id=1, source_target_pairs={{0,7},{1,0},{2,1},{3,2},{4,3},{5,4},{6,5},{7,6},{8,15},{9,8},{10,9... | collective-permute-start | bytes 1179656 | tf_op jit(solution)/shard_map/ppermute | solution.py:78
  39.6 1.9 %fusion.44 = bf16[128,384]{1,0:T(8,128)(2,1)} fusion(f32[128,384]{1,0:T(8,128)S(1)} %collective-permute-done.5, bf16[512,384]{1,0:T(8,128)(2,1)} %collective-permute-done.4, bf16[128,1024]{1,0:T(8,128)(2,1)S(1)} %fusion.63, s32[]{:T(128)S(6)} %select_n.100), kind=kOutput, calls=%fused_computation.40 | convolution fusion | flops 50429952 | bytes 819204 | tf_op jit(solution)/shard_map/dot_general | solution.py:114
  41.5 1.9 %fusion.48 = bf16[128,384]{1,0:T(8,128)(2,1)} fusion(f32[128,384]{1,0:T(8,128)S(1)} %collective-permute-done.14, bf16[512,384]{1,0:T(8,128)(2,1)} %collective-permute-done.9, bf16[128,1024]{1,0:T(8,128)(2,1)S(1)} %fusion.63, s32[]{:T(128)S(6)} %select_n.100), kind=kOutput, calls=%fused_computation.44 | convolution fusion | flops 50429952 | bytes 819204 | tf_op jit(solution)/shard_map/dot_general | solution.py:114
  43.4 1.6 copy.42
  45.1 1.6 copy.46
  46.7 1.5 constant_dynamic-update-slice_fusion.13
  48.7 1.2 fusion.89
  50.0 1.9 %collective-permute-start.11 = (bf16[512,384]{1,0:T(8,128)(2,1)}, bf16[512,384]{1,0:T(8,128)(2,1)S(1)}, u32[]{:S(2)}, u32[]{:S(2)}) collective-permute-start(bf16[512,384]{1,0:T(8,128)(2,1)} %collective-permute-done.10), channel_id=1, source_target_pairs={{0,1},{1,2},{2,3},{3,4},{4,5},{5,6},{6,7},{7,0},{8,9},{9,10},{10,1... | collective-permute-start | bytes 1179656 | tf_op jit(solution)/shard_map/ppermute | solution.py:74
  51.9 1.2 fusion.85
  53.6 1.9 %fusion.45 = bf16[128,384]{1,0:T(8,128)(2,1)} fusion(f32[128,384]{1,0:T(8,128)S(1)} %collective-permute-done.7, bf16[512,384]{1,0:T(8,128)(2,1)} %collective-permute-done.6, bf16[128,1024]{1,0:T(8,128)(2,1)S(1)} %fusion.63, s32[]{:T(128)S(6)} %select_n.100), kind=kOutput, calls=%fused_computation.41 | convolution fusion | flops 50429952 | bytes 819204 | tf_op jit(solution)/shard_map/dot_general | solution.py:114
  55.5 7.8 %collective-permute-done.11 = bf16[512,384]{1,0:T(8,128)(2,1)S(1)} collective-permute-done((bf16[512,384]{1,0:T(8,128)(2,1)}, bf16[512,384]{1,0:T(8,128)(2,1)S(1)}, u32[]{:S(2)}, u32[]{:S(2)}) %collective-permute-start.11) | collective-permute-done | bytes 393248 | tf_op jit(solution)/shard_map/ppermute | solution.py:74
  63.3 0.9 fusion.87
  64.2 1.9 %fusion.47 = bf16[128,384]{1,0:T(8,128)(2,1)} fusion(f32[128,384]{1,0:T(8,128)S(1)} %collective-permute-done.13, bf16[512,384]{1,0:T(8,128)(2,1)} %collective-permute-done.10, bf16[128,1024]{1,0:T(8,128)(2,1)S(1)} %fusion.63, s32[]{:T(128)S(6)} %select_n.100), kind=kOutput, calls=%fused_computation.43 | convolution fusion | flops 50429952 | bytes 819204 | tf_op jit(solution)/shard_map/dot_general | solution.py:114
  66.1 1.0 copy.43
  67.1 1.0 copy.45
  68.8 1.3 fusion.46
  70.8 1.6 constant_dynamic-update-slice_fusion.11
  73.0 1.6 constant_dynamic-update-slice_fusion.9
  75.2 2.1 %copy.48 = bf16[16,3,64,128]{3,2,1,0:T(8,128)(2,1)} copy(bf16[16,3,64,128]{3,2,0,1:T(8,128)(2,1)} %bitcast.22) | data formatting | bytes 1572864 | tf_op jit(solution)/shard_map/transpose | solution.py:125
  77.3 5.4 %all-to-all-start = ((bf16[16,3,64,128]{3,2,1,0:T(8,128)(2,1)}), bf16[16,3,64,128]{3,2,1,0:T(8,128)(2,1)}, u32[]{:S(2)}, u32[]{:S(2)}) async-start(bf16[16,3,64,128]{3,2,1,0:T(8,128)(2,1)} %copy.48), calls=%async_computation | async-start | bytes 1572864 | tf_op jit(solution)/shard_map/all_to_all | solution.py:56
  82.7 0.9 constant_dynamic-update-slice_fusion.6
  83.5 1.9 %constant_dynamic-update-slice_fusion.5 = bf16[512,3072]{1,0:T(8,128)(2,1)} fusion(bf16[512,3072]{1,0:T(8,128)(2,1)} %constant_dynamic-update-slice_fusion.6, bf16[512,384]{1,0:T(8,128)(2,1)} %collective-permute-done.4), kind=kLoop, calls=%fused_computation.115 | loop fusion | bytes 786432
  85.4 1.8 %constant_dynamic-update-slice_fusion.4 = bf16[512,3072]{1,0:T(8,128)(2,1)} fusion(bf16[512,3072]{1,0:T(8,128)(2,1)} %constant_dynamic-update-slice_fusion.5, bf16[512,384]{1,0:T(8,128)(2,1)} %collective-permute-done.6), kind=kLoop, calls=%fused_computation.114 | loop fusion | bytes 786432
  88.0 1.8 %constant_dynamic-update-slice_fusion.2 = bf16[512,3072]{1,0:T(8,128)(2,1)} fusion(bf16[512,3072]{1,0:T(8,128)(2,1)} %constant_dynamic-update-slice_fusion.3, bf16[512,384]{1,0:T(8,128)(2,1)} %collective-permute-done.10), kind=kLoop, calls=%fused_computation.112 | loop fusion | bytes 786432
  89.8 1.8 %constant_dynamic-update-slice_fusion.1 = bf16[512,3072]{1,0:T(8,128)(2,1)} fusion(bf16[512,3072]{1,0:T(8,128)(2,1)} %constant_dynamic-update-slice_fusion.2, bf16[512,384]{1,0:T(8,128)(2,1)} %collective-permute-done.9), kind=kLoop, calls=%fused_computation.111 | loop fusion | bytes 786432
  92.8 3.6 %all-to-all-done = bf16[16,3,64,128]{3,2,1,0:T(8,128)(2,1)} async-done(((bf16[16,3,64,128]{3,2,1,0:T(8,128)(2,1)}), bf16[16,3,64,128]{3,2,1,0:T(8,128)(2,1)}, u32[]{:S(2)}, u32[]{:S(2)}) %all-to-all-start) | async-done | bytes 786464 | tf_op jit(solution)/shard_map/all_to_all | solution.py:56
  96.4 1.2 fusion.125
  98.0 2.8 %select_reduce_fusion.1 = (f32[2048]{0:T(1024)S(1)}, f32[2048,2048]{0,1:T(8,128)S(1)}) fusion(pred[2048]{0:T(1024)(128)(4,1)S(1)} %iota_compare_fusion, bf16[8,8,16,128]{3,2,1,0:T(8,128)(2,1)S(1)} %bitcast.174, bf16[8,8,16,128]{3,2,1,0:T(8,128)(2,1)S(1)} %bitcast.172), kind=kOutput, calls=%fused_computation.3 | convolution fusion | flops 549451776 | bytes 17311744 | tf_op jit(solution)/shard_map/dq,dk->qk/dot_general | solution.py:25
  100.7 5.1 %fusion = (bf16[2048,2048]{0,1:T(8,128)(2,1)S(1)}, f32[2048]{0:T(1024)S(1)}) fusion(f32[2048,2048]{0,1:T(8,128)S(1)} %get-tuple-element.26, f32[2048]{0:T(1024)S(1)} %get-tuple-element.25, pred[2048]{0:T(1024)(128)(4,1)S(1)} %iota_compare_fusion), kind=kLoop, calls=%fused_computation.4 | loop fusion | flops 20969472 | bytes 25184256 | tf_op jit(solution)/shard_map/convert_element_type | solution.py:32
  106.1 1.6 fusion.42
  107.8 10.6 %all_to_all.40 = bf16[16,64,128]{2,1,0:T(8,128)(2,1)S(1)} all-to-all(bf16[16,64,128]{2,1,0:T(8,128)(2,1)S(1)} %bitcast.176), channel_id=1, replica_groups=mesh['pipe'=2,'ctx'=16,'dp'=8] {'ctx'}, dimensions={0} | all-to-all | bytes 524288 | tf_op jit(solution)/shard_map/all_to_all | solution.py:59
  118.9 1.3 collective-permute-start.16
  120.2 9.8 %collective-permute-done.16 = bf16[128,1024]{1,0:T(8,128)(2,1)S(1)} collective-permute-done((bf16[128,1024]{1,0:T(8,128)(2,1)S(1)}, bf16[128,1024]{1,0:T(8,128)(2,1)S(1)}, u32[]{:S(2)}, u32[]{:S(2)}) %collective-permute-start.16) | collective-permute-done | bytes 262176 | tf_op jit(solution)/shard_map/ppermute | solution.py:135
  130.7 2.5 %fusion.78 = f32[128,3072]{1,0:T(8,128)S(1)} fusion(bf16[512,3072]{1,0:T(8,128)(2,1)} %collective-permute-done.17, bf16[128,1024]{1,0:T(8,128)(2,1)S(1)} %fusion.59, s32[]{:T(128)S(6)} %select_n.119), kind=kOutput, calls=%fused_computation.82 | convolution fusion | flops 402653184 | bytes 4849668 | tf_op jit(solution)/shard_map/dot_general | solution.py:49
  134.2 1.2 copy.53
  135.4 1.2 copy.54
  136.6 16.5 %all_to_all.41 = bf16[16,3,64,128]{3,2,1,0:T(8,128)(2,1)S(1)} all-to-all(bf16[16,3,64,128]{3,2,1,0:T(8,128)(2,1)S(1)} %copy.54), channel_id=1, replica_groups=mesh['pipe'=2,'ctx'=16,'dp'=8] {'ctx'}, dimensions={0} | all-to-all | bytes 1572864 | tf_op jit(solution)/shard_map/all_to_all | solution.py:56
  153.6 2.8 %select_reduce_fusion = (f32[2048]{0:T(1024)S(1)}, f32[2048,2048]{0,1:T(8,128)S(1)}) fusion(pred[2048]{0:T(1024)(128)(4,1)S(1)} %iota_compare_fusion, bf16[8,8,16,128]{3,2,1,0:T(8,128)(2,1)S(1)} %bitcast.175, bf16[8,8,16,128]{3,2,1,0:T(8,128)(2,1)S(1)} %bitcast.173), kind=kOutput, calls=%fused_computation.1 | convolution fusion | flops 549451776 | bytes 17311744 | tf_op jit(solution)/shard_map/dq,dk->qk/dot_general | solution.py:25
  156.3 5.1 %fusion.2 = (bf16[2048,2048]{0,1:T(8,128)(2,1)S(1)}, f32[2048]{0:T(1024)S(1)}) fusion(f32[2048,2048]{0,1:T(8,128)S(1)} %get-tuple-element.28, f32[2048]{0:T(1024)S(1)} %get-tuple-element.27, pred[2048]{0:T(1024)(128)(4,1)S(1)} %iota_compare_fusion), kind=kLoop, calls=%fused_computation.6 | loop fusion | flops 20969472 | bytes 25184256 | tf_op jit(solution)/shard_map/convert_element_type | solution.py:32
  161.7 1.6 fusion.41
  164.0 3.5 %all-to-all-start.3 = ((bf16[16,64,128]{2,1,0:T(8,128)(2,1)}), bf16[16,64,128]{2,1,0:T(8,128)(2,1)S(1)}, u32[]{:S(2)}, u32[]{:S(2)}) async-start(bf16[16,64,128]{2,1,0:T(8,128)(2,1)} %bitcast.164), calls=%async_computation.3 | async-start | bytes 524288 | tf_op jit(solution)/shard_map/all_to_all | solution.py:59
  167.5 8.0 %all-to-all-done.3 = bf16[16,64,128]{2,1,0:T(8,128)(2,1)S(1)} async-done(((bf16[16,64,128]{2,1,0:T(8,128)(2,1)}), bf16[16,64,128]{2,1,0:T(8,128)(2,1)S(1)}, u32[]{:S(2)}, u32[]{:S(2)}) %all-to-all-start.3) | async-done | bytes 262176 | tf_op jit(solution)/shard_map/all_to_all | solution.py:59
  175.5 1.2 fusion.38
  (77 shorter events, 14.1 us)
Async XLA Ops:
  0.0 118.4 %copy-start = (bf16[1,1024,1024]{2,1,0:T(8,128)(2,1)S(1)}, bf16[1,1024,1024]{2,1,0:T(8,128)(2,1)}, u32[]{:S(2)}) copy-start(bf16[1,1024,1024]{2,1,0:T(8,128)(2,1)} %param.13) | copy-start | bytes 6291460
  2.1 15.5 %collective-permute-start.8 = (bf16[512,384]{1,0:T(8,128)(2,1)}, bf16[512,384]{1,0:T(8,128)(2,1)S(1)}, u32[]{:S(2)}, u32[]{:S(2)}) collective-permute-start(bf16[512,384]{1,0:T(8,128)(2,1)} %get-tuple-element.14), channel_id=1, source_target_pairs={{0,1},{1,2},{2,3},{3,4},{4,5},{5,6},{6,7},{7,0},{8,9},{9,10},{10,1... | collective-permute-start | bytes 1179656 | tf_op jit(solution)/shard_map/ppermute | solution.py:74
  4.0 12.6 %collective-permute-start.2 = (bf16[512,384]{1,0:T(8,128)(2,1)}, bf16[512,384]{1,0:T(8,128)(2,1)S(1)}, u32[]{:S(2)}, u32[]{:S(2)}) collective-permute-start(bf16[512,384]{1,0:T(8,128)(2,1)} %get-tuple-element.14), channel_id=1, source_target_pairs={{0,7},{1,0},{2,1},{3,2},{4,3},{5,4},{6,5},{7,6},{8,15},{9,8},{10,9... | collective-permute-start | bytes 1179656 | tf_op jit(solution)/shard_map/ppermute | solution.py:78
  11.5 2.7 %collective-permute-start = (bf16[128,1024]{1,0:T(8,128)(2,1)S(1)}, bf16[128,1024]{1,0:T(8,128)(2,1)S(1)}, u32[]{:S(2)}, u32[]{:S(2)}) collective-permute-start(bf16[128,1024]{1,0:T(8,128)(2,1)S(1)} %fusion.63), channel_id=1, source_target_pairs={{0,8},{8,0},{16,24},{24,16},{32,40},{40,32},{48,56},{56,48},{64,72... | collective-permute-start | bytes 786440 | tf_op jit(solution)/shard_map/ppermute | solution.py:104
  15.4 7.2 %collective-permute-start.1 = (f32[128,384]{1,0:T(8,128)S(1)}, f32[128,384]{1,0:T(8,128)S(1)}, u32[]{:S(2)}, u32[]{:S(2)}) collective-permute-start(f32[128,384]{1,0:T(8,128)S(1)} %fusion.95), channel_id=1, source_target_pairs={{0,8},{8,0},{16,24},{24,16},{32,40},{40,32},{48,56},{56,48},{64,72... | collective-permute-start | bytes 589832 | tf_op jit(solution)/shard_map/ppermute | solution.py:116
  17.6 9.4 %collective-permute-start.3 = (f32[128,384]{1,0:T(8,128)}, f32[128,384]{1,0:T(8,128)}, u32[]{:S(2)}, u32[]{:S(2)}) collective-permute-start(f32[128,384]{1,0:T(8,128)} %fusion.93), channel_id=1, source_target_pairs={{0,8},{8,0},{16,24},{24,16},{32,40},{40,32},{48,56},{56,48},{64,72... | collective-permute-start | bytes 589832 | tf_op jit(solution)/shard_map/ppermute | solution.py:116
  18.5 9.6 %collective-permute-start.15 = (f32[128,384]{1,0:T(8,128)}, f32[128,384]{1,0:T(8,128)}, u32[]{:S(2)}, u32[]{:S(2)}) collective-permute-start(f32[128,384]{1,0:T(8,128)} %fusion.81), channel_id=1, source_target_pairs={{0,8},{8,0},{16,24},{24,16},{32,40},{40,32},{48,56},{56,48},{64,72... | collective-permute-start | bytes 589832 | tf_op jit(solution)/shard_map/ppermute | solution.py:116
  19.0 15.6 %collective-permute-start.9 = (bf16[512,384]{1,0:T(8,128)(2,1)S(1)}, bf16[512,384]{1,0:T(8,128)(2,1)}, u32[]{:S(2)}, u32[]{:S(2)}) collective-permute-start(bf16[512,384]{1,0:T(8,128)(2,1)S(1)} %collective-permute-done.8), channel_id=1, source_target_pairs={{0,1},{1,2},{2,3},{3,4},{4,5},{5,6},{6,7},{7,0},{8,9},{9,10},{10,1... | collective-permute-start | bytes 1179656 | tf_op jit(solution)/shard_map/ppermute | solution.py:74
  19.3 14.0 %collective-permute-start.4 = (bf16[512,384]{1,0:T(8,128)(2,1)S(1)}, bf16[512,384]{1,0:T(8,128)(2,1)}, u32[]{:S(2)}, u32[]{:S(2)}) collective-permute-start(bf16[512,384]{1,0:T(8,128)(2,1)S(1)} %collective-permute-done.2), channel_id=1, source_target_pairs={{0,7},{1,0},{2,1},{3,2},{4,3},{5,4},{6,5},{7,6},{8,15},{9,8},{10,9... | collective-permute-start | bytes 1179656 | tf_op jit(solution)/shard_map/ppermute | solution.py:78
  34.5 5.1 %collective-permute-start.5 = (f32[128,384]{1,0:T(8,128)S(1)}, f32[128,384]{1,0:T(8,128)S(1)}, u32[]{:S(2)}, u32[]{:S(2)}) collective-permute-start(f32[128,384]{1,0:T(8,128)S(1)} %fusion.91), channel_id=1, source_target_pairs={{0,8},{8,0},{16,24},{24,16},{32,40},{40,32},{48,56},{56,48},{64,72... | collective-permute-start | bytes 589832 | tf_op jit(solution)/shard_map/ppermute | solution.py:116
  35.8 5.7 %collective-permute-start.14 = (f32[128,384]{1,0:T(8,128)S(1)}, f32[128,384]{1,0:T(8,128)S(1)}, u32[]{:S(2)}, u32[]{:S(2)}) collective-permute-start(f32[128,384]{1,0:T(8,128)S(1)} %fusion.83), channel_id=1, source_target_pairs={{0,8},{8,0},{16,24},{24,16},{32,40},{40,32},{48,56},{56,48},{64,72... | collective-permute-start | bytes 589832 | tf_op jit(solution)/shard_map/ppermute | solution.py:116
  36.4 13.7 %collective-permute-start.10 = (bf16[512,384]{1,0:T(8,128)(2,1)}, bf16[512,384]{1,0:T(8,128)(2,1)}, u32[]{:S(2)}, u32[]{:S(2)}) collective-permute-start(bf16[512,384]{1,0:T(8,128)(2,1)} %collective-permute-done.9), channel_id=1, source_target_pairs={{0,1},{1,2},{2,3},{3,4},{4,5},{5,6},{6,7},{7,0},{8,9},{9,10},{10,1... | collective-permute-start | bytes 1179656 | tf_op jit(solution)/shard_map/ppermute | solution.py:74
  37.6 11.1 %collective-permute-start.6 = (bf16[512,384]{1,0:T(8,128)(2,1)}, bf16[512,384]{1,0:T(8,128)(2,1)}, u32[]{:S(2)}, u32[]{:S(2)}) collective-permute-start(bf16[512,384]{1,0:T(8,128)(2,1)} %collective-permute-done.4), channel_id=1, source_target_pairs={{0,7},{1,0},{2,1},{3,2},{4,3},{5,4},{6,5},{7,6},{8,15},{9,8},{10,9... | collective-permute-start | bytes 1179656 | tf_op jit(solution)/shard_map/ppermute | solution.py:78
  49.9 3.7 %collective-permute-start.7 = (f32[128,384]{1,0:T(8,128)S(1)}, f32[128,384]{1,0:T(8,128)S(1)}, u32[]{:S(2)}, u32[]{:S(2)}) collective-permute-start(f32[128,384]{1,0:T(8,128)S(1)} %fusion.89), channel_id=1, source_target_pairs={{0,8},{8,0},{16,24},{24,16},{32,40},{40,32},{48,56},{56,48},{64,72... | collective-permute-start | bytes 589832 | tf_op jit(solution)/shard_map/ppermute | solution.py:116
  50.0 13.2 %collective-permute-start.11 = (bf16[512,384]{1,0:T(8,128)(2,1)}, bf16[512,384]{1,0:T(8,128)(2,1)S(1)}, u32[]{:S(2)}, u32[]{:S(2)}) collective-permute-start(bf16[512,384]{1,0:T(8,128)(2,1)} %collective-permute-done.10), channel_id=1, source_target_pairs={{0,1},{1,2},{2,3},{3,4},{4,5},{5,6},{6,7},{7,0},{8,9},{9,10},{10,1... | collective-permute-start | bytes 1179656 | tf_op jit(solution)/shard_map/ppermute | solution.py:74
  53.2 11.0 %collective-permute-start.13 = (f32[128,384]{1,0:T(8,128)S(1)}, f32[128,384]{1,0:T(8,128)S(1)}, u32[]{:S(2)}, u32[]{:S(2)}) collective-permute-start(f32[128,384]{1,0:T(8,128)S(1)} %fusion.85), channel_id=1, source_target_pairs={{0,8},{8,0},{16,24},{24,16},{32,40},{40,32},{48,56},{56,48},{64,72... | collective-permute-start | bytes 589832 | tf_op jit(solution)/shard_map/ppermute | solution.py:116
  63.3 0.9 copy-start.3
  64.2 4.5 %collective-permute-start.12 = (f32[128,384]{1,0:T(8,128)}, f32[128,384]{1,0:T(8,128)}, u32[]{:S(2)}, u32[]{:S(2)}) collective-permute-start(f32[128,384]{1,0:T(8,128)} %fusion.87), channel_id=1, source_target_pairs={{0,8},{8,0},{16,24},{24,16},{32,40},{40,32},{48,56},{56,48},{64,72... | collective-permute-start | bytes 589832 | tf_op jit(solution)/shard_map/ppermute | solution.py:116
  70.8 16.4 %copy-start.4 = (bf16[512,384]{1,0:T(8,128)(2,1)S(1)}, bf16[512,384]{1,0:T(8,128)(2,1)}, u32[]{:S(2)}) copy-start(bf16[512,384]{1,0:T(8,128)(2,1)} %copy-done.3) | copy-start | bytes 1179652
  77.3 19.1 %all-to-all-start = ((bf16[16,3,64,128]{3,2,1,0:T(8,128)(2,1)}), bf16[16,3,64,128]{3,2,1,0:T(8,128)(2,1)}, u32[]{:S(2)}, u32[]{:S(2)}) async-start(bf16[16,3,64,128]{3,2,1,0:T(8,128)(2,1)} %copy.48), calls=%async_computation | async-start | bytes 1572864 | tf_op jit(solution)/shard_map/all_to_all | solution.py:56
  92.5 38.2 %collective-permute-start.17 = (bf16[512,3072]{1,0:T(8,128)(2,1)}, bf16[512,3072]{1,0:T(8,128)(2,1)}, u32[]{:S(2)}, u32[]{:S(2)}) collective-permute-start(bf16[512,3072]{1,0:T(8,128)(2,1)} %constant_dynamic-update-slice_fusion), channel_id=1, source_target_pairs={{0,8},{8,0},{16,24},{24,16},{32,40},{40,32},{48,56},{56,48},{64,72... | collective-permute-start | bytes 9437192 | tf_op jit(solution)/shard_map/ppermute | solution.py:126
  106.1 12.3 %copy-start.1 = (bf16[1,1,128,1024]{3,2,1,0:T(8,128)(2,1)S(1)}, bf16[1,1,128,1024]{3,2,1,0:T(8,128)(2,1)}, u32[]{:S(2)}) copy-start(bf16[1,1,128,1024]{3,2,1,0:T(8,128)(2,1)} %param.8) | copy-start | bytes 786436
  106.1 12.3 %copy-start.9 = (f32[1,1024]{1,0:T(1,128)S(1)}, f32[1,1024]{1,0:T(1,128)}, u32[]{:S(2)}) copy-start(f32[1,1024]{1,0:T(1,128)} %param.14) | copy-start | bytes 12292
  106.1 12.3 %copy-start.10 = (f32[1,1024]{1,0:T(1,128)S(1)}, f32[1,1024]{1,0:T(1,128)}, u32[]{:S(2)}) copy-start(f32[1,1024]{1,0:T(1,128)} %param.15) | copy-start | bytes 12292
  107.7 22.8 %copy-start.7 = (f32[1,1024]{1,0:T(1,128)S(1)}, f32[1,1024]{1,0:T(1,128)}, u32[]{:S(2)}) copy-start(f32[1,1024]{1,0:T(1,128)} %param.11) | copy-start | bytes 12292
  107.7 22.8 %copy-start.8 = (f32[1,1024]{1,0:T(1,128)S(1)}, f32[1,1024]{1,0:T(1,128)}, u32[]{:S(2)}) copy-start(f32[1,1024]{1,0:T(1,128)} %param.10) | copy-start | bytes 12292
  118.9 11.5 %copy-start.5 = (bf16[128,1024]{1,0:T(8,128)(2,1)}, bf16[128,1024]{1,0:T(8,128)(2,1)S(1)}, u32[]{:S(2)}) copy-start(bf16[128,1024]{1,0:T(8,128)(2,1)S(1)} %fusion.32) | copy-start | bytes 786436
  118.9 11.2 %collective-permute-start.16 = (bf16[128,1024]{1,0:T(8,128)(2,1)S(1)}, bf16[128,1024]{1,0:T(8,128)(2,1)S(1)}, u32[]{:S(2)}, u32[]{:S(2)}) collective-permute-start(bf16[128,1024]{1,0:T(8,128)(2,1)S(1)} %fusion.32), channel_id=1, source_target_pairs={{0,128},{1,129},{2,130},{3,131},{4,132},{5,133},{6,134},{7,135},{8... | collective-permute-start | bytes 786440 | tf_op jit(solution)/shard_map/ppermute | solution.py:135
  120.2 13.0 %copy-start.2 = (bf16[512,3072]{1,0:T(8,128)(2,1)S(1)}, bf16[512,3072]{1,0:T(8,128)(2,1)}, u32[]{:S(2)}) copy-start(bf16[512,3072]{1,0:T(8,128)(2,1)} %constant_dynamic-update-slice_fusion) | copy-start | bytes 9437188
  161.6 13.9 %copy-start.6 = (bf16[128,1024]{1,0:T(8,128)(2,1)S(1)}, bf16[128,1024]{1,0:T(8,128)(2,1)}, u32[]{:S(2)}) copy-start(bf16[128,1024]{1,0:T(8,128)(2,1)} %copy-done.5) | copy-start | bytes 786436
  164.0 11.5 %all-to-all-start.3 = ((bf16[16,64,128]{2,1,0:T(8,128)(2,1)}), bf16[16,64,128]{2,1,0:T(8,128)(2,1)S(1)}, u32[]{:S(2)}, u32[]{:S(2)}) async-start(bf16[16,64,128]{2,1,0:T(8,128)(2,1)} %bitcast.164), calls=%async_computation.3 | async-start | bytes 524288 | tf_op jit(solution)/shard_map/all_to_all | solution.py:59

commit v13 on v10

--- a/solution.py
+++ b/solution.py
@@ -78,6 +78,7 @@
             backward = lax.ppermute(backward, axis, left)
             k = 1 + step
             blocks[k], made[k] = backward, on_block(backward)
+    blocks = lax.optimization_barrier(blocks)
     return jnp.concatenate(blocks, axis=1), jnp.concatenate(made, axis=made_axis)
 
 

time: 163 us -> 162 us (level)
  no operation moved by 1% of the time
where the time goes in v13:
time: 162 us; the launch traced here: 161 us
  waiting for transfers between devices  52.5 us (32%)
  blocking collectives  27.2 us (17%)
  starting transfers between devices  23.5 us (15%)
  local copies, waits for them, and re-layouts  22.6 us (14%)
  other arithmetic  17.2 us (11%)
  matrix products  16.9 us (10%)
    ppermute x4, waiting for transfers between devices, ring_gather(): forward = lax.ppermute(forward, axis, right)  23.8 us
    all_to_all x1, blocking collectives, sublayer(): gathered = lax.all_to_all(projected, 'ctx', 0, 3, tiled=True)  16.5 us
    ppermute x3, starting transfers between devices, ring_gather(): backward = lax.ppermute(backward, axis, left)  12.9 us
    unnamed x39, local copies, waits for them, and re-layouts  11.6 us
    all_to_all x1, blocking collectives, sublayer(): lax.all_to_all(context, 'ctx', 0, 0, tiled=True).reshape(width, tok_rows)  10.6 us
    convert_element_type x2, other arithmetic, head_attention(): weights.astype(jnp.bfloat16)  10.2 us
    ppermute x1, waiting for transfers between devices, per_device(): current = lax.ppermute(produced, 'pipe', pairs)  9.85 us
    all_to_all x1, waiting for transfers between devices, sublayer(): lax.all_to_all(context, 'ctx', 0, 0, tiled=True).reshape(width, tok_rows)  7.98 us
  transfers between devices with their start and end apart: 13, of which 10 were waited for; matrix products, arithmetic and copies ran while one was open for 17% of the time, Pallas kernels for 0%

profile of v13, /device:TPU:4, one launch (start us, length us, event | category | flops | bytes accessed | tf_op | source)
XLA Modules:
  0.0 161.1 jit_solution(12368829448177146393)
XLA Ops:
  0.0 1.2 dynamic-slice_bitcast_fusion
  1.2 5.9 %collective-permute-start.1 = (bf16[512,384]{1,0:T(8,128)(2,1)S(1)}, bf16[512,384]{1,0:T(8,128)(2,1)S(1)}, u32[]{:S(2)}, u32[]{:S(2)}) collective-permute-start(bf16[512,384]{1,0:T(8,128)(2,1)S(1)} %dynamic-slice_bitcast_fusion), channel_id=1, source_target_pairs={{0,7},{1,0},{2,1},{3,2},{4,3},{5,4},{6,5},{7,6},{8,15},{9,8},{10,9... | collective-permute-start | bytes 1179656 | tf_op jit(solution)/shard_map/ppermute | solution.py:78
  7.1 1.1 convert_reduce_fusion.1
  8.2 1.2 fusion.64
  9.4 9.5 %collective-permute-done.4 = bf16[512,384]{1,0:T(8,128)(2,1)S(1)} collective-permute-done((bf16[512,384]{1,0:T(8,128)(2,1)S(1)}, bf16[512,384]{1,0:T(8,128)(2,1)S(1)}, u32[]{:S(2)}, u32[]{:S(2)}) %collective-permute-start.4) | collective-permute-done | bytes 393248 | tf_op jit(solution)/shard_map/ppermute | solution.py:74
  18.9 1.2 fusion.67
  20.2 3.3 %collective-permute-start.2 = (bf16[512,384]{1,0:T(8,128)(2,1)S(1)}, bf16[512,384]{1,0:T(8,128)(2,1)S(1)}, u32[]{:S(2)}, u32[]{:S(2)}) collective-permute-start(bf16[512,384]{1,0:T(8,128)(2,1)S(1)} %collective-permute-done.1), channel_id=1, source_target_pairs={{0,7},{1,0},{2,1},{3,2},{4,3},{5,4},{6,5},{7,6},{8,15},{9,8},{10,9... | collective-permute-start | bytes 1179656 | tf_op jit(solution)/shard_map/ppermute | solution.py:78
  23.6 6.3 %collective-permute-done.5 = bf16[512,384]{1,0:T(8,128)(2,1)S(1)} collective-permute-done((bf16[512,384]{1,0:T(8,128)(2,1)S(1)}, bf16[512,384]{1,0:T(8,128)(2,1)S(1)}, u32[]{:S(2)}, u32[]{:S(2)}) %collective-permute-start.5) | collective-permute-done | bytes 393248 | tf_op jit(solution)/shard_map/ppermute | solution.py:74
  29.9 1.4 fusion.44
  31.3 1.2 collective-permute-done.2
  32.5 3.7 %collective-permute-start.3 = (bf16[512,384]{1,0:T(8,128)(2,1)S(1)}, bf16[512,384]{1,0:T(8,128)(2,1)S(1)}, u32[]{:S(2)}, u32[]{:S(2)}) collective-permute-start(bf16[512,384]{1,0:T(8,128)(2,1)S(1)} %collective-permute-done.2), channel_id=1, source_target_pairs={{0,7},{1,0},{2,1},{3,2},{4,3},{5,4},{6,5},{7,6},{8,15},{9,8},{10,9... | collective-permute-start | bytes 1179656 | tf_op jit(solution)/shard_map/ppermute | solution.py:78
  36.2 0.3 fusion.43
  36.5 3.4 %collective-permute-done.6 = bf16[512,384]{1,0:T(8,128)(2,1)S(1)} collective-permute-done((bf16[512,384]{1,0:T(8,128)(2,1)S(1)}, bf16[512,384]{1,0:T(8,128)(2,1)S(1)}, u32[]{:S(2)}, u32[]{:S(2)}) %collective-permute-start.6) | collective-permute-done | bytes 393248 | tf_op jit(solution)/shard_map/ppermute | solution.py:74
  39.9 0.3 fusion.42
  40.2 4.1 %collective-permute-done.3 = bf16[512,384]{1,0:T(8,128)(2,1)S(1)} collective-permute-done((bf16[512,384]{1,0:T(8,128)(2,1)S(1)}, bf16[512,384]{1,0:T(8,128)(2,1)S(1)}, u32[]{:S(2)}, u32[]{:S(2)}) %collective-permute-start.3) | collective-permute-done | bytes 393248 | tf_op jit(solution)/shard_map/ppermute | solution.py:78
  44.3 0.3 fusion.41
  44.6 4.6 %collective-permute-done.7 = bf16[512,384]{1,0:T(8,128)(2,1)S(1)} collective-permute-done((bf16[512,384]{1,0:T(8,128)(2,1)S(1)}, bf16[512,384]{1,0:T(8,128)(2,1)S(1)}, u32[]{:S(2)}, u32[]{:S(2)}) %collective-permute-start.7) | collective-permute-done | bytes 393248 | tf_op jit(solution)/shard_map/ppermute | solution.py:74
  49.1 0.3 fusion.40
  49.4 0.3 fusion.39
  49.8 0.3 fusion.38
  50.1 0.3 fusion.37
  50.4 1.7 %copy-done.3 = f32[2,3072,128]{1,2,0:T(8,128)} copy-done((f32[2,3072,128]{1,2,0:T(8,128)}, f32[2,3072,128]{1,2,0:T(8,128)S(1)}, u32[]{:S(2)}) %copy-start.3) | copy-done | bytes 3145752
  52.1 1.4 slice_bitcast_fusion
  54.1 0.8 constant_dynamic-update-slice_fusion.7
  54.9 2.3 %collective-permute-done.8 = f32[3072,128]{0,1:T(8,128)} collective-permute-done((f32[3072,128]{0,1:T(8,128)}, f32[3072,128]{0,1:T(8,128)}, u32[]{:S(2)}, u32[]{:S(2)}) %collective-permute-start.8) | collective-permute-done | bytes 1572896 | tf_op jit(solution)/shard_map/ppermute | solution.py:114
  57.2 2.0 %fusion.12 = bf16[3072,128]{0,1:T(8,128)(2,1)S(1)} fusion(f32[3072,128]{0,1:T(8,128)} %collective-permute-done.8, f32[2,3072,128]{1,2,0:T(8,128)} %copy-done.3), kind=kLoop, calls=%fused_computation.21 | loop fusion | flops 786432 | bytes 3932160 | tf_op jit(solution)/shard_map/convert_element_type | solution.py:115
  59.2 0.4 fusion.54
  59.7 1.2 copy.19
  60.8 2.1 %copy.20 = bf16[16,3,64,128]{3,2,1,0:T(8,128)(2,1)} copy(bf16[16,3,64,128]{3,2,0,1:T(8,128)(2,1)} %bitcast.197) | data formatting | bytes 1572864 | tf_op jit(solution)/shard_map/transpose | solution.py:116
  62.9 5.2 %all-to-all-start = ((bf16[16,3,64,128]{3,2,1,0:T(8,128)(2,1)}), bf16[16,3,64,128]{3,2,1,0:T(8,128)(2,1)S(1)}, u32[]{:S(2)}, u32[]{:S(2)}) async-start(bf16[16,3,64,128]{3,2,1,0:T(8,128)(2,1)} %copy.20), calls=%async_computation | async-start | bytes 1572864 | tf_op jit(solution)/shard_map/all_to_all | solution.py:56
  68.2 1.9 %constant_dynamic-update-slice_fusion.6 = bf16[512,3072]{1,0:T(8,128)(2,1)} fusion(bf16[512,3072]{1,0:T(8,128)(2,1)} %constant_dynamic-update-slice_fusion.7, bf16[512,384]{1,0:T(8,128)(2,1)} %copy-done.4), kind=kLoop, calls=%fused_computation.111 | loop fusion | bytes 786432
  70.1 1.9 %constant_dynamic-update-slice_fusion.5 = bf16[512,3072]{1,0:T(8,128)(2,1)} fusion(bf16[512,3072]{1,0:T(8,128)(2,1)} %constant_dynamic-update-slice_fusion.6, bf16[512,384]{1,0:T(8,128)(2,1)} %copy-done.9), kind=kLoop, calls=%fused_computation.110 | loop fusion | bytes 786432
  71.9 1.8 %constant_dynamic-update-slice_fusion.4 = bf16[512,3072]{1,0:T(8,128)(2,1)} fusion(bf16[512,3072]{1,0:T(8,128)(2,1)} %constant_dynamic-update-slice_fusion.5, bf16[512,384]{1,0:T(8,128)(2,1)} %copy-done.10), kind=kLoop, calls=%fused_computation.109 | loop fusion | bytes 786432
  73.8 1.8 %constant_dynamic-update-slice_fusion.3 = bf16[512,3072]{1,0:T(8,128)(2,1)} fusion(bf16[512,3072]{1,0:T(8,128)(2,1)} %constant_dynamic-update-slice_fusion.4, bf16[512,384]{1,0:T(8,128)(2,1)} %copy-done.11), kind=kLoop, calls=%fused_computation.108 | loop fusion | bytes 786432
  75.6 0.8 constant_dynamic-update-slice_fusion.2
  76.4 0.8 constant_dynamic-update-slice_fusion.1
  77.3 0.8 constant_dynamic-update-slice_fusion
  78.1 0.4 collective-permute-start.10
  78.5 3.4 %all-to-all-done = bf16[16,3,64,128]{3,2,1,0:T(8,128)(2,1)S(1)} async-done(((bf16[16,3,64,128]{3,2,1,0:T(8,128)(2,1)}), bf16[16,3,64,128]{3,2,1,0:T(8,128)(2,1)S(1)}, u32[]{:S(2)}, u32[]{:S(2)}) %all-to-all-start) | async-done | bytes 786464 | tf_op jit(solution)/shard_map/all_to_all | solution.py:56
  81.9 0.2 copy.22
  82.3 2.8 %select_reduce_fusion.1 = (f32[2048]{0:T(1024)S(1)}, f32[2048,2048]{0,1:T(8,128)S(1)}) fusion(pred[2048]{0:T(1024)(128)(4,1)S(1)} %iota_compare_fusion, bf16[8,8,16,128]{3,2,1,0:T(8,128)(2,1)S(1)} %bitcast.203, bf16[8,8,16,128]{3,2,1,0:T(8,128)(2,1)S(1)} %bitcast.201), kind=kOutput, calls=%fused_computation.3 | convolution fusion | flops 549451776 | bytes 17311744 | tf_op jit(solution)/shard_map/dq,dk->qk/dot_general | solution.py:25
  85.1 5.1 %fusion = (bf16[2048,2048]{0,1:T(8,128)(2,1)S(1)}, f32[2048]{0:T(1024)S(1)}) fusion(f32[2048,2048]{0,1:T(8,128)S(1)} %get-tuple-element.40, f32[2048]{0:T(1024)S(1)} %get-tuple-element.39, pred[2048]{0:T(1024)(128)(4,1)S(1)} %iota_compare_fusion), kind=kLoop, calls=%fused_computation.4 | loop fusion | flops 20969472 | bytes 25184256 | tf_op jit(solution)/shard_map/convert_element_type | solution.py:32
  90.2 0.2 copy.21
  90.4 1.6 fusion.52
  92.1 10.6 %all_to_all.40 = bf16[16,64,128]{2,1,0:T(8,128)(2,1)S(1)} all-to-all(bf16[16,64,128]{2,1,0:T(8,128)(2,1)S(1)} %bitcast.205), channel_id=1, replica_groups=mesh['pipe'=2,'ctx'=16,'dp'=8] {'ctx'}, dimensions={0} | all-to-all | bytes 524288 | tf_op jit(solution)/shard_map/all_to_all | solution.py:59
  102.7 0.5 fusion.34
  103.2 1.3 collective-permute-start.9
  104.5 9.8 %collective-permute-done.9 = bf16[128,1024]{1,0:T(8,128)(2,1)S(1)} collective-permute-done((bf16[128,1024]{1,0:T(8,128)(2,1)S(1)}, bf16[128,1024]{1,0:T(8,128)(2,1)S(1)}, u32[]{:S(2)}, u32[]{:S(2)}) %collective-permute-start.9) | collective-permute-done | bytes 262176 | tf_op jit(solution)/shard_map/ppermute | solution.py:126
  114.5 0.2 fusion.60
  114.8 0.2 fusion.63
  115.0 2.5 %fusion.91 = f32[128,3072]{1,0:T(8,128)S(1)} fusion(bf16[512,3072]{1,0:T(8,128)(2,1)} %collective-permute-done.10, bf16[128,1024]{1,0:T(8,128)(2,1)S(1)} %fusion.63, s32[]{:T(128)S(6)} %select_n.49), kind=kOutput, calls=%fused_computation.100 | convolution fusion | flops 402653184 | bytes 4849668 | tf_op jit(solution)/shard_map/dot_general | solution.py:49
  117.5 0.6 fusion.4
  118.1 0.4 fusion.53
  118.5 1.2 copy.25
  119.7 1.2 copy.26
  120.9 16.5 %all_to_all.41 = bf16[16,3,64,128]{3,2,1,0:T(8,128)(2,1)S(1)} all-to-all(bf16[16,3,64,128]{3,2,1,0:T(8,128)(2,1)S(1)} %copy.26), channel_id=1, replica_groups=mesh['pipe'=2,'ctx'=16,'dp'=8] {'ctx'}, dimensions={0} | all-to-all | bytes 1572864 | tf_op jit(solution)/shard_map/all_to_all | solution.py:56
  137.5 0.2 copy.28
  137.9 2.8 %select_reduce_fusion = (f32[2048]{0:T(1024)S(1)}, f32[2048,2048]{0,1:T(8,128)S(1)}) fusion(pred[2048]{0:T(1024)(128)(4,1)S(1)} %iota_compare_fusion, bf16[8,8,16,128]{3,2,1,0:T(8,128)(2,1)S(1)} %bitcast.204, bf16[8,8,16,128]{3,2,1,0:T(8,128)(2,1)S(1)} %bitcast.202), kind=kOutput, calls=%fused_computation.1 | convolution fusion | flops 549451776 | bytes 17311744 | tf_op jit(solution)/shard_map/dq,dk->qk/dot_general | solution.py:25
  140.7 5.1 %fusion.2 = (bf16[2048,2048]{0,1:T(8,128)(2,1)S(1)}, f32[2048]{0:T(1024)S(1)}) fusion(f32[2048,2048]{0,1:T(8,128)S(1)} %get-tuple-element.42, f32[2048]{0:T(1024)S(1)} %get-tuple-element.41, pred[2048]{0:T(1024)(128)(4,1)S(1)} %iota_compare_fusion), kind=kLoop, calls=%fused_computation.6 | loop fusion | flops 20969472 | bytes 25184256 | tf_op jit(solution)/shard_map/convert_element_type | solution.py:32
  146.0 1.6 fusion.51
  147.5 0.8 copy.73
  148.3 3.5 %all-to-all-start.3 = ((bf16[16,64,128]{2,1,0:T(8,128)(2,1)}), bf16[16,64,128]{2,1,0:T(8,128)(2,1)S(1)}, u32[]{:S(2)}, u32[]{:S(2)}) async-start(bf16[16,64,128]{2,1,0:T(8,128)(2,1)} %bitcast.191), calls=%async_computation.3 | async-start | bytes 524288 | tf_op jit(solution)/shard_map/all_to_all | solution.py:59
  151.9 8.0 %all-to-all-done.3 = bf16[16,64,128]{2,1,0:T(8,128)(2,1)S(1)} async-done(((bf16[16,64,128]{2,1,0:T(8,128)(2,1)}), bf16[16,64,128]{2,1,0:T(8,128)(2,1)S(1)}, u32[]{:S(2)}, u32[]{:S(2)}) %all-to-all-start.3) | async-done | bytes 262176 | tf_op jit(solution)/shard_map/all_to_all | solution.py:59
  159.8 1.2 fusion.48
  (54 shorter events, 1.1 us)
Async XLA Ops:
  0.0 102.7 %copy-start = (bf16[1,1024,1024]{2,1,0:T(8,128)(2,1)S(1)}, bf16[1,1024,1024]{2,1,0:T(8,128)(2,1)}, u32[]{:S(2)}) copy-start(bf16[1,1024,1024]{2,1,0:T(8,128)(2,1)} %param.13) | copy-start | bytes 6291460
  1.2 19.0 %collective-permute-start.1 = (bf16[512,384]{1,0:T(8,128)(2,1)S(1)}, bf16[512,384]{1,0:T(8,128)(2,1)S(1)}, u32[]{:S(2)}, u32[]{:S(2)}) collective-permute-start(bf16[512,384]{1,0:T(8,128)(2,1)S(1)} %dynamic-slice_bitcast_fusion), channel_id=1, source_target_pairs={{0,7},{1,0},{2,1},{3,2},{4,3},{5,4},{6,5},{7,6},{8,15},{9,8},{10,9... | collective-permute-start | bytes 1179656 | tf_op jit(solution)/shard_map/ppermute | solution.py:78
  7.1 11.8 %collective-permute-start.4 = (bf16[512,384]{1,0:T(8,128)(2,1)S(1)}, bf16[512,384]{1,0:T(8,128)(2,1)S(1)}, u32[]{:S(2)}, u32[]{:S(2)}) collective-permute-start(bf16[512,384]{1,0:T(8,128)(2,1)S(1)} %dynamic-slice_bitcast_fusion), channel_id=1, source_target_pairs={{0,1},{1,2},{2,3},{3,4},{4,5},{5,6},{6,7},{7,0},{8,9},{9,10},{10,1... | collective-permute-start | bytes 1179656 | tf_op jit(solution)/shard_map/ppermute | solution.py:74
  18.9 10.9 %collective-permute-start.5 = (bf16[512,384]{1,0:T(8,128)(2,1)S(1)}, bf16[512,384]{1,0:T(8,128)(2,1)S(1)}, u32[]{:S(2)}, u32[]{:S(2)}) collective-permute-start(bf16[512,384]{1,0:T(8,128)(2,1)S(1)} %collective-permute-done.4), channel_id=1, source_target_pairs={{0,1},{1,2},{2,3},{3,4},{4,5},{5,6},{6,7},{7,0},{8,9},{9,10},{10,1... | collective-permute-start | bytes 1179656 | tf_op jit(solution)/shard_map/ppermute | solution.py:74
  20.1 9.7 %collective-permute-start = (bf16[128,1024]{1,0:T(8,128)(2,1)S(1)}, bf16[128,1024]{1,0:T(8,128)(2,1)S(1)}, u32[]{:S(2)}, u32[]{:S(2)}) collective-permute-start(bf16[128,1024]{1,0:T(8,128)(2,1)S(1)} %fusion.67), channel_id=1, source_target_pairs={{0,8},{8,0},{16,24},{24,16},{32,40},{40,32},{48,56},{56,48},{64,72... | collective-permute-start | bytes 786440 | tf_op jit(solution)/shard_map/ppermute | solution.py:103
  20.2 29.5 %copy-start.4 = (bf16[512,384]{1,0:T(8,128)(2,1)}, bf16[512,384]{1,0:T(8,128)(2,1)S(1)}, u32[]{:S(2)}) copy-start(bf16[512,384]{1,0:T(8,128)(2,1)S(1)} %collective-permute-done.1) | copy-start | bytes 1179652
  20.2 12.3 %collective-permute-start.2 = (bf16[512,384]{1,0:T(8,128)(2,1)S(1)}, bf16[512,384]{1,0:T(8,128)(2,1)S(1)}, u32[]{:S(2)}, u32[]{:S(2)}) collective-permute-start(bf16[512,384]{1,0:T(8,128)(2,1)S(1)} %collective-permute-done.1), channel_id=1, source_target_pairs={{0,7},{1,0},{2,1},{3,2},{4,3},{5,4},{6,5},{7,6},{8,15},{9,8},{10,9... | collective-permute-start | bytes 1179656 | tf_op jit(solution)/shard_map/ppermute | solution.py:78
  29.8 19.9 %copy-start.5 = (bf16[512,384]{1,0:T(8,128)(2,1)}, bf16[512,384]{1,0:T(8,128)(2,1)S(1)}, u32[]{:S(2)}) copy-start(bf16[512,384]{1,0:T(8,128)(2,1)S(1)} %collective-permute-done.5) | copy-start | bytes 1179652
  29.8 10.1 %collective-permute-start.6 = (bf16[512,384]{1,0:T(8,128)(2,1)S(1)}, bf16[512,384]{1,0:T(8,128)(2,1)S(1)}, u32[]{:S(2)}, u32[]{:S(2)}) collective-permute-start(bf16[512,384]{1,0:T(8,128)(2,1)S(1)} %collective-permute-done.5), channel_id=1, source_target_pairs={{0,1},{1,2},{2,3},{3,4},{4,5},{5,6},{6,7},{7,0},{8,9},{9,10},{10,1... | collective-permute-start | bytes 1179656 | tf_op jit(solution)/shard_map/ppermute | solution.py:74
  32.5 17.6 %copy-start.9 = (bf16[512,384]{1,0:T(8,128)(2,1)}, bf16[512,384]{1,0:T(8,128)(2,1)S(1)}, u32[]{:S(2)}) copy-start(bf16[512,384]{1,0:T(8,128)(2,1)S(1)} %collective-permute-done.2) | copy-start | bytes 1179652
  32.5 11.8 %collective-permute-start.3 = (bf16[512,384]{1,0:T(8,128)(2,1)S(1)}, bf16[512,384]{1,0:T(8,128)(2,1)S(1)}, u32[]{:S(2)}, u32[]{:S(2)}) collective-permute-start(bf16[512,384]{1,0:T(8,128)(2,1)S(1)} %collective-permute-done.2), channel_id=1, source_target_pairs={{0,7},{1,0},{2,1},{3,2},{4,3},{5,4},{6,5},{7,6},{8,15},{9,8},{10,9... | collective-permute-start | bytes 1179656 | tf_op jit(solution)/shard_map/ppermute | solution.py:78
  39.9 10.5 %copy-start.7 = (bf16[512,384]{1,0:T(8,128)(2,1)}, bf16[512,384]{1,0:T(8,128)(2,1)S(1)}, u32[]{:S(2)}) copy-start(bf16[512,384]{1,0:T(8,128)(2,1)S(1)} %collective-permute-done.6) | copy-start | bytes 1179652
  39.9 9.2 %collective-permute-start.7 = (bf16[512,384]{1,0:T(8,128)(2,1)S(1)}, bf16[512,384]{1,0:T(8,128)(2,1)S(1)}, u32[]{:S(2)}, u32[]{:S(2)}) collective-permute-start(bf16[512,384]{1,0:T(8,128)(2,1)S(1)} %collective-permute-done.6), channel_id=1, source_target_pairs={{0,1},{1,2},{2,3},{3,4},{4,5},{5,6},{6,7},{7,0},{8,9},{9,10},{10,1... | collective-permute-start | bytes 1179656 | tf_op jit(solution)/shard_map/ppermute | solution.py:74
  44.3 5.8 %copy-start.10 = (bf16[512,384]{1,0:T(8,128)(2,1)}, bf16[512,384]{1,0:T(8,128)(2,1)S(1)}, u32[]{:S(2)}) copy-start(bf16[512,384]{1,0:T(8,128)(2,1)S(1)} %collective-permute-done.3) | copy-start | bytes 1179652
  49.1 0.9 copy-start.11
  50.4 1.7 %copy-start.3 = (f32[2,3072,128]{1,2,0:T(8,128)}, f32[2,3072,128]{1,2,0:T(8,128)S(1)}, u32[]{:S(2)}) copy-start(f32[2,3072,128]{1,2,0:T(8,128)S(1)} %fusion.37) | copy-start | bytes 9437188
  53.4 3.8 %collective-permute-start.8 = (f32[3072,128]{0,1:T(8,128)}, f32[3072,128]{0,1:T(8,128)}, u32[]{:S(2)}, u32[]{:S(2)}) collective-permute-start(f32[3072,128]{0,1:T(8,128)} %slice_bitcast_fusion), channel_id=1, source_target_pairs={{0,8},{8,0},{16,24},{24,16},{32,40},{40,32},{48,56},{56,48},{64,72... | collective-permute-start | bytes 4718600 | tf_op jit(solution)/shard_map/ppermute | solution.py:114
  62.9 18.9 %all-to-all-start = ((bf16[16,3,64,128]{3,2,1,0:T(8,128)(2,1)}), bf16[16,3,64,128]{3,2,1,0:T(8,128)(2,1)S(1)}, u32[]{:S(2)}, u32[]{:S(2)}) async-start(bf16[16,3,64,128]{3,2,1,0:T(8,128)(2,1)} %copy.20), calls=%async_computation | async-start | bytes 1572864 | tf_op jit(solution)/shard_map/all_to_all | solution.py:56
  68.1 7.5 %copy-start.8 = (bf16[512,384]{1,0:T(8,128)(2,1)S(1)}, bf16[512,384]{1,0:T(8,128)(2,1)}, u32[]{:S(2)}) copy-start(bf16[512,384]{1,0:T(8,128)(2,1)} %copy-done.7) | copy-start | bytes 1179652
  68.2 8.3 %copy-start.6 = (bf16[512,384]{1,0:T(8,128)(2,1)S(1)}, bf16[512,384]{1,0:T(8,128)(2,1)}, u32[]{:S(2)}) copy-start(bf16[512,384]{1,0:T(8,128)(2,1)} %copy-done.5) | copy-start | bytes 1179652
  78.1 36.9 %collective-permute-start.10 = (bf16[512,3072]{1,0:T(8,128)(2,1)}, bf16[512,3072]{1,0:T(8,128)(2,1)}, u32[]{:S(2)}, u32[]{:S(2)}) collective-permute-start(bf16[512,3072]{1,0:T(8,128)(2,1)} %constant_dynamic-update-slice_fusion), channel_id=1, source_target_pairs={{0,8},{8,0},{16,24},{24,16},{32,40},{40,32},{48,56},{56,48},{64,72... | collective-permute-start | bytes 9437192 | tf_op jit(solution)/shard_map/ppermute | solution.py:117
  90.4 12.3 %copy-start.1 = (bf16[1,1,128,1024]{3,2,1,0:T(8,128)(2,1)S(1)}, bf16[1,1,128,1024]{3,2,1,0:T(8,128)(2,1)}, u32[]{:S(2)}) copy-start(bf16[1,1,128,1024]{3,2,1,0:T(8,128)(2,1)} %param.8) | copy-start | bytes 786436
  90.4 12.3 %copy-start.14 = (f32[1,1024]{1,0:T(1,128)S(1)}, f32[1,1024]{1,0:T(1,128)}, u32[]{:S(2)}) copy-start(f32[1,1024]{1,0:T(1,128)} %param.14) | copy-start | bytes 12292
  90.4 12.3 %copy-start.15 = (f32[1,1024]{1,0:T(1,128)S(1)}, f32[1,1024]{1,0:T(1,128)}, u32[]{:S(2)}) copy-start(f32[1,1024]{1,0:T(1,128)} %param.15) | copy-start | bytes 12292
  92.0 22.8 %copy-start.12 = (f32[1,1024]{1,0:T(1,128)S(1)}, f32[1,1024]{1,0:T(1,128)}, u32[]{:S(2)}) copy-start(f32[1,1024]{1,0:T(1,128)} %param.11) | copy-start | bytes 12292
  92.0 22.7 %copy-start.13 = (f32[1,1024]{1,0:T(1,128)S(1)}, f32[1,1024]{1,0:T(1,128)}, u32[]{:S(2)}) copy-start(f32[1,1024]{1,0:T(1,128)} %param.10) | copy-start | bytes 12292
  103.2 11.2 %collective-permute-start.9 = (bf16[128,1024]{1,0:T(8,128)(2,1)S(1)}, bf16[128,1024]{1,0:T(8,128)(2,1)S(1)}, u32[]{:S(2)}, u32[]{:S(2)}) collective-permute-start(bf16[128,1024]{1,0:T(8,128)(2,1)S(1)} %fusion.34), channel_id=1, source_target_pairs={{0,128},{1,129},{2,130},{3,131},{4,132},{5,133},{6,134},{7,135},{8... | collective-permute-start | bytes 786440 | tf_op jit(solution)/shard_map/ppermute | solution.py:126
  104.5 13.0 %copy-start.2 = (bf16[512,3072]{1,0:T(8,128)(2,1)S(1)}, bf16[512,3072]{1,0:T(8,128)(2,1)}, u32[]{:S(2)}) copy-start(bf16[512,3072]{1,0:T(8,128)(2,1)} %constant_dynamic-update-slice_fusion) | copy-start | bytes 9437188
  148.3 11.5 %all-to-all-start.3 = ((bf16[16,64,128]{2,1,0:T(8,128)(2,1)}), bf16[16,64,128]{2,1,0:T(8,128)(2,1)S(1)}, u32[]{:S(2)}, u32[]{:S(2)}) async-start(bf16[16,64,128]{2,1,0:T(8,128)(2,1)} %bitcast.191), calls=%async_computation.3 | async-start | bytes 524288 | tf_op jit(solution)/shard_map/all_to_all | solution.py:59

commit v14 on v13

--- a/solution.py
+++ b/solution.py
@@ -79,6 +79,8 @@
             k = 1 + step
             blocks[k], made[k] = backward, on_block(backward)
     blocks = lax.optimization_barrier(blocks)
+    if made_axis is None:
+        return jnp.concatenate(blocks, axis=1), made
     return jnp.concatenate(blocks, axis=1), jnp.concatenate(made, axis=made_axis)
 
 
@@ -107,13 +109,20 @@
     both = jnp.stack([mine_rows, sibling_rows])
 
     def on_block(block):
-        return jnp.einsum("kc,stk->sct", block, both, preferred_element_type=jnp.float32)
+        return jnp.einsum("stk,kc->stc", both, block, preferred_element_type=jnp.float32)
 
-    qkv_mine, partial = ring_gather(rows_mine, "dp", on_block, made_axis=1)
+    qkv_mine, made = ring_gather(rows_mine, "dp", on_block, made_axis=None)
+    dp_count = lax.axis_size("dp")
+    dp_index = lax.axis_index("dp")
+    shard_width = made[0].shape[-1]
+    partial = jnp.zeros(made[0].shape[:-1] + (shard_width * dp_count,), jnp.float32)
+    for k, piece in enumerate(made):
+        owner = (dp_index + k) % dp_count
+        partial = lax.dynamic_update_slice_in_dim(partial, piece, owner * shard_width, axis=2)
     tok_rows = current.shape[0]
     partial_other = lax.ppermute(partial[1], "ctx", sibling)
-    first = unrotate((partial[0] + partial_other).astype(jnp.bfloat16), "dp", along=0)
-    first = jnp.transpose(first.reshape(3, HEADS, width // HEADS, tok_rows), (1, 0, 2, 3))
+    first = (partial[0] + partial_other).astype(jnp.bfloat16)
+    first = jnp.transpose(first.reshape(tok_rows, 3, HEADS, width // HEADS), (2, 1, 3, 0))
     qkv_other = lax.ppermute(qkv_mine, "ctx", sibling)
     args = (qkv_mine, qkv_other, w_out[0], norm_gain[0], norm_bias[0], out_bias[0], scale_gain[0])
     length = lengths[0, 0]

time: 162 us -> 154 us (0.951)
  local copies, waits for them, and re-layouts: 22.6 us -> 18.8 us
  other arithmetic: 17.2 us -> 14.9 us
  waiting for transfers between devices: 52.5 us -> 50.6 us
    convert_element_type x1, other arithmetic: 2.04 us -> 0.16 us  [per_device(): first = (partial[0] + partial_other).astype(jnp.bfloat16)]
    unnamed x39 -> x41, local copies, waits for them, and re-layouts: 11.6 us -> 10 us
  transfers between devices with their start and end apart: 13 -> 13, of which waited for: 10 -> 10; matrix products, arithmetic and copies ran while one was open for 17% -> 19% of each run, Pallas kernels for 0% -> 0%
where the time goes in v14:
time: 154 us; the launch traced here: 153 us
  waiting for transfers between devices  50.6 us (33%)
  blocking collectives  27.2 us (18%)
  starting transfers between devices  23.7 us (15%)
  local copies, waits for them, and re-layouts  18.8 us (12%)
  matrix products  17.2 us (11%)
  other arithmetic  14.9 us (10%)
    ppermute x4, waiting for transfers between devices, ring_gather(): forward = lax.ppermute(forward, axis, right)  23 us
    all_to_all x1, blocking collectives, sublayer(): gathered = lax.all_to_all(projected, 'ctx', 0, 3, tiled=True)  16.5 us
    ppermute x3, starting transfers between devices, ring_gather(): backward = lax.ppermute(backward, axis, left)  13 us
    all_to_all x1, blocking collectives, sublayer(): lax.all_to_all(context, 'ctx', 0, 0, tiled=True).reshape(width, tok_rows)  10.6 us
    convert_element_type x2, other arithmetic, head_attention(): weights.astype(jnp.bfloat16)  10.2 us
    unnamed x41, local copies, waits for them, and re-layouts  10 us
    ppermute x1, waiting for transfers between devices, per_device(): current = lax.ppermute(produced, 'pipe', pairs)  9.84 us
    all_to_all x1, waiting for transfers between devices, sublayer(): lax.all_to_all(context, 'ctx', 0, 0, tiled=True).reshape(width, tok_rows)  7.98 us
  transfers between devices with their start and end apart: 13, of which 10 were waited for; matrix products, arithmetic and copies ran while one was open for 19% of the time, Pallas kernels for 0%

profile of v14, /device:TPU:4, one launch (start us, length us, event | category | flops | bytes accessed | tf_op | source)
XLA Modules:
  0.0 153.4 jit_solution(14455271251418198784)
XLA Ops:
  0.0 1.2 dynamic-slice_bitcast_fusion
  1.2 5.9 %collective-permute-start.1 = (bf16[512,384]{1,0:T(8,128)(2,1)S(1)}, bf16[512,384]{1,0:T(8,128)(2,1)S(1)}, u32[]{:S(2)}, u32[]{:S(2)}) collective-permute-start(bf16[512,384]{1,0:T(8,128)(2,1)S(1)} %dynamic-slice_bitcast_fusion), channel_id=1, source_target_pairs={{0,7},{1,0},{2,1},{3,2},{4,3},{5,4},{6,5},{7,6},{8,15},{9,8},{10,9... | collective-permute-start | bytes 1179656 | tf_op jit(solution)/shard_map/ppermute | solution.py:78
  7.1 1.1 convert_reduce_fusion.1
  8.2 1.2 fusion.55
  9.4 9.5 %collective-permute-done.4 = bf16[512,384]{1,0:T(8,128)(2,1)S(1)} collective-permute-done((bf16[512,384]{1,0:T(8,128)(2,1)S(1)}, bf16[512,384]{1,0:T(8,128)(2,1)S(1)}, u32[]{:S(2)}, u32[]{:S(2)}) %collective-permute-start.4) | collective-permute-done | bytes 393248 | tf_op jit(solution)/shard_map/ppermute | solution.py:74
  18.9 1.2 fusion.58
  20.3 3.3 %collective-permute-start.2 = (bf16[512,384]{1,0:T(8,128)(2,1)S(1)}, bf16[512,384]{1,0:T(8,128)(2,1)}, u32[]{:S(2)}, u32[]{:S(2)}) collective-permute-start(bf16[512,384]{1,0:T(8,128)(2,1)S(1)} %collective-permute-done.1), channel_id=1, source_target_pairs={{0,7},{1,0},{2,1},{3,2},{4,3},{5,4},{6,5},{7,6},{8,15},{9,8},{10,9... | collective-permute-start | bytes 1179656 | tf_op jit(solution)/shard_map/ppermute | solution.py:78
  23.6 6.3 %collective-permute-done.5 = bf16[512,384]{1,0:T(8,128)(2,1)S(1)} collective-permute-done((bf16[512,384]{1,0:T(8,128)(2,1)S(1)}, bf16[512,384]{1,0:T(8,128)(2,1)S(1)}, u32[]{:S(2)}, u32[]{:S(2)}) %collective-permute-start.5) | collective-permute-done | bytes 393248 | tf_op jit(solution)/shard_map/ppermute | solution.py:74
  29.9 1.1 dynamic-slice_bitcast_fusion.1
  30.9 0.2 broadcast_in_dim.44
  31.1 0.3 convolution_dynamic-update-slice_fusion.7
  31.5 1.1 collective-permute-done.2
  32.6 3.8 %collective-permute-start.3 = (bf16[512,384]{1,0:T(8,128)(2,1)}, bf16[512,384]{1,0:T(8,128)(2,1)S(1)}, u32[]{:S(2)}, u32[]{:S(2)}) collective-permute-start(bf16[512,384]{1,0:T(8,128)(2,1)} %collective-permute-done.2), channel_id=1, source_target_pairs={{0,7},{1,0},{2,1},{3,2},{4,3},{5,4},{6,5},{7,6},{8,15},{9,8},{10,9... | collective-permute-start | bytes 1179656 | tf_op jit(solution)/shard_map/ppermute | solution.py:78
  36.4 0.3 convolution_dynamic-update-slice_fusion.6
  36.7 3.2 %collective-permute-done.6 = bf16[512,384]{1,0:T(8,128)(2,1)S(1)} collective-permute-done((bf16[512,384]{1,0:T(8,128)(2,1)S(1)}, bf16[512,384]{1,0:T(8,128)(2,1)S(1)}, u32[]{:S(2)}, u32[]{:S(2)}) %collective-permute-start.6) | collective-permute-done | bytes 393248 | tf_op jit(solution)/shard_map/ppermute | solution.py:74
  39.9 1.5 convolution_dynamic-update-slice_fusion.5
  41.4 3.4 %collective-permute-done.3 = bf16[512,384]{1,0:T(8,128)(2,1)S(1)} collective-permute-done((bf16[512,384]{1,0:T(8,128)(2,1)}, bf16[512,384]{1,0:T(8,128)(2,1)S(1)}, u32[]{:S(2)}, u32[]{:S(2)}) %collective-permute-start.3) | collective-permute-done | bytes 393248 | tf_op jit(solution)/shard_map/ppermute | solution.py:78
  44.8 0.3 convolution_dynamic-update-slice_fusion.4
  45.2 4.0 %collective-permute-done.7 = bf16[512,384]{1,0:T(8,128)(2,1)S(1)} collective-permute-done((bf16[512,384]{1,0:T(8,128)(2,1)S(1)}, bf16[512,384]{1,0:T(8,128)(2,1)S(1)}, u32[]{:S(2)}, u32[]{:S(2)}) %collective-permute-start.7) | collective-permute-done | bytes 393248 | tf_op jit(solution)/shard_map/ppermute | solution.py:74
  49.2 0.3 convolution_dynamic-update-slice_fusion.3
  49.5 0.3 convolution_dynamic-update-slice_fusion.2
  49.8 0.3 convolution_dynamic-update-slice_fusion.1
  50.2 0.3 convolution_dynamic-update-slice_fusion
  51.4 0.9 constant_dynamic-update-slice_fusion.7
  52.3 1.9 %collective-permute-done.8 = f32[128,3072]{0,1:T(8,128)S(1)} collective-permute-done((f32[128,3072]{0,1:T(8,128)S(1)}, f32[128,3072]{0,1:T(8,128)S(1)}, u32[]{:S(2)}, u32[]{:S(2)}) %collective-permute-start.8) | collective-permute-done | bytes 1572896 | tf_op jit(solution)/shard_map/ppermute | solution.py:123
  54.3 1.0 copy.34
  55.2 5.2 %all-to-all-start = ((bf16[16,3,64,128]{3,2,1,0:T(8,128)(2,1)}), bf16[16,3,64,128]{3,2,1,0:T(8,128)(2,1)S(1)}, u32[]{:S(2)}, u32[]{:S(2)}) async-start(bf16[16,3,64,128]{3,2,1,0:T(8,128)(2,1)} %copy.34), calls=%async_computation | async-start | bytes 1572864 | tf_op jit(solution)/shard_map/all_to_all | solution.py:56
  60.5 1.9 %constant_dynamic-update-slice_fusion.6 = bf16[512,3072]{1,0:T(8,128)(2,1)} fusion(bf16[512,3072]{1,0:T(8,128)(2,1)} %constant_dynamic-update-slice_fusion.7, bf16[512,384]{1,0:T(8,128)(2,1)} %copy-done.3), kind=kLoop, calls=%fused_computation.100 | loop fusion | bytes 786432
  62.4 1.8 %constant_dynamic-update-slice_fusion.5 = bf16[512,3072]{1,0:T(8,128)(2,1)} fusion(bf16[512,3072]{1,0:T(8,128)(2,1)} %constant_dynamic-update-slice_fusion.6, bf16[512,384]{1,0:T(8,128)(2,1)} %collective-permute-done.2), kind=kLoop, calls=%fused_computation.99 | loop fusion | bytes 786432
  64.2 1.8 %constant_dynamic-update-slice_fusion.4 = bf16[512,3072]{1,0:T(8,128)(2,1)} fusion(bf16[512,3072]{1,0:T(8,128)(2,1)} %constant_dynamic-update-slice_fusion.5, bf16[512,384]{1,0:T(8,128)(2,1)} %copy-done.10), kind=kLoop, calls=%fused_computation.98 | loop fusion | bytes 786432
  66.1 1.8 %constant_dynamic-update-slice_fusion.3 = bf16[512,3072]{1,0:T(8,128)(2,1)} fusion(bf16[512,3072]{1,0:T(8,128)(2,1)} %constant_dynamic-update-slice_fusion.4, bf16[512,384]{1,0:T(8,128)(2,1)} %copy-done.11), kind=kLoop, calls=%fused_computation.97 | loop fusion | bytes 786432
  67.9 0.8 constant_dynamic-update-slice_fusion.2
  68.7 0.8 constant_dynamic-update-slice_fusion.1
  69.6 0.9 constant_dynamic-update-slice_fusion
  70.4 0.4 collective-permute-start.10
  70.8 3.3 %all-to-all-done = bf16[16,3,64,128]{3,2,1,0:T(8,128)(2,1)S(1)} async-done(((bf16[16,3,64,128]{3,2,1,0:T(8,128)(2,1)}), bf16[16,3,64,128]{3,2,1,0:T(8,128)(2,1)S(1)}, u32[]{:S(2)}, u32[]{:S(2)}) %all-to-all-start) | async-done | bytes 786464 | tf_op jit(solution)/shard_map/all_to_all | solution.py:56
  74.2 0.2 copy.36
  74.4 0.2 copy.37
  74.6 2.8 %select_reduce_fusion.1 = (f32[2048]{0:T(1024)S(1)}, f32[2048,2048]{0,1:T(8,128)S(1)}) fusion(pred[2048]{0:T(1024)(128)(4,1)S(1)} %iota_compare_fusion, bf16[8,8,16,128]{3,2,1,0:T(8,128)(2,1)S(1)} %bitcast.171, bf16[8,8,16,128]{3,2,1,0:T(8,128)(2,1)S(1)} %bitcast.169), kind=kOutput, calls=%fused_computation.3 | convolution fusion | flops 549451776 | bytes 17311744 | tf_op jit(solution)/shard_map/dq,dk->qk/dot_general | solution.py:25
  77.4 5.1 %fusion = (bf16[2048,2048]{0,1:T(8,128)(2,1)S(1)}, f32[2048]{0:T(1024)S(1)}) fusion(f32[2048,2048]{0,1:T(8,128)S(1)} %get-tuple-element.40, f32[2048]{0:T(1024)S(1)} %get-tuple-element.39, pred[2048]{0:T(1024)(128)(4,1)S(1)} %iota_compare_fusion), kind=kLoop, calls=%fused_computation.4 | loop fusion | flops 20969472 | bytes 25184256 | tf_op jit(solution)/shard_map/convert_element_type | solution.py:32
  82.5 0.2 copy.35
  82.7 1.6 %fusion.44 = bf16[8,16,8,128]{3,2,1,0:T(8,128)(2,1)S(1)} fusion(bf16[2048,2048]{0,1:T(8,128)(2,1)S(1)} %get-tuple-element.17, bf16[8,8,16,128]{3,2,1,0:T(8,128)(2,1)S(1)} %bitcast.167, f32[2048]{0:T(1024)S(1)} %get-tuple-element.18), kind=kOutput, calls=%fused_computation.43 | convolution fusion | flops 537133056 | bytes 8921088 | tf_op jit(solution)/shard_map/qk,dk->dq/dot_general | solution.py:34
  84.4 10.6 %all_to_all.40 = bf16[16,64,128]{2,1,0:T(8,128)(2,1)S(1)} all-to-all(bf16[16,64,128]{2,1,0:T(8,128)(2,1)S(1)} %bitcast.173), channel_id=1, replica_groups=mesh['pipe'=2,'ctx'=16,'dp'=8] {'ctx'}, dimensions={0} | all-to-all | bytes 524288 | tf_op jit(solution)/shard_map/all_to_all | solution.py:59
  95.0 0.5 fusion.34
  95.5 1.3 collective-permute-start.9
  96.9 9.8 %collective-permute-done.9 = bf16[128,1024]{1,0:T(8,128)(2,1)S(1)} collective-permute-done((bf16[128,1024]{1,0:T(8,128)(2,1)S(1)}, bf16[128,1024]{1,0:T(8,128)(2,1)S(1)}, u32[]{:S(2)}, u32[]{:S(2)}) %collective-permute-start.9) | collective-permute-done | bytes 262176 | tf_op jit(solution)/shard_map/ppermute | solution.py:135
  106.8 0.2 fusion.51
  107.1 0.2 fusion.54
  107.3 2.5 %fusion.82 = f32[128,3072]{1,0:T(8,128)S(1)} fusion(bf16[512,3072]{1,0:T(8,128)(2,1)} %collective-permute-done.10, bf16[128,1024]{1,0:T(8,128)(2,1)S(1)} %fusion.54, s32[]{:T(128)S(6)} %select_n.119), kind=kOutput, calls=%fused_computation.89 | convolution fusion | flops 402653184 | bytes 4849668 | tf_op jit(solution)/shard_map/dot_general | solution.py:49
  109.8 0.6 fusion.4
  110.4 0.4 fusion.45
  110.9 1.2 copy.39
  112.0 1.2 copy.40
  113.2 16.5 %all_to_all.41 = bf16[16,3,64,128]{3,2,1,0:T(8,128)(2,1)S(1)} all-to-all(bf16[16,3,64,128]{3,2,1,0:T(8,128)(2,1)S(1)} %copy.40), channel_id=1, replica_groups=mesh['pipe'=2,'ctx'=16,'dp'=8] {'ctx'}, dimensions={0} | all-to-all | bytes 1572864 | tf_op jit(solution)/shard_map/all_to_all | solution.py:56
  129.8 0.2 copy.42
  130.0 0.2 copy.43
  130.2 2.8 %select_reduce_fusion = (f32[2048]{0:T(1024)S(1)}, f32[2048,2048]{0,1:T(8,128)S(1)}) fusion(pred[2048]{0:T(1024)(128)(4,1)S(1)} %iota_compare_fusion, bf16[8,8,16,128]{3,2,1,0:T(8,128)(2,1)S(1)} %bitcast.172, bf16[8,8,16,128]{3,2,1,0:T(8,128)(2,1)S(1)} %bitcast.170), kind=kOutput, calls=%fused_computation.1 | convolution fusion | flops 549451776 | bytes 17311744 | tf_op jit(solution)/shard_map/dq,dk->qk/dot_general | solution.py:25
  133.0 5.1 %fusion.2 = (bf16[2048,2048]{0,1:T(8,128)(2,1)S(1)}, f32[2048]{0:T(1024)S(1)}) fusion(f32[2048,2048]{0,1:T(8,128)S(1)} %get-tuple-element.42, f32[2048]{0:T(1024)S(1)} %get-tuple-element.41, pred[2048]{0:T(1024)(128)(4,1)S(1)} %iota_compare_fusion), kind=kLoop, calls=%fused_computation.6 | loop fusion | flops 20969472 | bytes 25184256 | tf_op jit(solution)/shard_map/convert_element_type | solution.py:32
  138.1 0.2 copy.41
  138.3 1.6 %fusion.43 = bf16[8,16,8,128]{3,2,1,0:T(8,128)(2,1)S(1)} fusion(bf16[2048,2048]{0,1:T(8,128)(2,1)S(1)} %get-tuple-element.27, bf16[8,8,16,128]{3,2,1,0:T(8,128)(2,1)S(1)} %bitcast.168, f32[2048]{0:T(1024)S(1)} %get-tuple-element.28), kind=kOutput, calls=%fused_computation.42 | convolution fusion | flops 537133056 | bytes 8921088 | tf_op jit(solution)/shard_map/qk,dk->dq/dot_general | solution.py:34
  139.9 0.8 copy.95
  140.6 3.5 %all-to-all-start.3 = ((bf16[16,64,128]{2,1,0:T(8,128)(2,1)}), bf16[16,64,128]{2,1,0:T(8,128)(2,1)S(1)}, u32[]{:S(2)}, u32[]{:S(2)}) async-start(bf16[16,64,128]{2,1,0:T(8,128)(2,1)} %bitcast.159), calls=%async_computation.3 | async-start | bytes 524288 | tf_op jit(solution)/shard_map/all_to_all | solution.py:59
  144.2 8.0 %all-to-all-done.3 = bf16[16,64,128]{2,1,0:T(8,128)(2,1)S(1)} async-done(((bf16[16,64,128]{2,1,0:T(8,128)(2,1)}), bf16[16,64,128]{2,1,0:T(8,128)(2,1)S(1)}, u32[]{:S(2)}, u32[]{:S(2)}) %all-to-all-start.3) | async-done | bytes 262176 | tf_op jit(solution)/shard_map/all_to_all | solution.py:59
  152.2 1.2 fusion.40
  (55 shorter events, 0.9 us)
Async XLA Ops:
  0.0 95.0 %copy-start = (bf16[1,1024,1024]{2,1,0:T(8,128)(2,1)S(1)}, bf16[1,1024,1024]{2,1,0:T(8,128)(2,1)}, u32[]{:S(2)}) copy-start(bf16[1,1024,1024]{2,1,0:T(8,128)(2,1)} %param.13) | copy-start | bytes 6291460
  1.2 19.1 %copy-start.6 = (bf16[512,384]{1,0:T(8,128)(2,1)}, bf16[512,384]{1,0:T(8,128)(2,1)S(1)}, u32[]{:S(2)}) copy-start(bf16[512,384]{1,0:T(8,128)(2,1)S(1)} %dynamic-slice_bitcast_fusion) | copy-start | bytes 1179652
  1.2 19.0 %collective-permute-start.1 = (bf16[512,384]{1,0:T(8,128)(2,1)S(1)}, bf16[512,384]{1,0:T(8,128)(2,1)S(1)}, u32[]{:S(2)}, u32[]{:S(2)}) collective-permute-start(bf16[512,384]{1,0:T(8,128)(2,1)S(1)} %dynamic-slice_bitcast_fusion), channel_id=1, source_target_pairs={{0,7},{1,0},{2,1},{3,2},{4,3},{5,4},{6,5},{7,6},{8,15},{9,8},{10,9... | collective-permute-start | bytes 1179656 | tf_op jit(solution)/shard_map/ppermute | solution.py:78
  7.1 11.8 %collective-permute-start.4 = (bf16[512,384]{1,0:T(8,128)(2,1)S(1)}, bf16[512,384]{1,0:T(8,128)(2,1)S(1)}, u32[]{:S(2)}, u32[]{:S(2)}) collective-permute-start(bf16[512,384]{1,0:T(8,128)(2,1)S(1)} %dynamic-slice_bitcast_fusion), channel_id=1, source_target_pairs={{0,1},{1,2},{2,3},{3,4},{4,5},{5,6},{6,7},{7,0},{8,9},{9,10},{10,1... | collective-permute-start | bytes 1179656 | tf_op jit(solution)/shard_map/ppermute | solution.py:74
  18.9 10.9 %collective-permute-start.5 = (bf16[512,384]{1,0:T(8,128)(2,1)S(1)}, bf16[512,384]{1,0:T(8,128)(2,1)S(1)}, u32[]{:S(2)}, u32[]{:S(2)}) collective-permute-start(bf16[512,384]{1,0:T(8,128)(2,1)S(1)} %collective-permute-done.4), channel_id=1, source_target_pairs={{0,1},{1,2},{2,3},{3,4},{4,5},{5,6},{6,7},{7,0},{8,9},{9,10},{10,1... | collective-permute-start | bytes 1179656 | tf_op jit(solution)/shard_map/ppermute | solution.py:74
  20.1 9.7 %collective-permute-start = (bf16[128,1024]{1,0:T(8,128)(2,1)S(1)}, bf16[128,1024]{1,0:T(8,128)(2,1)}, u32[]{:S(2)}, u32[]{:S(2)}) collective-permute-start(bf16[128,1024]{1,0:T(8,128)(2,1)S(1)} %fusion.58), channel_id=1, source_target_pairs={{0,8},{8,0},{16,24},{24,16},{32,40},{40,32},{48,56},{56,48},{64,72... | collective-permute-start | bytes 786440 | tf_op jit(solution)/shard_map/ppermute | solution.py:105
  20.3 21.1 %copy-start.3 = (bf16[512,384]{1,0:T(8,128)(2,1)}, bf16[512,384]{1,0:T(8,128)(2,1)S(1)}, u32[]{:S(2)}) copy-start(bf16[512,384]{1,0:T(8,128)(2,1)S(1)} %collective-permute-done.1) | copy-start | bytes 1179652
  20.3 12.3 %collective-permute-start.2 = (bf16[512,384]{1,0:T(8,128)(2,1)S(1)}, bf16[512,384]{1,0:T(8,128)(2,1)}, u32[]{:S(2)}, u32[]{:S(2)}) collective-permute-start(bf16[512,384]{1,0:T(8,128)(2,1)S(1)} %collective-permute-done.1), channel_id=1, source_target_pairs={{0,7},{1,0},{2,1},{3,2},{4,3},{5,4},{6,5},{7,6},{8,15},{9,8},{10,9... | collective-permute-start | bytes 1179656 | tf_op jit(solution)/shard_map/ppermute | solution.py:78
  23.6 7.6 %copy-start.12 = (bf16[1,1024,384]{2,1,0:T(8,128)(2,1)S(1)}, bf16[1,1024,384]{2,1,0:T(8,128)(2,1)}, u32[]{:S(2)}) copy-start(bf16[1,1024,384]{2,1,0:T(8,128)(2,1)} %param.12) | copy-start | bytes 2359300
  29.9 20.0 %copy-start.4 = (bf16[512,384]{1,0:T(8,128)(2,1)}, bf16[512,384]{1,0:T(8,128)(2,1)S(1)}, u32[]{:S(2)}) copy-start(bf16[512,384]{1,0:T(8,128)(2,1)S(1)} %collective-permute-done.5) | copy-start | bytes 1179652
  29.9 10.1 %collective-permute-start.6 = (bf16[512,384]{1,0:T(8,128)(2,1)S(1)}, bf16[512,384]{1,0:T(8,128)(2,1)S(1)}, u32[]{:S(2)}, u32[]{:S(2)}) collective-permute-start(bf16[512,384]{1,0:T(8,128)(2,1)S(1)} %collective-permute-done.5), channel_id=1, source_target_pairs={{0,1},{1,2},{2,3},{3,4},{4,5},{5,6},{6,7},{7,0},{8,9},{9,10},{10,1... | collective-permute-start | bytes 1179656 | tf_op jit(solution)/shard_map/ppermute | solution.py:74
  32.6 12.3 %collective-permute-start.3 = (bf16[512,384]{1,0:T(8,128)(2,1)}, bf16[512,384]{1,0:T(8,128)(2,1)S(1)}, u32[]{:S(2)}, u32[]{:S(2)}) collective-permute-start(bf16[512,384]{1,0:T(8,128)(2,1)} %collective-permute-done.2), channel_id=1, source_target_pairs={{0,7},{1,0},{2,1},{3,2},{4,3},{5,4},{6,5},{7,6},{8,15},{9,8},{10,9... | collective-permute-start | bytes 1179656 | tf_op jit(solution)/shard_map/ppermute | solution.py:78
  39.9 10.6 %copy-start.8 = (bf16[512,384]{1,0:T(8,128)(2,1)}, bf16[512,384]{1,0:T(8,128)(2,1)S(1)}, u32[]{:S(2)}) copy-start(bf16[512,384]{1,0:T(8,128)(2,1)S(1)} %collective-permute-done.6) | copy-start | bytes 1179652
  39.9 9.2 %collective-permute-start.7 = (bf16[512,384]{1,0:T(8,128)(2,1)S(1)}, bf16[512,384]{1,0:T(8,128)(2,1)S(1)}, u32[]{:S(2)}, u32[]{:S(2)}) collective-permute-start(bf16[512,384]{1,0:T(8,128)(2,1)S(1)} %collective-permute-done.6), channel_id=1, source_target_pairs={{0,1},{1,2},{2,3},{3,4},{4,5},{5,6},{6,7},{7,0},{8,9},{9,10},{10,1... | collective-permute-start | bytes 1179656 | tf_op jit(solution)/shard_map/ppermute | solution.py:74
  44.8 5.8 %copy-start.10 = (bf16[512,384]{1,0:T(8,128)(2,1)}, bf16[512,384]{1,0:T(8,128)(2,1)S(1)}, u32[]{:S(2)}) copy-start(bf16[512,384]{1,0:T(8,128)(2,1)S(1)} %collective-permute-done.3) | copy-start | bytes 1179652
  49.1 1.5 copy-start.11
  49.5 1.9 %copy-start.7 = (bf16[512,384]{1,0:T(8,128)(2,1)S(1)}, bf16[512,384]{1,0:T(8,128)(2,1)}, u32[]{:S(2)}) copy-start(bf16[512,384]{1,0:T(8,128)(2,1)} %copy-done.6) | copy-start | bytes 1179652
  50.6 3.5 %collective-permute-start.8 = (f32[128,3072]{0,1:T(8,128)S(1)}, f32[128,3072]{0,1:T(8,128)S(1)}, u32[]{:S(2)}, u32[]{:S(2)}) collective-permute-start(f32[128,3072]{0,1:T(8,128)S(1)} %slice_bitcast_fusion), channel_id=1, source_target_pairs={{0,8},{8,0},{16,24},{24,16},{32,40},{40,32},{48,56},{56,48},{64,72... | collective-permute-start | bytes 4718600 | tf_op jit(solution)/shard_map/ppermute | solution.py:123
  55.2 18.9 %all-to-all-start = ((bf16[16,3,64,128]{3,2,1,0:T(8,128)(2,1)}), bf16[16,3,64,128]{3,2,1,0:T(8,128)(2,1)S(1)}, u32[]{:S(2)}, u32[]{:S(2)}) async-start(bf16[16,3,64,128]{3,2,1,0:T(8,128)(2,1)} %copy.34), calls=%async_computation | async-start | bytes 1572864 | tf_op jit(solution)/shard_map/all_to_all | solution.py:56
  60.5 7.4 %copy-start.9 = (bf16[512,384]{1,0:T(8,128)(2,1)S(1)}, bf16[512,384]{1,0:T(8,128)(2,1)}, u32[]{:S(2)}) copy-start(bf16[512,384]{1,0:T(8,128)(2,1)} %copy-done.8) | copy-start | bytes 1179652
  60.5 8.3 %copy-start.5 = (bf16[512,384]{1,0:T(8,128)(2,1)S(1)}, bf16[512,384]{1,0:T(8,128)(2,1)}, u32[]{:S(2)}) copy-start(bf16[512,384]{1,0:T(8,128)(2,1)} %copy-done.4) | copy-start | bytes 1179652
  70.4 36.9 %collective-permute-start.10 = (bf16[512,3072]{1,0:T(8,128)(2,1)}, bf16[512,3072]{1,0:T(8,128)(2,1)}, u32[]{:S(2)}, u32[]{:S(2)}) collective-permute-start(bf16[512,3072]{1,0:T(8,128)(2,1)} %constant_dynamic-update-slice_fusion), channel_id=1, source_target_pairs={{0,8},{8,0},{16,24},{24,16},{32,40},{40,32},{48,56},{56,48},{64,72... | collective-permute-start | bytes 9437192 | tf_op jit(solution)/shard_map/ppermute | solution.py:126
  82.7 12.3 %copy-start.1 = (bf16[1,1,128,1024]{3,2,1,0:T(8,128)(2,1)S(1)}, bf16[1,1,128,1024]{3,2,1,0:T(8,128)(2,1)}, u32[]{:S(2)}) copy-start(bf16[1,1,128,1024]{3,2,1,0:T(8,128)(2,1)} %param.8) | copy-start | bytes 786436
  82.7 12.3 %copy-start.15 = (f32[1,1024]{1,0:T(1,128)S(1)}, f32[1,1024]{1,0:T(1,128)}, u32[]{:S(2)}) copy-start(f32[1,1024]{1,0:T(1,128)} %param.14) | copy-start | bytes 12292
  82.7 12.3 %copy-start.16 = (f32[1,1024]{1,0:T(1,128)S(1)}, f32[1,1024]{1,0:T(1,128)}, u32[]{:S(2)}) copy-start(f32[1,1024]{1,0:T(1,128)} %param.15) | copy-start | bytes 12292
  84.3 22.8 %copy-start.13 = (f32[1,1024]{1,0:T(1,128)S(1)}, f32[1,1024]{1,0:T(1,128)}, u32[]{:S(2)}) copy-start(f32[1,1024]{1,0:T(1,128)} %param.11) | copy-start | bytes 12292
  84.3 22.7 %copy-start.14 = (f32[1,1024]{1,0:T(1,128)S(1)}, f32[1,1024]{1,0:T(1,128)}, u32[]{:S(2)}) copy-start(f32[1,1024]{1,0:T(1,128)} %param.10) | copy-start | bytes 12292
  95.5 11.2 %collective-permute-start.9 = (bf16[128,1024]{1,0:T(8,128)(2,1)S(1)}, bf16[128,1024]{1,0:T(8,128)(2,1)S(1)}, u32[]{:S(2)}, u32[]{:S(2)}) collective-permute-start(bf16[128,1024]{1,0:T(8,128)(2,1)S(1)} %fusion.34), channel_id=1, source_target_pairs={{0,128},{1,129},{2,130},{3,131},{4,132},{5,133},{6,134},{7,135},{8... | collective-permute-start | bytes 786440 | tf_op jit(solution)/shard_map/ppermute | solution.py:135
  96.9 13.0 %copy-start.2 = (bf16[512,3072]{1,0:T(8,128)(2,1)S(1)}, bf16[512,3072]{1,0:T(8,128)(2,1)}, u32[]{:S(2)}) copy-start(bf16[512,3072]{1,0:T(8,128)(2,1)} %constant_dynamic-update-slice_fusion) | copy-start | bytes 9437188
  140.6 11.5 %all-to-all-start.3 = ((bf16[16,64,128]{2,1,0:T(8,128)(2,1)}), bf16[16,64,128]{2,1,0:T(8,128)(2,1)S(1)}, u32[]{:S(2)}, u32[]{:S(2)}) async-start(bf16[16,64,128]{2,1,0:T(8,128)(2,1)} %bitcast.159), calls=%async_computation.3 | async-start | bytes 524288 | tf_op jit(solution)/shard_map/all_to_all | solution.py:59

commit v15 on v14

--- a/solution.py
+++ b/solution.py
@@ -49,7 +49,7 @@
         projected = jnp.dot(normed_mine, qkv_mine, preferred_element_type=jnp.float32) + jnp.dot(
             normed_other, qkv_other, preferred_element_type=jnp.float32
         )
-        projected = unrotate(projected.astype(jnp.bfloat16), "dp")
+        projected = projected.astype(jnp.bfloat16)
         projected = jnp.transpose(
             projected.reshape(tok_rows, 3, HEADS, head_width), (2, 1, 3, 0)
         )
@@ -62,7 +62,7 @@
     return (current.astype(jnp.float32) + layer_scale * mixed).astype(jnp.bfloat16)
 
 
-def ring_gather(piece, axis, on_block, made_axis=1):
+def ring_gather(piece, axis, on_block):
     count = lax.axis_size(axis)
     right = [(i, (i + 1) % count) for i in range(count)]
     left = [(i, (i - 1) % count) for i in range(count)]
@@ -79,17 +79,12 @@
             k = 1 + step
             blocks[k], made[k] = backward, on_block(backward)
     blocks = lax.optimization_barrier(blocks)
-    if made_axis is None:
-        return jnp.concatenate(blocks, axis=1), made
-    return jnp.concatenate(blocks, axis=1), jnp.concatenate(made, axis=made_axis)
-
-
-def unrotate(rotated, axis, along=1):
-    count = lax.axis_size(axis)
-    cols = rotated.shape[along]
-    shift = lax.axis_index(axis) * (cols // count)
-    doubled = jnp.concatenate([rotated, rotated], axis=along)
-    return lax.dynamic_slice_in_dim(doubled, cols - shift, cols, axis=along)
+    index = lax.axis_index(axis)
+    rows, cols = piece.shape
+    whole = jnp.zeros((rows, cols * count), piece.dtype)
+    for k, block in enumerate(blocks):
+        whole = lax.dynamic_update_slice_in_dim(whole, block, ((index + k) % count) * cols, axis=1)
+    return whole, made
 
 
 def per_device(patches, lengths, norm_gain, norm_bias, w_qkv, w_out, out_bias, scale_gain):
@@ -111,7 +106,7 @@
     def on_block(block):
         return jnp.einsum("stk,kc->stc", both, block, preferred_element_type=jnp.float32)
 
-    qkv_mine, made = ring_gather(rows_mine, "dp", on_block, made_axis=None)
+    qkv_mine, made = ring_gather(rows_mine, "dp", on_block)
     dp_count = lax.axis_size("dp")
     dp_index = lax.axis_index("dp")
     shard_width = made[0].shape[-1]

time: 154 us -> 156 us (1.013)
  matrix products: 17.2 us -> 20 us
  waiting for transfers between devices: 50.6 us -> 48.7 us
    dynamic_update_slice x0 -> x8, local copies, waits for them, and re-layouts: none -> 10.7 us  [ring_gather(): lax.dynamic_update_slice_in_dim(whole, block, (index + k) % count * cols,...]
    unnamed x41 -> x32, local copies, waits for them, and re-layouts: 10 us -> 0.08 us
    dot_general x1, matrix products: 0.58 us -> 3.43 us  [sublayer(): jnp.dot(normed_mine, qkv_mine, preferred_element_type=jnp.float32)]
    broadcast_in_dim x0 -> x1, local copies, waits for them, and re-layouts: none -> 2.02 us  [ring_gather(): whole = jnp.zeros((rows, cols * count), piece.dtype)]
    ppermute x1, waiting for transfers between devices: 1.86 us -> 0.01 us  [per_device(): partial_other = lax.ppermute(partial[1], 'ctx', sibling)]
  transfers between devices with their start and end apart: 13 -> 13, of which waited for: 10 -> 9; matrix products, arithmetic and copies ran while one was open for 19% -> 20% of each run, Pallas kernels for 0% -> 0%
where the time goes in v15:
time: 156 us; the launch traced here: 155 us
  waiting for transfers between devices  48.7 us (31%)
  blocking collectives  27.2 us (17%)
  starting transfers between devices  23.8 us (15%)
  matrix products  20 us (13%)
  local copies, waits for them, and re-layouts  19.9 us (13%)
  other arithmetic  14.4 us (9%)
    ppermute x4, waiting for transfers between devices, ring_gather(): forward = lax.ppermute(forward, axis, right)  23 us
    all_to_all x1, blocking collectives, sublayer(): gathered = lax.all_to_all(projected, 'ctx', 0, 3, tiled=True)  16.5 us
    ppermute x3, starting transfers between devices, ring_gather(): backward = lax.ppermute(backward, axis, left)  13 us
    dynamic_update_slice x8, local copies, waits for them, and re-layouts, ring_gather(): lax.dynamic_update_slice_in_dim(whole, block, (index + k) % count * cols,...  10.7 us
    all_to_all x1, blocking collectives, sublayer(): lax.all_to_all(context, 'ctx', 0, 0, tiled=True).reshape(width, tok_rows)  10.6 us
    convert_element_type x2, other arithmetic, head_attention(): weights.astype(jnp.bfloat16)  10.2 us
    ppermute x1, waiting for transfers between devices, per_device(): current = lax.ppermute(produced, 'pipe', pairs)  9.86 us
    all_to_all x1, waiting for transfers between devices, sublayer(): lax.all_to_all(context, 'ctx', 0, 0, tiled=True).reshape(width, tok_rows)  7.98 us
  transfers between devices with their start and end apart: 13, of which 9 were waited for; matrix products, arithmetic and copies ran while one was open for 20% of the time, Pallas kernels for 0%

profile of v15, /device:TPU:4, one launch (start us, length us, event | category | flops | bytes accessed | tf_op | source)
XLA Modules:
  0.0 155.2 jit_solution(8717360615541721162)
XLA Ops:
  0.0 1.2 dynamic-slice_bitcast_fusion
  1.2 5.9 %collective-permute-start.1 = (bf16[512,384]{1,0:T(8,128)(2,1)S(1)}, bf16[512,384]{1,0:T(8,128)(2,1)S(1)}, u32[]{:S(2)}, u32[]{:S(2)}) collective-permute-start(bf16[512,384]{1,0:T(8,128)(2,1)S(1)} %dynamic-slice_bitcast_fusion), channel_id=1, source_target_pairs={{0,7},{1,0},{2,1},{3,2},{4,3},{5,4},{6,5},{7,6},{8,15},{9,8},{10,9... | collective-permute-start | bytes 1179656 | tf_op jit(solution)/shard_map/ppermute | solution.py:78
  7.1 1.1 convert_reduce_fusion.1
  8.2 1.2 fusion.54
  9.4 9.5 %collective-permute-done.4 = bf16[512,384]{1,0:T(8,128)(2,1)S(1)} collective-permute-done((bf16[512,384]{1,0:T(8,128)(2,1)S(1)}, bf16[512,384]{1,0:T(8,128)(2,1)S(1)}, u32[]{:S(2)}, u32[]{:S(2)}) %collective-permute-start.4) | collective-permute-done | bytes 393248 | tf_op jit(solution)/shard_map/ppermute | solution.py:74
  18.9 1.2 fusion.57
  20.3 3.3 %collective-permute-start.2 = (bf16[512,384]{1,0:T(8,128)(2,1)S(1)}, bf16[512,384]{1,0:T(8,128)(2,1)}, u32[]{:S(2)}, u32[]{:S(2)}) collective-permute-start(bf16[512,384]{1,0:T(8,128)(2,1)S(1)} %collective-permute-done.1), channel_id=1, source_target_pairs={{0,7},{1,0},{2,1},{3,2},{4,3},{5,4},{6,5},{7,6},{8,15},{9,8},{10,9... | collective-permute-start | bytes 1179656 | tf_op jit(solution)/shard_map/ppermute | solution.py:78
  23.6 6.3 %collective-permute-done.5 = bf16[512,384]{1,0:T(8,128)(2,1)S(1)} collective-permute-done((bf16[512,384]{1,0:T(8,128)(2,1)S(1)}, bf16[512,384]{1,0:T(8,128)(2,1)S(1)}, u32[]{:S(2)}, u32[]{:S(2)}) %collective-permute-start.5) | collective-permute-done | bytes 393248 | tf_op jit(solution)/shard_map/ppermute | solution.py:74
  29.9 1.1 dynamic-slice_bitcast_fusion.1
  30.9 0.2 broadcast_in_dim.47
  31.1 0.3 convolution_dynamic-update-slice_fusion.7
  31.5 1.1 collective-permute-done.2
  32.6 3.8 %collective-permute-start.3 = (bf16[512,384]{1,0:T(8,128)(2,1)}, bf16[512,384]{1,0:T(8,128)(2,1)S(1)}, u32[]{:S(2)}, u32[]{:S(2)}) collective-permute-start(bf16[512,384]{1,0:T(8,128)(2,1)} %collective-permute-done.2), channel_id=1, source_target_pairs={{0,7},{1,0},{2,1},{3,2},{4,3},{5,4},{6,5},{7,6},{8,15},{9,8},{10,9... | collective-permute-start | bytes 1179656 | tf_op jit(solution)/shard_map/ppermute | solution.py:78
  36.4 0.3 convolution_dynamic-update-slice_fusion.6
  36.7 3.2 %collective-permute-done.6 = bf16[512,384]{1,0:T(8,128)(2,1)S(1)} collective-permute-done((bf16[512,384]{1,0:T(8,128)(2,1)S(1)}, bf16[512,384]{1,0:T(8,128)(2,1)S(1)}, u32[]{:S(2)}, u32[]{:S(2)}) %collective-permute-start.6) | collective-permute-done | bytes 393248 | tf_op jit(solution)/shard_map/ppermute | solution.py:74
  39.9 1.5 convolution_dynamic-update-slice_fusion.5
  41.4 3.4 %collective-permute-done.3 = bf16[512,384]{1,0:T(8,128)(2,1)S(1)} collective-permute-done((bf16[512,384]{1,0:T(8,128)(2,1)}, bf16[512,384]{1,0:T(8,128)(2,1)S(1)}, u32[]{:S(2)}, u32[]{:S(2)}) %collective-permute-start.3) | collective-permute-done | bytes 393248 | tf_op jit(solution)/shard_map/ppermute | solution.py:78
  44.8 0.3 convolution_dynamic-update-slice_fusion.4
  45.2 4.0 %collective-permute-done.7 = bf16[512,384]{1,0:T(8,128)(2,1)S(1)} collective-permute-done((bf16[512,384]{1,0:T(8,128)(2,1)S(1)}, bf16[512,384]{1,0:T(8,128)(2,1)S(1)}, u32[]{:S(2)}, u32[]{:S(2)}) %collective-permute-start.7) | collective-permute-done | bytes 393248 | tf_op jit(solution)/shard_map/ppermute | solution.py:74
  49.2 0.3 convolution_dynamic-update-slice_fusion.3
  49.5 0.3 convolution_dynamic-update-slice_fusion.2
  49.8 0.3 convolution_dynamic-update-slice_fusion.1
  50.2 0.3 convolution_dynamic-update-slice_fusion
  51.4 2.0 %broadcast_in_dim.51 = bf16[512,3072]{1,0:T(8,128)(2,1)} broadcast(bf16[]{:T(256)} %constant.121.clone.1), dimensions={} | broadcast | bytes 3145730 | tf_op jit(solution)/shard_map/broadcast_in_dim | solution.py:84
  53.4 0.8 constant_dynamic-update-slice_fusion.7
  54.2 0.2 fusion.12
  54.4 0.9 copy.34
  55.3 5.3 %all-to-all-start = ((bf16[16,3,64,128]{3,2,1,0:T(8,128)(2,1)}), bf16[16,3,64,128]{3,2,1,0:T(8,128)(2,1)S(1)}, u32[]{:S(2)}, u32[]{:S(2)}) async-start(bf16[16,3,64,128]{3,2,1,0:T(8,128)(2,1)} %copy.34), calls=%async_computation | async-start | bytes 1572864 | tf_op jit(solution)/shard_map/all_to_all | solution.py:56
  60.7 1.9 %constant_dynamic-update-slice_fusion.6 = bf16[512,3072]{1,0:T(8,128)(2,1)} fusion(bf16[512,3072]{1,0:T(8,128)(2,1)} %constant_dynamic-update-slice_fusion.7, bf16[512,384]{1,0:T(8,128)(2,1)} %copy-done.4, s32[]{:T(128)S(6)} %select_n.125), kind=kLoop, calls=%fused_computation.99 | loop fusion | bytes 786436 | tf_op jit(solution)/shard_map/dynamic_update_slice | solution.py:86
  62.6 1.9 %constant_dynamic-update-slice_fusion.5 = bf16[512,3072]{1,0:T(8,128)(2,1)} fusion(bf16[512,3072]{1,0:T(8,128)(2,1)} %constant_dynamic-update-slice_fusion.6, bf16[512,384]{1,0:T(8,128)(2,1)} %collective-permute-done.2, s32[]{:T(128)S(6)} %select_n.127), kind=kLoop, calls=%fused_computation.98 | loop fusion | bytes 786436 | tf_op jit(solution)/shard_map/dynamic_update_slice | solution.py:86
  64.5 1.8 %constant_dynamic-update-slice_fusion.4 = bf16[512,3072]{1,0:T(8,128)(2,1)} fusion(bf16[512,3072]{1,0:T(8,128)(2,1)} %constant_dynamic-update-slice_fusion.5, bf16[512,384]{1,0:T(8,128)(2,1)} %copy-done.9, s32[]{:T(128)S(6)} %select_n.129), kind=kLoop, calls=%fused_computation.97 | loop fusion | bytes 786436 | tf_op jit(solution)/shard_map/dynamic_update_slice | solution.py:86
  66.3 1.8 %constant_dynamic-update-slice_fusion.3 = bf16[512,3072]{1,0:T(8,128)(2,1)} fusion(bf16[512,3072]{1,0:T(8,128)(2,1)} %constant_dynamic-update-slice_fusion.4, bf16[512,384]{1,0:T(8,128)(2,1)} %copy-done.10, s32[]{:T(128)S(6)} %select_n.131), kind=kLoop, calls=%fused_computation.96 | loop fusion | bytes 786436 | tf_op jit(solution)/shard_map/dynamic_update_slice | solution.py:86
  68.1 0.8 constant_dynamic-update-slice_fusion.2
  69.0 0.8 constant_dynamic-update-slice_fusion.1
  69.8 0.8 constant_dynamic-update-slice_fusion
  70.6 0.4 collective-permute-start.10
  71.0 3.4 %all-to-all-done = bf16[16,3,64,128]{3,2,1,0:T(8,128)(2,1)S(1)} async-done(((bf16[16,3,64,128]{3,2,1,0:T(8,128)(2,1)}), bf16[16,3,64,128]{3,2,1,0:T(8,128)(2,1)S(1)}, u32[]{:S(2)}, u32[]{:S(2)}) %all-to-all-start) | async-done | bytes 786464 | tf_op jit(solution)/shard_map/all_to_all | solution.py:56
  74.4 0.2 copy.36
  74.6 0.2 copy.37
  74.8 2.8 %select_reduce_fusion.1 = (f32[2048]{0:T(1024)S(1)}, f32[2048,2048]{0,1:T(8,128)S(1)}) fusion(pred[2048]{0:T(1024)(128)(4,1)S(1)} %iota_compare_fusion, bf16[8,8,16,128]{3,2,1,0:T(8,128)(2,1)S(1)} %bitcast.171, bf16[8,8,16,128]{3,2,1,0:T(8,128)(2,1)S(1)} %bitcast.169), kind=kOutput, calls=%fused_computation.3 | convolution fusion | flops 549451776 | bytes 17311744 | tf_op jit(solution)/shard_map/dq,dk->qk/dot_general | solution.py:25
  77.6 5.1 %fusion = (bf16[2048,2048]{0,1:T(8,128)(2,1)S(1)}, f32[2048]{0:T(1024)S(1)}) fusion(f32[2048,2048]{0,1:T(8,128)S(1)} %get-tuple-element.40, f32[2048]{0:T(1024)S(1)} %get-tuple-element.39, pred[2048]{0:T(1024)(128)(4,1)S(1)} %iota_compare_fusion), kind=kLoop, calls=%fused_computation.4 | loop fusion | flops 20969472 | bytes 25184256 | tf_op jit(solution)/shard_map/convert_element_type | solution.py:32
  82.7 0.2 copy.35
  82.9 1.6 %fusion.44 = bf16[8,16,8,128]{3,2,1,0:T(8,128)(2,1)S(1)} fusion(bf16[2048,2048]{0,1:T(8,128)(2,1)S(1)} %get-tuple-element.17, bf16[8,8,16,128]{3,2,1,0:T(8,128)(2,1)S(1)} %bitcast.167, f32[2048]{0:T(1024)S(1)} %get-tuple-element.18), kind=kOutput, calls=%fused_computation.41 | convolution fusion | flops 537133056 | bytes 8921088 | tf_op jit(solution)/shard_map/qk,dk->dq/dot_general | solution.py:34
  84.6 10.6 %all_to_all.40 = bf16[16,64,128]{2,1,0:T(8,128)(2,1)S(1)} all-to-all(bf16[16,64,128]{2,1,0:T(8,128)(2,1)S(1)} %bitcast.173), channel_id=1, replica_groups=mesh['pipe'=2,'ctx'=16,'dp'=8] {'ctx'}, dimensions={0} | all-to-all | bytes 524288 | tf_op jit(solution)/shard_map/all_to_all | solution.py:59
  95.3 0.5 fusion.34
  95.7 1.3 collective-permute-start.9
  97.1 9.9 %collective-permute-done.9 = bf16[128,1024]{1,0:T(8,128)(2,1)S(1)} collective-permute-done((bf16[128,1024]{1,0:T(8,128)(2,1)S(1)}, bf16[128,1024]{1,0:T(8,128)(2,1)S(1)}, u32[]{:S(2)}, u32[]{:S(2)}) %collective-permute-start.9) | collective-permute-done | bytes 262176 | tf_op jit(solution)/shard_map/ppermute | solution.py:130
  106.9 0.1 convert_reduce_fusion
  107.0 0.2 fusion.50
  107.3 0.2 fusion.53
  107.5 2.5 %fusion.81 = f32[128,3072]{1,0:T(8,128)S(1)} fusion(bf16[512,3072]{1,0:T(8,128)(2,1)} %collective-permute-done.10, bf16[128,1024]{1,0:T(8,128)(2,1)S(1)} %fusion.53, s32[]{:T(128)S(6)} %select_n.140), kind=kOutput, calls=%fused_computation.86 | convolution fusion | flops 402653184 | bytes 4849668 | tf_op jit(solution)/shard_map/dot_general | solution.py:49
  110.0 3.4 %fusion.4 = bf16[128,3072]{1,0:T(8,128)(2,1)} fusion(f32[128,3072]{1,0:T(8,128)S(1)} %fusion.81, bf16[512,3072]{1,0:T(8,128)(2,1)} %constant_dynamic-update-slice_fusion, bf16[128,1024]{1,0:T(8,128)(2,1)S(1)} %fusion.53, s32[]{:T(128)S(6)} %select_n.121), kind=kOutput, calls=%fused_computation.9 | convolution fusion | flops 403439616 | bytes 5636100 | tf_op jit(solution)/shard_map/dot_general | solution.py:49
  113.5 1.5 copy.39
  115.0 16.5 %all_to_all.41 = bf16[16,3,64,128]{3,2,1,0:T(8,128)(2,1)S(1)} all-to-all(bf16[16,3,64,128]{3,2,1,0:T(8,128)(2,1)S(1)} %copy.40), channel_id=1, replica_groups=mesh['pipe'=2,'ctx'=16,'dp'=8] {'ctx'}, dimensions={0} | all-to-all | bytes 1572864 | tf_op jit(solution)/shard_map/all_to_all | solution.py:56
  131.6 0.2 copy.42
  131.8 0.2 copy.43
  132.0 2.8 %select_reduce_fusion = (f32[2048]{0:T(1024)S(1)}, f32[2048,2048]{0,1:T(8,128)S(1)}) fusion(pred[2048]{0:T(1024)(128)(4,1)S(1)} %iota_compare_fusion, bf16[8,8,16,128]{3,2,1,0:T(8,128)(2,1)S(1)} %bitcast.172, bf16[8,8,16,128]{3,2,1,0:T(8,128)(2,1)S(1)} %bitcast.170), kind=kOutput, calls=%fused_computation.1 | convolution fusion | flops 549451776 | bytes 17311744 | tf_op jit(solution)/shard_map/dq,dk->qk/dot_general | solution.py:25
  134.8 5.1 %fusion.2 = (bf16[2048,2048]{0,1:T(8,128)(2,1)S(1)}, f32[2048]{0:T(1024)S(1)}) fusion(f32[2048,2048]{0,1:T(8,128)S(1)} %get-tuple-element.42, f32[2048]{0:T(1024)S(1)} %get-tuple-element.41, pred[2048]{0:T(1024)(128)(4,1)S(1)} %iota_compare_fusion), kind=kLoop, calls=%fused_computation.6 | loop fusion | flops 20969472 | bytes 25184256 | tf_op jit(solution)/shard_map/convert_element_type | solution.py:32
  139.9 0.2 copy.41
  140.1 1.6 %fusion.43 = bf16[8,16,8,128]{3,2,1,0:T(8,128)(2,1)S(1)} fusion(bf16[2048,2048]{0,1:T(8,128)(2,1)S(1)} %get-tuple-element.27, bf16[8,8,16,128]{3,2,1,0:T(8,128)(2,1)S(1)} %bitcast.168, f32[2048]{0:T(1024)S(1)} %get-tuple-element.28), kind=kOutput, calls=%fused_computation.40 | convolution fusion | flops 537133056 | bytes 8921088 | tf_op jit(solution)/shard_map/qk,dk->dq/dot_general | solution.py:34
  141.7 0.8 copy.95
  142.4 3.5 %all-to-all-start.3 = ((bf16[16,64,128]{2,1,0:T(8,128)(2,1)}), bf16[16,64,128]{2,1,0:T(8,128)(2,1)S(1)}, u32[]{:S(2)}, u32[]{:S(2)}) async-start(bf16[16,64,128]{2,1,0:T(8,128)(2,1)} %bitcast.159), calls=%async_computation.3 | async-start | bytes 524288 | tf_op jit(solution)/shard_map/all_to_all | solution.py:59
  146.0 8.0 %all-to-all-done.3 = bf16[16,64,128]{2,1,0:T(8,128)(2,1)S(1)} async-done(((bf16[16,64,128]{2,1,0:T(8,128)(2,1)}), bf16[16,64,128]{2,1,0:T(8,128)(2,1)S(1)}, u32[]{:S(2)}, u32[]{:S(2)}) %all-to-all-start.3) | async-done | bytes 262176 | tf_op jit(solution)/shard_map/all_to_all | solution.py:59
  154.0 1.2 fusion.40
  (53 shorter events, 0.7 us)
Async XLA Ops:
  0.0 95.2 %copy-start = (bf16[1,1024,1024]{2,1,0:T(8,128)(2,1)S(1)}, bf16[1,1024,1024]{2,1,0:T(8,128)(2,1)}, u32[]{:S(2)}) copy-start(bf16[1,1024,1024]{2,1,0:T(8,128)(2,1)} %param.13) | copy-start | bytes 6291460
  1.2 19.1 %copy-start.5 = (bf16[512,384]{1,0:T(8,128)(2,1)}, bf16[512,384]{1,0:T(8,128)(2,1)S(1)}, u32[]{:S(2)}) copy-start(bf16[512,384]{1,0:T(8,128)(2,1)S(1)} %dynamic-slice_bitcast_fusion) | copy-start | bytes 1179652
  1.2 19.0 %collective-permute-start.1 = (bf16[512,384]{1,0:T(8,128)(2,1)S(1)}, bf16[512,384]{1,0:T(8,128)(2,1)S(1)}, u32[]{:S(2)}, u32[]{:S(2)}) collective-permute-start(bf16[512,384]{1,0:T(8,128)(2,1)S(1)} %dynamic-slice_bitcast_fusion), channel_id=1, source_target_pairs={{0,7},{1,0},{2,1},{3,2},{4,3},{5,4},{6,5},{7,6},{8,15},{9,8},{10,9... | collective-permute-start | bytes 1179656 | tf_op jit(solution)/shard_map/ppermute | solution.py:78
  7.1 11.8 %collective-permute-start.4 = (bf16[512,384]{1,0:T(8,128)(2,1)S(1)}, bf16[512,384]{1,0:T(8,128)(2,1)S(1)}, u32[]{:S(2)}, u32[]{:S(2)}) collective-permute-start(bf16[512,384]{1,0:T(8,128)(2,1)S(1)} %dynamic-slice_bitcast_fusion), channel_id=1, source_target_pairs={{0,1},{1,2},{2,3},{3,4},{4,5},{5,6},{6,7},{7,0},{8,9},{9,10},{10,1... | collective-permute-start | bytes 1179656 | tf_op jit(solution)/shard_map/ppermute | solution.py:74
  18.9 10.9 %collective-permute-start.5 = (bf16[512,384]{1,0:T(8,128)(2,1)S(1)}, bf16[512,384]{1,0:T(8,128)(2,1)S(1)}, u32[]{:S(2)}, u32[]{:S(2)}) collective-permute-start(bf16[512,384]{1,0:T(8,128)(2,1)S(1)} %collective-permute-done.4), channel_id=1, source_target_pairs={{0,1},{1,2},{2,3},{3,4},{4,5},{5,6},{6,7},{7,0},{8,9},{9,10},{10,1... | collective-permute-start | bytes 1179656 | tf_op jit(solution)/shard_map/ppermute | solution.py:74
  20.1 9.7 %collective-permute-start = (bf16[128,1024]{1,0:T(8,128)(2,1)S(1)}, bf16[128,1024]{1,0:T(8,128)(2,1)}, u32[]{:S(2)}, u32[]{:S(2)}) collective-permute-start(bf16[128,1024]{1,0:T(8,128)(2,1)S(1)} %fusion.57), channel_id=1, source_target_pairs={{0,8},{8,0},{16,24},{24,16},{32,40},{40,32},{48,56},{56,48},{64,72... | collective-permute-start | bytes 786440 | tf_op jit(solution)/shard_map/ppermute | solution.py:100
  20.3 21.1 %copy-start.4 = (bf16[512,384]{1,0:T(8,128)(2,1)}, bf16[512,384]{1,0:T(8,128)(2,1)S(1)}, u32[]{:S(2)}) copy-start(bf16[512,384]{1,0:T(8,128)(2,1)S(1)} %collective-permute-done.1) | copy-start | bytes 1179652
  20.3 12.3 %collective-permute-start.2 = (bf16[512,384]{1,0:T(8,128)(2,1)S(1)}, bf16[512,384]{1,0:T(8,128)(2,1)}, u32[]{:S(2)}, u32[]{:S(2)}) collective-permute-start(bf16[512,384]{1,0:T(8,128)(2,1)S(1)} %collective-permute-done.1), channel_id=1, source_target_pairs={{0,7},{1,0},{2,1},{3,2},{4,3},{5,4},{6,5},{7,6},{8,15},{9,8},{10,9... | collective-permute-start | bytes 1179656 | tf_op jit(solution)/shard_map/ppermute | solution.py:78
  23.6 7.6 %copy-start.11 = (bf16[1,1024,384]{2,1,0:T(8,128)(2,1)S(1)}, bf16[1,1024,384]{2,1,0:T(8,128)(2,1)}, u32[]{:S(2)}) copy-start(bf16[1,1024,384]{2,1,0:T(8,128)(2,1)} %param.12) | copy-start | bytes 2359300
  29.9 20.0 %copy-start.2 = (bf16[512,384]{1,0:T(8,128)(2,1)}, bf16[512,384]{1,0:T(8,128)(2,1)S(1)}, u32[]{:S(2)}) copy-start(bf16[512,384]{1,0:T(8,128)(2,1)S(1)} %collective-permute-done.5) | copy-start | bytes 1179652
  29.9 10.1 %collective-permute-start.6 = (bf16[512,384]{1,0:T(8,128)(2,1)S(1)}, bf16[512,384]{1,0:T(8,128)(2,1)S(1)}, u32[]{:S(2)}, u32[]{:S(2)}) collective-permute-start(bf16[512,384]{1,0:T(8,128)(2,1)S(1)} %collective-permute-done.5), channel_id=1, source_target_pairs={{0,1},{1,2},{2,3},{3,4},{4,5},{5,6},{6,7},{7,0},{8,9},{9,10},{10,1... | collective-permute-start | bytes 1179656 | tf_op jit(solution)/shard_map/ppermute | solution.py:74
  32.6 12.3 %collective-permute-start.3 = (bf16[512,384]{1,0:T(8,128)(2,1)}, bf16[512,384]{1,0:T(8,128)(2,1)S(1)}, u32[]{:S(2)}, u32[]{:S(2)}) collective-permute-start(bf16[512,384]{1,0:T(8,128)(2,1)} %collective-permute-done.2), channel_id=1, source_target_pairs={{0,7},{1,0},{2,1},{3,2},{4,3},{5,4},{6,5},{7,6},{8,15},{9,8},{10,9... | collective-permute-start | bytes 1179656 | tf_op jit(solution)/shard_map/ppermute | solution.py:78
  39.9 10.6 %copy-start.7 = (bf16[512,384]{1,0:T(8,128)(2,1)}, bf16[512,384]{1,0:T(8,128)(2,1)S(1)}, u32[]{:S(2)}) copy-start(bf16[512,384]{1,0:T(8,128)(2,1)S(1)} %collective-permute-done.6) | copy-start | bytes 1179652
  39.9 9.2 %collective-permute-start.7 = (bf16[512,384]{1,0:T(8,128)(2,1)S(1)}, bf16[512,384]{1,0:T(8,128)(2,1)S(1)}, u32[]{:S(2)}, u32[]{:S(2)}) collective-permute-start(bf16[512,384]{1,0:T(8,128)(2,1)S(1)} %collective-permute-done.6), channel_id=1, source_target_pairs={{0,1},{1,2},{2,3},{3,4},{4,5},{5,6},{6,7},{7,0},{8,9},{9,10},{10,1... | collective-permute-start | bytes 1179656 | tf_op jit(solution)/shard_map/ppermute | solution.py:74
  44.8 5.3 %copy-start.9 = (bf16[512,384]{1,0:T(8,128)(2,1)}, bf16[512,384]{1,0:T(8,128)(2,1)S(1)}, u32[]{:S(2)}) copy-start(bf16[512,384]{1,0:T(8,128)(2,1)S(1)} %collective-permute-done.3) | copy-start | bytes 1179652
  49.1 1.0 copy-start.10
  50.5 2.9 %copy-start.6 = (bf16[512,384]{1,0:T(8,128)(2,1)S(1)}, bf16[512,384]{1,0:T(8,128)(2,1)}, u32[]{:S(2)}) copy-start(bf16[512,384]{1,0:T(8,128)(2,1)} %copy-done.5) | copy-start | bytes 1179652
  50.6 3.6 %collective-permute-start.8 = (f32[128,3072]{0,1:T(8,128)S(1)}, f32[128,3072]{0,1:T(8,128)S(1)}, u32[]{:S(2)}, u32[]{:S(2)}) collective-permute-start(f32[128,3072]{0,1:T(8,128)S(1)} %slice_bitcast_fusion), channel_id=1, source_target_pairs={{0,8},{8,0},{16,24},{24,16},{32,40},{40,32},{48,56},{56,48},{64,72... | collective-permute-start | bytes 4718600 | tf_op jit(solution)/shard_map/ppermute | solution.py:118
  55.3 19.0 %all-to-all-start = ((bf16[16,3,64,128]{3,2,1,0:T(8,128)(2,1)}), bf16[16,3,64,128]{3,2,1,0:T(8,128)(2,1)S(1)}, u32[]{:S(2)}, u32[]{:S(2)}) async-start(bf16[16,3,64,128]{3,2,1,0:T(8,128)(2,1)} %copy.34), calls=%async_computation | async-start | bytes 1572864 | tf_op jit(solution)/shard_map/all_to_all | solution.py:56
  60.7 7.5 %copy-start.8 = (bf16[512,384]{1,0:T(8,128)(2,1)S(1)}, bf16[512,384]{1,0:T(8,128)(2,1)}, u32[]{:S(2)}) copy-start(bf16[512,384]{1,0:T(8,128)(2,1)} %copy-done.7) | copy-start | bytes 1179652
  60.7 8.3 %copy-start.3 = (bf16[512,384]{1,0:T(8,128)(2,1)S(1)}, bf16[512,384]{1,0:T(8,128)(2,1)}, u32[]{:S(2)}) copy-start(bf16[512,384]{1,0:T(8,128)(2,1)} %copy-done.2) | copy-start | bytes 1179652
  70.6 36.9 %collective-permute-start.10 = (bf16[512,3072]{1,0:T(8,128)(2,1)}, bf16[512,3072]{1,0:T(8,128)(2,1)}, u32[]{:S(2)}, u32[]{:S(2)}) collective-permute-start(bf16[512,3072]{1,0:T(8,128)(2,1)} %constant_dynamic-update-slice_fusion), channel_id=1, source_target_pairs={{0,8},{8,0},{16,24},{24,16},{32,40},{40,32},{48,56},{56,48},{64,72... | collective-permute-start | bytes 9437192 | tf_op jit(solution)/shard_map/ppermute | solution.py:121
  82.9 12.3 %copy-start.1 = (bf16[1,1,128,1024]{3,2,1,0:T(8,128)(2,1)S(1)}, bf16[1,1,128,1024]{3,2,1,0:T(8,128)(2,1)}, u32[]{:S(2)}) copy-start(bf16[1,1,128,1024]{3,2,1,0:T(8,128)(2,1)} %param.8) | copy-start | bytes 786436
  82.9 12.3 %copy-start.14 = (f32[1,1024]{1,0:T(1,128)S(1)}, f32[1,1024]{1,0:T(1,128)}, u32[]{:S(2)}) copy-start(f32[1,1024]{1,0:T(1,128)} %param.14) | copy-start | bytes 12292
  82.9 12.3 %copy-start.15 = (f32[1,1024]{1,0:T(1,128)S(1)}, f32[1,1024]{1,0:T(1,128)}, u32[]{:S(2)}) copy-start(f32[1,1024]{1,0:T(1,128)} %param.15) | copy-start | bytes 12292
  84.5 22.8 %copy-start.12 = (f32[1,1024]{1,0:T(1,128)S(1)}, f32[1,1024]{1,0:T(1,128)}, u32[]{:S(2)}) copy-start(f32[1,1024]{1,0:T(1,128)} %param.11) | copy-start | bytes 12292
  84.5 22.8 %copy-start.13 = (f32[1,1024]{1,0:T(1,128)S(1)}, f32[1,1024]{1,0:T(1,128)}, u32[]{:S(2)}) copy-start(f32[1,1024]{1,0:T(1,128)} %param.10) | copy-start | bytes 12292
  95.7 11.2 %collective-permute-start.9 = (bf16[128,1024]{1,0:T(8,128)(2,1)S(1)}, bf16[128,1024]{1,0:T(8,128)(2,1)S(1)}, u32[]{:S(2)}, u32[]{:S(2)}) collective-permute-start(bf16[128,1024]{1,0:T(8,128)(2,1)S(1)} %fusion.34), channel_id=1, source_target_pairs={{0,128},{1,129},{2,130},{3,131},{4,132},{5,133},{6,134},{7,135},{8... | collective-permute-start | bytes 786440 | tf_op jit(solution)/shard_map/ppermute | solution.py:130
  142.4 11.5 %all-to-all-start.3 = ((bf16[16,64,128]{2,1,0:T(8,128)(2,1)}), bf16[16,64,128]{2,1,0:T(8,128)(2,1)S(1)}, u32[]{:S(2)}, u32[]{:S(2)}) async-start(bf16[16,64,128]{2,1,0:T(8,128)(2,1)} %bitcast.159), calls=%async_computation.3 | async-start | bytes 524288 | tf_op jit(solution)/shard_map/all_to_all | solution.py:59

commit v16 on v14

--- a/solution.py
+++ b/solution.py
@@ -49,10 +49,12 @@
         projected = jnp.dot(normed_mine, qkv_mine, preferred_element_type=jnp.float32) + jnp.dot(
             normed_other, qkv_other, preferred_element_type=jnp.float32
         )
-        projected = unrotate(projected.astype(jnp.bfloat16), "dp")
-        projected = jnp.transpose(
-            projected.reshape(tok_rows, 3, HEADS, head_width), (2, 1, 3, 0)
-        )
+        segments = jnp.transpose(projected.astype(jnp.bfloat16)).reshape(-1, head_width, tok_rows)
+        count = segments.shape[0]
+        shift = lax.axis_index("dp") * (count // lax.axis_size("dp"))
+        wanted = jnp.arange(HEADS)[:, None] + HEADS * jnp.arange(3)[None, :]
+        projected = jnp.take(segments, ((wanted - shift) % count).reshape(-1), axis=0, mode="clip")
+        projected = projected.reshape(HEADS, 3, head_width, tok_rows)
     gathered = lax.all_to_all(projected, "ctx", 0, 3, tiled=True)
     context = head_attention(gathered[0], length, head_width ** (-0.5))
     context = jnp.transpose(context.reshape(head_width, ctx_count, tok_rows), (1, 0, 2))

time: 154 us -> 156 us (1.013)
  blocking collectives: 27.2 us -> 17.2 us
  waiting for transfers between devices: 50.6 us -> 58.5 us
  starting transfers between devices: 23.7 us -> 27.2 us
    all_to_all x1 -> x0, blocking collectives: 10.6 us -> none  [sublayer(): lax.all_to_all(context, 'ctx', 0, 0, tiled=True).reshape(width, tok_rows)]
    all_to_all x1 -> x2, waiting for transfers between devices: 7.98 us -> 15.8 us  [sublayer(): lax.all_to_all(context, 'ctx', 0, 0, tiled=True).reshape(width, tok_rows)]
    all_to_all x1 -> x2, starting transfers between devices: 3.53 us -> 7.07 us  [sublayer(): lax.all_to_all(context, 'ctx', 0, 0, tiled=True).reshape(width, tok_rows)]
    gather x0 -> x1, local copies, waits for them, and re-layouts: none -> 1.58 us  [sublayer(): jnp.take(segments, ((wanted - shift) % count).reshape(-1), axis=0, mode='...]
  transfers between devices with their start and end apart: 13 -> 14, of which waited for: 10 -> 11; matrix products, arithmetic and copies ran while one was open for 19% -> 19% of each run, Pallas kernels for 0% -> 0%
where the time goes in v16:
time: 156 us; the launch traced here: 155 us
  waiting for transfers between devices  58.5 us (38%)
  starting transfers between devices  27.2 us (17%)
  local copies, waits for them, and re-layouts  18.7 us (12%)
  matrix products  18.2 us (12%)
  blocking collectives  17.2 us (11%)
  other arithmetic  14.5 us (9%)
    ppermute x4, waiting for transfers between devices, ring_gather(): forward = lax.ppermute(forward, axis, right)  23 us
    all_to_all x1, blocking collectives, sublayer(): gathered = lax.all_to_all(projected, 'ctx', 0, 3, tiled=True)  17.2 us
    all_to_all x2, waiting for transfers between devices, sublayer(): lax.all_to_all(context, 'ctx', 0, 0, tiled=True).reshape(width, tok_rows)  15.8 us
    ppermute x3, starting transfers between devices, ring_gather(): backward = lax.ppermute(backward, axis, left)  13 us
    convert_element_type x2, other arithmetic, head_attention(): weights.astype(jnp.bfloat16)  10.2 us
    unnamed x41, local copies, waits for them, and re-layouts  9.95 us
    ppermute x1, waiting for transfers between devices, per_device(): current = lax.ppermute(produced, 'pipe', pairs)  9.85 us
    all_to_all x2, starting transfers between devices, sublayer(): lax.all_to_all(context, 'ctx', 0, 0, tiled=True).reshape(width, tok_rows)  7.07 us
  transfers between devices with their start and end apart: 14, of which 11 were waited for; matrix products, arithmetic and copies ran while one was open for 19% of the time, Pallas kernels for 0%

profile of v16, /device:TPU:4, one launch (start us, length us, event | category | flops | bytes accessed | tf_op | source)
XLA Modules:
  0.0 155.5 jit_solution(4617193459348525053)
XLA Ops:
  0.0 1.2 dynamic-slice_bitcast_fusion
  1.2 5.9 %collective-permute-start.1 = (bf16[512,384]{1,0:T(8,128)(2,1)S(1)}, bf16[512,384]{1,0:T(8,128)(2,1)S(1)}, u32[]{:S(2)}, u32[]{:S(2)}) collective-permute-start(bf16[512,384]{1,0:T(8,128)(2,1)S(1)} %dynamic-slice_bitcast_fusion), channel_id=1, source_target_pairs={{0,7},{1,0},{2,1},{3,2},{4,3},{5,4},{6,5},{7,6},{8,15},{9,8},{10,9... | collective-permute-start | bytes 1179656 | tf_op jit(solution)/shard_map/ppermute | solution.py:80
  7.1 1.1 convert_reduce_fusion.1
  8.2 1.2 fusion.54
  9.4 9.5 %collective-permute-done.4 = bf16[512,384]{1,0:T(8,128)(2,1)S(1)} collective-permute-done((bf16[512,384]{1,0:T(8,128)(2,1)S(1)}, bf16[512,384]{1,0:T(8,128)(2,1)S(1)}, u32[]{:S(2)}, u32[]{:S(2)}) %collective-permute-start.4) | collective-permute-done | bytes 393248 | tf_op jit(solution)/shard_map/ppermute | solution.py:76
  18.9 1.2 fusion.57
  20.3 3.3 %collective-permute-start.2 = (bf16[512,384]{1,0:T(8,128)(2,1)S(1)}, bf16[512,384]{1,0:T(8,128)(2,1)}, u32[]{:S(2)}, u32[]{:S(2)}) collective-permute-start(bf16[512,384]{1,0:T(8,128)(2,1)S(1)} %collective-permute-done.1), channel_id=1, source_target_pairs={{0,7},{1,0},{2,1},{3,2},{4,3},{5,4},{6,5},{7,6},{8,15},{9,8},{10,9... | collective-permute-start | bytes 1179656 | tf_op jit(solution)/shard_map/ppermute | solution.py:80
  23.6 6.3 %collective-permute-done.5 = bf16[512,384]{1,0:T(8,128)(2,1)S(1)} collective-permute-done((bf16[512,384]{1,0:T(8,128)(2,1)S(1)}, bf16[512,384]{1,0:T(8,128)(2,1)S(1)}, u32[]{:S(2)}, u32[]{:S(2)}) %collective-permute-start.5) | collective-permute-done | bytes 393248 | tf_op jit(solution)/shard_map/ppermute | solution.py:76
  29.9 1.1 dynamic-slice_bitcast_fusion.1
  30.9 0.2 broadcast_in_dim.48
  31.1 0.3 convolution_dynamic-update-slice_fusion.7
  31.5 1.1 collective-permute-done.2
  32.6 3.8 %collective-permute-start.3 = (bf16[512,384]{1,0:T(8,128)(2,1)}, bf16[512,384]{1,0:T(8,128)(2,1)S(1)}, u32[]{:S(2)}, u32[]{:S(2)}) collective-permute-start(bf16[512,384]{1,0:T(8,128)(2,1)} %collective-permute-done.2), channel_id=1, source_target_pairs={{0,7},{1,0},{2,1},{3,2},{4,3},{5,4},{6,5},{7,6},{8,15},{9,8},{10,9... | collective-permute-start | bytes 1179656 | tf_op jit(solution)/shard_map/ppermute | solution.py:80
  36.4 0.3 convolution_dynamic-update-slice_fusion.6
  36.7 3.2 %collective-permute-done.6 = bf16[512,384]{1,0:T(8,128)(2,1)S(1)} collective-permute-done((bf16[512,384]{1,0:T(8,128)(2,1)S(1)}, bf16[512,384]{1,0:T(8,128)(2,1)S(1)}, u32[]{:S(2)}, u32[]{:S(2)}) %collective-permute-start.6) | collective-permute-done | bytes 393248 | tf_op jit(solution)/shard_map/ppermute | solution.py:76
  39.9 1.5 convolution_dynamic-update-slice_fusion.5
  41.4 3.4 %collective-permute-done.3 = bf16[512,384]{1,0:T(8,128)(2,1)S(1)} collective-permute-done((bf16[512,384]{1,0:T(8,128)(2,1)}, bf16[512,384]{1,0:T(8,128)(2,1)S(1)}, u32[]{:S(2)}, u32[]{:S(2)}) %collective-permute-start.3) | collective-permute-done | bytes 393248 | tf_op jit(solution)/shard_map/ppermute | solution.py:80
  44.8 0.3 convolution_dynamic-update-slice_fusion.4
  45.2 4.0 %collective-permute-done.7 = bf16[512,384]{1,0:T(8,128)(2,1)S(1)} collective-permute-done((bf16[512,384]{1,0:T(8,128)(2,1)S(1)}, bf16[512,384]{1,0:T(8,128)(2,1)S(1)}, u32[]{:S(2)}, u32[]{:S(2)}) %collective-permute-start.7) | collective-permute-done | bytes 393248 | tf_op jit(solution)/shard_map/ppermute | solution.py:76
  49.2 0.3 convolution_dynamic-update-slice_fusion.3
  49.5 0.3 convolution_dynamic-update-slice_fusion.2
  49.8 0.3 convolution_dynamic-update-slice_fusion.1
  50.2 0.3 convolution_dynamic-update-slice_fusion
  51.4 0.8 constant_dynamic-update-slice_fusion.7
  52.2 1.9 %collective-permute-done.8 = f32[128,3072]{0,1:T(8,128)S(1)} collective-permute-done((f32[128,3072]{0,1:T(8,128)S(1)}, f32[128,3072]{0,1:T(8,128)S(1)}, u32[]{:S(2)}, u32[]{:S(2)}) %collective-permute-start.8) | collective-permute-done | bytes 1572896 | tf_op jit(solution)/shard_map/ppermute | solution.py:125
  54.3 1.0 copy.46
  55.2 5.2 %all-to-all-start = ((bf16[16,3,64,128]{3,2,1,0:T(8,128)(2,1)}), bf16[16,3,64,128]{3,2,1,0:T(8,128)(2,1)S(1)}, u32[]{:S(2)}, u32[]{:S(2)}) async-start(bf16[16,3,64,128]{3,2,1,0:T(8,128)(2,1)} %copy.46), calls=%async_computation | async-start | bytes 1572864 | tf_op jit(solution)/shard_map/all_to_all | solution.py:58
  60.5 1.9 %constant_dynamic-update-slice_fusion.6 = bf16[512,3072]{1,0:T(8,128)(2,1)} fusion(bf16[512,3072]{1,0:T(8,128)(2,1)} %constant_dynamic-update-slice_fusion.7, bf16[512,384]{1,0:T(8,128)(2,1)} %copy-done.3), kind=kLoop, calls=%fused_computation.98 | loop fusion | bytes 786432
  62.4 1.9 %constant_dynamic-update-slice_fusion.5 = bf16[512,3072]{1,0:T(8,128)(2,1)} fusion(bf16[512,3072]{1,0:T(8,128)(2,1)} %constant_dynamic-update-slice_fusion.6, bf16[512,384]{1,0:T(8,128)(2,1)} %collective-permute-done.2), kind=kLoop, calls=%fused_computation.97 | loop fusion | bytes 786432
  64.3 1.8 %constant_dynamic-update-slice_fusion.4 = bf16[512,3072]{1,0:T(8,128)(2,1)} fusion(bf16[512,3072]{1,0:T(8,128)(2,1)} %constant_dynamic-update-slice_fusion.5, bf16[512,384]{1,0:T(8,128)(2,1)} %copy-done.10), kind=kLoop, calls=%fused_computation.96 | loop fusion | bytes 786432
  66.1 1.8 %constant_dynamic-update-slice_fusion.3 = bf16[512,3072]{1,0:T(8,128)(2,1)} fusion(bf16[512,3072]{1,0:T(8,128)(2,1)} %constant_dynamic-update-slice_fusion.4, bf16[512,384]{1,0:T(8,128)(2,1)} %copy-done.11), kind=kLoop, calls=%fused_computation.95 | loop fusion | bytes 786432
  67.9 0.8 constant_dynamic-update-slice_fusion.2
  68.7 0.8 constant_dynamic-update-slice_fusion.1
  69.5 0.8 constant_dynamic-update-slice_fusion
  70.4 0.4 collective-permute-start.10
  70.8 3.4 %all-to-all-done = bf16[16,3,64,128]{3,2,1,0:T(8,128)(2,1)S(1)} async-done(((bf16[16,3,64,128]{3,2,1,0:T(8,128)(2,1)}), bf16[16,3,64,128]{3,2,1,0:T(8,128)(2,1)S(1)}, u32[]{:S(2)}, u32[]{:S(2)}) %all-to-all-start) | async-done | bytes 786464 | tf_op jit(solution)/shard_map/all_to_all | solution.py:58
  74.2 0.2 copy.48
  74.4 0.2 copy.49
  74.6 2.8 %select_reduce_fusion.1 = (f32[2048]{0:T(1024)S(1)}, f32[2048,2048]{0,1:T(8,128)S(1)}) fusion(pred[2048]{0:T(1024)(128)(4,1)S(1)} %iota_compare_fusion, bf16[8,8,16,128]{3,2,1,0:T(8,128)(2,1)S(1)} %bitcast.173, bf16[8,8,16,128]{3,2,1,0:T(8,128)(2,1)S(1)} %bitcast.171), kind=kOutput, calls=%fused_computation.4 | convolution fusion | flops 549451776 | bytes 17311744 | tf_op jit(solution)/shard_map/dq,dk->qk/dot_general | solution.py:25
  77.4 5.1 %fusion = (bf16[2048,2048]{0,1:T(8,128)(2,1)S(1)}, f32[2048]{0:T(1024)S(1)}) fusion(f32[2048,2048]{0,1:T(8,128)S(1)} %get-tuple-element.40, f32[2048]{0:T(1024)S(1)} %get-tuple-element.39, pred[2048]{0:T(1024)(128)(4,1)S(1)} %iota_compare_fusion), kind=kLoop, calls=%fused_computation.5 | loop fusion | flops 20969472 | bytes 25184256 | tf_op jit(solution)/shard_map/convert_element_type | solution.py:32
  82.5 0.2 copy.47
  82.7 1.6 %fusion.44 = bf16[8,16,8,128]{3,2,1,0:T(8,128)(2,1)S(1)} fusion(bf16[2048,2048]{0,1:T(8,128)(2,1)S(1)} %get-tuple-element.17, bf16[8,8,16,128]{3,2,1,0:T(8,128)(2,1)S(1)} %bitcast.169, f32[2048]{0:T(1024)S(1)} %get-tuple-element.18), kind=kOutput, calls=%fused_computation.42 | convolution fusion | flops 537133056 | bytes 8921088 | tf_op jit(solution)/shard_map/qk,dk->dq/dot_general | solution.py:34
  84.3 0.8 copy.106
  85.1 3.5 %all-to-all-start.1 = ((bf16[16,64,128]{2,1,0:T(8,128)(2,1)}), bf16[16,64,128]{2,1,0:T(8,128)(2,1)S(1)}, u32[]{:S(2)}, u32[]{:S(2)}) async-start(bf16[16,64,128]{2,1,0:T(8,128)(2,1)} %bitcast.162), calls=%async_computation.1 | async-start | bytes 524288 | tf_op jit(solution)/shard_map/all_to_all | solution.py:61
  88.8 7.9 %all-to-all-done.1 = bf16[16,64,128]{2,1,0:T(8,128)(2,1)S(1)} async-done(((bf16[16,64,128]{2,1,0:T(8,128)(2,1)}), bf16[16,64,128]{2,1,0:T(8,128)(2,1)S(1)}, u32[]{:S(2)}, u32[]{:S(2)}) %all-to-all-start.1) | async-done | bytes 262176 | tf_op jit(solution)/shard_map/all_to_all | solution.py:61
  96.7 0.5 fusion.34
  97.1 1.3 collective-permute-start.9
  98.5 9.8 %collective-permute-done.9 = bf16[128,1024]{1,0:T(8,128)(2,1)S(1)} collective-permute-done((bf16[128,1024]{1,0:T(8,128)(2,1)S(1)}, bf16[128,1024]{1,0:T(8,128)(2,1)S(1)}, u32[]{:S(2)}, u32[]{:S(2)}) %collective-permute-start.9) | collective-permute-done | bytes 262176 | tf_op jit(solution)/shard_map/ppermute | solution.py:137
  108.4 0.2 fusion.50
  108.7 0.2 fusion.53
  109.0 3.1 %fusion.81 = f32[3072,128]{1,0:T(8,128)S(1)} fusion(bf16[512,3072]{1,0:T(8,128)(2,1)} %collective-permute-done.10, bf16[128,1024]{1,0:T(8,128)(2,1)S(1)} %fusion.53, s32[]{:T(128)S(6)} %select_n.129), kind=kOutput, calls=%fused_computation.87 | convolution fusion | flops 402653184 | bytes 4849668 | tf_op jit(solution)/shard_map/dot_general | solution.py:49
  112.0 1.0 fusion.4
  113.1 1.6 %gather_fusion = bf16[48,64,128]{2,1,0:T(8,128)(2,1)} fusion(bf16[48,64,128]{2,1,0:T(8,128)(2,1)S(1)} %bitcast.164, s32[1024]{0:T(1024)S(1)} %pad_clamp_fusion), kind=kCustom, calls=%fused_computation | custom fusion | bytes 1573056 | tf_op jit(solution)/shard_map/jit(_take)/gather | solution.py:56
  114.6 17.2 %all_to_all.40 = bf16[16,3,64,128]{3,2,1,0:T(8,128)(2,1)S(1)} all-to-all(bf16[16,3,64,128]{3,2,1,0:T(8,128)(2,1)} %bitcast.167), channel_id=1, replica_groups=mesh['pipe'=2,'ctx'=16,'dp'=8] {'ctx'}, dimensions={0} | all-to-all | bytes 1572864 | tf_op jit(solution)/shard_map/all_to_all | solution.py:58
  131.9 0.2 copy.52
  132.1 0.2 copy.53
  132.3 2.8 %select_reduce_fusion = (f32[2048]{0:T(1024)S(1)}, f32[2048,2048]{0,1:T(8,128)S(1)}) fusion(pred[2048]{0:T(1024)(128)(4,1)S(1)} %iota_compare_fusion, bf16[8,8,16,128]{3,2,1,0:T(8,128)(2,1)S(1)} %bitcast.174, bf16[8,8,16,128]{3,2,1,0:T(8,128)(2,1)S(1)} %bitcast.172), kind=kOutput, calls=%fused_computation.2 | convolution fusion | flops 549451776 | bytes 17311744 | tf_op jit(solution)/shard_map/dq,dk->qk/dot_general | solution.py:25
  135.1 5.1 %fusion.2 = (bf16[2048,2048]{0,1:T(8,128)(2,1)S(1)}, f32[2048]{0:T(1024)S(1)}) fusion(f32[2048,2048]{0,1:T(8,128)S(1)} %get-tuple-element.42, f32[2048]{0:T(1024)S(1)} %get-tuple-element.41, pred[2048]{0:T(1024)(128)(4,1)S(1)} %iota_compare_fusion), kind=kLoop, calls=%fused_computation.7 | loop fusion | flops 20969472 | bytes 25184256 | tf_op jit(solution)/shard_map/convert_element_type | solution.py:32
  140.2 0.2 copy.51
  140.4 1.6 %fusion.43 = bf16[8,16,8,128]{3,2,1,0:T(8,128)(2,1)S(1)} fusion(bf16[2048,2048]{0,1:T(8,128)(2,1)S(1)} %get-tuple-element.27, bf16[8,8,16,128]{3,2,1,0:T(8,128)(2,1)S(1)} %bitcast.170, f32[2048]{0:T(1024)S(1)} %get-tuple-element.28), kind=kOutput, calls=%fused_computation.41 | convolution fusion | flops 537133056 | bytes 8921088 | tf_op jit(solution)/shard_map/qk,dk->dq/dot_general | solution.py:34
  142.0 0.8 copy.105
  142.7 3.5 %all-to-all-start.3 = ((bf16[16,64,128]{2,1,0:T(8,128)(2,1)}), bf16[16,64,128]{2,1,0:T(8,128)(2,1)S(1)}, u32[]{:S(2)}, u32[]{:S(2)}) async-start(bf16[16,64,128]{2,1,0:T(8,128)(2,1)} %bitcast.160), calls=%async_computation.3 | async-start | bytes 524288 | tf_op jit(solution)/shard_map/all_to_all | solution.py:61
  146.3 8.0 %all-to-all-done.3 = bf16[16,64,128]{2,1,0:T(8,128)(2,1)S(1)} async-done(((bf16[16,64,128]{2,1,0:T(8,128)(2,1)}), bf16[16,64,128]{2,1,0:T(8,128)(2,1)S(1)}, u32[]{:S(2)}, u32[]{:S(2)}) %all-to-all-start.3) | async-done | bytes 262176 | tf_op jit(solution)/shard_map/all_to_all | solution.py:61
  154.3 1.2 fusion.40
  (59 shorter events, 0.9 us)
Async XLA Ops:
  0.0 96.6 %copy-start = (bf16[1,1024,1024]{2,1,0:T(8,128)(2,1)S(1)}, bf16[1,1024,1024]{2,1,0:T(8,128)(2,1)}, u32[]{:S(2)}) copy-start(bf16[1,1024,1024]{2,1,0:T(8,128)(2,1)} %param.13) | copy-start | bytes 6291460
  1.2 19.1 %copy-start.6 = (bf16[512,384]{1,0:T(8,128)(2,1)}, bf16[512,384]{1,0:T(8,128)(2,1)S(1)}, u32[]{:S(2)}) copy-start(bf16[512,384]{1,0:T(8,128)(2,1)S(1)} %dynamic-slice_bitcast_fusion) | copy-start | bytes 1179652
  1.2 19.0 %collective-permute-start.1 = (bf16[512,384]{1,0:T(8,128)(2,1)S(1)}, bf16[512,384]{1,0:T(8,128)(2,1)S(1)}, u32[]{:S(2)}, u32[]{:S(2)}) collective-permute-start(bf16[512,384]{1,0:T(8,128)(2,1)S(1)} %dynamic-slice_bitcast_fusion), channel_id=1, source_target_pairs={{0,7},{1,0},{2,1},{3,2},{4,3},{5,4},{6,5},{7,6},{8,15},{9,8},{10,9... | collective-permute-start | bytes 1179656 | tf_op jit(solution)/shard_map/ppermute | solution.py:80
  7.1 11.8 %collective-permute-start.4 = (bf16[512,384]{1,0:T(8,128)(2,1)S(1)}, bf16[512,384]{1,0:T(8,128)(2,1)S(1)}, u32[]{:S(2)}, u32[]{:S(2)}) collective-permute-start(bf16[512,384]{1,0:T(8,128)(2,1)S(1)} %dynamic-slice_bitcast_fusion), channel_id=1, source_target_pairs={{0,1},{1,2},{2,3},{3,4},{4,5},{5,6},{6,7},{7,0},{8,9},{9,10},{10,1... | collective-permute-start | bytes 1179656 | tf_op jit(solution)/shard_map/ppermute | solution.py:76
  18.9 10.9 %collective-permute-start.5 = (bf16[512,384]{1,0:T(8,128)(2,1)S(1)}, bf16[512,384]{1,0:T(8,128)(2,1)S(1)}, u32[]{:S(2)}, u32[]{:S(2)}) collective-permute-start(bf16[512,384]{1,0:T(8,128)(2,1)S(1)} %collective-permute-done.4), channel_id=1, source_target_pairs={{0,1},{1,2},{2,3},{3,4},{4,5},{5,6},{6,7},{7,0},{8,9},{9,10},{10,1... | collective-permute-start | bytes 1179656 | tf_op jit(solution)/shard_map/ppermute | solution.py:76
  20.1 9.7 %collective-permute-start = (bf16[128,1024]{1,0:T(8,128)(2,1)S(1)}, bf16[128,1024]{1,0:T(8,128)(2,1)}, u32[]{:S(2)}, u32[]{:S(2)}) collective-permute-start(bf16[128,1024]{1,0:T(8,128)(2,1)S(1)} %fusion.57), channel_id=1, source_target_pairs={{0,8},{8,0},{16,24},{24,16},{32,40},{40,32},{48,56},{56,48},{64,72... | collective-permute-start | bytes 786440 | tf_op jit(solution)/shard_map/ppermute | solution.py:107
  20.3 21.1 %copy-start.3 = (bf16[512,384]{1,0:T(8,128)(2,1)}, bf16[512,384]{1,0:T(8,128)(2,1)S(1)}, u32[]{:S(2)}) copy-start(bf16[512,384]{1,0:T(8,128)(2,1)S(1)} %collective-permute-done.1) | copy-start | bytes 1179652
  20.3 12.3 %collective-permute-start.2 = (bf16[512,384]{1,0:T(8,128)(2,1)S(1)}, bf16[512,384]{1,0:T(8,128)(2,1)}, u32[]{:S(2)}, u32[]{:S(2)}) collective-permute-start(bf16[512,384]{1,0:T(8,128)(2,1)S(1)} %collective-permute-done.1), channel_id=1, source_target_pairs={{0,7},{1,0},{2,1},{3,2},{4,3},{5,4},{6,5},{7,6},{8,15},{9,8},{10,9... | collective-permute-start | bytes 1179656 | tf_op jit(solution)/shard_map/ppermute | solution.py:80
  23.6 7.6 %copy-start.12 = (bf16[1,1024,384]{2,1,0:T(8,128)(2,1)S(1)}, bf16[1,1024,384]{2,1,0:T(8,128)(2,1)}, u32[]{:S(2)}) copy-start(bf16[1,1024,384]{2,1,0:T(8,128)(2,1)} %param.12) | copy-start | bytes 2359300
  29.9 20.0 %copy-start.4 = (bf16[512,384]{1,0:T(8,128)(2,1)}, bf16[512,384]{1,0:T(8,128)(2,1)S(1)}, u32[]{:S(2)}) copy-start(bf16[512,384]{1,0:T(8,128)(2,1)S(1)} %collective-permute-done.5) | copy-start | bytes 1179652
  29.9 10.1 %collective-permute-start.6 = (bf16[512,384]{1,0:T(8,128)(2,1)S(1)}, bf16[512,384]{1,0:T(8,128)(2,1)S(1)}, u32[]{:S(2)}, u32[]{:S(2)}) collective-permute-start(bf16[512,384]{1,0:T(8,128)(2,1)S(1)} %collective-permute-done.5), channel_id=1, source_target_pairs={{0,1},{1,2},{2,3},{3,4},{4,5},{5,6},{6,7},{7,0},{8,9},{9,10},{10,1... | collective-permute-start | bytes 1179656 | tf_op jit(solution)/shard_map/ppermute | solution.py:76
  32.6 12.3 %collective-permute-start.3 = (bf16[512,384]{1,0:T(8,128)(2,1)}, bf16[512,384]{1,0:T(8,128)(2,1)S(1)}, u32[]{:S(2)}, u32[]{:S(2)}) collective-permute-start(bf16[512,384]{1,0:T(8,128)(2,1)} %collective-permute-done.2), channel_id=1, source_target_pairs={{0,7},{1,0},{2,1},{3,2},{4,3},{5,4},{6,5},{7,6},{8,15},{9,8},{10,9... | collective-permute-start | bytes 1179656 | tf_op jit(solution)/shard_map/ppermute | solution.py:80
  39.9 10.6 %copy-start.8 = (bf16[512,384]{1,0:T(8,128)(2,1)}, bf16[512,384]{1,0:T(8,128)(2,1)S(1)}, u32[]{:S(2)}) copy-start(bf16[512,384]{1,0:T(8,128)(2,1)S(1)} %collective-permute-done.6) | copy-start | bytes 1179652
  39.9 9.2 %collective-permute-start.7 = (bf16[512,384]{1,0:T(8,128)(2,1)S(1)}, bf16[512,384]{1,0:T(8,128)(2,1)S(1)}, u32[]{:S(2)}, u32[]{:S(2)}) collective-permute-start(bf16[512,384]{1,0:T(8,128)(2,1)S(1)} %collective-permute-done.6), channel_id=1, source_target_pairs={{0,1},{1,2},{2,3},{3,4},{4,5},{5,6},{6,7},{7,0},{8,9},{9,10},{10,1... | collective-permute-start | bytes 1179656 | tf_op jit(solution)/shard_map/ppermute | solution.py:76
  44.8 5.8 %copy-start.10 = (bf16[512,384]{1,0:T(8,128)(2,1)}, bf16[512,384]{1,0:T(8,128)(2,1)S(1)}, u32[]{:S(2)}) copy-start(bf16[512,384]{1,0:T(8,128)(2,1)S(1)} %collective-permute-done.3) | copy-start | bytes 1179652
  49.1 1.5 copy-start.11
  49.5 1.9 %copy-start.7 = (bf16[512,384]{1,0:T(8,128)(2,1)S(1)}, bf16[512,384]{1,0:T(8,128)(2,1)}, u32[]{:S(2)}) copy-start(bf16[512,384]{1,0:T(8,128)(2,1)} %copy-done.6) | copy-start | bytes 1179652
  50.6 3.5 %collective-permute-start.8 = (f32[128,3072]{0,1:T(8,128)S(1)}, f32[128,3072]{0,1:T(8,128)S(1)}, u32[]{:S(2)}, u32[]{:S(2)}) collective-permute-start(f32[128,3072]{0,1:T(8,128)S(1)} %slice_bitcast_fusion), channel_id=1, source_target_pairs={{0,8},{8,0},{16,24},{24,16},{32,40},{40,32},{48,56},{56,48},{64,72... | collective-permute-start | bytes 4718600 | tf_op jit(solution)/shard_map/ppermute | solution.py:125
  55.2 18.9 %all-to-all-start = ((bf16[16,3,64,128]{3,2,1,0:T(8,128)(2,1)}), bf16[16,3,64,128]{3,2,1,0:T(8,128)(2,1)S(1)}, u32[]{:S(2)}, u32[]{:S(2)}) async-start(bf16[16,3,64,128]{3,2,1,0:T(8,128)(2,1)} %copy.46), calls=%async_computation | async-start | bytes 1572864 | tf_op jit(solution)/shard_map/all_to_all | solution.py:58
  60.5 7.4 %copy-start.9 = (bf16[512,384]{1,0:T(8,128)(2,1)S(1)}, bf16[512,384]{1,0:T(8,128)(2,1)}, u32[]{:S(2)}) copy-start(bf16[512,384]{1,0:T(8,128)(2,1)} %copy-done.8) | copy-start | bytes 1179652
  60.5 8.3 %copy-start.5 = (bf16[512,384]{1,0:T(8,128)(2,1)S(1)}, bf16[512,384]{1,0:T(8,128)(2,1)}, u32[]{:S(2)}) copy-start(bf16[512,384]{1,0:T(8,128)(2,1)} %copy-done.4) | copy-start | bytes 1179652
  70.4 38.6 %collective-permute-start.10 = (bf16[512,3072]{1,0:T(8,128)(2,1)}, bf16[512,3072]{1,0:T(8,128)(2,1)}, u32[]{:S(2)}, u32[]{:S(2)}) collective-permute-start(bf16[512,3072]{1,0:T(8,128)(2,1)} %constant_dynamic-update-slice_fusion), channel_id=1, source_target_pairs={{0,8},{8,0},{16,24},{24,16},{32,40},{40,32},{48,56},{56,48},{64,72... | collective-permute-start | bytes 9437192 | tf_op jit(solution)/shard_map/ppermute | solution.py:128
  82.7 13.9 %copy-start.2 = (bf16[1,1,128,1024]{3,2,1,0:T(8,128)(2,1)S(1)}, bf16[1,1,128,1024]{3,2,1,0:T(8,128)(2,1)}, u32[]{:S(2)}) copy-start(bf16[1,1,128,1024]{3,2,1,0:T(8,128)(2,1)} %param.8) | copy-start | bytes 786436
  82.7 13.9 %copy-start.15 = (f32[1,1024]{1,0:T(1,128)S(1)}, f32[1,1024]{1,0:T(1,128)}, u32[]{:S(2)}) copy-start(f32[1,1024]{1,0:T(1,128)} %param.14) | copy-start | bytes 12292
  82.7 13.9 %copy-start.16 = (f32[1,1024]{1,0:T(1,128)S(1)}, f32[1,1024]{1,0:T(1,128)}, u32[]{:S(2)}) copy-start(f32[1,1024]{1,0:T(1,128)} %param.15) | copy-start | bytes 12292
  84.3 24.4 %copy-start.13 = (f32[1,1024]{1,0:T(1,128)S(1)}, f32[1,1024]{1,0:T(1,128)}, u32[]{:S(2)}) copy-start(f32[1,1024]{1,0:T(1,128)} %param.11) | copy-start | bytes 12292
  84.3 24.4 %copy-start.14 = (f32[1,1024]{1,0:T(1,128)S(1)}, f32[1,1024]{1,0:T(1,128)}, u32[]{:S(2)}) copy-start(f32[1,1024]{1,0:T(1,128)} %param.10) | copy-start | bytes 12292
  85.1 11.5 %all-to-all-start.1 = ((bf16[16,64,128]{2,1,0:T(8,128)(2,1)}), bf16[16,64,128]{2,1,0:T(8,128)(2,1)S(1)}, u32[]{:S(2)}, u32[]{:S(2)}) async-start(bf16[16,64,128]{2,1,0:T(8,128)(2,1)} %bitcast.162), calls=%async_computation.1 | async-start | bytes 524288 | tf_op jit(solution)/shard_map/all_to_all | solution.py:61
  97.1 11.2 %collective-permute-start.9 = (bf16[128,1024]{1,0:T(8,128)(2,1)S(1)}, bf16[128,1024]{1,0:T(8,128)(2,1)S(1)}, u32[]{:S(2)}, u32[]{:S(2)}) collective-permute-start(bf16[128,1024]{1,0:T(8,128)(2,1)S(1)} %fusion.34), channel_id=1, source_target_pairs={{0,128},{1,129},{2,130},{3,131},{4,132},{5,133},{6,134},{7,135},{8... | collective-permute-start | bytes 786440 | tf_op jit(solution)/shard_map/ppermute | solution.py:137
  108.9 3.1 %copy-start.1 = (bf16[512,3072]{1,0:T(8,128)(2,1)S(1)}, bf16[512,3072]{1,0:T(8,128)(2,1)}, u32[]{:S(2)}) copy-start(bf16[512,3072]{1,0:T(8,128)(2,1)} %constant_dynamic-update-slice_fusion) | copy-start | bytes 9437188
  142.7 11.5 %all-to-all-start.3 = ((bf16[16,64,128]{2,1,0:T(8,128)(2,1)}), bf16[16,64,128]{2,1,0:T(8,128)(2,1)S(1)}, u32[]{:S(2)}, u32[]{:S(2)}) async-start(bf16[16,64,128]{2,1,0:T(8,128)(2,1)} %bitcast.160), calls=%async_computation.3 | async-start | bytes 524288 | tf_op jit(solution)/shard_map/all_to_all | solution.py:61

commit v17 on v14

--- a/solution.py
+++ b/solution.py
@@ -49,9 +49,9 @@
         projected = jnp.dot(normed_mine, qkv_mine, preferred_element_type=jnp.float32) + jnp.dot(
             normed_other, qkv_other, preferred_element_type=jnp.float32
         )
-        projected = unrotate(projected.astype(jnp.bfloat16), "dp")
+        projected = unrotate(jnp.transpose(projected.astype(jnp.bfloat16)), "dp", along=0)
         projected = jnp.transpose(
-            projected.reshape(tok_rows, 3, HEADS, head_width), (2, 1, 3, 0)
+            projected.reshape(3, HEADS, head_width, tok_rows), (1, 0, 2, 3)
         )
     gathered = lax.all_to_all(projected, "ctx", 0, 3, tiled=True)
     context = head_attention(gathered[0], length, head_width ** (-0.5))

time: 154 us -> 155 us (level)
  local copies, waits for them, and re-layouts: 18.8 us -> 16.5 us
  other arithmetic: 14.9 us -> 17.2 us
    concatenate x1, other arithmetic: 0.42 us -> 2.75 us  [unrotate(): doubled = jnp.concatenate([rotated, rotated], axis=along)]
where the time goes in v17:
time: 155 us; the launch traced here: 154 us
  waiting for transfers between devices  50.3 us (32%)
  blocking collectives  27.2 us (18%)
  starting transfers between devices  23.9 us (15%)
  matrix products  18.2 us (12%)
  other arithmetic  17.2 us (11%)
  local copies, waits for them, and re-layouts  16.5 us (11%)
    ppermute x4, waiting for transfers between devices, ring_gather(): forward = lax.ppermute(forward, axis, right)  23 us
    all_to_all x1, blocking collectives, sublayer(): gathered = lax.all_to_all(projected, 'ctx', 0, 3, tiled=True)  16.5 us
    ppermute x3, starting transfers between devices, ring_gather(): backward = lax.ppermute(backward, axis, left)  13 us
    all_to_all x1, blocking collectives, sublayer(): lax.all_to_all(context, 'ctx', 0, 0, tiled=True).reshape(width, tok_rows)  10.6 us
    convert_element_type x2, other arithmetic, head_attention(): weights.astype(jnp.bfloat16)  10.2 us
    unnamed x41, local copies, waits for them, and re-layouts  10 us
    ppermute x1, waiting for transfers between devices, per_device(): current = lax.ppermute(produced, 'pipe', pairs)  9.63 us
    all_to_all x1, waiting for transfers between devices, sublayer(): lax.all_to_all(context, 'ctx', 0, 0, tiled=True).reshape(width, tok_rows)  7.98 us
  transfers between devices with their start and end apart: 13, of which 10 were waited for; matrix products, arithmetic and copies ran while one was open for 19% of the time, Pallas kernels for 0%

profile of v17, /device:TPU:4, one launch (start us, length us, event | category | flops | bytes accessed | tf_op | source)
XLA Modules:
  0.0 154.4 jit_solution(12604913213165839367)
XLA Ops:
  0.0 1.2 dynamic-slice_bitcast_fusion
  1.2 5.9 %collective-permute-start.1 = (bf16[512,384]{1,0:T(8,128)(2,1)S(1)}, bf16[512,384]{1,0:T(8,128)(2,1)S(1)}, u32[]{:S(2)}, u32[]{:S(2)}) collective-permute-start(bf16[512,384]{1,0:T(8,128)(2,1)S(1)} %dynamic-slice_bitcast_fusion), channel_id=1, source_target_pairs={{0,7},{1,0},{2,1},{3,2},{4,3},{5,4},{6,5},{7,6},{8,15},{9,8},{10,9... | collective-permute-start | bytes 1179656 | tf_op jit(solution)/shard_map/ppermute | solution.py:78
  7.1 1.1 convert_reduce_fusion.1
  8.2 1.2 fusion.55
  9.4 9.5 %collective-permute-done.4 = bf16[512,384]{1,0:T(8,128)(2,1)S(1)} collective-permute-done((bf16[512,384]{1,0:T(8,128)(2,1)S(1)}, bf16[512,384]{1,0:T(8,128)(2,1)S(1)}, u32[]{:S(2)}, u32[]{:S(2)}) %collective-permute-start.4) | collective-permute-done | bytes 393248 | tf_op jit(solution)/shard_map/ppermute | solution.py:74
  18.9 1.2 fusion.58
  20.3 3.3 %collective-permute-start.2 = (bf16[512,384]{1,0:T(8,128)(2,1)S(1)}, bf16[512,384]{1,0:T(8,128)(2,1)}, u32[]{:S(2)}, u32[]{:S(2)}) collective-permute-start(bf16[512,384]{1,0:T(8,128)(2,1)S(1)} %collective-permute-done.1), channel_id=1, source_target_pairs={{0,7},{1,0},{2,1},{3,2},{4,3},{5,4},{6,5},{7,6},{8,15},{9,8},{10,9... | collective-permute-start | bytes 1179656 | tf_op jit(solution)/shard_map/ppermute | solution.py:78
  23.6 6.3 %collective-permute-done.5 = bf16[512,384]{1,0:T(8,128)(2,1)S(1)} collective-permute-done((bf16[512,384]{1,0:T(8,128)(2,1)S(1)}, bf16[512,384]{1,0:T(8,128)(2,1)S(1)}, u32[]{:S(2)}, u32[]{:S(2)}) %collective-permute-start.5) | collective-permute-done | bytes 393248 | tf_op jit(solution)/shard_map/ppermute | solution.py:74
  29.9 1.1 dynamic-slice_bitcast_fusion.1
  30.9 0.2 broadcast_in_dim.44
  31.1 0.3 convolution_dynamic-update-slice_fusion.7
  31.5 1.1 collective-permute-done.2
  32.6 3.8 %collective-permute-start.3 = (bf16[512,384]{1,0:T(8,128)(2,1)}, bf16[512,384]{1,0:T(8,128)(2,1)S(1)}, u32[]{:S(2)}, u32[]{:S(2)}) collective-permute-start(bf16[512,384]{1,0:T(8,128)(2,1)} %collective-permute-done.2), channel_id=1, source_target_pairs={{0,7},{1,0},{2,1},{3,2},{4,3},{5,4},{6,5},{7,6},{8,15},{9,8},{10,9... | collective-permute-start | bytes 1179656 | tf_op jit(solution)/shard_map/ppermute | solution.py:78
  36.4 0.3 convolution_dynamic-update-slice_fusion.6
  36.7 3.2 %collective-permute-done.6 = bf16[512,384]{1,0:T(8,128)(2,1)S(1)} collective-permute-done((bf16[512,384]{1,0:T(8,128)(2,1)S(1)}, bf16[512,384]{1,0:T(8,128)(2,1)S(1)}, u32[]{:S(2)}, u32[]{:S(2)}) %collective-permute-start.6) | collective-permute-done | bytes 393248 | tf_op jit(solution)/shard_map/ppermute | solution.py:74
  39.9 1.5 convolution_dynamic-update-slice_fusion.5
  41.4 3.4 %collective-permute-done.3 = bf16[512,384]{1,0:T(8,128)(2,1)S(1)} collective-permute-done((bf16[512,384]{1,0:T(8,128)(2,1)}, bf16[512,384]{1,0:T(8,128)(2,1)S(1)}, u32[]{:S(2)}, u32[]{:S(2)}) %collective-permute-start.3) | collective-permute-done | bytes 393248 | tf_op jit(solution)/shard_map/ppermute | solution.py:78
  44.8 0.3 convolution_dynamic-update-slice_fusion.4
  45.2 4.0 %collective-permute-done.7 = bf16[512,384]{1,0:T(8,128)(2,1)S(1)} collective-permute-done((bf16[512,384]{1,0:T(8,128)(2,1)S(1)}, bf16[512,384]{1,0:T(8,128)(2,1)S(1)}, u32[]{:S(2)}, u32[]{:S(2)}) %collective-permute-start.7) | collective-permute-done | bytes 393248 | tf_op jit(solution)/shard_map/ppermute | solution.py:74
  49.2 0.3 convolution_dynamic-update-slice_fusion.3
  49.5 0.3 convolution_dynamic-update-slice_fusion.2
  49.8 0.3 convolution_dynamic-update-slice_fusion.1
  50.2 0.3 convolution_dynamic-update-slice_fusion
  51.4 0.9 constant_dynamic-update-slice_fusion.7
  52.3 1.9 %collective-permute-done.8 = f32[128,3072]{0,1:T(8,128)S(1)} collective-permute-done((f32[128,3072]{0,1:T(8,128)S(1)}, f32[128,3072]{0,1:T(8,128)S(1)}, u32[]{:S(2)}, u32[]{:S(2)}) %collective-permute-start.8) | collective-permute-done | bytes 1572896 | tf_op jit(solution)/shard_map/ppermute | solution.py:123
  54.1 0.2 fusion.12
  54.3 1.0 copy.46
  55.2 5.2 %all-to-all-start = ((bf16[16,3,64,128]{3,2,1,0:T(8,128)(2,1)}), bf16[16,3,64,128]{3,2,1,0:T(8,128)(2,1)S(1)}, u32[]{:S(2)}, u32[]{:S(2)}) async-start(bf16[16,3,64,128]{3,2,1,0:T(8,128)(2,1)} %copy.46), calls=%async_computation | async-start | bytes 1572864 | tf_op jit(solution)/shard_map/all_to_all | solution.py:56
  60.5 1.9 %constant_dynamic-update-slice_fusion.6 = bf16[512,3072]{1,0:T(8,128)(2,1)} fusion(bf16[512,3072]{1,0:T(8,128)(2,1)} %constant_dynamic-update-slice_fusion.7, bf16[512,384]{1,0:T(8,128)(2,1)} %copy-done.3), kind=kLoop, calls=%fused_computation.100 | loop fusion | bytes 786432
  62.4 1.8 %constant_dynamic-update-slice_fusion.5 = bf16[512,3072]{1,0:T(8,128)(2,1)} fusion(bf16[512,3072]{1,0:T(8,128)(2,1)} %constant_dynamic-update-slice_fusion.6, bf16[512,384]{1,0:T(8,128)(2,1)} %collective-permute-done.2), kind=kLoop, calls=%fused_computation.99 | loop fusion | bytes 786432
  64.2 1.8 %constant_dynamic-update-slice_fusion.4 = bf16[512,3072]{1,0:T(8,128)(2,1)} fusion(bf16[512,3072]{1,0:T(8,128)(2,1)} %constant_dynamic-update-slice_fusion.5, bf16[512,384]{1,0:T(8,128)(2,1)} %copy-done.10), kind=kLoop, calls=%fused_computation.98 | loop fusion | bytes 786432
  66.0 1.8 %constant_dynamic-update-slice_fusion.3 = bf16[512,3072]{1,0:T(8,128)(2,1)} fusion(bf16[512,3072]{1,0:T(8,128)(2,1)} %constant_dynamic-update-slice_fusion.4, bf16[512,384]{1,0:T(8,128)(2,1)} %copy-done.11), kind=kLoop, calls=%fused_computation.97 | loop fusion | bytes 786432
  67.9 0.8 constant_dynamic-update-slice_fusion.2
  68.7 0.8 constant_dynamic-update-slice_fusion.1
  69.6 0.9 constant_dynamic-update-slice_fusion
  70.4 0.4 collective-permute-start.10
  70.8 3.3 %all-to-all-done = bf16[16,3,64,128]{3,2,1,0:T(8,128)(2,1)S(1)} async-done(((bf16[16,3,64,128]{3,2,1,0:T(8,128)(2,1)}), bf16[16,3,64,128]{3,2,1,0:T(8,128)(2,1)S(1)}, u32[]{:S(2)}, u32[]{:S(2)}) %all-to-all-start) | async-done | bytes 786464 | tf_op jit(solution)/shard_map/all_to_all | solution.py:56
  74.2 0.2 copy.48
  74.4 0.2 copy.49
  74.6 2.8 %select_reduce_fusion.1 = (f32[2048]{0:T(1024)S(1)}, f32[2048,2048]{0,1:T(8,128)S(1)}) fusion(pred[2048]{0:T(1024)(128)(4,1)S(1)} %iota_compare_fusion, bf16[8,8,16,128]{3,2,1,0:T(8,128)(2,1)S(1)} %bitcast.171, bf16[8,8,16,128]{3,2,1,0:T(8,128)(2,1)S(1)} %bitcast.169), kind=kOutput, calls=%fused_computation.3 | convolution fusion | flops 549451776 | bytes 17311744 | tf_op jit(solution)/shard_map/dq,dk->qk/dot_general | solution.py:25
  77.4 5.1 %fusion = (bf16[2048,2048]{0,1:T(8,128)(2,1)S(1)}, f32[2048]{0:T(1024)S(1)}) fusion(f32[2048,2048]{0,1:T(8,128)S(1)} %get-tuple-element.40, f32[2048]{0:T(1024)S(1)} %get-tuple-element.39, pred[2048]{0:T(1024)(128)(4,1)S(1)} %iota_compare_fusion), kind=kLoop, calls=%fused_computation.4 | loop fusion | flops 20969472 | bytes 25184256 | tf_op jit(solution)/shard_map/convert_element_type | solution.py:32
  82.5 0.2 copy.47
  82.7 1.6 %fusion.44 = bf16[8,16,8,128]{3,2,1,0:T(8,128)(2,1)S(1)} fusion(bf16[2048,2048]{0,1:T(8,128)(2,1)S(1)} %get-tuple-element.17, bf16[8,8,16,128]{3,2,1,0:T(8,128)(2,1)S(1)} %bitcast.167, f32[2048]{0:T(1024)S(1)} %get-tuple-element.18), kind=kOutput, calls=%fused_computation.43 | convolution fusion | flops 537133056 | bytes 8921088 | tf_op jit(solution)/shard_map/qk,dk->dq/dot_general | solution.py:34
  84.4 10.6 %all_to_all.40 = bf16[16,64,128]{2,1,0:T(8,128)(2,1)S(1)} all-to-all(bf16[16,64,128]{2,1,0:T(8,128)(2,1)S(1)} %bitcast.173), channel_id=1, replica_groups=mesh['pipe'=2,'ctx'=16,'dp'=8] {'ctx'}, dimensions={0} | all-to-all | bytes 524288 | tf_op jit(solution)/shard_map/all_to_all | solution.py:59
  95.0 0.5 fusion.34
  95.5 1.5 collective-permute-start.9
  97.1 9.6 %collective-permute-done.9 = bf16[128,1024]{1,0:T(8,128)(2,1)S(1)} collective-permute-done((bf16[128,1024]{1,0:T(8,128)(2,1)S(1)}, bf16[128,1024]{1,0:T(8,128)(2,1)S(1)}, u32[]{:S(2)}, u32[]{:S(2)}) %collective-permute-start.9) | collective-permute-done | bytes 262176 | tf_op jit(solution)/shard_map/ppermute | solution.py:135
  106.7 0.1 convert_reduce_fusion
  106.8 0.2 fusion.51
  107.1 0.2 fusion.54
  107.3 3.1 %fusion.82 = f32[3072,128]{1,0:T(8,128)S(1)} fusion(bf16[512,3072]{1,0:T(8,128)(2,1)} %collective-permute-done.10, bf16[128,1024]{1,0:T(8,128)(2,1)S(1)} %fusion.54, s32[]{:T(128)S(6)} %select_n.119), kind=kOutput, calls=%fused_computation.89 | convolution fusion | flops 402653184 | bytes 4849668 | tf_op jit(solution)/shard_map/dot_general | solution.py:49
  110.4 1.0 fusion.4
  111.5 2.7 %fusion.45 = bf16[3072,128]{1,0:T(8,128)(2,1)S(1)} fusion(s32[]{:T(128)S(6)} %select_n.120, bf16[3072,128]{1,0:T(8,128)(2,1)S(1)} %fusion.4), kind=kLoop, calls=%fused_computation.44 | loop fusion | flops 1572864 | bytes 1572868 | tf_op jit(solution)/shard_map/concatenate | solution.py:91
  114.3 16.5 %all_to_all.41 = bf16[16,3,64,128]{3,2,1,0:T(8,128)(2,1)S(1)} all-to-all(bf16[16,3,64,128]{3,2,1,0:T(8,128)(2,1)S(1)} %copy.51), channel_id=1, replica_groups=mesh['pipe'=2,'ctx'=16,'dp'=8] {'ctx'}, dimensions={0} | all-to-all | bytes 1572864 | tf_op jit(solution)/shard_map/all_to_all | solution.py:56
  130.9 0.2 copy.53
  131.1 0.2 copy.54
  131.2 2.8 %select_reduce_fusion = (f32[2048]{0:T(1024)S(1)}, f32[2048,2048]{0,1:T(8,128)S(1)}) fusion(pred[2048]{0:T(1024)(128)(4,1)S(1)} %iota_compare_fusion, bf16[8,8,16,128]{3,2,1,0:T(8,128)(2,1)S(1)} %bitcast.172, bf16[8,8,16,128]{3,2,1,0:T(8,128)(2,1)S(1)} %bitcast.170), kind=kOutput, calls=%fused_computation.1 | convolution fusion | flops 549451776 | bytes 17311744 | tf_op jit(solution)/shard_map/dq,dk->qk/dot_general | solution.py:25
  134.0 5.1 %fusion.2 = (bf16[2048,2048]{0,1:T(8,128)(2,1)S(1)}, f32[2048]{0:T(1024)S(1)}) fusion(f32[2048,2048]{0,1:T(8,128)S(1)} %get-tuple-element.42, f32[2048]{0:T(1024)S(1)} %get-tuple-element.41, pred[2048]{0:T(1024)(128)(4,1)S(1)} %iota_compare_fusion), kind=kLoop, calls=%fused_computation.6 | loop fusion | flops 20969472 | bytes 25184256 | tf_op jit(solution)/shard_map/convert_element_type | solution.py:32
  139.1 0.2 copy.52
  139.3 1.6 %fusion.43 = bf16[8,16,8,128]{3,2,1,0:T(8,128)(2,1)S(1)} fusion(bf16[2048,2048]{0,1:T(8,128)(2,1)S(1)} %get-tuple-element.27, bf16[8,8,16,128]{3,2,1,0:T(8,128)(2,1)S(1)} %bitcast.168, f32[2048]{0:T(1024)S(1)} %get-tuple-element.28), kind=kOutput, calls=%fused_computation.42 | convolution fusion | flops 537133056 | bytes 8921088 | tf_op jit(solution)/shard_map/qk,dk->dq/dot_general | solution.py:34
  140.9 0.8 copy.106
  141.7 3.5 %all-to-all-start.3 = ((bf16[16,64,128]{2,1,0:T(8,128)(2,1)}), bf16[16,64,128]{2,1,0:T(8,128)(2,1)S(1)}, u32[]{:S(2)}, u32[]{:S(2)}) async-start(bf16[16,64,128]{2,1,0:T(8,128)(2,1)} %bitcast.159), calls=%async_computation.3 | async-start | bytes 524288 | tf_op jit(solution)/shard_map/all_to_all | solution.py:59
  145.2 8.0 %all-to-all-done.3 = bf16[16,64,128]{2,1,0:T(8,128)(2,1)S(1)} async-done(((bf16[16,64,128]{2,1,0:T(8,128)(2,1)}), bf16[16,64,128]{2,1,0:T(8,128)(2,1)S(1)}, u32[]{:S(2)}, u32[]{:S(2)}) %all-to-all-start.3) | async-done | bytes 262176 | tf_op jit(solution)/shard_map/all_to_all | solution.py:59
  153.2 1.2 fusion.40
  (54 shorter events, 0.7 us)
Async XLA Ops:
  0.0 95.0 %copy-start = (bf16[1,1024,1024]{2,1,0:T(8,128)(2,1)S(1)}, bf16[1,1024,1024]{2,1,0:T(8,128)(2,1)}, u32[]{:S(2)}) copy-start(bf16[1,1024,1024]{2,1,0:T(8,128)(2,1)} %param.13) | copy-start | bytes 6291460
  1.2 19.1 %copy-start.6 = (bf16[512,384]{1,0:T(8,128)(2,1)}, bf16[512,384]{1,0:T(8,128)(2,1)S(1)}, u32[]{:S(2)}) copy-start(bf16[512,384]{1,0:T(8,128)(2,1)S(1)} %dynamic-slice_bitcast_fusion) | copy-start | bytes 1179652
  1.2 19.0 %collective-permute-start.1 = (bf16[512,384]{1,0:T(8,128)(2,1)S(1)}, bf16[512,384]{1,0:T(8,128)(2,1)S(1)}, u32[]{:S(2)}, u32[]{:S(2)}) collective-permute-start(bf16[512,384]{1,0:T(8,128)(2,1)S(1)} %dynamic-slice_bitcast_fusion), channel_id=1, source_target_pairs={{0,7},{1,0},{2,1},{3,2},{4,3},{5,4},{6,5},{7,6},{8,15},{9,8},{10,9... | collective-permute-start | bytes 1179656 | tf_op jit(solution)/shard_map/ppermute | solution.py:78
  7.1 11.8 %collective-permute-start.4 = (bf16[512,384]{1,0:T(8,128)(2,1)S(1)}, bf16[512,384]{1,0:T(8,128)(2,1)S(1)}, u32[]{:S(2)}, u32[]{:S(2)}) collective-permute-start(bf16[512,384]{1,0:T(8,128)(2,1)S(1)} %dynamic-slice_bitcast_fusion), channel_id=1, source_target_pairs={{0,1},{1,2},{2,3},{3,4},{4,5},{5,6},{6,7},{7,0},{8,9},{9,10},{10,1... | collective-permute-start | bytes 1179656 | tf_op jit(solution)/shard_map/ppermute | solution.py:74
  18.9 10.9 %collective-permute-start.5 = (bf16[512,384]{1,0:T(8,128)(2,1)S(1)}, bf16[512,384]{1,0:T(8,128)(2,1)S(1)}, u32[]{:S(2)}, u32[]{:S(2)}) collective-permute-start(bf16[512,384]{1,0:T(8,128)(2,1)S(1)} %collective-permute-done.4), channel_id=1, source_target_pairs={{0,1},{1,2},{2,3},{3,4},{4,5},{5,6},{6,7},{7,0},{8,9},{9,10},{10,1... | collective-permute-start | bytes 1179656 | tf_op jit(solution)/shard_map/ppermute | solution.py:74
  20.1 9.7 %collective-permute-start = (bf16[128,1024]{1,0:T(8,128)(2,1)S(1)}, bf16[128,1024]{1,0:T(8,128)(2,1)}, u32[]{:S(2)}, u32[]{:S(2)}) collective-permute-start(bf16[128,1024]{1,0:T(8,128)(2,1)S(1)} %fusion.58), channel_id=1, source_target_pairs={{0,8},{8,0},{16,24},{24,16},{32,40},{40,32},{48,56},{56,48},{64,72... | collective-permute-start | bytes 786440 | tf_op jit(solution)/shard_map/ppermute | solution.py:105
  20.3 21.1 %copy-start.3 = (bf16[512,384]{1,0:T(8,128)(2,1)}, bf16[512,384]{1,0:T(8,128)(2,1)S(1)}, u32[]{:S(2)}) copy-start(bf16[512,384]{1,0:T(8,128)(2,1)S(1)} %collective-permute-done.1) | copy-start | bytes 1179652
  20.3 12.3 %collective-permute-start.2 = (bf16[512,384]{1,0:T(8,128)(2,1)S(1)}, bf16[512,384]{1,0:T(8,128)(2,1)}, u32[]{:S(2)}, u32[]{:S(2)}) collective-permute-start(bf16[512,384]{1,0:T(8,128)(2,1)S(1)} %collective-permute-done.1), channel_id=1, source_target_pairs={{0,7},{1,0},{2,1},{3,2},{4,3},{5,4},{6,5},{7,6},{8,15},{9,8},{10,9... | collective-permute-start | bytes 1179656 | tf_op jit(solution)/shard_map/ppermute | solution.py:78
  23.6 7.6 %copy-start.12 = (bf16[1,1024,384]{2,1,0:T(8,128)(2,1)S(1)}, bf16[1,1024,384]{2,1,0:T(8,128)(2,1)}, u32[]{:S(2)}) copy-start(bf16[1,1024,384]{2,1,0:T(8,128)(2,1)} %param.12) | copy-start | bytes 2359300
  29.9 20.0 %copy-start.4 = (bf16[512,384]{1,0:T(8,128)(2,1)}, bf16[512,384]{1,0:T(8,128)(2,1)S(1)}, u32[]{:S(2)}) copy-start(bf16[512,384]{1,0:T(8,128)(2,1)S(1)} %collective-permute-done.5) | copy-start | bytes 1179652
  29.9 10.1 %collective-permute-start.6 = (bf16[512,384]{1,0:T(8,128)(2,1)S(1)}, bf16[512,384]{1,0:T(8,128)(2,1)S(1)}, u32[]{:S(2)}, u32[]{:S(2)}) collective-permute-start(bf16[512,384]{1,0:T(8,128)(2,1)S(1)} %collective-permute-done.5), channel_id=1, source_target_pairs={{0,1},{1,2},{2,3},{3,4},{4,5},{5,6},{6,7},{7,0},{8,9},{9,10},{10,1... | collective-permute-start | bytes 1179656 | tf_op jit(solution)/shard_map/ppermute | solution.py:74
  32.6 12.3 %collective-permute-start.3 = (bf16[512,384]{1,0:T(8,128)(2,1)}, bf16[512,384]{1,0:T(8,128)(2,1)S(1)}, u32[]{:S(2)}, u32[]{:S(2)}) collective-permute-start(bf16[512,384]{1,0:T(8,128)(2,1)} %collective-permute-done.2), channel_id=1, source_target_pairs={{0,7},{1,0},{2,1},{3,2},{4,3},{5,4},{6,5},{7,6},{8,15},{9,8},{10,9... | collective-permute-start | bytes 1179656 | tf_op jit(solution)/shard_map/ppermute | solution.py:78
  39.9 10.6 %copy-start.8 = (bf16[512,384]{1,0:T(8,128)(2,1)}, bf16[512,384]{1,0:T(8,128)(2,1)S(1)}, u32[]{:S(2)}) copy-start(bf16[512,384]{1,0:T(8,128)(2,1)S(1)} %collective-permute-done.6) | copy-start | bytes 1179652
  39.9 9.2 %collective-permute-start.7 = (bf16[512,384]{1,0:T(8,128)(2,1)S(1)}, bf16[512,384]{1,0:T(8,128)(2,1)S(1)}, u32[]{:S(2)}, u32[]{:S(2)}) collective-permute-start(bf16[512,384]{1,0:T(8,128)(2,1)S(1)} %collective-permute-done.6), channel_id=1, source_target_pairs={{0,1},{1,2},{2,3},{3,4},{4,5},{5,6},{6,7},{7,0},{8,9},{9,10},{10,1... | collective-permute-start | bytes 1179656 | tf_op jit(solution)/shard_map/ppermute | solution.py:74
  44.8 4.3 %copy-start.10 = (bf16[512,384]{1,0:T(8,128)(2,1)}, bf16[512,384]{1,0:T(8,128)(2,1)S(1)}, u32[]{:S(2)}) copy-start(bf16[512,384]{1,0:T(8,128)(2,1)S(1)} %collective-permute-done.3) | copy-start | bytes 1179652
  49.2 1.0 copy-start.11
  49.5 1.9 %copy-start.7 = (bf16[512,384]{1,0:T(8,128)(2,1)S(1)}, bf16[512,384]{1,0:T(8,128)(2,1)}, u32[]{:S(2)}) copy-start(bf16[512,384]{1,0:T(8,128)(2,1)} %copy-done.6) | copy-start | bytes 1179652
  50.6 3.5 %collective-permute-start.8 = (f32[128,3072]{0,1:T(8,128)S(1)}, f32[128,3072]{0,1:T(8,128)S(1)}, u32[]{:S(2)}, u32[]{:S(2)}) collective-permute-start(f32[128,3072]{0,1:T(8,128)S(1)} %slice_bitcast_fusion), channel_id=1, source_target_pairs={{0,8},{8,0},{16,24},{24,16},{32,40},{40,32},{48,56},{56,48},{64,72... | collective-permute-start | bytes 4718600 | tf_op jit(solution)/shard_map/ppermute | solution.py:123
  55.2 18.9 %all-to-all-start = ((bf16[16,3,64,128]{3,2,1,0:T(8,128)(2,1)}), bf16[16,3,64,128]{3,2,1,0:T(8,128)(2,1)S(1)}, u32[]{:S(2)}, u32[]{:S(2)}) async-start(bf16[16,3,64,128]{3,2,1,0:T(8,128)(2,1)} %copy.46), calls=%async_computation | async-start | bytes 1572864 | tf_op jit(solution)/shard_map/all_to_all | solution.py:56
  60.5 7.4 %copy-start.9 = (bf16[512,384]{1,0:T(8,128)(2,1)S(1)}, bf16[512,384]{1,0:T(8,128)(2,1)}, u32[]{:S(2)}) copy-start(bf16[512,384]{1,0:T(8,128)(2,1)} %copy-done.8) | copy-start | bytes 1179652
  60.5 8.3 %copy-start.5 = (bf16[512,384]{1,0:T(8,128)(2,1)S(1)}, bf16[512,384]{1,0:T(8,128)(2,1)}, u32[]{:S(2)}) copy-start(bf16[512,384]{1,0:T(8,128)(2,1)} %copy-done.4) | copy-start | bytes 1179652
  70.4 36.9 %collective-permute-start.10 = (bf16[512,3072]{1,0:T(8,128)(2,1)}, bf16[512,3072]{1,0:T(8,128)(2,1)}, u32[]{:S(2)}, u32[]{:S(2)}) collective-permute-start(bf16[512,3072]{1,0:T(8,128)(2,1)} %constant_dynamic-update-slice_fusion), channel_id=1, source_target_pairs={{0,8},{8,0},{16,24},{24,16},{32,40},{40,32},{48,56},{56,48},{64,72... | collective-permute-start | bytes 9437192 | tf_op jit(solution)/shard_map/ppermute | solution.py:126
  82.7 12.3 %copy-start.2 = (bf16[1,1,128,1024]{3,2,1,0:T(8,128)(2,1)S(1)}, bf16[1,1,128,1024]{3,2,1,0:T(8,128)(2,1)}, u32[]{:S(2)}) copy-start(bf16[1,1,128,1024]{3,2,1,0:T(8,128)(2,1)} %param.8) | copy-start | bytes 786436
  82.7 12.3 %copy-start.15 = (f32[1,1024]{1,0:T(1,128)S(1)}, f32[1,1024]{1,0:T(1,128)}, u32[]{:S(2)}) copy-start(f32[1,1024]{1,0:T(1,128)} %param.14) | copy-start | bytes 12292
  82.7 12.3 %copy-start.16 = (f32[1,1024]{1,0:T(1,128)S(1)}, f32[1,1024]{1,0:T(1,128)}, u32[]{:S(2)}) copy-start(f32[1,1024]{1,0:T(1,128)} %param.15) | copy-start | bytes 12292
  84.3 22.8 %copy-start.13 = (f32[1,1024]{1,0:T(1,128)S(1)}, f32[1,1024]{1,0:T(1,128)}, u32[]{:S(2)}) copy-start(f32[1,1024]{1,0:T(1,128)} %param.11) | copy-start | bytes 12292
  84.3 22.7 %copy-start.14 = (f32[1,1024]{1,0:T(1,128)S(1)}, f32[1,1024]{1,0:T(1,128)}, u32[]{:S(2)}) copy-start(f32[1,1024]{1,0:T(1,128)} %param.10) | copy-start | bytes 12292
  95.5 11.2 %collective-permute-start.9 = (bf16[128,1024]{1,0:T(8,128)(2,1)S(1)}, bf16[128,1024]{1,0:T(8,128)(2,1)S(1)}, u32[]{:S(2)}, u32[]{:S(2)}) collective-permute-start(bf16[128,1024]{1,0:T(8,128)(2,1)S(1)} %fusion.34), channel_id=1, source_target_pairs={{0,128},{1,129},{2,130},{3,131},{4,132},{5,133},{6,134},{7,135},{8... | collective-permute-start | bytes 786440 | tf_op jit(solution)/shard_map/ppermute | solution.py:135
  107.3 3.1 %copy-start.1 = (bf16[512,3072]{1,0:T(8,128)(2,1)S(1)}, bf16[512,3072]{1,0:T(8,128)(2,1)}, u32[]{:S(2)}) copy-start(bf16[512,3072]{1,0:T(8,128)(2,1)} %constant_dynamic-update-slice_fusion) | copy-start | bytes 9437188
  141.7 11.5 %all-to-all-start.3 = ((bf16[16,64,128]{2,1,0:T(8,128)(2,1)}), bf16[16,64,128]{2,1,0:T(8,128)(2,1)S(1)}, u32[]{:S(2)}, u32[]{:S(2)}) async-start(bf16[16,64,128]{2,1,0:T(8,128)(2,1)} %bitcast.159), calls=%async_computation.3 | async-start | bytes 524288 | tf_op jit(solution)/shard_map/all_to_all | solution.py:59
